TPU v7x, 512 devices: a whole 4x8x8 slice. The times are simulated.
512 devices in a mesh: grp: 32 (over x, y), tp: 16 (over z, core).
Axes of the slice: x: 4, y: 8, z: 8, core: 2. Of those that a mesh axis runs over, the one named last changes fastest.
Arguments:
- patches: bfloat16 [16384, 1664], P('grp'), may hold values from -6 to 6
- patch_image: int32 [16384], P('grp'), may hold values from 0 to 4095, as said below
- vis_gain: float32 [1664], replicated, may hold values from 0.25 to 1.75
- vis_bias: float32 [1664], replicated, may hold values from -3 to 3
- vis_qkv: bfloat16 [3, 1664, 1664], P(None, None, 'tp'), may hold values from -2 to 2
- vis_out: bfloat16 [1664, 1664], P('tp'), may hold values from -0.15625 to 0.15625
- merge_weight: bfloat16 [4, 1664, 1024], P(None, 'tp'), may hold values from -0.078125 to 0.078125
- positions: int32 [4096], P('grp'), may hold values from 0 to 12287, as said below
- text: bfloat16 [8192, 1024], P('grp'), may hold values from -6 to 6
- dec_gain: float32 [1024], replicated, may hold values from 0.25 to 1.75
- dec_bias: float32 [1024], replicated, may hold values from -3 to 3
- dec_qkv: bfloat16 [3, 1024, 1024], P(None, None, 'tp'), may hold values from -2 to 2
Outputs:
- dec_attn: bfloat16 [12288, 1024], P('grp', 'tp')
Inputs may be any that keep to these rules, and one draw needn't show every extreme that they name: `patch_image`: each aligned run of four patches belongs to one image. Groups 2j and 2j+1 are partners: the last image of group 2j continues as the first image of group 2j+1; no other image is shared between groups. All positions are distinct; each group's block of 384 positions holds exactly 128 of them; the 128 merged rows of one group put at most 8 positions into any one group's block.
All inputs are finite; a program needn't handle non-finite values.
Results may differ from a plain program's by a relative error of at most 0.025.
Values may be sent and summed in bfloat16 or wider, within the bound.
No kernel may reach another device: no remote copies, remote signals or barrier semaphores. Data moves between devices by JAX's collectives and lax.ppermute only.
A program may use at most 128 MiB of HBM per device.

v0:
```python
import jax
import jax.numpy as jnp
from jax import lax
from jax.sharding import PartitionSpec as P

HD = 104
DH = 64


layer_eps = 1e-05


def swapped(value, axis, stride):
    return lax.ppermute(value, axis, [(i, i ^ 1 << stride) for i in range(lax.axis_size(axis))])


def normalize(values, gain, bias):
    mean = jnp.mean(values, axis=-1, keepdims=True)
    centred = values - mean
    spread = jnp.mean(centred * centred, axis=-1, keepdims=True)
    return centred * lax.rsqrt(spread + layer_eps) * gain + bias


def body(
    patches,
    patch_image,
    vis_gain,
    vis_bias,
    vis_qkv,
    vis_out,
    merge_weight,
    positions,
    text,
    dec_gain,
    dec_bias,
    dec_qkv,
):
    rows = patches.shape[0]
    heads = vis_qkv.shape[2] // HD
    patches_f = patches.astype(jnp.float32)
    normed = normalize(patches_f, vis_gain, vis_bias).astype(jnp.bfloat16)
    proj = jnp.einsum("pd,sde->spe", normed, vis_qkv, preferred_element_type=jnp.float32).astype(
        jnp.bfloat16
    )
    query = proj[0].reshape(rows, heads, HD)
    partner_kv, partner_ids = swapped((proj[1:], patch_image), "grp", 0)
    both_kv = jnp.concatenate([proj[1:], partner_kv], axis=1)
    both_ids = jnp.concatenate([patch_image, partner_ids], axis=0)
    keys = both_kv[0].reshape(2 * rows, heads, HD)
    values = both_kv[1].reshape(2 * rows, heads, HD)
    scores = jnp.einsum("phe,khe->hpk", query, keys, preferred_element_type=jnp.float32) * HD ** (
        -0.5
    )
    same = patch_image[:, None] == both_ids[None, :]
    top = jnp.max(jnp.where(same, scores, -1e30), axis=2, keepdims=True)
    expo = jnp.where(same, jnp.exp(scores - top), 0.0)
    weights = (expo / jnp.sum(expo, axis=2, keepdims=True)).astype(jnp.bfloat16)
    attended = jnp.einsum(
        "hpk,khe->phe", weights, values, preferred_element_type=jnp.float32
    ).astype(jnp.bfloat16)
    attended = attended.reshape(rows, heads * HD)
    width = patches.shape[1] // lax.axis_size("tp")
    mixed = lax.psum_scatter(
        lax.dot_general(
            vis_out, attended, (((0,), (1,)), ((), ())), preferred_element_type=jnp.float32
        ).astype(jnp.bfloat16),
        "tp",
        scatter_dimension=0,
        tiled=True,
    ).astype(jnp.float32)
    own_cols = lax.dynamic_slice_in_dim(patches_f, lax.axis_index("tp") * width, width, 1)
    visual = (mixed + own_cols.T).astype(jnp.bfloat16)
    windows = visual.reshape(width, rows // 4, 4)
    partial_rows = jnp.einsum(
        "cmk,kce->me", windows, merge_weight, preferred_element_type=jnp.float32
    )
    groups = lax.axis_size("grp")
    here = lax.axis_index("grp")
    merged_count = rows // 4
    text_count = text.shape[0]
    tok = text_count + merged_count
    cap = merged_count // min(groups, 16)
    target = positions // tok
    member = (target[:, None] == jnp.arange(groups, dtype=jnp.int32)[None, :]).astype(jnp.int32)
    rank = jnp.sum(jnp.cumsum(member, axis=0) * member, axis=1) - 1
    slot = target * cap + rank
    select = slot[None, :] == jnp.arange(groups * cap, dtype=jnp.int32)[:, None]
    select_bf = select.astype(jnp.bfloat16)
    bucket_pos = jnp.sum(jnp.where(select, positions[None, :] + 1, 0), axis=1) - 1
    merged = lax.psum(partial_rows.astype(jnp.bfloat16), "tp")
    packed = jnp.dot(select_bf, merged, preferred_element_type=jnp.float32).astype(jnp.bfloat16)
    got_rows, got_pos = (
        lax.all_to_all(packed, "grp", split_axis=0, concat_axis=0, tiled=True),
        lax.all_to_all(bucket_pos, "grp", split_axis=0, concat_axis=0, tiled=True),
    )
    local_pos = got_pos - here * tok
    place = jnp.arange(tok, dtype=jnp.int32)
    landing = (local_pos[None, :] == place[:, None]) & (got_pos[None, :] >= 0)
    image_here = jnp.any(landing, axis=1).astype(jnp.int32)
    text_index = place - (jnp.cumsum(image_here) - image_here)
    text_pick = (image_here[:, None] == 0) & (
        text_index[:, None] == jnp.arange(text_count, dtype=jnp.int32)[None, :]
    )
    prompt = jnp.dot(landing.astype(jnp.bfloat16), got_rows, preferred_element_type=jnp.float32)
    prompt = prompt + jnp.dot(
        text_pick.astype(jnp.bfloat16), text, preferred_element_type=jnp.float32
    )
    dnorm = normalize(prompt, dec_gain, dec_bias).astype(jnp.bfloat16)
    dproj = jnp.einsum("td,sde->ste", dnorm, dec_qkv, preferred_element_type=jnp.float32).astype(
        jnp.bfloat16
    )
    dheads = dec_qkv.shape[2] // DH
    dquery = dproj[0].reshape(tok, dheads, DH)
    query_pos = here * tok + place
    best = jnp.full((dheads, tok), -1e30, jnp.float32)
    key_rows = lax.all_gather(dproj[1], "grp", axis=0, tiled=True).reshape(-1, dheads, DH)
    value_rows = lax.all_gather(dproj[2], "grp", axis=0, tiled=True).reshape(-1, dheads, DH)
    key_pos = jnp.arange(key_rows.shape[0], dtype=jnp.int32)
    score = jnp.einsum(
        "the,rhe->htr", dquery, key_rows, preferred_element_type=jnp.float32
    ) * DH ** (-0.5)
    allowed = key_pos[None, :] <= query_pos[:, None]
    new_best = jnp.maximum(best, jnp.max(jnp.where(allowed[None], score, -1e30), axis=2))
    expo_d = jnp.where(allowed[None], jnp.exp(score - new_best[:, :, None]), 0.0)
    total = jnp.sum(expo_d, axis=2)
    acc = jnp.einsum(
        "htr,rhe->hte", expo_d.astype(jnp.bfloat16), value_rows, preferred_element_type=jnp.float32
    )
    best, total, acc = (new_best, total, acc)
    result = acc / total[:, :, None]
    return result.transpose(1, 0, 2).reshape(tok, dheads * DH).astype(jnp.bfloat16)


def solution(mesh):
    in_specs = (
        P("grp", None),
        P("grp"),
        P(),
        P(),
        P(None, None, "tp"),
        P("tp", None),
        P(None, "tp", None),
        P("grp"),
        P("grp", None),
        P(),
        P(),
        P(None, None, "tp"),
    )
    out_specs = P("grp", "tp")
    return jax.shard_map(body, mesh=mesh, in_specs=in_specs, out_specs=out_specs, check_vma=False)
```

profile of v0, /device:TPU:6, one launch (start us, length us, event | category | flops | bytes accessed | tf_op | source)
XLA Modules:
  0.0 415.6 jit_solution(2915710087922539153)
XLA Ops:
  6.6 1.9 convert_reduce_fusion
  8.5 0.1 copy-done.1
  8.6 0.6 multiply_reduce_fusion
  9.2 1.0 fusion.6
  10.3 3.5 collective-permute-start
  13.8 2.4 collective-permute-start.1
  16.2 3.1 collective-permute-done.1
  19.3 0.6 fusion.5
  19.9 1.4 copy-done.2
  21.3 0.7 fusion.13
  22.0 4.3 %fusion.4 = bf16[1664,512]{0,1:T(8,128)(2,1)} fusion(bf16[104,1664]{1,0:T(8,128)(2,1)S(1)} %copy-done.6, f32[512,1024]{1,0:T(8,128)} %copy-done.2, f32[512]{0:T(512)S(1)} %fusion.13, f32[512]{0:T(512)S(1)} %get-tuple-element.11, s32[1024]{0:T(1024)S(1)} %pad_add_fusion, s32[512]{0:T(512)S(1)} %copy-done.4, bf16[2,512,104]{1,2,0:T(8,128)(2,1)S(1)} %slice.38, ...), kind=kOutput, calls=%fused_computation.10 | convolution fusion | flops 290738176 | bytes 4583424 | tf_op jit(solution)/shard_map/dot_general | solution.py:64
  26.2 3.6 copy.17
  30.0 2.0 convert_element_type.82
  31.9 0.1 fusion.64
  32.0 0.2 reduce_window_sum.30
  32.2 0.2 select_reduce_fusion.2
  32.4 0.1 select_reduce_fusion.1
  32.5 63.8 %reduce-scatter.4.cloned.1.call-done = bf16[104,512]{1,0:T(8,128)(2,1)} async-done(((bf16[1664,512]{1,0:T(8,128)(2,1)}), bf16[104,512]{1,0:T(8,128)(2,1)}) %reduce-scatter.4.cloned.1.call-update) | async-done | bytes 106512
  96.3 1.0 copy.18
  97.4 1.2 fusion.49
  98.5 2.2 fusion.15
  100.8 0.7 sub.80
  101.5 10.1 %all-to-all-start = ((s32[32,8,1]{1,2,0:T(1,128)}), s32[32,8,1]{1,2,0:T(1,128)S(1)}, u32[]{:S(2)}, u32[]{:S(2)}) async-start(s32[32,8,1]{1,2,0:T(1,128)} %bitcast), calls=%async_computation | async-start | bytes 32768 | tf_op jit(solution)/shard_map/all_to_all | solution.py:94
  111.6 101.9 %all-reduce.2.cloned.1.call-done = bf16[128,1024]{1,0:T(8,128)(2,1)} async-done(((bf16[128,1024]{1,0:T(8,128)(2,1)}), bf16[128,1024]{1,0:T(8,128)(2,1)}) %all-reduce.2.cloned.1.call-update) | async-done | bytes 262160 | tf_op jit(solution)/shard_map/psum | solution.py:90
  213.5 2.0 fusion.14
  215.5 9.9 %all-to-all-start.1 = ((bf16[32,8,1024]{2,1,0:T(8,128)(2,1)}), bf16[32,8,1024]{2,1,0:T(8,128)(2,1)S(1)}, u32[]{:S(2)}, u32[]{:S(2)}) async-start(bf16[32,8,1024]{2,1,0:T(8,128)(2,1)} %fusion.14), calls=%async_computation.1 | async-start | bytes 1048576 | tf_op jit(solution)/shard_map/all_to_all | solution.py:93
  225.5 0.1 sub.83
  225.6 0.1 compare_reduce_fusion
  225.7 0.1 ge.16
  225.8 0.2 fusion.45
  226.0 0.3 reduce-window.9
  226.3 0.1 slice.33
  226.4 0.1 slice_reduce_fusion
  226.5 0.1 fusion.65
  226.6 14.0 %all-to-all-done.1 = bf16[32,8,1024]{2,1,0:T(8,128)(2,1)S(1)} async-done(((bf16[32,8,1024]{2,1,0:T(8,128)(2,1)}), bf16[32,8,1024]{2,1,0:T(8,128)(2,1)S(1)}, u32[]{:S(2)}, u32[]{:S(2)}) %all-to-all-start.1) | async-done | bytes 524320 | tf_op jit(solution)/shard_map/all_to_all | solution.py:93
  240.6 0.4 fusion.42
  241.1 0.5 fusion.75
  241.6 0.3 multiply_reduce_fusion.1
  241.9 0.1 copy-done.5
  242.0 0.6 fusion.37
  242.6 0.6 fusion.74
  243.3 0.2 all-gather.7.cloned.1.call-start
  243.5 0.3 all-gather.7.cloned.1.call-update
  243.9 73.6 %all-gather.5.cloned.1.call-done = bf16[1,12288,64]{1,2,0:T(8,128)(2,1)} async-done(((bf16[1,384,64]{1,2,0:T(8,128)(2,1)}), bf16[1,12288,64]{1,2,0:T(8,128)(2,1)}) %all-gather.5.cloned.1.call-update) | async-done | bytes 1572880 | tf_op jit(solution)/shard_map/all_gather | solution.py:116
  317.4 9.3 %select_reduce_fusion = (f32[384]{0:T(512)S(1)}, f32[384,12288]{1,0:T(8,128)}) fusion(s32[384]{0:T(512)S(1)} %iota_add_fusion, bf16[1,12288,64]{1,2,0:T(8,128)(2,1)} %all-gather.5.cloned.1.call-done, bf16[3,384,64]{1,2,0:T(8,128)(2,1)S(1)} %convert_bitcast_fusion.1), kind=kOutput, calls=%fused_computation.1 | convolution fusion | flops 622853760 | bytes 20499968 | tf_op jit(solution)/shard_map/the,rhe->htr/dot_general | solution.py:119
  326.7 11.1 %fusion = f32[384]{0:T(512)S(1)} fusion(f32[384,12288]{1,0:T(8,128)} %get-tuple-element.16, f32[384]{0:T(512)S(1)} %broadcast_maximum_fusion, s32[384]{0:T(512)S(1)} %iota_add_fusion), kind=kLoop, calls=%fused_computation.4 | loop fusion | flops 18873984 | bytes 18878976 | tf_op jit(solution)/shard_map/reduce_sum | solution.py:125
  337.8 60.2 %all-gather.7.cloned.1.call-done = bf16[1,12288,64]{1,2,0:T(8,128)(2,1)} async-done(((bf16[1,384,64]{1,2,0:T(8,128)(2,1)}), bf16[1,12288,64]{1,2,0:T(8,128)(2,1)}) %all-gather.7.cloned.1.call-update) | async-done | bytes 1572880 | tf_op jit(solution)/shard_map/all_gather | solution.py:117
  398.0 11.1 %fusion.22 = bf16[384,64]{0,1:T(8,128)(2,1)} fusion(bf16[1,12288,64]{1,2,0:T(8,128)(2,1)} %all-gather.7.cloned.1.call-done, f32[384,12288]{1,0:T(8,128)} %get-tuple-element.16, f32[384]{0:T(512)S(1)} %broadcast_maximum_fusion, s32[384]{0:T(512)S(1)} %iota_add_fusion, f32[384]{0:T(512)S(1)} %fusion), kind=kOutput, calls=%fused_computation.34 | convolution fusion | flops 622903296 | bytes 20500992 | tf_op jit(solution)/shard_map/htr,rhe->hte/dot_general | solution.py:126
  (45 shorter events, 0.5 us)
Async XLA Ops:
  6.5 2.6 copy-start
  6.5 2.1 copy-start.1
  6.5 2.7 copy-start.8
  6.5 2.7 copy-start.7
  6.5 89.8 %reduce-scatter.4.cloned.1.call-start = ((), (), s32[]{:S(2)}) async-start(), calls=%async_computation.6 | async-start | bytes 1810432
  9.2 4.6 %copy-start.4 = (s32[512]{0:T(512)S(1)}, s32[512]{0:T(512)}, u32[]{:S(2)}) copy-start(s32[512]{0:T(512)} %param.13) | copy-start | bytes 6148
  10.3 9.0 %collective-permute-start = (bf16[2,512,104]{1,2,0:T(8,128)(2,1)S(1)}, bf16[2,512,104]{1,2,0:T(8,128)(2,1)S(1)}, u32[]{:S(2)}, u32[]{:S(2)}) collective-permute-start(bf16[2,512,104]{1,2,0:T(8,128)(2,1)S(1)} %slice.38), channel_id=1, source_target_pairs={{0,16},{16,0},{32,48},{48,32},{64,80},{80,64},{96,112},{112,96},{1... | collective-permute-start | bytes 638984 | tf_op jit(solution)/shard_map/ppermute | solution.py:14
  13.8 5.5 %collective-permute-start.1 = (s32[512]{0:T(512)S(1)}, s32[512]{0:T(512)S(1)}, u32[]{:S(2)}, u32[]{:S(2)}) collective-permute-start(s32[512]{0:T(512)S(1)} %copy-done.4), channel_id=1, source_target_pairs={{0,16},{16,0},{32,48},{48,32},{64,80},{80,64},{96,112},{112,96},{1... | collective-permute-start | bytes 6152 | tf_op jit(solution)/shard_map/ppermute | solution.py:14
  19.3 2.6 copy-start.6
  19.9 1.4 copy-start.2
  29.9 183.6 %all-reduce.2.cloned.1.call-start = ((), (), s32[]{:S(2)}) async-start(), calls=%async_computation.3 | async-start | bytes 524288 | tf_op jit(solution)/shard_map/psum | solution.py:90
  29.9 2.0 copy-start.11
  100.8 140.2 %copy-start.3 = (bf16[256,1024]{1,0:T(8,128)(2,1)S(1)}, bf16[256,1024]{1,0:T(8,128)(2,1)}, u32[]{:S(2)}) copy-start(bf16[256,1024]{1,0:T(8,128)(2,1)} %param.20) | copy-start | bytes 1572868
  101.5 114.0 %all-to-all-start = ((s32[32,8,1]{1,2,0:T(1,128)}), s32[32,8,1]{1,2,0:T(1,128)S(1)}, u32[]{:S(2)}, u32[]{:S(2)}) async-start(s32[32,8,1]{1,2,0:T(1,128)} %bitcast), calls=%async_computation | async-start | bytes 32768 | tf_op jit(solution)/shard_map/all_to_all | solution.py:94
  215.5 25.1 %all-to-all-start.1 = ((bf16[32,8,1024]{2,1,0:T(8,128)(2,1)}), bf16[32,8,1024]{2,1,0:T(8,128)(2,1)S(1)}, u32[]{:S(2)}, u32[]{:S(2)}) async-start(bf16[32,8,1024]{2,1,0:T(8,128)(2,1)} %fusion.14), calls=%async_computation.1 | async-start | bytes 1048576 | tf_op jit(solution)/shard_map/all_to_all | solution.py:93
  225.4 92.0 %all-gather.5.cloned.1.call-start = ((), (), s32[]{:S(2)}) async-start(), calls=%async_computation.4 | async-start | bytes 1622016 | tf_op jit(solution)/shard_map/all_gather | solution.py:116
  241.0 1.0 copy-start.5
  241.0 1.0 copy-start.9
  241.0 1.0 copy-start.10
  243.3 154.7 %all-gather.7.cloned.1.call-start = ((), (), s32[]{:S(2)}) async-start(), calls=%async_computation.5 | async-start | bytes 1622016 | tf_op jit(solution)/shard_map/all_gather | solution.py:117
Sparse Core Ops, SparseCore 0:
  30.0 66.2 reduce-scatter.3
  100.9 112.5 all-reduce.1
  243.4 73.9 all-gather.4
  320.4 77.5 all-gather.6
where the time goes:
time: 416 us
  waiting for transfers between devices  317 us (76%)
  matrix products  32 us (8%)
  starting transfers between devices  26.2 us (6%)
  other arithmetic  19 us (5%)
  between operations  13.4 us (3%)
  local copies, waits for them, and re-layouts  8.01 us (2%)
    psum x1, waiting for transfers between devices, body(): merged = lax.psum(partial_rows.astype(jnp.bfloat16), 'tp')  102 us
    all_gather x1, waiting for transfers between devices, body(): lax.all_gather(dproj[1], 'grp', axis=0, tiled=True).reshape(-1, dheads, DH)  73.6 us
    unnamed x5, waiting for transfers between devices  64.2 us
    all_gather x1, waiting for transfers between devices, body(): lax.all_gather(dproj[2], 'grp', axis=0, tiled=True).reshape(-1, dheads, DH)  60.2 us
    all_to_all x1, waiting for transfers between devices, body(): lax.all_to_all(packed, 'grp', split_axis=0, concat_axis=0, tiled=True)  14 us
    dot_general x1, matrix products, body(): jnp.einsum('htr,rhe->hte', expo_d.astype(jnp.bfloat16), value_rows, prefe...  11.1 us
    reduce_sum x1, other arithmetic, body(): total = jnp.sum(expo_d, axis=2)  11.1 us
    all_to_all x1, starting transfers between devices, body(): lax.all_to_all(bucket_pos, 'grp', split_axis=0, concat_axis=0, tiled=True)  10.1 us
  transfers between devices with their start and end apart: 8, of which 6 were waited for; matrix products, arithmetic and copies ran while one was open for 6% of the time, Pallas kernels for 0%

commit v1 on v0

--- a/solution.py
+++ b/solution.py
@@ -12,6 +12,20 @@
 
 def swapped(value, axis, stride):
     return lax.ppermute(value, axis, [(i, i ^ 1 << stride) for i in range(lax.axis_size(axis))])
+
+
+def a2a_gather(value, axis):
+    n = lax.axis_size(axis)
+    spread = jnp.broadcast_to(value[None], (n,) + value.shape)
+    got = lax.all_to_all(spread, axis, 0, 0, tiled=True)
+    return got.reshape((n * value.shape[0],) + value.shape[1:])
+
+
+def a2a_reduce_scatter(value, axis):
+    n = lax.axis_size(axis)
+    parts = value.reshape((n, value.shape[0] // n) + value.shape[1:])
+    got = lax.all_to_all(parts, axis, 0, 0, tiled=True)
+    return jnp.sum(got.astype(jnp.float32), axis=0)
 
 
 def normalize(values, gain, bias):
@@ -60,14 +74,12 @@
     ).astype(jnp.bfloat16)
     attended = attended.reshape(rows, heads * HD)
     width = patches.shape[1] // lax.axis_size("tp")
-    mixed = lax.psum_scatter(
+    mixed = a2a_reduce_scatter(
         lax.dot_general(
             vis_out, attended, (((0,), (1,)), ((), ())), preferred_element_type=jnp.float32
         ).astype(jnp.bfloat16),
         "tp",
-        scatter_dimension=0,
-        tiled=True,
-    ).astype(jnp.float32)
+    )
     own_cols = lax.dynamic_slice_in_dim(patches_f, lax.axis_index("tp") * width, width, 1)
     visual = (mixed + own_cols.T).astype(jnp.bfloat16)
     windows = visual.reshape(width, rows // 4, 4)
@@ -87,7 +99,9 @@
     select = slot[None, :] == jnp.arange(groups * cap, dtype=jnp.int32)[:, None]
     select_bf = select.astype(jnp.bfloat16)
     bucket_pos = jnp.sum(jnp.where(select, positions[None, :] + 1, 0), axis=1) - 1
-    merged = lax.psum(partial_rows.astype(jnp.bfloat16), "tp")
+    merged = a2a_gather(
+        a2a_reduce_scatter(partial_rows.astype(jnp.bfloat16), "tp").astype(jnp.bfloat16), "tp"
+    )
     packed = jnp.dot(select_bf, merged, preferred_element_type=jnp.float32).astype(jnp.bfloat16)
     got_rows, got_pos = (
         lax.all_to_all(packed, "grp", split_axis=0, concat_axis=0, tiled=True),
@@ -113,8 +127,9 @@
     dquery = dproj[0].reshape(tok, dheads, DH)
     query_pos = here * tok + place
     best = jnp.full((dheads, tok), -1e30, jnp.float32)
-    key_rows = lax.all_gather(dproj[1], "grp", axis=0, tiled=True).reshape(-1, dheads, DH)
-    value_rows = lax.all_gather(dproj[2], "grp", axis=0, tiled=True).reshape(-1, dheads, DH)
+    kv_rows = a2a_gather(jnp.swapaxes(dproj[1:], 0, 1), "grp")
+    key_rows = kv_rows[:, 0].reshape(-1, dheads, DH)
+    value_rows = kv_rows[:, 1].reshape(-1, dheads, DH)
     key_pos = jnp.arange(key_rows.shape[0], dtype=jnp.int32)
     score = jnp.einsum(
         "the,rhe->htr", dquery, key_rows, preferred_element_type=jnp.float32

time: 416 us -> 268 us (0.64)
  waiting for transfers between devices: 317 us -> 155 us
  starting transfers between devices: 26.2 us -> 48.1 us
  between operations: 13.4 us -> 0.36 us
  local copies, waits for them, and re-layouts: 8.01 us -> 14.6 us
    all_gather x2 -> x0, waiting for transfers between devices: 134 us -> none  [the longest x1 73.6 us: body(): lax.all_gather(dproj[1], 'grp', axis=0, tiled=True).reshape(-1, dheads, DH)]
    all_to_all x0 -> x4, waiting for transfers between devices: none -> 132 us  [the longest x2 82.6 us: a2a_gather(): got = lax.all_to_all(spread, axis, 0, 0, tiled=True)]
    psum x1 -> x0, waiting for transfers between devices: 102 us -> none  [body(): merged = lax.psum(partial_rows.astype(jnp.bfloat16), 'tp')]
    unnamed x5 -> x0, waiting for transfers between devices: 64.2 us -> none
    all_to_all x0 -> x4, starting transfers between devices: none -> 26.3 us  [the longest x2 15.3 us: a2a_reduce_scatter(): got = lax.all_to_all(parts, axis, 0, 0, tiled=True)]
    all_to_all x1, waiting for transfers between devices: 0.01 us -> 6.75 us  [body(): lax.all_to_all(bucket_pos, 'grp', split_axis=0, concat_axis=0, tiled=True)]
  transfers between devices with their start and end apart: 8 -> 8, of which waited for: 6 -> 7; matrix products, arithmetic and copies ran while one was open for 6% -> 2% of each run, Pallas kernels for 0% -> 0%
where the time goes in v1:
time: 268 us; the launch traced here: 266 us
  waiting for transfers between devices  155 us (58%)
  starting transfers between devices  48.1 us (18%)
  matrix products  28.8 us (11%)
  other arithmetic  19.2 us (7%)
  local copies, waits for them, and re-layouts  14.6 us (5%)
    all_to_all x2, waiting for transfers between devices, a2a_gather(): got = lax.all_to_all(spread, axis, 0, 0, tiled=True)  82.6 us
    all_to_all x2, waiting for transfers between devices, a2a_reduce_scatter(): got = lax.all_to_all(parts, axis, 0, 0, tiled=True)  49.2 us
    all_to_all x2, starting transfers between devices, a2a_reduce_scatter(): got = lax.all_to_all(parts, axis, 0, 0, tiled=True)  15.3 us
    all_to_all x1, waiting for transfers between devices, body(): lax.all_to_all(packed, 'grp', split_axis=0, concat_axis=0, tiled=True)  13.7 us
    dot_general x1, matrix products, body(): jnp.einsum('htr,rhe->hte', expo_d.astype(jnp.bfloat16), value_rows, prefe...  11.1 us
    reduce_sum x1, other arithmetic, body(): total = jnp.sum(expo_d, axis=2)  11.1 us
    all_to_all x2, starting transfers between devices, a2a_gather(): got = lax.all_to_all(spread, axis, 0, 0, tiled=True)  11 us
    all_to_all x1, starting transfers between devices, body(): lax.all_to_all(bucket_pos, 'grp', split_axis=0, concat_axis=0, tiled=True)  10.2 us
  transfers between devices with their start and end apart: 8, of which 7 were waited for; matrix products, arithmetic and copies ran while one was open for 2% of the time, Pallas kernels for 0%

profile of v1, /device:TPU:6, one launch (start us, length us, event | category | flops | bytes accessed | tf_op | source)
XLA Modules:
  0.0 266.3 jit_solution(7555404254238633154)
XLA Ops:
  0.0 2.9 %copy.31 = bf16[512,1664]{0,1:T(8,128)(2,1)S(1)} copy(bf16[512,1664]{1,0:T(8,128)(2,1)} %param.12) | data formatting | bytes 3407872 | tf_op args[0]
  3.0 0.3 convert_reduce_fusion.1
  3.3 0.5 multiply_reduce_fusion
  3.8 1.0 fusion.6
  4.8 3.5 %collective-permute-start = (bf16[2,512,104]{1,2,0:T(8,128)(2,1)S(1)}, bf16[2,512,104]{1,2,0:T(8,128)(2,1)S(1)}, u32[]{:S(2)}, u32[]{:S(2)}) collective-permute-start(bf16[2,512,104]{1,2,0:T(8,128)(2,1)S(1)} %slice.42), channel_id=1, source_target_pairs={{0,16},{16,0},{32,48},{48,32},{64,80},{80,64},{96,112},{112,96},{1... | collective-permute-start | bytes 638984 | tf_op jit(solution)/shard_map/ppermute | solution.py:14
  8.3 2.4 collective-permute-start.1
  10.7 3.1 %collective-permute-done.1 = s32[512]{0:T(512)S(1)} collective-permute-done((s32[512]{0:T(512)S(1)}, s32[512]{0:T(512)S(1)}, u32[]{:S(2)}, u32[]{:S(2)}) %collective-permute-start.1) | collective-permute-done | bytes 2080 | tf_op jit(solution)/shard_map/ppermute | solution.py:14
  13.8 0.6 fusion.5
  14.4 1.4 copy-done.2
  15.8 0.7 fusion.11
  16.5 4.3 %fusion.4 = bf16[1664,512]{0,1:T(8,128)(2,1)} fusion(bf16[104,1664]{1,0:T(8,128)(2,1)S(1)} %copy-done.7, f32[512,1024]{1,0:T(8,128)} %copy-done.2, f32[512]{0:T(512)S(1)} %fusion.11, f32[512]{0:T(512)S(1)} %get-tuple-element.9, s32[1024]{0:T(1024)S(1)} %pad_add_fusion, s32[512]{0:T(512)S(1)} %copy-done.5, bf16[2,512,104]{1,2,0:T(8,128)(2,1)S(1)} %slice.42, ...), kind=kOutput, calls=%fused_computation.11 | convolution fusion | flops 290738176 | bytes 4583424 | tf_op jit(solution)/shard_map/dot_general | solution.py:78
  20.8 3.6 %copy.33 = bf16[1664,512]{1,0:T(8,128)(2,1)} copy(bf16[1664,512]{0,1:T(8,128)(2,1)} %fusion.4) | data formatting | bytes 3407872 | tf_op jit(solution)/shard_map/convert_element_type | solution.py:80
  24.4 10.5 %all-to-all-start.1 = ((bf16[16,104,512]{2,1,0:T(8,128)(2,1)}), bf16[16,104,512]{2,1,0:T(8,128)(2,1)}, u32[]{:S(2)}, u32[]{:S(2)}) async-start(bf16[16,104,512]{2,1,0:T(8,128)(2,1)} %bitcast.92), calls=%async_computation.1 | async-start | bytes 3407872 | tf_op jit(solution)/shard_map/all_to_all | solution.py:27
  34.9 2.2 convert_element_type.84
  37.1 38.5 %all-to-all-done.1 = bf16[16,104,512]{2,1,0:T(8,128)(2,1)} async-done(((bf16[16,104,512]{2,1,0:T(8,128)(2,1)}), bf16[16,104,512]{2,1,0:T(8,128)(2,1)}, u32[]{:S(2)}, u32[]{:S(2)}) %all-to-all-start.1) | async-done | bytes 1703968 | tf_op jit(solution)/shard_map/all_to_all | solution.py:27
  75.6 1.7 convert_reduce_fusion
  77.3 1.0 fusion.53
  78.3 0.1 copy.34
  78.4 1.0 fusion.14
  79.5 4.8 %all-to-all-start.2 = ((bf16[16,8,1024]{2,1,0:T(8,128)(2,1)}), bf16[16,8,1024]{2,1,0:T(8,128)(2,1)S(1)}, u32[]{:S(2)}, u32[]{:S(2)}) async-start(bf16[16,8,1024]{2,1,0:T(8,128)(2,1)} %fusion.14), calls=%async_computation.2 | async-start | bytes 524288 | tf_op jit(solution)/shard_map/all_to_all | solution.py:27
  84.4 0.2 reduce_window_sum.30
  84.6 0.2 select_reduce_fusion.2
  84.8 10.7 %all-to-all-done.2 = bf16[16,8,1024]{2,1,0:T(8,128)(2,1)S(1)} async-done(((bf16[16,8,1024]{2,1,0:T(8,128)(2,1)}), bf16[16,8,1024]{2,1,0:T(8,128)(2,1)S(1)}, u32[]{:S(2)}, u32[]{:S(2)}) %all-to-all-start.2) | async-done | bytes 262176 | tf_op jit(solution)/shard_map/all_to_all | solution.py:27
  95.5 0.7 broadcast_in_dim.38
  96.2 3.5 %all-to-all-start.3 = ((bf16[16,8,1024]{2,1,0:T(8,128)(2,1)}), bf16[16,8,1024]{2,1,0:T(8,128)(2,1)S(1)}, u32[]{:S(2)}, u32[]{:S(2)}) async-start(bf16[16,8,1024]{2,1,0:T(8,128)(2,1)} %broadcast_in_dim.38), calls=%async_computation.3 | async-start | bytes 524288 | tf_op jit(solution)/shard_map/all_to_all | solution.py:20
  99.8 0.1 select_reduce_fusion.1
  99.9 0.7 sub.80
  100.6 10.5 %all-to-all-done.3 = bf16[16,8,1024]{2,1,0:T(8,128)(2,1)S(1)} async-done(((bf16[16,8,1024]{2,1,0:T(8,128)(2,1)}), bf16[16,8,1024]{2,1,0:T(8,128)(2,1)S(1)}, u32[]{:S(2)}, u32[]{:S(2)}) %all-to-all-start.3) | async-done | bytes 262176 | tf_op jit(solution)/shard_map/all_to_all | solution.py:20
  111.1 10.2 %all-to-all-start = ((s32[32,8,1]{1,2,0:T(1,128)}), s32[32,8,1]{1,2,0:T(1,128)S(1)}, u32[]{:S(2)}, u32[]{:S(2)}) async-start(s32[32,8,1]{1,2,0:T(1,128)} %bitcast), calls=%async_computation | async-start | bytes 32768 | tf_op jit(solution)/shard_map/all_to_all | solution.py:108
  121.3 1.1 fusion.12
  122.4 6.8 %all-to-all-done = s32[32,8,1]{1,2,0:T(1,128)S(1)} async-done(((s32[32,8,1]{1,2,0:T(1,128)}), s32[32,8,1]{1,2,0:T(1,128)S(1)}, u32[]{:S(2)}, u32[]{:S(2)}) %all-to-all-start) | async-done | bytes 1056 | tf_op jit(solution)/shard_map/all_to_all | solution.py:108
  129.1 5.8 %all-to-all-start.4 = ((bf16[32,8,1024]{2,1,0:T(8,128)(2,1)}), bf16[32,8,1024]{2,1,0:T(8,128)(2,1)S(1)}, u32[]{:S(2)}, u32[]{:S(2)}) async-start(bf16[32,8,1024]{2,1,0:T(8,128)(2,1)} %fusion.12), calls=%async_computation.4 | async-start | bytes 1048576 | tf_op jit(solution)/shard_map/all_to_all | solution.py:107
  135.2 0.2 fusion.40
  135.4 0.3 reduce-window.9
  135.8 0.1 slice_reduce_fusion
  136.0 13.7 %all-to-all-done.4 = bf16[32,8,1024]{2,1,0:T(8,128)(2,1)S(1)} async-done(((bf16[32,8,1024]{2,1,0:T(8,128)(2,1)}), bf16[32,8,1024]{2,1,0:T(8,128)(2,1)S(1)}, u32[]{:S(2)}, u32[]{:S(2)}) %all-to-all-start.4) | async-done | bytes 524320 | tf_op jit(solution)/shard_map/all_to_all | solution.py:107
  149.7 0.4 fusion.37
  150.1 0.5 fusion.70
  150.6 0.3 multiply_reduce_fusion.1
  150.9 0.1 copy-done.6
  151.1 0.5 fusion.32
  151.7 2.2 broadcast_in_dim.39
  153.9 7.4 %all-to-all-start.5 = ((bf16[32,384,2,64]{1,3,2,0:T(8,128)(2,1)}), bf16[32,384,2,64]{1,3,2,0:T(8,128)(2,1)}, u32[]{:S(2)}, u32[]{:S(2)}) async-start(bf16[32,384,2,64]{1,3,2,0:T(8,128)(2,1)} %broadcast_in_dim.39), calls=%async_computation.5 | async-start | bytes 6291456 | tf_op jit(solution)/shard_map/all_to_all | solution.py:20
  161.3 72.2 %all-to-all-done.5 = bf16[32,384,2,64]{1,3,2,0:T(8,128)(2,1)} async-done(((bf16[32,384,2,64]{1,3,2,0:T(8,128)(2,1)}), bf16[32,384,2,64]{1,3,2,0:T(8,128)(2,1)}, u32[]{:S(2)}, u32[]{:S(2)}) %all-to-all-start.5) | async-done | bytes 3145760 | tf_op jit(solution)/shard_map/all_to_all | solution.py:20
  233.5 2.4 copy.38
  235.9 8.3 %select_reduce_fusion = (f32[384]{0:T(512)S(1)}, f32[384,12288]{1,0:T(8,128)}) fusion(s32[384]{0:T(512)S(1)} %iota_add_fusion, bf16[12288,2,64]{0,2,1:T(8,128)(2,1)S(1)} %bitcast.90, bf16[3,384,64]{1,2,0:T(8,128)(2,1)S(1)} %convert_bitcast_fusion.1), kind=kOutput, calls=%fused_computation.1 | convolution fusion | flops 622853760 | bytes 20499968 | tf_op jit(solution)/shard_map/the,rhe->htr/dot_general | solution.py:134
  244.2 11.1 %fusion = f32[384]{0:T(512)S(1)} fusion(f32[384,12288]{1,0:T(8,128)} %get-tuple-element.14, f32[384]{0:T(512)S(1)} %broadcast_maximum_fusion, s32[384]{0:T(512)S(1)} %iota_add_fusion), kind=kLoop, calls=%fused_computation.4 | loop fusion | flops 18873984 | bytes 18878976 | tf_op jit(solution)/shard_map/reduce_sum | solution.py:140
  255.2 11.1 %fusion.19 = bf16[384,64]{0,1:T(8,128)(2,1)} fusion(bf16[12288,2,64]{0,2,1:T(8,128)(2,1)} %bitcast.91, f32[384,12288]{1,0:T(8,128)} %get-tuple-element.14, f32[384]{0:T(512)S(1)} %broadcast_maximum_fusion, s32[384]{0:T(512)S(1)} %iota_add_fusion, f32[384]{0:T(512)S(1)} %fusion), kind=kOutput, calls=%fused_computation.36 | convolution fusion | flops 622903296 | bytes 20500992 | tf_op jit(solution)/shard_map/htr,rhe->hte/dot_general | solution.py:141
  (49 shorter events, 0.8 us)
Async XLA Ops:
  0.0 3.8 %copy-start = (bf16[3,1664,104]{1,2,0:T(8,128)(2,1)S(1)}, bf16[3,1664,104]{1,2,0:T(8,128)(2,1)}, u32[]{:S(2)}) copy-start(bf16[3,1664,104]{1,2,0:T(8,128)(2,1)} %param.16) | copy-start | bytes 3115012
  2.9 0.9 copy-start.8
  2.9 0.9 copy-start.9
  3.8 4.5 %copy-start.5 = (s32[512]{0:T(512)S(1)}, s32[512]{0:T(512)}, u32[]{:S(2)}) copy-start(s32[512]{0:T(512)} %param.13) | copy-start | bytes 6148
  4.8 9.0 %collective-permute-start = (bf16[2,512,104]{1,2,0:T(8,128)(2,1)S(1)}, bf16[2,512,104]{1,2,0:T(8,128)(2,1)S(1)}, u32[]{:S(2)}, u32[]{:S(2)}) collective-permute-start(bf16[2,512,104]{1,2,0:T(8,128)(2,1)S(1)} %slice.42), channel_id=1, source_target_pairs={{0,16},{16,0},{32,48},{48,32},{64,80},{80,64},{96,112},{112,96},{1... | collective-permute-start | bytes 638984 | tf_op jit(solution)/shard_map/ppermute | solution.py:14
  8.3 5.5 %collective-permute-start.1 = (s32[512]{0:T(512)S(1)}, s32[512]{0:T(512)S(1)}, u32[]{:S(2)}, u32[]{:S(2)}) collective-permute-start(s32[512]{0:T(512)S(1)} %copy-done.5), channel_id=1, source_target_pairs={{0,16},{16,0},{32,48},{48,32},{64,80},{80,64},{96,112},{112,96},{1... | collective-permute-start | bytes 6152 | tf_op jit(solution)/shard_map/ppermute | solution.py:14
  13.8 2.6 copy-start.7
  14.4 1.4 copy-start.2
  24.4 51.2 %all-to-all-start.1 = ((bf16[16,104,512]{2,1,0:T(8,128)(2,1)}), bf16[16,104,512]{2,1,0:T(8,128)(2,1)}, u32[]{:S(2)}, u32[]{:S(2)}) async-start(bf16[16,104,512]{2,1,0:T(8,128)(2,1)} %bitcast.92), calls=%async_computation.1 | async-start | bytes 3407872 | tf_op jit(solution)/shard_map/all_to_all | solution.py:27
  37.1 41.3 %copy-start.3 = (bf16[4,104,1024]{2,1,0:T(8,128)(2,1)S(1)}, bf16[4,104,1024]{2,1,0:T(8,128)(2,1)}, u32[]{:S(2)}) copy-start(bf16[4,104,1024]{2,1,0:T(8,128)(2,1)} %param.18) | copy-start | bytes 2555908
  37.1 47.2 %copy-start.12 = (s32[128]{0:T(128)S(1)}, s32[128]{0:T(128)}, u32[]{:S(2)}) copy-start(s32[128]{0:T(128)} %param.19) | copy-start | bytes 1540
  79.5 16.0 %all-to-all-start.2 = ((bf16[16,8,1024]{2,1,0:T(8,128)(2,1)}), bf16[16,8,1024]{2,1,0:T(8,128)(2,1)S(1)}, u32[]{:S(2)}, u32[]{:S(2)}) async-start(bf16[16,8,1024]{2,1,0:T(8,128)(2,1)} %fusion.14), calls=%async_computation.2 | async-start | bytes 524288 | tf_op jit(solution)/shard_map/all_to_all | solution.py:27
  96.2 14.9 %all-to-all-start.3 = ((bf16[16,8,1024]{2,1,0:T(8,128)(2,1)}), bf16[16,8,1024]{2,1,0:T(8,128)(2,1)S(1)}, u32[]{:S(2)}, u32[]{:S(2)}) async-start(bf16[16,8,1024]{2,1,0:T(8,128)(2,1)} %broadcast_in_dim.38), calls=%async_computation.3 | async-start | bytes 524288 | tf_op jit(solution)/shard_map/all_to_all | solution.py:20
  99.8 50.3 %copy-start.4 = (bf16[256,1024]{1,0:T(8,128)(2,1)S(1)}, bf16[256,1024]{1,0:T(8,128)(2,1)}, u32[]{:S(2)}) copy-start(bf16[256,1024]{1,0:T(8,128)(2,1)} %param.20) | copy-start | bytes 1572868
  111.1 18.0 %all-to-all-start = ((s32[32,8,1]{1,2,0:T(1,128)}), s32[32,8,1]{1,2,0:T(1,128)S(1)}, u32[]{:S(2)}, u32[]{:S(2)}) async-start(s32[32,8,1]{1,2,0:T(1,128)} %bitcast), calls=%async_computation | async-start | bytes 32768 | tf_op jit(solution)/shard_map/all_to_all | solution.py:108
  129.1 20.5 %all-to-all-start.4 = ((bf16[32,8,1024]{2,1,0:T(8,128)(2,1)}), bf16[32,8,1024]{2,1,0:T(8,128)(2,1)S(1)}, u32[]{:S(2)}, u32[]{:S(2)}) async-start(bf16[32,8,1024]{2,1,0:T(8,128)(2,1)} %fusion.12), calls=%async_computation.4 | async-start | bytes 1048576 | tf_op jit(solution)/shard_map/all_to_all | solution.py:107
  150.1 1.0 copy-start.6
  150.1 1.0 copy-start.10
  150.1 1.0 copy-start.11
  153.9 79.6 %all-to-all-start.5 = ((bf16[32,384,2,64]{1,3,2,0:T(8,128)(2,1)}), bf16[32,384,2,64]{1,3,2,0:T(8,128)(2,1)}, u32[]{:S(2)}, u32[]{:S(2)}) async-start(bf16[32,384,2,64]{1,3,2,0:T(8,128)(2,1)} %broadcast_in_dim.39), calls=%async_computation.5 | async-start | bytes 6291456 | tf_op jit(solution)/shard_map/all_to_all | solution.py:20
  235.9 8.3 %copy-start.1 = (bf16[32,2,8,8,384]{4,3,0,2,1:T(8,128)(2,1)}, bf16[32,2,8,8,384]{4,3,0,2,1:T(8,128)(2,1)S(1)}, u32[]{:S(2)}) copy-start(bf16[32,2,8,8,384]{4,3,0,2,1:T(8,128)(2,1)S(1)} %copy.38) | copy-start | bytes 9437188

commit v2 on v0

v2 whole, which is shorter than its diff:
```python
import jax
import jax.numpy as jnp
from jax import lax
from jax.sharding import Mesh
from jax.sharding import PartitionSpec as P

HD = 104
DH = 64

layer_eps = 1e-05

GRP = ("gx", "gy")
TP = ("z", "core")


def normalize(values, gain, bias):
    mean = jnp.mean(values, axis=-1, keepdims=True)
    centred = values - mean
    spread = jnp.mean(centred * centred, axis=-1, keepdims=True)
    return centred * lax.rsqrt(spread + layer_eps) * gain + bias


def a2a_gather(value, axis):
    n = lax.axis_size(axis)
    spread = jnp.broadcast_to(value[None], (n,) + value.shape)
    got = lax.all_to_all(spread, axis, 0, 0, tiled=True)
    return got.reshape((n * value.shape[0],) + value.shape[1:])


def grp_gather(value):
    return a2a_gather(a2a_gather(value, "gy"), "gx")


def a2a_sum(parts, axis):
    got = lax.all_to_all(parts, axis, 0, 0, tiled=True)
    return jnp.sum(got.astype(jnp.float32), axis=0)


def attend_part(query, qpos, keys, kpos, values):
    score = jnp.dot(query, keys.T, preferred_element_type=jnp.float32) * DH ** (-0.5)
    allowed = kpos[None, :] <= qpos[:, None]
    top = jnp.max(jnp.where(allowed, score, -1e30), axis=1)
    expo = jnp.where(allowed, jnp.exp(score - top[:, None]), 0.0)
    total = jnp.sum(expo, axis=1)
    acc = jnp.dot(expo.astype(jnp.bfloat16), values, preferred_element_type=jnp.float32)
    return top, total, acc


def body(
    patches,
    patch_image,
    vis_gain,
    vis_bias,
    vis_qkv,
    vis_out,
    merge_weight,
    positions,
    text,
    dec_gain,
    dec_bias,
    dec_qkv,
):
    groups = lax.axis_size(GRP)
    here = lax.axis_index(GRP)
    rows = patches.shape[0]
    merged_count = rows // 4
    text_count = text.shape[0]
    tok = text_count + merged_count
    cap = merged_count // min(groups, 16)

    tnorm = normalize(text.astype(jnp.float32), dec_gain, dec_bias).astype(jnp.bfloat16)
    tproj = jnp.einsum("td,sde->ste", tnorm, dec_qkv, preferred_element_type=jnp.float32).astype(
        jnp.bfloat16
    )
    text_kv = grp_gather(jnp.stack([tproj[1], tproj[2]], axis=1))

    all_pos = a2a_gather(positions, GRP)
    flags = jnp.zeros((groups * tok,), jnp.int32).at[all_pos].add(1).reshape(groups, tok)
    free = 1 - flags
    text_rank = jnp.cumsum(free, axis=1) - 1
    place = jnp.arange(tok, dtype=jnp.int32)
    pick = (free[:, :, None] == 1) & (
        text_rank[:, :, None] == jnp.arange(text_count, dtype=jnp.int32)[None, None, :]
    )
    text_pos = jnp.sum(jnp.where(pick, place[None, :, None], 0), axis=1) + (
        jnp.arange(groups, dtype=jnp.int32) * tok
    )[:, None]

    heads = vis_qkv.shape[2] // HD
    patches_f = patches.astype(jnp.float32)
    normed = normalize(patches_f, vis_gain, vis_bias).astype(jnp.bfloat16)
    proj = jnp.einsum("pd,sde->spe", normed, vis_qkv, preferred_element_type=jnp.float32).astype(
        jnp.bfloat16
    )
    query = proj[0].reshape(rows, heads, HD)
    swap = [(i, i ^ 1) for i in range(lax.axis_size("gy"))]
    partner_kv, partner_ids = lax.ppermute((proj[1:], patch_image), "gy", swap)
    both_kv = jnp.concatenate([proj[1:], partner_kv], axis=1)
    both_ids = jnp.concatenate([patch_image, partner_ids], axis=0)
    keys = both_kv[0].reshape(2 * rows, heads, HD)
    values = both_kv[1].reshape(2 * rows, heads, HD)
    scores = jnp.einsum("phe,khe->hpk", query, keys, preferred_element_type=jnp.float32) * HD ** (
        -0.5
    )
    same = patch_image[:, None] == both_ids[None, :]
    top = jnp.max(jnp.where(same, scores, -1e30), axis=2, keepdims=True)
    expo = jnp.where(same, jnp.exp(scores - top), 0.0)
    weights = (expo / jnp.sum(expo, axis=2, keepdims=True)).astype(jnp.bfloat16)
    attended = jnp.einsum(
        "hpk,khe->phe", weights, values, preferred_element_type=jnp.float32
    ).astype(jnp.bfloat16)
    attended = attended.reshape(rows, heads * HD)

    nz = lax.axis_size("z")
    ncore = lax.axis_size("core")
    width = patches.shape[1] // (nz * ncore)
    mixed_parts = lax.dot_general(
        vis_out, attended, (((0,), (1,)), ((), ())), preferred_element_type=jnp.float32
    ).astype(jnp.bfloat16)
    mixed_parts = mixed_parts.reshape(nz, ncore, width, rows).transpose(1, 0, 2, 3)
    half = a2a_sum(mixed_parts, "core").astype(jnp.bfloat16)
    mixed = a2a_sum(half, "z")
    own_cols = lax.dynamic_slice_in_dim(patches_f, lax.axis_index(TP) * width, width, 1)
    visual = (mixed + own_cols.T).astype(jnp.bfloat16)
    windows = visual.reshape(width, merged_count, 4)
    partial_rows = jnp.einsum(
        "cmk,kce->me", windows, merge_weight, preferred_element_type=jnp.float32
    ).astype(jnp.bfloat16)
    ntp = nz * ncore
    merged = a2a_gather(
        a2a_sum(partial_rows.reshape(ntp, merged_count // ntp, -1), TP).astype(jnp.bfloat16), TP
    )

    mnorm = normalize(merged.astype(jnp.float32), dec_gain, dec_bias).astype(jnp.bfloat16)
    mproj = jnp.einsum("td,sde->ste", mnorm, dec_qkv, preferred_element_type=jnp.float32).astype(
        jnp.bfloat16
    )
    merged_kv = grp_gather(jnp.stack([mproj[1], mproj[2]], axis=1))

    own_text_pos = lax.dynamic_index_in_dim(text_pos, here, 0, keepdims=False)
    dquery = jnp.concatenate([tproj[0], mproj[0]], axis=0)
    query_pos = jnp.concatenate([own_text_pos, positions], axis=0)
    top_t, total_t, acc_t = attend_part(
        dquery, query_pos, text_kv[:, 0], text_pos.reshape(-1), text_kv[:, 1]
    )
    top_m, total_m, acc_m = attend_part(dquery, query_pos, merged_kv[:, 0], all_pos, merged_kv[:, 1])
    best = jnp.maximum(top_t, top_m)
    scale_t = jnp.exp(top_t - best)
    scale_m = jnp.exp(top_m - best)
    total = total_t * scale_t + total_m * scale_m
    acc = acc_t * scale_t[:, None] + acc_m * scale_m[:, None]
    result = (acc / total[:, None]).astype(jnp.bfloat16)
    text_out = result[:text_count]
    merged_out = result[text_count:]

    target = positions // tok
    member = (target[:, None] == jnp.arange(groups, dtype=jnp.int32)[None, :]).astype(jnp.int32)
    rank = jnp.sum(jnp.cumsum(member, axis=0) * member, axis=1) - 1
    slot = target * cap + rank
    select = slot[None, :] == jnp.arange(groups * cap, dtype=jnp.int32)[:, None]
    packed = jnp.dot(
        select.astype(jnp.bfloat16), merged_out, preferred_element_type=jnp.float32
    ).astype(jnp.bfloat16)
    got = lax.all_to_all(packed, GRP, 0, 0, tiled=True)

    src_pos = all_pos.reshape(groups, merged_count)
    to_me = (src_pos // tok) == here
    src_rank = jnp.cumsum(to_me.astype(jnp.int32), axis=1) - 1
    slot_hit = to_me[:, :, None] & (
        src_rank[:, :, None] == jnp.arange(cap, dtype=jnp.int32)[None, None, :]
    )
    got_pos = jnp.sum(jnp.where(slot_hit, src_pos[:, :, None] + 1, 0), axis=1).reshape(-1) - 1
    local = got_pos - here * tok
    landing = (local[None, :] == place[:, None]) & (got_pos[None, :] >= 0)
    text_land = own_text_pos[None, :] - here * tok == place[:, None]
    out = jnp.dot(landing.astype(jnp.bfloat16), got, preferred_element_type=jnp.float32)
    out = out + jnp.dot(
        text_land.astype(jnp.bfloat16), text_out, preferred_element_type=jnp.float32
    )
    return out.astype(jnp.bfloat16)


def solution(mesh):
    grid = mesh.devices.reshape(4, mesh.devices.shape[0] // 4, mesh.devices.shape[1] // 2, 2)
    mesh4 = Mesh(grid, GRP + TP)
    in_specs = (
        P(GRP, None),
        P(GRP),
        P(),
        P(),
        P(None, None, TP),
        P(TP, None),
        P(None, TP, None),
        P(GRP),
        P(GRP, None),
        P(),
        P(),
        P(None, None, TP),
    )
    out_specs = P(GRP, TP)
    return jax.shard_map(body, mesh=mesh4, in_specs=in_specs, out_specs=out_specs, check_vma=False)
```

time: 416 us -> 243 us (0.58)
  waiting for transfers between devices: 317 us -> 77.1 us
  starting transfers between devices: 26.2 us -> 61.7 us
  other arithmetic: 19 us -> 51.4 us
  between operations: 13.4 us -> 0.57 us
  local copies, waits for them, and re-layouts: 8.01 us -> 19.9 us
  matrix products: 32 us -> 24 us
  blocking collectives: 0 us -> 5.95 us
    all_gather x2 -> x0, waiting for transfers between devices: 134 us -> none  [the longest x1 73.6 us: body(): lax.all_gather(dproj[1], 'grp', axis=0, tiled=True).reshape(-1, dheads, DH)]
    psum x1 -> x0, waiting for transfers between devices: 102 us -> none  [body(): merged = lax.psum(partial_rows.astype(jnp.bfloat16), 'tp')]
    unnamed x5 -> x0, waiting for transfers between devices: 64.2 us -> none
    all_to_all x2 -> x9, waiting for transfers between devices: 14 us -> 75 us  [the longest x6 56.6 us: a2a_gather(): got = lax.all_to_all(spread, axis, 0, 0, tiled=True)]
    all_to_all x2 -> x9, starting transfers between devices: 20 us -> 55.8 us  [the longest x6 32.7 us: a2a_gather(): got = lax.all_to_all(spread, axis, 0, 0, tiled=True)]
    scatter-add x0 -> x1, other arithmetic: none -> 21.9 us  [body(): jnp.zeros((groups * tok,), jnp.int32).at[all_pos].add(1)]
    dot_general x5 -> x7, matrix products: 23.3 us -> 15.3 us  [the longest x2 7.13 us: attend_part(): jnp.dot(expo.astype(jnp.bfloat16), values, preferred_element_type=jnp.flo...]
    reduce_sum x2 -> x7, other arithmetic: 11.2 us -> 18.2 us  [the longest x2 7.93 us: attend_part(): total = jnp.sum(expo, axis=1)]
  transfers between devices with their start and end apart: 8 -> 11, of which waited for: 6 -> 9; matrix products, arithmetic and copies ran while one was open for 6% -> 24% of each run, Pallas kernels for 0% -> 0%
where the time goes in v2:
time: 243 us; the launch traced here: 241 us
  waiting for transfers between devices  77.1 us (32%)
  starting transfers between devices  61.7 us (25%)
  other arithmetic  51.4 us (21%)
  matrix products  24 us (10%)
  local copies, waits for them, and re-layouts  19.9 us (8%)
  blocking collectives  5.95 us (2%)
    all_to_all x6, waiting for transfers between devices, a2a_gather(): got = lax.all_to_all(spread, axis, 0, 0, tiled=True)  56.6 us
    all_to_all x6, starting transfers between devices, a2a_gather(): got = lax.all_to_all(spread, axis, 0, 0, tiled=True)  32.7 us
    scatter-add x1, other arithmetic, body(): jnp.zeros((groups * tok,), jnp.int32).at[all_pos].add(1)  21.9 us
    all_to_all x2, starting transfers between devices, a2a_sum(): got = lax.all_to_all(parts, axis, 0, 0, tiled=True)  17.3 us
    all_to_all x2, waiting for transfers between devices, a2a_sum(): got = lax.all_to_all(parts, axis, 0, 0, tiled=True)  10.8 us
    reduce_sum x2, other arithmetic, attend_part(): total = jnp.sum(expo, axis=1)  7.93 us
    all_to_all x1, waiting for transfers between devices, body(): got = lax.all_to_all(packed, GRP, 0, 0, tiled=True)  7.71 us
    dot_general x2, matrix products, attend_part(): jnp.dot(expo.astype(jnp.bfloat16), values, preferred_element_type=jnp.flo...  7.13 us
  transfers between devices with their start and end apart: 11, of which 9 were waited for; matrix products, arithmetic and copies ran while one was open for 24% of the time, Pallas kernels for 0%

profile of v2, /device:TPU:6, one launch (start us, length us, event | category | flops | bytes accessed | tf_op | source)
XLA Modules:
  0.0 240.6 jit_solution(9514494556852948400)
XLA Ops:
  0.0 2.9 %copy.69 = bf16[512,1664]{0,1:T(8,128)(2,1)S(1)} copy(bf16[512,1664]{1,0:T(8,128)(2,1)} %param.12) | data formatting | bytes 3407872 | tf_op args[0]
  3.8 1.0 fusion.13
  4.9 3.5 %collective-permute-start = (bf16[2,512,104]{1,2,0:T(8,128)(2,1)S(1)}, bf16[2,512,104]{1,2,0:T(8,128)(2,1)S(1)}, u32[]{:S(2)}, u32[]{:S(2)}) collective-permute-start(bf16[2,512,104]{1,2,0:T(8,128)(2,1)S(1)} %slice.75), channel_id=1, source_target_pairs={{0,16},{16,0},{32,48},{48,32},{64,80},{80,64},{96,112},{112,96},{1... | collective-permute-start | bytes 638984 | tf_op jit(solution)/shard_map/ppermute | solution.py:97
  8.4 2.4 collective-permute-start.1
  11.8 2.1 collective-permute-done.1
  14.6 1.3 copy-done.2
  16.5 4.3 %fusion.11 = bf16[1664,512]{0,1:T(8,128)(2,1)} fusion(bf16[104,1664]{1,0:T(8,128)(2,1)S(1)} %copy-done.8, f32[512,1024]{1,0:T(8,128)} %copy-done.2, f32[512]{0:T(512)S(1)} %fusion.18, f32[512]{0:T(512)S(1)} %get-tuple-element.18, s32[1024]{0:T(1024)S(1)} %pad_add_fusion, s32[512]{0:T(512)S(1)} %copy-done.5, bf16[2,512,104]{1,2,0:T(8,128)(2,1)S(1)} %slice.75, ...), kind=kOutput, calls=%fused_computation.21 | convolution fusion | flops 290738176 | bytes 4583424 | tf_op jit(solution)/shard_map/dot_general | solution.py:117
  20.8 3.6 %copy.71 = bf16[1664,512]{1,0:T(8,128)(2,1)} copy(bf16[1664,512]{0,1:T(8,128)(2,1)} %fusion.11) | data formatting | bytes 3407872 | tf_op jit(solution)/shard_map/convert_element_type | solution.py:119
  24.4 1.6 copy.72
  26.0 6.0 %all_to_all.58 = bf16[2,8,104,512]{3,2,1,0:T(8,128)(2,1)} all-to-all(bf16[2,8,104,512]{3,2,1,0:T(8,128)(2,1)S(1)} %copy.72), channel_id=1, replica_groups=mesh['gx'=4,'gy'=8,'z'=8,'core'=2] {'core'}, dimensions={0} | all-to-all | bytes 3407872 | tf_op jit(solution)/shard_map/all_to_all | solution.py:35
  32.6 10.2 %all-to-all-start = ((s32[32,1,128]{2,1,0:T(1,128)}), s32[32,1,128]{2,1,0:T(1,128)S(1)}, u32[]{:S(2)}, u32[]{:S(2)}) async-start(s32[32,1,128]{2,1,0:T(1,128)} %broadcast_in_dim.63), calls=%async_computation | async-start | bytes 32768 | tf_op jit(solution)/shard_map/all_to_all | solution.py:26
  42.9 2.9 %reduce_sum.149 = bf16[8,104,512]{2,1,0:T(8,128)(2,1)} reduce(bf16[2,8,104,512]{3,2,1,0:T(8,128)(2,1)} %all_to_all.58, bf16[]{:T(256)} %constant.98.clone.1), dimensions={0}, to_apply=%region_14.15 | reduce | flops 425984 | bytes 2555906 | tf_op jit(solution)/shard_map/reduce_sum | solution.py:36
  45.8 4.8 %all-to-all-done = s32[32,1,128]{2,1,0:T(1,128)S(1)} async-done(((s32[32,1,128]{2,1,0:T(1,128)}), s32[32,1,128]{2,1,0:T(1,128)S(1)}, u32[]{:S(2)}, u32[]{:S(2)}) %all-to-all-start) | async-done | bytes 16416 | tf_op jit(solution)/shard_map/all_to_all | solution.py:26
  50.6 10.3 %all-to-all-start.2 = ((bf16[8,104,512]{2,1,0:T(8,128)(2,1)}), bf16[8,104,512]{2,1,0:T(8,128)(2,1)}, u32[]{:S(2)}, u32[]{:S(2)}) async-start(bf16[8,104,512]{2,1,0:T(8,128)(2,1)} %reduce_sum.149), calls=%async_computation.2 | async-start | bytes 1703936 | tf_op jit(solution)/shard_map/all_to_all | solution.py:35
  61.0 2.2 convert_element_type.109
  64.2 21.9 %scatter_custom_fusion = s32[12288]{0:T(1024)S(1)} fusion(s32[4096]{0:T(1024)S(1)} %bitcast.169, s32[4096]{0:T(1024)S(1)} %broadcast.258, s32[]{:T(128)} %constant.37.clone.1), kind=kCustom, calls=%fused_computation.127 | custom fusion | flops 4096 | bytes 49156 | tf_op jit(solution)/shard_map/scatter-add | solution.py:78
  86.1 0.9 broadcast_in_dim.74
  86.9 3.5 %all-to-all-start.5 = ((bf16[8,256,2,64]{1,3,2,0:T(8,128)(2,1)}), bf16[8,256,2,64]{1,3,2,0:T(8,128)(2,1)S(1)}, u32[]{:S(2)}, u32[]{:S(2)}) async-start(bf16[8,256,2,64]{1,3,2,0:T(8,128)(2,1)} %broadcast_in_dim.74), calls=%async_computation.5 | async-start | bytes 1048576 | tf_op jit(solution)/shard_map/all_to_all | solution.py:26
  90.5 0.9 reduce-window.6
  91.6 1.3 convert_reduce_fusion.1
  92.9 1.0 fusion.84
  94.0 1.0 fusion.22
  95.1 11.6 %all-to-all-done.5 = bf16[8,256,2,64]{1,3,2,0:T(8,128)(2,1)S(1)} async-done(((bf16[8,256,2,64]{1,3,2,0:T(8,128)(2,1)}), bf16[8,256,2,64]{1,3,2,0:T(8,128)(2,1)S(1)}, u32[]{:S(2)}, u32[]{:S(2)}) %all-to-all-start.5) | async-done | bytes 524320 | tf_op jit(solution)/shard_map/all_to_all | solution.py:26
  106.7 7.0 %all-to-all-start.3 = ((bf16[16,8,1024]{2,1,0:T(8,128)(2,1)}), bf16[16,8,1024]{2,1,0:T(8,128)(2,1)S(1)}, u32[]{:S(2)}, u32[]{:S(2)}) async-start(bf16[16,8,1024]{2,1,0:T(8,128)(2,1)} %fusion.22), calls=%async_computation.3 | async-start | bytes 524288 | tf_op jit(solution)/shard_map/all_to_all | solution.py:35
  114.2 10.8 %all-to-all-done.3 = bf16[16,8,1024]{2,1,0:T(8,128)(2,1)S(1)} async-done(((bf16[16,8,1024]{2,1,0:T(8,128)(2,1)}), bf16[16,8,1024]{2,1,0:T(8,128)(2,1)S(1)}, u32[]{:S(2)}, u32[]{:S(2)}) %all-to-all-start.3) | async-done | bytes 262176 | tf_op jit(solution)/shard_map/all_to_all | solution.py:35
  124.9 1.6 broadcast_in_dim.76
  126.6 5.7 %all-to-all-start.6 = ((bf16[4,2048,2,64]{1,3,2,0:T(8,128)(2,1)}), bf16[4,2048,2,64]{1,3,2,0:T(8,128)(2,1)S(1)}, u32[]{:S(2)}, u32[]{:S(2)}) async-start(bf16[4,2048,2,64]{1,3,2,0:T(8,128)(2,1)} %broadcast_in_dim.76), calls=%async_computation.6 | async-start | bytes 4194304 | tf_op jit(solution)/shard_map/all_to_all | solution.py:26
  133.5 4.6 %select_reduce_fusion = s32[32,256]{1,0:T(8,128)S(1)} fusion(s32[32,384]{1,0:T(8,128)S(1)} %copy_bitcast_fusion.1, pred[32,384]{1,0:T(8,128)(4,1)S(1)} %eq.134), kind=kLoop, calls=%fused_computation.4 | loop fusion | flops 12574720 | bytes 94208 | tf_op jit(solution)/shard_map/reduce_sum | solution.py:85
  138.9 18.9 %all-to-all-done.6 = bf16[4,2048,2,64]{1,3,2,0:T(8,128)(2,1)S(1)} async-done(((bf16[4,2048,2,64]{1,3,2,0:T(8,128)(2,1)}), bf16[4,2048,2,64]{1,3,2,0:T(8,128)(2,1)S(1)}, u32[]{:S(2)}, u32[]{:S(2)}) %all-to-all-start.6) | async-done | bytes 2097184 | tf_op jit(solution)/shard_map/all_to_all | solution.py:26
  158.6 3.7 %all-to-all-start.4 = ((bf16[16,8,1024]{2,1,0:T(8,128)(2,1)}), bf16[16,8,1024]{2,1,0:T(8,128)(2,1)S(1)}, u32[]{:S(2)}, u32[]{:S(2)}) async-start(bf16[16,8,1024]{2,1,0:T(8,128)(2,1)} %broadcast_in_dim.73), calls=%async_computation.4 | async-start | bytes 524288 | tf_op jit(solution)/shard_map/all_to_all | solution.py:26
  163.7 1.4 select_reduce_fusion.1
  165.1 1.5 copy.83
  166.6 6.6 %all-to-all-done.4 = bf16[16,8,1024]{2,1,0:T(8,128)(2,1)S(1)} async-done(((bf16[16,8,1024]{2,1,0:T(8,128)(2,1)}), bf16[16,8,1024]{2,1,0:T(8,128)(2,1)S(1)}, u32[]{:S(2)}, u32[]{:S(2)}) %all-to-all-start.4) | async-done | bytes 262176 | tf_op jit(solution)/shard_map/all_to_all | solution.py:26
  173.7 1.4 fusion.70
  175.9 3.4 %all-to-all-start.7 = ((bf16[8,128,2,64]{1,3,2,0:T(8,128)(2,1)}), bf16[8,128,2,64]{1,3,2,0:T(8,128)(2,1)S(1)}, u32[]{:S(2)}, u32[]{:S(2)}) async-start(bf16[8,128,2,64]{1,3,2,0:T(8,128)(2,1)} %broadcast_in_dim.79), calls=%async_computation.7 | async-start | bytes 524288 | tf_op jit(solution)/shard_map/all_to_all | solution.py:26
  179.3 5.7 %fusion = (f32[384]{0:T(512)S(1)}, f32[384,8192]{1,0:T(8,128)}) fusion(s32[8192]{0:T(1024)S(1)} %bitcast.156, s32[384]{0:T(512)S(1)} %pad_add_fusion.1, bf16[8192,2,64]{0,2,1:T(8,128)(2,1)S(1)} %bitcast.150, bf16[128,64]{0,1:T(8,128)(2,1)S(1)} %get-tuple-element.17, bf16[256,64]{0,1:T(8,128)(2,1)S(1)} %get-tuple-element.12), kind=kOutput, calls=%fused_computation.3 | convolution fusion | flops 415334016 | bytes 13716992 | tf_op jit(solution)/shard_map/dot_general | solution.py:40
  185.0 7.5 %all-to-all-done.7 = bf16[8,128,2,64]{1,3,2,0:T(8,128)(2,1)S(1)} async-done(((bf16[8,128,2,64]{1,3,2,0:T(8,128)(2,1)}), bf16[8,128,2,64]{1,3,2,0:T(8,128)(2,1)S(1)}, u32[]{:S(2)}, u32[]{:S(2)}) %all-to-all-start.7) | async-done | bytes 262176 | tf_op jit(solution)/shard_map/all_to_all | solution.py:26
  192.5 1.1 broadcast_in_dim.85
  193.6 6.3 %all-to-all-start.8 = ((bf16[4,1024,2,64]{1,3,2,0:T(8,128)(2,1)}), bf16[4,1024,2,64]{1,3,2,0:T(8,128)(2,1)}, u32[]{:S(2)}, u32[]{:S(2)}) async-start(bf16[4,1024,2,64]{1,3,2,0:T(8,128)(2,1)} %broadcast_in_dim.85), calls=%async_computation.8 | async-start | bytes 2097152 | tf_op jit(solution)/shard_map/all_to_all | solution.py:26
  199.9 6.5 %fusion.2 = f32[384]{0:T(512)S(1)} fusion(f32[384,8192]{1,0:T(8,128)} %get-tuple-element.21, f32[384]{0:T(512)S(1)} %get-tuple-element.20, s32[8192]{0:T(1024)S(1)} %bitcast.157, s32[384]{0:T(512)S(1)} %pad_add_fusion.1), kind=kLoop, calls=%fused_computation.8 | loop fusion | flops 12582528 | bytes 12620288 | tf_op jit(solution)/shard_map/reduce_sum | solution.py:44
  206.4 7.2 %all-to-all-done.8 = bf16[4,1024,2,64]{1,3,2,0:T(8,128)(2,1)} async-done(((bf16[4,1024,2,64]{1,3,2,0:T(8,128)(2,1)}), bf16[4,1024,2,64]{1,3,2,0:T(8,128)(2,1)}, u32[]{:S(2)}, u32[]{:S(2)}) %all-to-all-start.8) | async-done | bytes 1048608 | tf_op jit(solution)/shard_map/all_to_all | solution.py:26
  213.6 1.3 copy.85
  214.9 1.2 fusion.4
  216.1 1.4 fusion.7
  217.6 5.9 %fusion.30 = f32[384,64]{0,1:T(8,128)S(1)} fusion(f32[384,8192]{1,0:T(8,128)} %get-tuple-element.21, f32[384]{0:T(512)S(1)} %get-tuple-element.20, s32[8192]{0:T(1024)S(1)} %bitcast.158, s32[384]{0:T(512)S(1)} %pad_add_fusion.1, bf16[8192,2,64]{0,2,1:T(8,128)(2,1)S(1)} %bitcast.151, f32[384]{0:T(512)S(1)} %get-tuple-element.9), kind=kOutput, calls=%fused_computation.46 | convolution fusion | flops 415260672 | bytes 13768704 | tf_op jit(solution)/shard_map/dot_general | solution.py:45
  223.5 1.2 fusion.37
  225.8 5.7 %all-to-all-start.9 = ((bf16[32,2,256]{2,1,0:T(2,128)(2,1)}), bf16[32,2,256]{2,1,0:T(2,128)(2,1)S(1)}, u32[]{:S(2)}, u32[]{:S(2)}) async-start(bf16[32,2,256]{2,1,0:T(2,128)(2,1)} %reshape.356), calls=%async_computation.9 | async-start | bytes 65536 | tf_op jit(solution)/shard_map/all_to_all | solution.py:164
  231.7 7.7 %all-to-all-done.9 = bf16[32,2,256]{2,1,0:T(2,128)(2,1)S(1)} async-done(((bf16[32,2,256]{2,1,0:T(2,128)(2,1)}), bf16[32,2,256]{2,1,0:T(2,128)(2,1)S(1)}, u32[]{:S(2)}, u32[]{:S(2)}) %all-to-all-start.9) | async-done | bytes 32800 | tf_op jit(solution)/shard_map/all_to_all | solution.py:164
  (100 shorter events, 13.6 us)
Async XLA Ops:
  0.0 3.8 %copy-start = (bf16[3,1664,104]{1,2,0:T(8,128)(2,1)S(1)}, bf16[3,1664,104]{1,2,0:T(8,128)(2,1)}, u32[]{:S(2)}) copy-start(bf16[3,1664,104]{1,2,0:T(8,128)(2,1)} %param.16) | copy-start | bytes 3115012
  0.0 3.8 %copy-start.11 = (f32[1664]{0:T(1024)S(1)}, f32[1664]{0:T(1024)}, u32[]{:S(2)}) copy-start(f32[1664]{0:T(1024)} %param.14) | copy-start | bytes 19972
  0.0 3.8 %copy-start.10 = (f32[1664]{0:T(1024)S(1)}, f32[1664]{0:T(1024)}, u32[]{:S(2)}) copy-start(f32[1664]{0:T(1024)} %param.15) | copy-start | bytes 19972
  3.8 4.6 %copy-start.5 = (s32[512]{0:T(512)S(1)}, s32[512]{0:T(512)}, u32[]{:S(2)}) copy-start(s32[512]{0:T(512)} %param.13) | copy-start | bytes 6148
  3.8 7.0 %copy-start.3 = (bf16[256,1024]{1,0:T(8,128)(2,1)S(1)}, bf16[256,1024]{1,0:T(8,128)(2,1)}, u32[]{:S(2)}) copy-start(bf16[256,1024]{1,0:T(8,128)(2,1)} %param.20) | copy-start | bytes 1572868
  3.8 7.4 %copy-start.7 = (bf16[3,1024,64]{1,2,0:T(8,128)(2,1)S(1)}, bf16[3,1024,64]{1,2,0:T(8,128)(2,1)}, u32[]{:S(2)}) copy-start(bf16[3,1024,64]{1,2,0:T(8,128)(2,1)} %param.23) | copy-start | bytes 1179652
  3.8 7.4 %copy-start.12 = (f32[1024]{0:T(1024)S(1)}, f32[1024]{0:T(1024)}, u32[]{:S(2)}) copy-start(f32[1024]{0:T(1024)} %param.22) | copy-start | bytes 12292
  3.8 7.4 %copy-start.13 = (f32[1024]{0:T(1024)S(1)}, f32[1024]{0:T(1024)}, u32[]{:S(2)}) copy-start(f32[1024]{0:T(1024)} %param.21) | copy-start | bytes 12292
  4.8 6.9 %copy-start.6 = (s32[128]{0:T(128)S(1)}, s32[128]{0:T(128)}, u32[]{:S(2)}) copy-start(s32[128]{0:T(128)} %param.19) | copy-start | bytes 1540
  4.9 9.0 %collective-permute-start = (bf16[2,512,104]{1,2,0:T(8,128)(2,1)S(1)}, bf16[2,512,104]{1,2,0:T(8,128)(2,1)S(1)}, u32[]{:S(2)}, u32[]{:S(2)}) collective-permute-start(bf16[2,512,104]{1,2,0:T(8,128)(2,1)S(1)} %slice.75), channel_id=1, source_target_pairs={{0,16},{16,0},{32,48},{48,32},{64,80},{80,64},{96,112},{112,96},{1... | collective-permute-start | bytes 638984 | tf_op jit(solution)/shard_map/ppermute | solution.py:97
  8.4 5.5 %collective-permute-start.1 = (s32[512]{0:T(512)S(1)}, s32[512]{0:T(512)S(1)}, u32[]{:S(2)}, u32[]{:S(2)}) collective-permute-start(s32[512]{0:T(512)S(1)} %copy-done.5), channel_id=1, source_target_pairs={{0,16},{16,0},{32,48},{48,32},{64,80},{80,64},{96,112},{112,96},{1... | collective-permute-start | bytes 6152 | tf_op jit(solution)/shard_map/ppermute | solution.py:97
  11.7 4.8 %copy-start.8 = (bf16[104,1664]{1,0:T(8,128)(2,1)S(1)}, bf16[104,1664]{1,0:T(8,128)(2,1)}, u32[]{:S(2)}) copy-start(bf16[104,1664]{1,0:T(8,128)(2,1)} %param.17) | copy-start | bytes 1038340
  13.9 0.7 copy-start.9
  14.5 1.4 copy-start.2
  32.6 18.0 %all-to-all-start = ((s32[32,1,128]{2,1,0:T(1,128)}), s32[32,1,128]{2,1,0:T(1,128)S(1)}, u32[]{:S(2)}, u32[]{:S(2)}) async-start(s32[32,1,128]{2,1,0:T(1,128)} %broadcast_in_dim.63), calls=%async_computation | async-start | bytes 32768 | tf_op jit(solution)/shard_map/all_to_all | solution.py:26
  50.6 35.4 %all-to-all-start.2 = ((bf16[8,104,512]{2,1,0:T(8,128)(2,1)}), bf16[8,104,512]{2,1,0:T(8,128)(2,1)}, u32[]{:S(2)}, u32[]{:S(2)}) async-start(bf16[8,104,512]{2,1,0:T(8,128)(2,1)} %reduce_sum.149), calls=%async_computation.2 | async-start | bytes 1703936 | tf_op jit(solution)/shard_map/all_to_all | solution.py:35
  63.2 30.9 %copy-start.4 = (bf16[4,104,1024]{2,1,0:T(8,128)(2,1)S(1)}, bf16[4,104,1024]{2,1,0:T(8,128)(2,1)}, u32[]{:S(2)}) copy-start(bf16[4,104,1024]{2,1,0:T(8,128)(2,1)} %param.18) | copy-start | bytes 2555908
  86.9 19.8 %all-to-all-start.5 = ((bf16[8,256,2,64]{1,3,2,0:T(8,128)(2,1)}), bf16[8,256,2,64]{1,3,2,0:T(8,128)(2,1)S(1)}, u32[]{:S(2)}, u32[]{:S(2)}) async-start(bf16[8,256,2,64]{1,3,2,0:T(8,128)(2,1)} %broadcast_in_dim.74), calls=%async_computation.5 | async-start | bytes 1048576 | tf_op jit(solution)/shard_map/all_to_all | solution.py:26
  106.7 18.2 %all-to-all-start.3 = ((bf16[16,8,1024]{2,1,0:T(8,128)(2,1)}), bf16[16,8,1024]{2,1,0:T(8,128)(2,1)S(1)}, u32[]{:S(2)}, u32[]{:S(2)}) async-start(bf16[16,8,1024]{2,1,0:T(8,128)(2,1)} %fusion.22), calls=%async_computation.3 | async-start | bytes 524288 | tf_op jit(solution)/shard_map/all_to_all | solution.py:35
  126.6 31.3 %all-to-all-start.6 = ((bf16[4,2048,2,64]{1,3,2,0:T(8,128)(2,1)}), bf16[4,2048,2,64]{1,3,2,0:T(8,128)(2,1)S(1)}, u32[]{:S(2)}, u32[]{:S(2)}) async-start(bf16[4,2048,2,64]{1,3,2,0:T(8,128)(2,1)} %broadcast_in_dim.76), calls=%async_computation.6 | async-start | bytes 4194304 | tf_op jit(solution)/shard_map/all_to_all | solution.py:26
  158.6 14.5 %all-to-all-start.4 = ((bf16[16,8,1024]{2,1,0:T(8,128)(2,1)}), bf16[16,8,1024]{2,1,0:T(8,128)(2,1)S(1)}, u32[]{:S(2)}, u32[]{:S(2)}) async-start(bf16[16,8,1024]{2,1,0:T(8,128)(2,1)} %broadcast_in_dim.73), calls=%async_computation.4 | async-start | bytes 524288 | tf_op jit(solution)/shard_map/all_to_all | solution.py:26
  166.6 12.7 %copy-start.1 = (bf16[4,2,8,8,2048]{4,3,0,2,1:T(8,128)(2,1)S(1)}, bf16[4,2,8,8,2048]{4,3,0,2,1:T(8,128)(2,1)}, u32[]{:S(2)}) copy-start(bf16[4,2,8,8,2048]{4,3,0,2,1:T(8,128)(2,1)} %copy.83) | copy-start | bytes 6291460
  175.9 16.6 %all-to-all-start.7 = ((bf16[8,128,2,64]{1,3,2,0:T(8,128)(2,1)}), bf16[8,128,2,64]{1,3,2,0:T(8,128)(2,1)S(1)}, u32[]{:S(2)}, u32[]{:S(2)}) async-start(bf16[8,128,2,64]{1,3,2,0:T(8,128)(2,1)} %broadcast_in_dim.79), calls=%async_computation.7 | async-start | bytes 524288 | tf_op jit(solution)/shard_map/all_to_all | solution.py:26
  193.6 20.0 %all-to-all-start.8 = ((bf16[4,1024,2,64]{1,3,2,0:T(8,128)(2,1)}), bf16[4,1024,2,64]{1,3,2,0:T(8,128)(2,1)}, u32[]{:S(2)}, u32[]{:S(2)}) async-start(bf16[4,1024,2,64]{1,3,2,0:T(8,128)(2,1)} %broadcast_in_dim.85), calls=%async_computation.8 | async-start | bytes 2097152 | tf_op jit(solution)/shard_map/all_to_all | solution.py:26
  223.5 1.3 copy-start.14
  225.8 13.7 %all-to-all-start.9 = ((bf16[32,2,256]{2,1,0:T(2,128)(2,1)}), bf16[32,2,256]{2,1,0:T(2,128)(2,1)S(1)}, u32[]{:S(2)}, u32[]{:S(2)}) async-start(bf16[32,2,256]{2,1,0:T(2,128)(2,1)} %reshape.356), calls=%async_computation.9 | async-start | bytes 65536 | tf_op jit(solution)/shard_map/all_to_all | solution.py:164

commit v3 on v2

--- a/solution.py
+++ b/solution.py
@@ -36,9 +36,8 @@
     return jnp.sum(got.astype(jnp.float32), axis=0)
 
 
-def attend_part(query, qpos, keys, kpos, values):
+def attend_part(query, allowed, keys, values):
     score = jnp.dot(query, keys.T, preferred_element_type=jnp.float32) * DH ** (-0.5)
-    allowed = kpos[None, :] <= qpos[:, None]
     top = jnp.max(jnp.where(allowed, score, -1e30), axis=1)
     expo = jnp.where(allowed, jnp.exp(score - top[:, None]), 0.0)
     total = jnp.sum(expo, axis=1)
@@ -72,19 +71,15 @@
     tproj = jnp.einsum("td,sde->ste", tnorm, dec_qkv, preferred_element_type=jnp.float32).astype(
         jnp.bfloat16
     )
-    text_kv = grp_gather(jnp.stack([tproj[1], tproj[2]], axis=1))
-
-    all_pos = a2a_gather(positions, GRP)
-    flags = jnp.zeros((groups * tok,), jnp.int32).at[all_pos].add(1).reshape(groups, tok)
+    text_kv = lax.all_gather(jnp.stack([tproj[1], tproj[2]], axis=1), GRP, axis=0, tiled=True)
+
+    all_pos = lax.all_gather(positions, GRP, axis=0, tiled=True)
+    place = jnp.arange(tok, dtype=jnp.int32)
+    flags = jnp.sum((all_pos[None, :] == (here * tok + place)[:, None]).astype(jnp.int32), axis=1)
     free = 1 - flags
-    text_rank = jnp.cumsum(free, axis=1) - 1
-    place = jnp.arange(tok, dtype=jnp.int32)
-    pick = (free[:, :, None] == 1) & (
-        text_rank[:, :, None] == jnp.arange(text_count, dtype=jnp.int32)[None, None, :]
-    )
-    text_pos = jnp.sum(jnp.where(pick, place[None, :, None], 0), axis=1) + (
-        jnp.arange(groups, dtype=jnp.int32) * tok
-    )[:, None]
+    text_rank = jnp.cumsum(free) - 1
+    pick = (free[:, None] == 1) & (text_rank[:, None] == jnp.arange(text_count, dtype=jnp.int32)[None, :])
+    own_text_pos = jnp.sum(jnp.where(pick, place[:, None], 0), axis=0) + here * tok
 
     heads = vis_qkv.shape[2] // HD
     patches_f = patches.astype(jnp.float32)
@@ -137,13 +132,25 @@
     )
     merged_kv = grp_gather(jnp.stack([mproj[1], mproj[2]], axis=1))
 
-    own_text_pos = lax.dynamic_index_in_dim(text_pos, here, 0, keepdims=False)
     dquery = jnp.concatenate([tproj[0], mproj[0]], axis=0)
     query_pos = jnp.concatenate([own_text_pos, positions], axis=0)
+    block = positions // tok
+    seen = jnp.sum(
+        ((all_pos[None, :] >= (block * tok)[:, None]) & (all_pos[None, :] <= positions[:, None])).astype(
+            jnp.int32
+        ),
+        axis=1,
+    )
+    merged_limit = block * text_count + (positions - block * tok + 1 - seen)
+    text_limit = here * text_count + jnp.arange(text_count, dtype=jnp.int32) + 1
+    limit = jnp.concatenate([text_limit, merged_limit], axis=0)
+    text_key = jnp.arange(groups * text_count, dtype=jnp.int32)
     top_t, total_t, acc_t = attend_part(
-        dquery, query_pos, text_kv[:, 0], text_pos.reshape(-1), text_kv[:, 1]
-    )
-    top_m, total_m, acc_m = attend_part(dquery, query_pos, merged_kv[:, 0], all_pos, merged_kv[:, 1])
+        dquery, text_key[None, :] < limit[:, None], text_kv[:, 0], text_kv[:, 1]
+    )
+    top_m, total_m, acc_m = attend_part(
+        dquery, all_pos[None, :] <= query_pos[:, None], merged_kv[:, 0], merged_kv[:, 1]
+    )
     best = jnp.maximum(top_t, top_m)
     scale_t = jnp.exp(top_t - best)
     scale_m = jnp.exp(top_m - best)

time: 243 us -> 210 us (0.86)
  blocking collectives: 5.95 us -> 40.7 us
  other arithmetic: 51.4 us -> 18.6 us
  waiting for transfers between devices: 77.1 us -> 56.5 us
  starting transfers between devices: 61.7 us -> 43.2 us
  between operations: 0.57 us -> 13.9 us
  matrix products: 24 us -> 18.8 us
  local copies, waits for them, and re-layouts: 19.9 us -> 16.6 us
    all_gather x0 -> x1, blocking collectives: none -> 34.8 us  [body(): all_pos = lax.all_gather(positions, GRP, axis=0, tiled=True)]
    scatter-add x1 -> x0, other arithmetic: 21.9 us -> none  [body(): jnp.zeros((groups * tok,), jnp.int32).at[all_pos].add(1)]
    all_to_all x6 -> x3, waiting for transfers between devices: 56.6 us -> 35.6 us  [a2a_gather(): got = lax.all_to_all(spread, axis, 0, 0, tiled=True)]
    all_to_all x6 -> x3, starting transfers between devices: 32.7 us -> 13.9 us  [a2a_gather(): got = lax.all_to_all(spread, axis, 0, 0, tiled=True)]
    dot_general x2, matrix products: 7.13 us -> 3.79 us  [attend_part(): jnp.dot(expo.astype(jnp.bfloat16), values, preferred_element_type=jnp.flo...]
    reduce_sum x1 -> x3, other arithmetic: 4.65 us -> 1.45 us  [the longest x1 0.78 us: body(): jnp.sum((all_pos[None, :] == (here * tok + place)[:, None]).astype(jnp.in...]
    broadcast_in_dim x8 -> x4, local copies, waits for them, and re-layouts: 5.79 us -> 2.62 us  [a2a_gather(): spread = jnp.broadcast_to(value[None], (n,) + value.shape)]
    reduce_sum x2, other arithmetic: 7.93 us -> 4.83 us  [attend_part(): total = jnp.sum(expo, axis=1)]
  transfers between devices with their start and end apart: 11 -> 9, of which waited for: 9 -> 6; matrix products, arithmetic and copies ran while one was open for 24% -> 9% of each run, Pallas kernels for 0% -> 0%
where the time goes in v3:
time: 210 us; the launch traced here: 208 us
  waiting for transfers between devices  56.5 us (27%)
  starting transfers between devices  43.2 us (21%)
  blocking collectives  40.7 us (19%)
  matrix products  18.8 us (9%)
  other arithmetic  18.6 us (9%)
  local copies, waits for them, and re-layouts  16.6 us (8%)
  between operations  13.9 us (7%)
    all_to_all x3, waiting for transfers between devices, a2a_gather(): got = lax.all_to_all(spread, axis, 0, 0, tiled=True)  35.6 us
    all_gather x1, blocking collectives, body(): all_pos = lax.all_gather(positions, GRP, axis=0, tiled=True)  34.8 us
    all_to_all x2, starting transfers between devices, a2a_sum(): got = lax.all_to_all(parts, axis, 0, 0, tiled=True)  17.8 us
    all_to_all x3, starting transfers between devices, a2a_gather(): got = lax.all_to_all(spread, axis, 0, 0, tiled=True)  13.9 us
    all_to_all x2, waiting for transfers between devices, a2a_sum(): got = lax.all_to_all(parts, axis, 0, 0, tiled=True)  11 us
    unnamed x37, local copies, waits for them, and re-layouts  7.84 us
    all_to_all x1, waiting for transfers between devices, body(): got = lax.all_to_all(packed, GRP, 0, 0, tiled=True)  7.71 us
    all_to_all x1, blocking collectives, a2a_sum(): got = lax.all_to_all(parts, axis, 0, 0, tiled=True)  5.95 us
  transfers between devices with their start and end apart: 9, of which 6 were waited for; matrix products, arithmetic and copies ran while one was open for 9% of the time, Pallas kernels for 0%

profile of v3, /device:TPU:6, one launch (start us, length us, event | category | flops | bytes accessed | tf_op | source)
XLA Modules:
  0.0 208.3 jit_solution(17210847224180489849)
XLA Ops:
  6.5 2.9 %copy.37 = bf16[512,1664]{0,1:T(8,128)(2,1)S(1)} copy(bf16[512,1664]{1,0:T(8,128)(2,1)} %param.12) | data formatting | bytes 3407872 | tf_op args[0]
  9.8 0.5 multiply_reduce_fusion
  10.4 1.0 fusion.11
  11.4 3.5 %collective-permute-start = (bf16[2,512,104]{1,2,0:T(8,128)(2,1)S(1)}, bf16[2,512,104]{1,2,0:T(8,128)(2,1)S(1)}, u32[]{:S(2)}, u32[]{:S(2)}) collective-permute-start(bf16[2,512,104]{1,2,0:T(8,128)(2,1)S(1)} %slice.75), channel_id=1, source_target_pairs={{0,16},{16,0},{32,48},{48,32},{64,80},{80,64},{96,112},{112,96},{1... | collective-permute-start | bytes 638984 | tf_op jit(solution)/shard_map/ppermute | solution.py:92
  14.9 2.4 %collective-permute-start.1 = (s32[512]{0:T(512)S(1)}, s32[512]{0:T(512)S(1)}, u32[]{:S(2)}, u32[]{:S(2)}) collective-permute-start(s32[512]{0:T(512)S(1)} %copy-done.5), channel_id=1, source_target_pairs={{0,16},{16,0},{32,48},{48,32},{64,80},{80,64},{96,112},{112,96},{1... | collective-permute-start | bytes 6152 | tf_op jit(solution)/shard_map/ppermute | solution.py:92
  17.8 0.5 fusion.59
  18.3 2.1 %collective-permute-done.1 = s32[512]{0:T(512)S(1)} collective-permute-done((s32[512]{0:T(512)S(1)}, s32[512]{0:T(512)S(1)}, u32[]{:S(2)}, u32[]{:S(2)}) %collective-permute-start.1) | collective-permute-done | bytes 2080 | tf_op jit(solution)/shard_map/ppermute | solution.py:92
  20.4 0.6 fusion.10
  21.1 1.3 copy-done.2
  22.4 0.7 fusion.16
  23.0 4.3 %fusion.9 = bf16[1664,512]{0,1:T(8,128)(2,1)} fusion(bf16[104,1664]{1,0:T(8,128)(2,1)S(1)} %copy-done.9, f32[512,1024]{1,0:T(8,128)} %copy-done.2, f32[512]{0:T(512)S(1)} %fusion.16, f32[512]{0:T(512)S(1)} %get-tuple-element.20, s32[1024]{0:T(1024)S(1)} %pad_add_fusion, s32[512]{0:T(512)S(1)} %copy-done.5, bf16[2,512,104]{1,2,0:T(8,128)(2,1)S(1)} %slice.75, ...), kind=kOutput, calls=%fused_computation.18 | convolution fusion | flops 290738176 | bytes 4583424 | tf_op jit(solution)/shard_map/dot_general | solution.py:112
  27.3 3.6 %copy.39 = bf16[1664,512]{1,0:T(8,128)(2,1)} copy(bf16[1664,512]{0,1:T(8,128)(2,1)} %fusion.9) | data formatting | bytes 3407872 | tf_op jit(solution)/shard_map/convert_element_type | solution.py:114
  31.0 1.6 copy.40
  32.5 6.0 %all_to_all.42 = bf16[2,8,104,512]{3,2,1,0:T(8,128)(2,1)} all-to-all(bf16[2,8,104,512]{3,2,1,0:T(8,128)(2,1)S(1)} %copy.40), channel_id=1, replica_groups=mesh['gx'=4,'gy'=8,'z'=8,'core'=2] {'core'}, dimensions={0} | all-to-all | bytes 3407872 | tf_op jit(solution)/shard_map/all_to_all | solution.py:35
  38.5 2.9 %reduce_sum.167 = bf16[8,104,512]{2,1,0:T(8,128)(2,1)} reduce(bf16[2,8,104,512]{3,2,1,0:T(8,128)(2,1)} %all_to_all.42, bf16[]{:T(256)} %constant.93.clone.1), dimensions={0}, to_apply=%region_11.12 | reduce | flops 425984 | bytes 2555906 | tf_op jit(solution)/shard_map/reduce_sum | solution.py:36
  41.4 10.4 %all-to-all-start.1 = ((bf16[8,104,512]{2,1,0:T(8,128)(2,1)}), bf16[8,104,512]{2,1,0:T(8,128)(2,1)}, u32[]{:S(2)}, u32[]{:S(2)}) async-start(bf16[8,104,512]{2,1,0:T(8,128)(2,1)} %reduce_sum.167), calls=%async_computation.1 | async-start | bytes 1703936 | tf_op jit(solution)/shard_map/all_to_all | solution.py:35
  51.9 0.6 pad_maximum_fusion.1
  52.6 2.2 %convert_element_type.116 = f32[512,1664]{0,1:T(8,128)} convert(bf16[512,1664]{0,1:T(8,128)(2,1)S(1)} %copy.37) | non-fusion elementwise | flops 851968 | bytes 5111808 | tf_op jit(solution)/shard_map/convert_element_type | solution.py:85
  54.8 34.8 %all-gather = s32[32,1,128]{2,1,0:T(1,128)S(1)} all-gather(s32[1,1,128]{2,1,0:T(1,128)S(1)} %bitcast.149), channel_id=1, replica_groups=mesh['gx'=4,'gy'=8,'z'=8,'core'=2] {'gx','gy'}, dimensions={0}, use_global_device_ids=true | all-gather | bytes 16896 | tf_op jit(solution)/shard_map/all_gather | solution.py:76
  89.6 0.8 convert_reduce_fusion
  91.0 1.3 convert_reduce_fusion.3
  92.3 1.0 fusion.83
  93.4 2.2 %fusion.20 = bf16[16,8,1024]{2,1,0:T(8,128)(2,1)} fusion(bf16[4,104,1024]{2,1,0:T(8,128)(2,1)} %param.18, bf16[104,128,4]{0,2,1:T(4,128)(2,1)S(1)} %bitcast.145), kind=kOutput, calls=%fused_computation.38 | convolution fusion | flops 109182976 | bytes 1220608 | tf_op jit(solution)/shard_map/cmk,kce->me/dot_general | solution.py:121
  95.7 7.3 %all-to-all-start.2 = ((bf16[16,8,1024]{2,1,0:T(8,128)(2,1)}), bf16[16,8,1024]{2,1,0:T(8,128)(2,1)S(1)}, u32[]{:S(2)}, u32[]{:S(2)}) async-start(bf16[16,8,1024]{2,1,0:T(8,128)(2,1)} %fusion.20), calls=%async_computation.2 | async-start | bytes 524288 | tf_op jit(solution)/shard_map/all_to_all | solution.py:35
  103.2 11.0 %all-to-all-done.2 = bf16[16,8,1024]{2,1,0:T(8,128)(2,1)S(1)} async-done(((bf16[16,8,1024]{2,1,0:T(8,128)(2,1)}), bf16[16,8,1024]{2,1,0:T(8,128)(2,1)S(1)}, u32[]{:S(2)}, u32[]{:S(2)}) %all-to-all-start.2) | async-done | bytes 262176 | tf_op jit(solution)/shard_map/all_to_all | solution.py:35
  114.2 0.7 broadcast_in_dim.53
  114.9 3.5 %all-to-all-start.3 = ((bf16[16,8,1024]{2,1,0:T(8,128)(2,1)}), bf16[16,8,1024]{2,1,0:T(8,128)(2,1)S(1)}, u32[]{:S(2)}, u32[]{:S(2)}) async-start(bf16[16,8,1024]{2,1,0:T(8,128)(2,1)} %broadcast_in_dim.53), calls=%async_computation.3 | async-start | bytes 524288 | tf_op jit(solution)/shard_map/all_to_all | solution.py:26
  118.5 0.5 convert_reduce_fusion.2
  119.1 10.7 %all-to-all-done.3 = bf16[16,8,1024]{2,1,0:T(8,128)(2,1)S(1)} async-done(((bf16[16,8,1024]{2,1,0:T(8,128)(2,1)}), bf16[16,8,1024]{2,1,0:T(8,128)(2,1)S(1)}, u32[]{:S(2)}, u32[]{:S(2)}) %all-to-all-start.3) | async-done | bytes 262176 | tf_op jit(solution)/shard_map/all_to_all | solution.py:26
  130.3 0.4 fusion.69
  130.7 0.7 broadcast_in_dim.58
  131.5 4.5 %all-to-all-start.4 = ((bf16[8,128,2,64]{1,3,2,0:T(8,128)(2,1)}), bf16[8,128,2,64]{1,3,2,0:T(8,128)(2,1)S(1)}, u32[]{:S(2)}, u32[]{:S(2)}) async-start(bf16[8,128,2,64]{1,3,2,0:T(8,128)(2,1)} %broadcast_in_dim.58), calls=%async_computation.4 | async-start | bytes 524288 | tf_op jit(solution)/shard_map/all_to_all | solution.py:26
  136.6 12.0 %all-to-all-done.4 = bf16[8,128,2,64]{1,3,2,0:T(8,128)(2,1)S(1)} async-done(((bf16[8,128,2,64]{1,3,2,0:T(8,128)(2,1)}), bf16[8,128,2,64]{1,3,2,0:T(8,128)(2,1)S(1)}, u32[]{:S(2)}, u32[]{:S(2)}) %all-to-all-start.4) | async-done | bytes 262176 | tf_op jit(solution)/shard_map/all_to_all | solution.py:26
  148.6 1.1 broadcast_in_dim.60
  149.8 5.9 %all-to-all-start.5 = ((bf16[4,1024,2,64]{1,3,2,0:T(8,128)(2,1)}), bf16[4,1024,2,64]{1,3,2,0:T(8,128)(2,1)S(1)}, u32[]{:S(2)}, u32[]{:S(2)}) async-start(bf16[4,1024,2,64]{1,3,2,0:T(8,128)(2,1)} %broadcast_in_dim.60), calls=%async_computation.5 | async-start | bytes 2097152 | tf_op jit(solution)/shard_map/all_to_all | solution.py:26
  155.7 0.6 select_reduce_fusion.2
  156.3 12.9 %all-to-all-done.5 = bf16[4,1024,2,64]{1,3,2,0:T(8,128)(2,1)S(1)} async-done(((bf16[4,1024,2,64]{1,3,2,0:T(8,128)(2,1)}), bf16[4,1024,2,64]{1,3,2,0:T(8,128)(2,1)S(1)}, u32[]{:S(2)}, u32[]{:S(2)}) %all-to-all-start.5) | async-done | bytes 1048608 | tf_op jit(solution)/shard_map/all_to_all | solution.py:26
  169.3 1.3 fusion.2
  170.5 2.7 %copy-done.1 = f32[384,4096]{1,0:T(8,128)} copy-done((f32[384,4096]{1,0:T(8,128)}, f32[384,4096]{1,0:T(8,128)S(1)}, u32[]{:S(2)}) %copy-start.1) | copy-done | bytes 6291480
  173.2 1.4 fusion.5
  174.6 3.7 %select_reduce_fusion = (f32[384]{0:T(512)S(1)}, f32[384,8192]{1,0:T(8,128)S(1)}) fusion(s32[384]{0:T(512)S(1)} %pad_add_fusion.1, bf16[8192,2,64]{0,2,1:T(8,128)(2,1)} %all-gather.3.cloned.1.call-done, bf16[128,64]{0,1:T(8,128)(2,1)S(1)} %get-tuple-element.17, bf16[256,64]{0,1:T(8,128)(2,1)S(1)} %get-tuple-element.12), kind=kOutput, calls=%fused_computation.1 | convolution fusion | flops 415334016 | bytes 13683712 | tf_op jit(solution)/shard_map/dot_general | solution.py:40
  178.4 3.4 %fusion = f32[384]{0:T(512)S(1)} fusion(f32[384,8192]{1,0:T(8,128)S(1)} %get-tuple-element.23, f32[384]{0:T(512)S(1)} %get-tuple-element.22, s32[384]{0:T(512)S(1)} %pad_add_fusion.1), kind=kLoop, calls=%fused_computation.4 | loop fusion | flops 12582528 | bytes 12587520 | tf_op jit(solution)/shard_map/reduce_sum | solution.py:43
  181.8 2.5 %fusion.28 = f32[384,64]{0,1:T(8,128)S(1)} fusion(f32[384,8192]{1,0:T(8,128)S(1)} %get-tuple-element.23, f32[384]{0:T(512)S(1)} %get-tuple-element.22, s32[384]{0:T(512)S(1)} %pad_add_fusion.1, bf16[8192,2,64]{0,2,1:T(8,128)(2,1)S(1)} %copy-done.4, f32[384]{0:T(512)S(1)} %get-tuple-element.7), kind=kOutput, calls=%fused_computation.44 | convolution fusion | flops 415260672 | bytes 13735936 | tf_op jit(solution)/shard_map/dot_general | solution.py:44
  184.4 1.3 fusion.35
  185.9 0.7 reshape.295
  186.7 5.7 %all-to-all-start.6 = ((bf16[32,2,256]{2,1,0:T(2,128)(2,1)}), bf16[32,2,256]{2,1,0:T(2,128)(2,1)S(1)}, u32[]{:S(2)}, u32[]{:S(2)}) async-start(bf16[32,2,256]{2,1,0:T(2,128)(2,1)} %reshape.295), calls=%async_computation.6 | async-start | bytes 65536 | tf_op jit(solution)/shard_map/all_to_all | solution.py:171
  192.6 7.7 %all-to-all-done.6 = bf16[32,2,256]{2,1,0:T(2,128)(2,1)S(1)} async-done(((bf16[32,2,256]{2,1,0:T(2,128)(2,1)}), bf16[32,2,256]{2,1,0:T(2,128)(2,1)S(1)}, u32[]{:S(2)}, u32[]{:S(2)}) %all-to-all-start.6) | async-done | bytes 32800 | tf_op jit(solution)/shard_map/all_to_all | solution.py:171
  200.7 0.8 fusion.31
  (94 shorter events, 4.3 us)
Async XLA Ops:
  6.5 3.8 %copy-start = (bf16[3,1664,104]{1,2,0:T(8,128)(2,1)S(1)}, bf16[3,1664,104]{1,2,0:T(8,128)(2,1)}, u32[]{:S(2)}) copy-start(bf16[3,1664,104]{1,2,0:T(8,128)(2,1)} %param.16) | copy-start | bytes 3115012
  6.5 3.8 %copy-start.12 = (f32[1664]{0:T(1024)S(1)}, f32[1664]{0:T(1024)}, u32[]{:S(2)}) copy-start(f32[1664]{0:T(1024)} %param.14) | copy-start | bytes 19972
  6.5 3.8 %copy-start.11 = (f32[1664]{0:T(1024)S(1)}, f32[1664]{0:T(1024)}, u32[]{:S(2)}) copy-start(f32[1664]{0:T(1024)} %param.15) | copy-start | bytes 19972
  10.3 4.6 %copy-start.5 = (s32[512]{0:T(512)S(1)}, s32[512]{0:T(512)}, u32[]{:S(2)}) copy-start(s32[512]{0:T(512)} %param.13) | copy-start | bytes 6148
  10.3 7.0 %copy-start.3 = (bf16[256,1024]{1,0:T(8,128)(2,1)S(1)}, bf16[256,1024]{1,0:T(8,128)(2,1)}, u32[]{:S(2)}) copy-start(bf16[256,1024]{1,0:T(8,128)(2,1)} %param.20) | copy-start | bytes 1572868
  10.3 7.4 %copy-start.7 = (bf16[3,1024,64]{1,2,0:T(8,128)(2,1)S(1)}, bf16[3,1024,64]{1,2,0:T(8,128)(2,1)}, u32[]{:S(2)}) copy-start(bf16[3,1024,64]{1,2,0:T(8,128)(2,1)} %param.23) | copy-start | bytes 1179652
  10.3 7.4 %copy-start.13 = (f32[1024]{0:T(1024)S(1)}, f32[1024]{0:T(1024)}, u32[]{:S(2)}) copy-start(f32[1024]{0:T(1024)} %param.22) | copy-start | bytes 12292
  10.4 7.4 %copy-start.14 = (f32[1024]{0:T(1024)S(1)}, f32[1024]{0:T(1024)}, u32[]{:S(2)}) copy-start(f32[1024]{0:T(1024)} %param.21) | copy-start | bytes 12292
  11.4 9.0 %collective-permute-start = (bf16[2,512,104]{1,2,0:T(8,128)(2,1)S(1)}, bf16[2,512,104]{1,2,0:T(8,128)(2,1)S(1)}, u32[]{:S(2)}, u32[]{:S(2)}) collective-permute-start(bf16[2,512,104]{1,2,0:T(8,128)(2,1)S(1)} %slice.75), channel_id=1, source_target_pairs={{0,16},{16,0},{32,48},{48,32},{64,80},{80,64},{96,112},{112,96},{1... | collective-permute-start | bytes 638984 | tf_op jit(solution)/shard_map/ppermute | solution.py:92
  14.9 5.5 %collective-permute-start.1 = (s32[512]{0:T(512)S(1)}, s32[512]{0:T(512)S(1)}, u32[]{:S(2)}, u32[]{:S(2)}) collective-permute-start(s32[512]{0:T(512)S(1)} %copy-done.5), channel_id=1, source_target_pairs={{0,16},{16,0},{32,48},{48,32},{64,80},{80,64},{96,112},{112,96},{1... | collective-permute-start | bytes 6152 | tf_op jit(solution)/shard_map/ppermute | solution.py:92
  17.8 5.3 %copy-start.9 = (bf16[104,1664]{1,0:T(8,128)(2,1)S(1)}, bf16[104,1664]{1,0:T(8,128)(2,1)}, u32[]{:S(2)}) copy-start(bf16[104,1664]{1,0:T(8,128)(2,1)} %param.17) | copy-start | bytes 1038340
  20.4 0.7 copy-start.10
  21.0 1.4 copy-start.2
  41.4 13.4 %copy-start.6 = (s32[128]{0:T(128)S(1)}, s32[128]{0:T(128)}, u32[]{:S(2)}) copy-start(s32[128]{0:T(128)} %param.19) | copy-start | bytes 1540
  41.4 49.6 %all-to-all-start.1 = ((bf16[8,104,512]{2,1,0:T(8,128)(2,1)}), bf16[8,104,512]{2,1,0:T(8,128)(2,1)}, u32[]{:S(2)}, u32[]{:S(2)}) async-start(bf16[8,104,512]{2,1,0:T(8,128)(2,1)} %reduce_sum.167), calls=%async_computation.1 | async-start | bytes 1703936 | tf_op jit(solution)/shard_map/all_to_all | solution.py:35
  51.9 122.8 %all-gather.3.cloned.1.call-start = ((), (), s32[]{:S(2)}) async-start(), calls=%async_computation.7 | async-start | bytes 2162688 | tf_op jit(solution)/shard_map/all_gather | solution.py:74
  54.8 75.5 %copy-start.8 = (bf16[3,1024,64]{1,2,0:T(8,128)(2,1)S(1)}, bf16[3,1024,64]{1,2,0:T(8,128)(2,1)}, u32[]{:S(2)}) copy-start(bf16[3,1024,64]{1,2,0:T(8,128)(2,1)} %param.23) | copy-start | bytes 1179652
  95.7 18.5 %all-to-all-start.2 = ((bf16[16,8,1024]{2,1,0:T(8,128)(2,1)}), bf16[16,8,1024]{2,1,0:T(8,128)(2,1)S(1)}, u32[]{:S(2)}, u32[]{:S(2)}) async-start(bf16[16,8,1024]{2,1,0:T(8,128)(2,1)} %fusion.20), calls=%async_computation.2 | async-start | bytes 524288 | tf_op jit(solution)/shard_map/all_to_all | solution.py:35
  114.9 14.9 %all-to-all-start.3 = ((bf16[16,8,1024]{2,1,0:T(8,128)(2,1)}), bf16[16,8,1024]{2,1,0:T(8,128)(2,1)S(1)}, u32[]{:S(2)}, u32[]{:S(2)}) async-start(bf16[16,8,1024]{2,1,0:T(8,128)(2,1)} %broadcast_in_dim.53), calls=%async_computation.3 | async-start | bytes 524288 | tf_op jit(solution)/shard_map/all_to_all | solution.py:26
  131.5 17.1 %all-to-all-start.4 = ((bf16[8,128,2,64]{1,3,2,0:T(8,128)(2,1)}), bf16[8,128,2,64]{1,3,2,0:T(8,128)(2,1)S(1)}, u32[]{:S(2)}, u32[]{:S(2)}) async-start(bf16[8,128,2,64]{1,3,2,0:T(8,128)(2,1)} %broadcast_in_dim.58), calls=%async_computation.4 | async-start | bytes 524288 | tf_op jit(solution)/shard_map/all_to_all | solution.py:26
  149.8 19.4 %all-to-all-start.5 = ((bf16[4,1024,2,64]{1,3,2,0:T(8,128)(2,1)}), bf16[4,1024,2,64]{1,3,2,0:T(8,128)(2,1)S(1)}, u32[]{:S(2)}, u32[]{:S(2)}) async-start(bf16[4,1024,2,64]{1,3,2,0:T(8,128)(2,1)} %broadcast_in_dim.60), calls=%async_computation.5 | async-start | bytes 2097152 | tf_op jit(solution)/shard_map/all_to_all | solution.py:26
  170.5 2.7 %copy-start.1 = (f32[384,4096]{1,0:T(8,128)}, f32[384,4096]{1,0:T(8,128)S(1)}, u32[]{:S(2)}) copy-start(f32[384,4096]{1,0:T(8,128)S(1)} %get-tuple-element.25) | copy-start | bytes 18874372
  178.3 3.4 %copy-start.4 = (bf16[8192,2,64]{0,2,1:T(8,128)(2,1)S(1)}, bf16[8192,2,64]{0,2,1:T(8,128)(2,1)}, u32[]{:S(2)}) copy-start(bf16[8192,2,64]{0,2,1:T(8,128)(2,1)} %all-gather.3.cloned.1.call-done) | copy-start | bytes 6291460
  178.4 6.0 %slice-start = ((s8[6291456]{0:T(1024)(128)(4,1)}), s8[4194304]{0:T(1024)(128)(4,1)S(1)}, s32[]{:S(2)}) async-start(s8[6291456]{0:T(1024)(128)(4,1)} %bitcast.132), calls=%async_computation.8 | async-start | bytes 8388608
  181.8 2.6 %slice-start.1 = ((s8[6291456]{0:T(1024)(128)(4,1)}), s8[2097152]{0:T(1024)(128)(4,1)S(1)}, s32[]{:S(2)}) async-start(s8[6291456]{0:T(1024)(128)(4,1)} %bitcast.132), calls=%async_computation.9 | async-start | bytes 4194304
  186.7 13.7 %all-to-all-start.6 = ((bf16[32,2,256]{2,1,0:T(2,128)(2,1)}), bf16[32,2,256]{2,1,0:T(2,128)(2,1)S(1)}, u32[]{:S(2)}, u32[]{:S(2)}) async-start(bf16[32,2,256]{2,1,0:T(2,128)(2,1)} %reshape.295), calls=%async_computation.6 | async-start | bytes 65536 | tf_op jit(solution)/shard_map/all_to_all | solution.py:171
Sparse Core Ops, SparseCore 0:
  55.8 81.6 all-gather.2

commit v4 on v3

--- a/solution.py
+++ b/solution.py
@@ -71,9 +71,17 @@
     tproj = jnp.einsum("td,sde->ste", tnorm, dec_qkv, preferred_element_type=jnp.float32).astype(
         jnp.bfloat16
     )
-    text_kv = lax.all_gather(jnp.stack([tproj[1], tproj[2]], axis=1), GRP, axis=0, tiled=True)
-
-    all_pos = lax.all_gather(positions, GRP, axis=0, tiled=True)
+    digit = 128
+    pos_rows = jnp.stack([positions // digit, positions % digit]).astype(jnp.bfloat16)
+    extra = jnp.zeros((8, 2, DH), jnp.bfloat16).at[:2].set(pos_rows.reshape(2, 2, DH))
+    payload = jnp.concatenate([jnp.stack([tproj[1], tproj[2]], axis=1), extra], axis=0)
+    gathered = lax.all_gather(payload, GRP, axis=0, tiled=True).reshape(
+        groups, text_count + 8, 2, DH
+    )
+    text_kv = gathered[:, :text_count].reshape(groups * text_count, 2, DH)
+    digits = gathered[:, text_count : text_count + 2].reshape(groups, 2, 2 * DH).astype(jnp.int32)
+    all_pos = (digits[:, 0] * digit + digits[:, 1]).reshape(-1)
+
     place = jnp.arange(tok, dtype=jnp.int32)
     flags = jnp.sum((all_pos[None, :] == (here * tok + place)[:, None]).astype(jnp.int32), axis=1)
     free = 1 - flags

time: 210 us -> 231 us (1.10)
  local copies, waits for them, and re-layouts: 16.6 us -> 50 us
  starting transfers between devices: 43.2 us -> 26.9 us
  blocking collectives: 40.7 us -> 55.8 us
  waiting for transfers between devices: 56.5 us -> 45.8 us
    all_to_all x0 -> x2, blocking collectives: none -> 36.2 us  [a2a_gather(): got = lax.all_to_all(spread, axis, 0, 0, tiled=True)]
    all_gather x1 -> x0, blocking collectives: 34.8 us -> none  [body(): all_pos = lax.all_gather(positions, GRP, axis=0, tiled=True)]
    all_to_all x3 -> x1, waiting for transfers between devices: 35.6 us -> 12.5 us  [a2a_gather(): got = lax.all_to_all(spread, axis, 0, 0, tiled=True)]
    slice x1 -> x2, local copies, waits for them, and re-layouts: 0.07 us -> 19 us  [the longest x1 9.87 us: body(): text_kv[:, 1]]
    all_to_all x1 -> x2, blocking collectives: 5.95 us -> 19.6 us  [a2a_sum(): got = lax.all_to_all(parts, axis, 0, 0, tiled=True)]
    unnamed x37 -> x31, local copies, waits for them, and re-layouts: 7.84 us -> 21.4 us
    all_to_all x3 -> x1, starting transfers between devices: 13.9 us -> 4.74 us  [a2a_gather(): got = lax.all_to_all(spread, axis, 0, 0, tiled=True)]
    all_to_all x2 -> x1, waiting for transfers between devices: 11 us -> 19.7 us  [a2a_sum(): got = lax.all_to_all(parts, axis, 0, 0, tiled=True)]
  transfers between devices with their start and end apart: 9 -> 6, of which waited for: 6 -> 4; matrix products, arithmetic and copies ran while one was open for 9% -> 7% of each run, Pallas kernels for 0% -> 0%
where the time goes in v4:
time: 231 us; the launch traced here: 228 us
  blocking collectives  55.8 us (24%)
  local copies, waits for them, and re-layouts  50 us (22%)
  waiting for transfers between devices  45.8 us (20%)
  starting transfers between devices  26.9 us (12%)
  matrix products  18 us (8%)
  other arithmetic  17.9 us (8%)
  between operations  13.9 us (6%)
    all_to_all x2, blocking collectives, a2a_gather(): got = lax.all_to_all(spread, axis, 0, 0, tiled=True)  36.2 us
    unnamed x31, local copies, waits for them, and re-layouts  21.4 us
    all_to_all x1, waiting for transfers between devices, a2a_sum(): got = lax.all_to_all(parts, axis, 0, 0, tiled=True)  19.7 us
    all_to_all x2, blocking collectives, a2a_sum(): got = lax.all_to_all(parts, axis, 0, 0, tiled=True)  19.6 us
    all_to_all x1, waiting for transfers between devices, a2a_gather(): got = lax.all_to_all(spread, axis, 0, 0, tiled=True)  12.5 us
    all_to_all x1, starting transfers between devices, a2a_sum(): got = lax.all_to_all(parts, axis, 0, 0, tiled=True)  10.3 us
    slice x1, local copies, waits for them, and re-layouts, body(): text_kv[:, 1]  9.87 us
    slice x1, local copies, waits for them, and re-layouts, body(): text_kv = gathered[:, :text_count].reshape(groups * text_count, 2, DH)  9.17 us
  transfers between devices with their start and end apart: 6, of which 4 were waited for; matrix products, arithmetic and copies ran while one was open for 7% of the time, Pallas kernels for 0%

profile of v4, /device:TPU:6, one launch (start us, length us, event | category | flops | bytes accessed | tf_op | source)
XLA Modules:
  0.0 228.5 jit_solution(15894062635021470558)
XLA Ops:
  6.5 3.6 %collective-permute-start.1 = (s32[512]{0:T(512)}, s32[512]{0:T(512)S(1)}, u32[]{:S(2)}, u32[]{:S(2)}) collective-permute-start(s32[512]{0:T(512)} %param.15), channel_id=1, source_target_pairs={{0,16},{16,0},{32,48},{48,32},{64,80},{80,64},{96,112},{112,96},{1... | collective-permute-start | bytes 6152 | tf_op jit(solution)/shard_map/ppermute | solution.py:100
  10.2 2.8 %copy.57 = bf16[512,1664]{0,1:T(8,128)(2,1)S(1)} copy(bf16[512,1664]{1,0:T(8,128)(2,1)} %param.14) | data formatting | bytes 3407872 | tf_op args[0]
  13.3 0.5 multiply_reduce_fusion
  13.9 1.0 fusion.11
  14.9 2.5 %collective-permute-start = (bf16[2,512,104]{1,2,0:T(8,128)(2,1)S(1)}, bf16[2,512,104]{1,2,0:T(8,128)(2,1)S(1)}, u32[]{:S(2)}, u32[]{:S(2)}) collective-permute-start(bf16[2,512,104]{1,2,0:T(8,128)(2,1)S(1)} %slice.117), channel_id=1, source_target_pairs={{0,16},{16,0},{32,48},{48,32},{64,80},{80,64},{96,112},{112,96},{1... | collective-permute-start | bytes 638984 | tf_op jit(solution)/shard_map/ppermute | solution.py:100
  17.8 5.9 %collective-permute-done = bf16[2,512,104]{1,2,0:T(8,128)(2,1)S(1)} collective-permute-done((bf16[2,512,104]{1,2,0:T(8,128)(2,1)S(1)}, bf16[2,512,104]{1,2,0:T(8,128)(2,1)S(1)}, u32[]{:S(2)}, u32[]{:S(2)}) %collective-permute-start) | collective-permute-done | bytes 213024 | tf_op jit(solution)/shard_map/ppermute | solution.py:100
  23.7 0.6 fusion.10
  24.3 1.4 copy-done.2
  25.6 0.7 fusion.16
  26.3 4.2 %fusion.9 = bf16[1664,512]{0,1:T(8,128)(2,1)} fusion(bf16[104,1664]{1,0:T(8,128)(2,1)S(1)} %copy-done.8, f32[512,1024]{1,0:T(8,128)} %copy-done.2, f32[512]{0:T(512)S(1)} %fusion.16, f32[512]{0:T(512)S(1)} %get-tuple-element.38, s32[1024]{0:T(1024)S(1)} %pad_add_fusion, s32[512]{0:T(512)S(1)} %copy-done.5, bf16[2,512,104]{1,2,0:T(8,128)(2,1)S(1)} %slice.117, ...), kind=kOutput, calls=%fused_computation.18 | convolution fusion | flops 290738176 | bytes 4583424 | tf_op jit(solution)/shard_map/dot_general | solution.py:120
  30.5 3.6 %copy.59 = bf16[1664,512]{1,0:T(8,128)(2,1)} copy(bf16[1664,512]{0,1:T(8,128)(2,1)} %fusion.9) | data formatting | bytes 3407872 | tf_op jit(solution)/shard_map/convert_element_type | solution.py:122
  34.1 1.6 copy.60
  35.7 6.0 %all_to_all.42 = bf16[2,8,104,512]{3,2,1,0:T(8,128)(2,1)} all-to-all(bf16[2,8,104,512]{3,2,1,0:T(8,128)(2,1)S(1)} %copy.60), channel_id=1, replica_groups=mesh['gx'=4,'gy'=8,'z'=8,'core'=2] {'core'}, dimensions={0} | all-to-all | bytes 3407872 | tf_op jit(solution)/shard_map/all_to_all | solution.py:35
  41.7 3.0 %reduce_sum.167 = bf16[8,104,512]{2,1,0:T(8,128)(2,1)} reduce(bf16[2,8,104,512]{3,2,1,0:T(8,128)(2,1)} %all_to_all.42, bf16[]{:T(256)} %constant.133.clone.1), dimensions={0}, to_apply=%region_11.12 | reduce | flops 425984 | bytes 2555906 | tf_op jit(solution)/shard_map/reduce_sum | solution.py:36
  44.7 10.3 %all-to-all-start.1 = ((bf16[8,104,512]{2,1,0:T(8,128)(2,1)}), bf16[8,104,512]{2,1,0:T(8,128)(2,1)S(1)}, u32[]{:S(2)}, u32[]{:S(2)}) async-start(bf16[8,104,512]{2,1,0:T(8,128)(2,1)} %reduce_sum.167), calls=%async_computation.1 | async-start | bytes 1703936 | tf_op jit(solution)/shard_map/all_to_all | solution.py:35
  55.5 1.5 fusion.61
  57.0 0.8 copy.55
  57.9 2.2 convert_element_type.126
  60.1 19.7 %all-to-all-done.1 = bf16[8,104,512]{2,1,0:T(8,128)(2,1)S(1)} async-done(((bf16[8,104,512]{2,1,0:T(8,128)(2,1)}), bf16[8,104,512]{2,1,0:T(8,128)(2,1)S(1)}, u32[]{:S(2)}, u32[]{:S(2)}) %all-to-all-start.1) | async-done | bytes 852000 | tf_op jit(solution)/shard_map/all_to_all | solution.py:35
  79.9 1.0 fusion.85
  81.0 1.5 fusion.20
  82.6 13.6 %all_to_all.43 = bf16[16,8,1024]{2,1,0:T(8,128)(2,1)S(1)} all-to-all(bf16[16,8,1024]{2,1,0:T(8,128)(2,1)S(1)} %fusion.20), channel_id=1, replica_groups=mesh['gx'=4,'gy'=8,'z'=8,'core'=2] {'z','core'}, dimensions={0} | all-to-all | bytes 524288 | tf_op jit(solution)/shard_map/all_to_all | solution.py:35
  96.3 14.5 %all_to_all.44 = bf16[16,8,1024]{2,1,0:T(8,128)(2,1)S(1)} all-to-all(bf16[16,8,1024]{2,1,0:T(8,128)(2,1)S(1)} %broadcast_in_dim.53), channel_id=1, replica_groups=mesh['gx'=4,'gy'=8,'z'=8,'core'=2] {'z','core'}, dimensions={0} | all-to-all | bytes 524288 | tf_op jit(solution)/shard_map/all_to_all | solution.py:26
  111.3 0.4 fusion.71
  111.8 21.7 %all_to_all.45 = bf16[8,128,2,64]{1,3,2,0:T(8,128)(2,1)S(1)} all-to-all(bf16[8,128,2,64]{1,3,2,0:T(8,128)(2,1)S(1)} %broadcast_in_dim.58), channel_id=1, replica_groups=mesh['gx'=4,'gy'=8,'z'=8,'core'=2] {'gy'}, dimensions={0} | all-to-all | bytes 524288 | tf_op jit(solution)/shard_map/all_to_all | solution.py:26
  133.6 1.1 broadcast_in_dim.60
  134.7 4.7 %all-to-all-start.5 = ((bf16[4,1024,2,64]{1,3,2,0:T(8,128)(2,1)}), bf16[4,1024,2,64]{1,3,2,0:T(8,128)(2,1)S(1)}, u32[]{:S(2)}, u32[]{:S(2)}) async-start(bf16[4,1024,2,64]{1,3,2,0:T(8,128)(2,1)} %broadcast_in_dim.60), calls=%async_computation.5 | async-start | bytes 2097152 | tf_op jit(solution)/shard_map/all_to_all | solution.py:26
  139.9 12.5 %all-to-all-done.5 = bf16[4,1024,2,64]{1,3,2,0:T(8,128)(2,1)S(1)} async-done(((bf16[4,1024,2,64]{1,3,2,0:T(8,128)(2,1)}), bf16[4,1024,2,64]{1,3,2,0:T(8,128)(2,1)S(1)}, u32[]{:S(2)}, u32[]{:S(2)}) %all-to-all-start.5) | async-done | bytes 1048608 | tf_op jit(solution)/shard_map/all_to_all | solution.py:26
  152.4 1.1 copy.74
  153.5 0.8 copy_convert_fusion
  154.4 9.2 %slice.122 = bf16[32,256,2,64]{3,2,1,0:T(2,128)(2,1)} slice(bf16[32,264,2,64]{3,2,1,0:T(2,128)(2,1)} %bitcast.139), slice={[0:32], [0:256], [0:2], [0:64]} | slice | bytes 4194304 | tf_op jit(solution)/shard_map/slice | solution.py:81
  163.6 0.8 convert_reduce_fusion
  164.7 0.6 select_reduce_fusion.2
  165.3 0.5 convert_reduce_fusion.2
  165.8 9.9 %fusion.121 = (bf16[8192,1,64]{2,1,0:T(2,128)(2,1)}, bf16[8192,1,64]{2,1,0:T(2,128)(2,1)}) fusion(bf16[8192,2,64]{2,1,0:T(2,128)(2,1)} %bitcast.135), kind=kLoop, calls=%fused_computation.186 | loop fusion | bytes 4194304 | tf_op jit(solution)/shard_map/slice | solution.py:157
  175.7 8.2 %copy.71 = bf16[8192,1,64]{0,2,1:T(8,128)(2,1)S(1)} copy(bf16[8192,1,64]{2,1,0:T(2,128)(2,1)} %get-tuple-element.25) | data formatting | bytes 2097152
  183.9 8.2 %copy.72 = bf16[8192,1,64]{0,2,1:T(8,128)(2,1)S(1)} copy(bf16[8192,1,64]{2,1,0:T(2,128)(2,1)} %get-tuple-element.24) | data formatting | bytes 2097152
  192.0 0.3 reduce-window.9
  192.9 2.5 %select_reduce_fusion = (f32[384]{0:T(512)S(1)}, f32[384,8192]{1,0:T(8,128)S(1)}) fusion(s32[384]{0:T(512)S(1)} %pad_add_fusion.1, bf16[8192,1,64]{0,2,1:T(8,128)(2,1)S(1)} %copy.71, bf16[128,64]{0,1:T(8,128)(2,1)S(1)} %get-tuple-element.31, bf16[256,64]{0,1:T(8,128)(2,1)S(1)} %get-tuple-element.26), kind=kOutput, calls=%fused_computation.1 | convolution fusion | flops 415334016 | bytes 13683712 | tf_op jit(solution)/shard_map/dot_general | solution.py:40
  195.4 1.3 fusion.2
  196.7 1.4 fusion.5
  198.1 3.6 %fusion = f32[384]{0:T(512)S(1)} fusion(f32[384,8192]{1,0:T(8,128)S(1)} %get-tuple-element.41, f32[384]{0:T(512)S(1)} %get-tuple-element.40, s32[384]{0:T(512)S(1)} %pad_add_fusion.1), kind=kLoop, calls=%fused_computation.4 | loop fusion | flops 12582528 | bytes 12587520 | tf_op jit(solution)/shard_map/reduce_sum | solution.py:43
  201.8 2.7 %fusion.28 = f32[384,64]{0,1:T(8,128)S(1)} fusion(f32[384,8192]{1,0:T(8,128)S(1)} %get-tuple-element.41, f32[384]{0:T(512)S(1)} %get-tuple-element.40, s32[384]{0:T(512)S(1)} %pad_add_fusion.1, bf16[8192,1,64]{0,2,1:T(8,128)(2,1)S(1)} %copy.72, f32[384]{0:T(512)S(1)} %get-tuple-element.19), kind=kOutput, calls=%fused_computation.44 | convolution fusion | flops 415260672 | bytes 13734400 | tf_op jit(solution)/shard_map/dot_general | solution.py:44
  204.5 1.3 fusion.35
  206.1 0.7 reshape.359
  206.8 5.7 %all-to-all-start.6 = ((bf16[32,2,256]{2,1,0:T(2,128)(2,1)}), bf16[32,2,256]{2,1,0:T(2,128)(2,1)S(1)}, u32[]{:S(2)}, u32[]{:S(2)}) async-start(bf16[32,2,256]{2,1,0:T(2,128)(2,1)} %reshape.359), calls=%async_computation.6 | async-start | bytes 65536 | tf_op jit(solution)/shard_map/all_to_all | solution.py:179
  212.7 7.7 %all-to-all-done.6 = bf16[32,2,256]{2,1,0:T(2,128)(2,1)S(1)} async-done(((bf16[32,2,256]{2,1,0:T(2,128)(2,1)}), bf16[32,2,256]{2,1,0:T(2,128)(2,1)S(1)}, u32[]{:S(2)}, u32[]{:S(2)}) %all-to-all-start.6) | async-done | bytes 32800 | tf_op jit(solution)/shard_map/all_to_all | solution.py:179
  220.8 0.8 fusion.31
  (92 shorter events, 4.4 us)
Async XLA Ops:
  6.5 7.3 %copy-start = (bf16[3,1664,104]{1,2,0:T(8,128)(2,1)S(1)}, bf16[3,1664,104]{1,2,0:T(8,128)(2,1)}, u32[]{:S(2)}) copy-start(bf16[3,1664,104]{1,2,0:T(8,128)(2,1)} %param.18) | copy-start | bytes 3115012
  6.5 7.3 %copy-start.9 = (f32[1664]{0:T(1024)S(1)}, f32[1664]{0:T(1024)}, u32[]{:S(2)}) copy-start(f32[1664]{0:T(1024)} %param.17) | copy-start | bytes 19972
  6.5 7.3 %copy-start.10 = (f32[1664]{0:T(1024)S(1)}, f32[1664]{0:T(1024)}, u32[]{:S(2)}) copy-start(f32[1664]{0:T(1024)} %param.16) | copy-start | bytes 19972
  6.5 11.2 %collective-permute-start.1 = (s32[512]{0:T(512)}, s32[512]{0:T(512)S(1)}, u32[]{:S(2)}, u32[]{:S(2)}) collective-permute-start(s32[512]{0:T(512)} %param.15), channel_id=1, source_target_pairs={{0,16},{16,0},{32,48},{48,32},{64,80},{80,64},{96,112},{112,96},{1... | collective-permute-start | bytes 6152 | tf_op jit(solution)/shard_map/ppermute | solution.py:100
  13.8 3.6 %copy-start.6 = (s32[128]{0:T(128)S(1)}, s32[128]{0:T(128)}, u32[]{:S(2)}) copy-start(s32[128]{0:T(128)} %param.21) | copy-start | bytes 1540
  13.9 3.6 %copy-start.3 = (bf16[256,1024]{1,0:T(8,128)(2,1)S(1)}, bf16[256,1024]{1,0:T(8,128)(2,1)}, u32[]{:S(2)}) copy-start(bf16[256,1024]{1,0:T(8,128)(2,1)} %param.22) | copy-start | bytes 1572868
  13.9 3.9 %copy-start.5 = (s32[512]{0:T(512)S(1)}, s32[512]{0:T(512)}, u32[]{:S(2)}) copy-start(s32[512]{0:T(512)} %param.15) | copy-start | bytes 6148
  14.8 11.4 %copy-start.8 = (bf16[104,1664]{1,0:T(8,128)(2,1)S(1)}, bf16[104,1664]{1,0:T(8,128)(2,1)}, u32[]{:S(2)}) copy-start(bf16[104,1664]{1,0:T(8,128)(2,1)} %param.19) | copy-start | bytes 1038340
  14.9 8.7 %collective-permute-start = (bf16[2,512,104]{1,2,0:T(8,128)(2,1)S(1)}, bf16[2,512,104]{1,2,0:T(8,128)(2,1)S(1)}, u32[]{:S(2)}, u32[]{:S(2)}) collective-permute-start(bf16[2,512,104]{1,2,0:T(8,128)(2,1)S(1)} %slice.117), channel_id=1, source_target_pairs={{0,16},{16,0},{32,48},{48,32},{64,80},{80,64},{96,112},{112,96},{1... | collective-permute-start | bytes 638984 | tf_op jit(solution)/shard_map/ppermute | solution.py:100
  24.3 1.4 copy-start.2
  35.7 19.8 %copy-start.11 = (f32[1024]{0:T(1024)S(1)}, f32[1024]{0:T(1024)}, u32[]{:S(2)}) copy-start(f32[1024]{0:T(1024)} %param.24) | copy-start | bytes 12292
  35.7 19.7 %copy-start.12 = (f32[1024]{0:T(1024)S(1)}, f32[1024]{0:T(1024)}, u32[]{:S(2)}) copy-start(f32[1024]{0:T(1024)} %param.23) | copy-start | bytes 12292
  44.7 35.2 %all-to-all-start.1 = ((bf16[8,104,512]{2,1,0:T(8,128)(2,1)}), bf16[8,104,512]{2,1,0:T(8,128)(2,1)S(1)}, u32[]{:S(2)}, u32[]{:S(2)}) async-start(bf16[8,104,512]{2,1,0:T(8,128)(2,1)} %reduce_sum.167), calls=%async_computation.1 | async-start | bytes 1703936 | tf_op jit(solution)/shard_map/all_to_all | solution.py:35
  55.0 98.5 %all-gather.2.cloned.1.call-start = ((), (), s32[]{:S(2)}) async-start(), calls=%async_computation.7 | async-start | bytes 4460544 | tf_op jit(solution)/shard_map/all_gather | solution.py:78
  60.1 51.2 %copy-start.7 = (bf16[3,1024,64]{1,2,0:T(8,128)(2,1)S(1)}, bf16[3,1024,64]{1,2,0:T(8,128)(2,1)}, u32[]{:S(2)}) copy-start(bf16[3,1024,64]{1,2,0:T(8,128)(2,1)} %param.25) | copy-start | bytes 1179652
  134.7 17.7 %all-to-all-start.5 = ((bf16[4,1024,2,64]{1,3,2,0:T(8,128)(2,1)}), bf16[4,1024,2,64]{1,3,2,0:T(8,128)(2,1)S(1)}, u32[]{:S(2)}, u32[]{:S(2)}) async-start(bf16[4,1024,2,64]{1,3,2,0:T(8,128)(2,1)} %broadcast_in_dim.60), calls=%async_computation.5 | async-start | bytes 2097152 | tf_op jit(solution)/shard_map/all_to_all | solution.py:26
  192.9 2.5 %copy-start.4 = (bf16[4,2,8,8,1024]{4,3,0,2,1:T(8,128)(2,1)S(1)}, bf16[4,2,8,8,1024]{4,3,0,2,1:T(8,128)(2,1)}, u32[]{:S(2)}) copy-start(bf16[4,2,8,8,1024]{4,3,0,2,1:T(8,128)(2,1)} %copy.74) | copy-start | bytes 3145732
  204.4 17.2 %copy-start.1 = (bf16[3,1664,104]{1,2,0:T(8,128)(2,1)S(1)}, bf16[3,1664,104]{1,2,0:T(8,128)(2,1)}, u32[]{:S(2)}) copy-start(bf16[3,1664,104]{1,2,0:T(8,128)(2,1)} %param.18) | copy-start | bytes 3115012
  206.8 13.7 %all-to-all-start.6 = ((bf16[32,2,256]{2,1,0:T(2,128)(2,1)}), bf16[32,2,256]{2,1,0:T(2,128)(2,1)S(1)}, u32[]{:S(2)}, u32[]{:S(2)}) async-start(bf16[32,2,256]{2,1,0:T(2,128)(2,1)} %reshape.359), calls=%async_computation.6 | async-start | bytes 65536 | tf_op jit(solution)/shard_map/all_to_all | solution.py:179
Sparse Core Ops, SparseCore 0:
  59.0 90.5 all-gather.1

commit v5 on v3

--- a/solution.py
+++ b/solution.py
@@ -71,9 +71,17 @@
     tproj = jnp.einsum("td,sde->ste", tnorm, dec_qkv, preferred_element_type=jnp.float32).astype(
         jnp.bfloat16
     )
-    text_kv = lax.all_gather(jnp.stack([tproj[1], tproj[2]], axis=1), GRP, axis=0, tiled=True)
-
-    all_pos = lax.all_gather(positions, GRP, axis=0, tiled=True)
+    digit = 128
+    pad_rows = 8
+    lanes = 2 * DH
+    pos_rows = jnp.stack([positions // digit, positions % digit]).astype(jnp.bfloat16)
+    extra = jnp.zeros((pad_rows, lanes), jnp.bfloat16).at[:2].set(pos_rows.reshape(2, lanes))
+    payload = jnp.concatenate([jnp.concatenate([tproj[1], tproj[2]], axis=1), extra], axis=0)
+    text_kv = lax.all_gather(payload, GRP, axis=0, tiled=True)
+    digits = text_kv.reshape(groups, text_count + pad_rows, lanes)[:, text_count : text_count + 2]
+    digits = digits.astype(jnp.int32)
+    all_pos = (digits[:, 0] * digit + digits[:, 1]).reshape(-1)
+
     place = jnp.arange(tok, dtype=jnp.int32)
     flags = jnp.sum((all_pos[None, :] == (here * tok + place)[:, None]).astype(jnp.int32), axis=1)
     free = 1 - flags
@@ -130,7 +138,7 @@
     mproj = jnp.einsum("td,sde->ste", mnorm, dec_qkv, preferred_element_type=jnp.float32).astype(
         jnp.bfloat16
     )
-    merged_kv = grp_gather(jnp.stack([mproj[1], mproj[2]], axis=1))
+    merged_kv = grp_gather(jnp.concatenate([mproj[1], mproj[2]], axis=1))
 
     dquery = jnp.concatenate([tproj[0], mproj[0]], axis=0)
     query_pos = jnp.concatenate([own_text_pos, positions], axis=0)
@@ -144,12 +152,15 @@
     merged_limit = block * text_count + (positions - block * tok + 1 - seen)
     text_limit = here * text_count + jnp.arange(text_count, dtype=jnp.int32) + 1
     limit = jnp.concatenate([text_limit, merged_limit], axis=0)
-    text_key = jnp.arange(groups * text_count, dtype=jnp.int32)
+    key_row = jnp.arange(groups * (text_count + pad_rows), dtype=jnp.int32)
+    key_grp = key_row // (text_count + pad_rows)
+    key_in = key_row % (text_count + pad_rows)
+    text_key = jnp.where(key_in < text_count, key_grp * text_count + key_in, groups * tok)
     top_t, total_t, acc_t = attend_part(
-        dquery, text_key[None, :] < limit[:, None], text_kv[:, 0], text_kv[:, 1]
+        dquery, text_key[None, :] < limit[:, None], text_kv[:, :DH], text_kv[:, DH:]
     )
     top_m, total_m, acc_m = attend_part(
-        dquery, all_pos[None, :] <= query_pos[:, None], merged_kv[:, 0], merged_kv[:, 1]
+        dquery, all_pos[None, :] <= query_pos[:, None], merged_kv[:, :DH], merged_kv[:, DH:]
     )
     best = jnp.maximum(top_t, top_m)
     scale_t = jnp.exp(top_t - best)

time: 210 us -> 199 us (0.948)
  blocking collectives: 40.7 us -> 19.6 us
  waiting for transfers between devices: 56.5 us -> 69.1 us
  starting transfers between devices: 43.2 us -> 36.6 us
  matrix products: 18.8 us -> 23 us
    all_gather x1 -> x0, blocking collectives: 34.8 us -> none  [body(): all_pos = lax.all_gather(positions, GRP, axis=0, tiled=True)]
    all_to_all x1 -> x2, blocking collectives: 5.95 us -> 19.6 us  [a2a_sum(): got = lax.all_to_all(parts, axis, 0, 0, tiled=True)]
    all_to_all x2 -> x1, waiting for transfers between devices: 11 us -> 20.2 us  [a2a_sum(): got = lax.all_to_all(parts, axis, 0, 0, tiled=True)]
    all_to_all x2 -> x1, starting transfers between devices: 17.8 us -> 10.3 us  [a2a_sum(): got = lax.all_to_all(parts, axis, 0, 0, tiled=True)]
    dot_general x2, matrix products: 3.79 us -> 8.05 us  [attend_part(): jnp.dot(expo.astype(jnp.bfloat16), values, preferred_element_type=jnp.flo...]
    ppermute x2, waiting for transfers between devices: 2.13 us -> 5.71 us  [body(): partner_kv, partner_ids = lax.ppermute((proj[1:], patch_image), 'gy', swap)]
    all_to_all x3, waiting for transfers between devices: 35.6 us -> 33.2 us  [a2a_gather(): got = lax.all_to_all(spread, axis, 0, 0, tiled=True)]
    all_gather x1, waiting for transfers between devices: 0.02 us -> 2.31 us  [body(): text_kv = lax.all_gather(payload, GRP, axis=0, tiled=True)]
  transfers between devices with their start and end apart: 9 -> 8, of which waited for: 6 -> 7; matrix products, arithmetic and copies ran while one was open for 9% -> 11% of each run, Pallas kernels for 0% -> 0%
where the time goes in v5:
time: 199 us; the launch traced here: 197 us
  waiting for transfers between devices  69.1 us (35%)
  starting transfers between devices  36.6 us (18%)
  matrix products  23 us (12%)
  blocking collectives  19.6 us (10%)
  other arithmetic  17.9 us (9%)
  local copies, waits for them, and re-layouts  17.3 us (9%)
  between operations  13.9 us (7%)
    all_to_all x3, waiting for transfers between devices, a2a_gather(): got = lax.all_to_all(spread, axis, 0, 0, tiled=True)  33.2 us
    all_to_all x1, waiting for transfers between devices, a2a_sum(): got = lax.all_to_all(parts, axis, 0, 0, tiled=True)  20.2 us
    all_to_all x2, blocking collectives, a2a_sum(): got = lax.all_to_all(parts, axis, 0, 0, tiled=True)  19.6 us
    all_to_all x3, starting transfers between devices, a2a_gather(): got = lax.all_to_all(spread, axis, 0, 0, tiled=True)  14.5 us
    all_to_all x1, starting transfers between devices, a2a_sum(): got = lax.all_to_all(parts, axis, 0, 0, tiled=True)  10.3 us
    dot_general x2, matrix products, attend_part(): jnp.dot(expo.astype(jnp.bfloat16), values, preferred_element_type=jnp.flo...  8.05 us
    all_to_all x1, waiting for transfers between devices, body(): got = lax.all_to_all(packed, GRP, 0, 0, tiled=True)  7.71 us
    unnamed x31, local copies, waits for them, and re-layouts  6.85 us
  transfers between devices with their start and end apart: 8, of which 7 were waited for; matrix products, arithmetic and copies ran while one was open for 11% of the time, Pallas kernels for 0%

profile of v5, /device:TPU:6, one launch (start us, length us, event | category | flops | bytes accessed | tf_op | source)
XLA Modules:
  0.0 197.4 jit_solution(2782912515790446769)
XLA Ops:
  6.5 3.6 %collective-permute-start.1 = (s32[512]{0:T(512)}, s32[512]{0:T(512)S(1)}, u32[]{:S(2)}, u32[]{:S(2)}) collective-permute-start(s32[512]{0:T(512)} %param.15), channel_id=1, source_target_pairs={{0,16},{16,0},{32,48},{48,32},{64,80},{80,64},{96,112},{112,96},{1... | collective-permute-start | bytes 6152 | tf_op jit(solution)/shard_map/ppermute | solution.py:100
  10.2 2.8 %copy.47 = bf16[512,1664]{0,1:T(8,128)(2,1)S(1)} copy(bf16[512,1664]{1,0:T(8,128)(2,1)} %param.14) | data formatting | bytes 3407872 | tf_op args[0]
  13.3 0.5 multiply_reduce_fusion
  13.9 1.0 fusion.14
  14.9 2.4 %collective-permute-start = (bf16[2,512,104]{1,2,0:T(8,128)(2,1)S(1)}, bf16[2,512,104]{1,2,0:T(8,128)(2,1)S(1)}, u32[]{:S(2)}, u32[]{:S(2)}) collective-permute-start(bf16[2,512,104]{1,2,0:T(8,128)(2,1)S(1)} %slice.108), channel_id=1, source_target_pairs={{0,16},{16,0},{32,48},{48,32},{64,80},{80,64},{96,112},{112,96},{1... | collective-permute-start | bytes 638984 | tf_op jit(solution)/shard_map/ppermute | solution.py:100
  17.8 5.7 %collective-permute-done = bf16[2,512,104]{1,2,0:T(8,128)(2,1)S(1)} collective-permute-done((bf16[2,512,104]{1,2,0:T(8,128)(2,1)S(1)}, bf16[2,512,104]{1,2,0:T(8,128)(2,1)S(1)}, u32[]{:S(2)}, u32[]{:S(2)}) %collective-permute-start) | collective-permute-done | bytes 213024 | tf_op jit(solution)/shard_map/ppermute | solution.py:100
  23.5 0.6 fusion.13
  24.2 1.3 copy-done.2
  25.5 0.7 fusion.19
  26.1 4.3 %fusion.10 = bf16[1664,512]{0,1:T(8,128)(2,1)} fusion(bf16[104,1664]{1,0:T(8,128)(2,1)} %param.19, f32[512,1024]{1,0:T(8,128)} %copy-done.2, f32[512]{0:T(512)S(1)} %fusion.19, f32[512]{0:T(512)S(1)} %get-tuple-element.36, s32[1024]{0:T(1024)S(1)} %pad_add_fusion, s32[512]{0:T(512)S(1)} %copy-done.4, bf16[2,512,104]{1,2,0:T(8,128)(2,1)S(1)} %slice.108, ...), kind=kOutput, calls=%fused_computation.18 | convolution fusion | flops 290738176 | bytes 4583424 | tf_op jit(solution)/shard_map/dot_general | solution.py:120
  30.4 3.6 %copy.49 = bf16[1664,512]{1,0:T(8,128)(2,1)} copy(bf16[1664,512]{0,1:T(8,128)(2,1)} %fusion.10) | data formatting | bytes 3407872 | tf_op jit(solution)/shard_map/convert_element_type | solution.py:122
  34.0 1.6 copy.50
  35.7 6.0 %all_to_all.42 = bf16[2,8,104,512]{3,2,1,0:T(8,128)(2,1)} all-to-all(bf16[2,8,104,512]{3,2,1,0:T(8,128)(2,1)S(1)} %copy.50), channel_id=1, replica_groups=mesh['gx'=4,'gy'=8,'z'=8,'core'=2] {'core'}, dimensions={0} | all-to-all | bytes 3407872 | tf_op jit(solution)/shard_map/all_to_all | solution.py:35
  41.6 2.9 %reduce_sum.167 = bf16[8,104,512]{2,1,0:T(8,128)(2,1)} reduce(bf16[2,8,104,512]{3,2,1,0:T(8,128)(2,1)} %all_to_all.42, bf16[]{:T(256)} %constant.152.clone.1), dimensions={0}, to_apply=%region_11.12 | reduce | flops 425984 | bytes 2555906 | tf_op jit(solution)/shard_map/reduce_sum | solution.py:36
  44.5 10.3 %all-to-all-start.1 = ((bf16[8,104,512]{2,1,0:T(8,128)(2,1)}), bf16[8,104,512]{2,1,0:T(8,128)(2,1)}, u32[]{:S(2)}, u32[]{:S(2)}) async-start(bf16[8,104,512]{2,1,0:T(8,128)(2,1)} %reduce_sum.167), calls=%async_computation.1 | async-start | bytes 1703936 | tf_op jit(solution)/shard_map/all_to_all | solution.py:35
  55.1 1.4 fusion.72
  56.6 0.7 copy.45
  57.3 2.2 %convert_element_type.121 = f32[512,1664]{0,1:T(8,128)} convert(bf16[512,1664]{0,1:T(8,128)(2,1)S(1)} %copy.47) | non-fusion elementwise | flops 851968 | bytes 5111808 | tf_op jit(solution)/shard_map/convert_element_type | solution.py:93
  59.6 20.2 %all-to-all-done.1 = bf16[8,104,512]{2,1,0:T(8,128)(2,1)} async-done(((bf16[8,104,512]{2,1,0:T(8,128)(2,1)}), bf16[8,104,512]{2,1,0:T(8,128)(2,1)}, u32[]{:S(2)}, u32[]{:S(2)}) %all-to-all-start.1) | async-done | bytes 852000 | tf_op jit(solution)/shard_map/all_to_all | solution.py:35
  79.8 1.3 convert_reduce_fusion.3
  81.1 1.0 fusion.96
  82.2 1.5 fusion.23
  83.7 13.6 %all_to_all.43 = bf16[16,8,1024]{2,1,0:T(8,128)(2,1)S(1)} all-to-all(bf16[16,8,1024]{2,1,0:T(8,128)(2,1)S(1)} %fusion.23), channel_id=1, replica_groups=mesh['gx'=4,'gy'=8,'z'=8,'core'=2] {'z','core'}, dimensions={0} | all-to-all | bytes 524288 | tf_op jit(solution)/shard_map/all_to_all | solution.py:35
  97.4 0.7 broadcast_in_dim.59
  98.1 3.5 %all-to-all-start.3 = ((bf16[16,8,1024]{2,1,0:T(8,128)(2,1)}), bf16[16,8,1024]{2,1,0:T(8,128)(2,1)S(1)}, u32[]{:S(2)}, u32[]{:S(2)}) async-start(bf16[16,8,1024]{2,1,0:T(8,128)(2,1)} %broadcast_in_dim.59), calls=%async_computation.3 | async-start | bytes 524288 | tf_op jit(solution)/shard_map/all_to_all | solution.py:26
  101.8 11.2 %all-to-all-done.3 = bf16[16,8,1024]{2,1,0:T(8,128)(2,1)S(1)} async-done(((bf16[16,8,1024]{2,1,0:T(8,128)(2,1)}), bf16[16,8,1024]{2,1,0:T(8,128)(2,1)S(1)}, u32[]{:S(2)}, u32[]{:S(2)}) %all-to-all-start.3) | async-done | bytes 262176 | tf_op jit(solution)/shard_map/all_to_all | solution.py:26
  114.1 0.7 broadcast_in_dim.63
  114.8 6.2 %all-to-all-start.4 = ((bf16[8,128,128]{2,1,0:T(8,128)(2,1)}), bf16[8,128,128]{2,1,0:T(8,128)(2,1)S(1)}, u32[]{:S(2)}, u32[]{:S(2)}) async-start(bf16[8,128,128]{2,1,0:T(8,128)(2,1)} %broadcast_in_dim.63), calls=%async_computation.4 | async-start | bytes 524288 | tf_op jit(solution)/shard_map/all_to_all | solution.py:26
  121.4 14.9 %all-to-all-done.4 = bf16[8,128,128]{2,1,0:T(8,128)(2,1)S(1)} async-done(((bf16[8,128,128]{2,1,0:T(8,128)(2,1)}), bf16[8,128,128]{2,1,0:T(8,128)(2,1)S(1)}, u32[]{:S(2)}, u32[]{:S(2)}) %all-to-all-start.4) | async-done | bytes 262176 | tf_op jit(solution)/shard_map/all_to_all | solution.py:26
  136.3 1.1 broadcast_in_dim.65
  137.4 4.8 %all-to-all-start.5 = ((bf16[4,1024,128]{2,1,0:T(8,128)(2,1)}), bf16[4,1024,128]{2,1,0:T(8,128)(2,1)S(1)}, u32[]{:S(2)}, u32[]{:S(2)}) async-start(bf16[4,1024,128]{2,1,0:T(8,128)(2,1)} %broadcast_in_dim.65), calls=%async_computation.5 | async-start | bytes 2097152 | tf_op jit(solution)/shard_map/all_to_all | solution.py:26
  142.2 2.3 %all-gather.2.cloned.1.call-done = bf16[8448,128]{1,0:T(8,128)(2,1)} async-done(((bf16[264,128]{1,0:T(8,128)(2,1)}), bf16[8448,128]{1,0:T(8,128)(2,1)}) %all-gather.2.cloned.1.call-update) | async-done | bytes 2162704 | tf_op jit(solution)/shard_map/all_gather | solution.py:80
  144.5 0.8 slice.104
  145.4 0.8 convert_reduce_fusion
  146.5 0.5 convert_reduce_fusion.2
  147.9 0.6 select_reduce_fusion.1
  148.5 7.0 %all-to-all-done.5 = bf16[4,1024,128]{2,1,0:T(8,128)(2,1)S(1)} async-done(((bf16[4,1024,128]{2,1,0:T(8,128)(2,1)}), bf16[4,1024,128]{2,1,0:T(8,128)(2,1)S(1)}, u32[]{:S(2)}, u32[]{:S(2)}) %all-to-all-start.5) | async-done | bytes 1048608 | tf_op jit(solution)/shard_map/all_to_all | solution.py:26
  155.5 1.6 fusion.5
  157.1 1.4 fusion.6
  158.5 1.8 copy-done.6
  160.3 3.0 %fusion = (f32[384]{0:T(512)S(1)}, f32[384,8448]{1,0:T(8,128)S(1)}) fusion(s32[8448]{0:T(1024)S(1)} %fusion.115, s32[384]{0:T(512)S(1)} %pad_add_fusion.1, bf16[8448,128]{1,0:T(8,128)(2,1)S(1)} %copy-done.6, bf16[128,64]{0,1:T(8,128)(2,1)S(1)} %get-tuple-element.27, bf16[256,64]{0,1:T(8,128)(2,1)S(1)} %get-tuple-element.24), kind=kOutput, calls=%fused_computation.3 | convolution fusion | flops 428310144 | bytes 15224832 | tf_op jit(solution)/shard_map/dot_general | solution.py:40
  163.3 3.2 %fusion.1 = f32[384]{0:T(512)S(1)} fusion(f32[384,8448]{1,0:T(8,128)S(1)} %get-tuple-element.41, f32[384]{0:T(512)S(1)} %get-tuple-element.40, s32[8448]{0:T(1024)S(1)} %fusion.115, s32[384]{0:T(512)S(1)} %pad_add_fusion.1), kind=kLoop, calls=%fused_computation.4 | loop fusion | flops 12975744 | bytes 13014528 | tf_op jit(solution)/shard_map/reduce_sum | solution.py:43
  166.6 4.7 %fusion.25 = f32[384,64]{0,1:T(8,128)S(1)} fusion(f32[384,4096]{1,0:T(8,128)} %copy-done.1, f32[384]{0:T(512)S(1)} %get-tuple-element.38, s32[4096]{0:T(1024)S(1)} %get-tuple-element.30, s32[384]{0:T(512)S(1)} %pad_add_fusion.2, bf16[4096,128]{1,0:T(8,128)(2,1)S(1)} %bitcast.118, f32[384]{0:T(512)S(1)} %get-tuple-element.19), kind=kOutput, calls=%fused_computation.44 | convolution fusion | flops 207642624 | bytes 7459328 | tf_op jit(solution)/shard_map/dot_general | solution.py:44
  171.3 3.4 %fusion.44 = bf16[384,64]{0,1:T(8,128)(2,1)S(1)} fusion(f32[384,64]{0,1:T(8,128)S(1)} %fusion.25, bf16[8448,128]{1,0:T(8,128)(2,1)S(1)} %copy-done.7, f32[384,8448]{1,0:T(8,128)S(1)} %get-tuple-element.41, f32[384]{0:T(512)S(1)} %get-tuple-element.40, s32[8448]{0:T(1024)S(1)} %fusion.115, s32[384]{0:T(512)S(1)} %pad_add_fusion.1, ...), kind=kOutput, calls=%fused_computation.50 | convolution fusion | flops 428310528 | bytes 15326208 | tf_op jit(solution)/shard_map/dot_general | solution.py:44
  175.0 0.7 reshape.359
  175.7 5.7 %all-to-all-start.6 = ((bf16[32,2,256]{2,1,0:T(2,128)(2,1)}), bf16[32,2,256]{2,1,0:T(2,128)(2,1)S(1)}, u32[]{:S(2)}, u32[]{:S(2)}) async-start(bf16[32,2,256]{2,1,0:T(2,128)(2,1)} %reshape.359), calls=%async_computation.6 | async-start | bytes 65536 | tf_op jit(solution)/shard_map/all_to_all | solution.py:182
  181.7 7.7 %all-to-all-done.6 = bf16[32,2,256]{2,1,0:T(2,128)(2,1)S(1)} async-done(((bf16[32,2,256]{2,1,0:T(2,128)(2,1)}), bf16[32,2,256]{2,1,0:T(2,128)(2,1)S(1)}, u32[]{:S(2)}, u32[]{:S(2)}) %all-to-all-start.6) | async-done | bytes 32800 | tf_op jit(solution)/shard_map/all_to_all | solution.py:182
  189.7 0.8 fusion.38
  (90 shorter events, 4.8 us)
Async XLA Ops:
  6.5 7.3 %copy-start = (bf16[3,1664,104]{1,2,0:T(8,128)(2,1)S(1)}, bf16[3,1664,104]{1,2,0:T(8,128)(2,1)}, u32[]{:S(2)}) copy-start(bf16[3,1664,104]{1,2,0:T(8,128)(2,1)} %param.18) | copy-start | bytes 3115012
  6.5 7.3 %copy-start.10 = (f32[1664]{0:T(1024)S(1)}, f32[1664]{0:T(1024)}, u32[]{:S(2)}) copy-start(f32[1664]{0:T(1024)} %param.17) | copy-start | bytes 19972
  6.5 7.3 %copy-start.11 = (f32[1664]{0:T(1024)S(1)}, f32[1664]{0:T(1024)}, u32[]{:S(2)}) copy-start(f32[1664]{0:T(1024)} %param.16) | copy-start | bytes 19972
  6.5 11.2 %collective-permute-start.1 = (s32[512]{0:T(512)}, s32[512]{0:T(512)S(1)}, u32[]{:S(2)}, u32[]{:S(2)}) collective-permute-start(s32[512]{0:T(512)} %param.15), channel_id=1, source_target_pairs={{0,16},{16,0},{32,48},{48,32},{64,80},{80,64},{96,112},{112,96},{1... | collective-permute-start | bytes 6152 | tf_op jit(solution)/shard_map/ppermute | solution.py:100
  13.8 3.4 %copy-start.3 = (bf16[256,1024]{1,0:T(8,128)(2,1)S(1)}, bf16[256,1024]{1,0:T(8,128)(2,1)}, u32[]{:S(2)}) copy-start(bf16[256,1024]{1,0:T(8,128)(2,1)} %param.22) | copy-start | bytes 1572868
  13.9 3.9 %copy-start.5 = (s32[128]{0:T(128)S(1)}, s32[128]{0:T(128)}, u32[]{:S(2)}) copy-start(s32[128]{0:T(128)} %param.21) | copy-start | bytes 1540
  13.9 3.9 %copy-start.4 = (s32[512]{0:T(512)S(1)}, s32[512]{0:T(512)}, u32[]{:S(2)}) copy-start(s32[512]{0:T(512)} %param.15) | copy-start | bytes 6148
  14.9 8.6 %collective-permute-start = (bf16[2,512,104]{1,2,0:T(8,128)(2,1)S(1)}, bf16[2,512,104]{1,2,0:T(8,128)(2,1)S(1)}, u32[]{:S(2)}, u32[]{:S(2)}) collective-permute-start(bf16[2,512,104]{1,2,0:T(8,128)(2,1)S(1)} %slice.108), channel_id=1, source_target_pairs={{0,16},{16,0},{32,48},{48,32},{64,80},{80,64},{96,112},{112,96},{1... | collective-permute-start | bytes 638984 | tf_op jit(solution)/shard_map/ppermute | solution.py:100
  23.5 0.7 copy-start.9
  24.1 1.4 copy-start.2
  35.6 19.4 %copy-start.12 = (f32[1024]{0:T(1024)S(1)}, f32[1024]{0:T(1024)}, u32[]{:S(2)}) copy-start(f32[1024]{0:T(1024)} %param.24) | copy-start | bytes 12292
  35.6 19.4 %copy-start.13 = (f32[1024]{0:T(1024)S(1)}, f32[1024]{0:T(1024)}, u32[]{:S(2)}) copy-start(f32[1024]{0:T(1024)} %param.23) | copy-start | bytes 12292
  44.5 35.3 %all-to-all-start.1 = ((bf16[8,104,512]{2,1,0:T(8,128)(2,1)}), bf16[8,104,512]{2,1,0:T(8,128)(2,1)}, u32[]{:S(2)}, u32[]{:S(2)}) async-start(bf16[8,104,512]{2,1,0:T(8,128)(2,1)} %reduce_sum.167), calls=%async_computation.1 | async-start | bytes 1703936 | tf_op jit(solution)/shard_map/all_to_all | solution.py:35
  54.9 89.7 %all-gather.2.cloned.1.call-start = ((), (), s32[]{:S(2)}) async-start(), calls=%async_computation.7 | async-start | bytes 2230272 | tf_op jit(solution)/shard_map/all_gather | solution.py:80
  59.6 54.0 %copy-start.8 = (bf16[3,1024,64]{1,2,0:T(8,128)(2,1)S(1)}, bf16[3,1024,64]{1,2,0:T(8,128)(2,1)}, u32[]{:S(2)}) copy-start(bf16[3,1024,64]{1,2,0:T(8,128)(2,1)} %param.25) | copy-start | bytes 1179652
  98.1 14.9 %all-to-all-start.3 = ((bf16[16,8,1024]{2,1,0:T(8,128)(2,1)}), bf16[16,8,1024]{2,1,0:T(8,128)(2,1)S(1)}, u32[]{:S(2)}, u32[]{:S(2)}) async-start(bf16[16,8,1024]{2,1,0:T(8,128)(2,1)} %broadcast_in_dim.59), calls=%async_computation.3 | async-start | bytes 524288 | tf_op jit(solution)/shard_map/all_to_all | solution.py:26
  114.8 21.5 %all-to-all-start.4 = ((bf16[8,128,128]{2,1,0:T(8,128)(2,1)}), bf16[8,128,128]{2,1,0:T(8,128)(2,1)S(1)}, u32[]{:S(2)}, u32[]{:S(2)}) async-start(bf16[8,128,128]{2,1,0:T(8,128)(2,1)} %broadcast_in_dim.63), calls=%async_computation.4 | async-start | bytes 524288 | tf_op jit(solution)/shard_map/all_to_all | solution.py:26
  137.4 18.1 %all-to-all-start.5 = ((bf16[4,1024,128]{2,1,0:T(8,128)(2,1)}), bf16[4,1024,128]{2,1,0:T(8,128)(2,1)S(1)}, u32[]{:S(2)}, u32[]{:S(2)}) async-start(bf16[4,1024,128]{2,1,0:T(8,128)(2,1)} %broadcast_in_dim.65), calls=%async_computation.5 | async-start | bytes 2097152 | tf_op jit(solution)/shard_map/all_to_all | solution.py:26
  157.1 6.3 %copy-start.1 = (f32[384,4096]{1,0:T(8,128)}, f32[384,4096]{1,0:T(8,128)S(1)}, u32[]{:S(2)}) copy-start(f32[384,4096]{1,0:T(8,128)S(1)} %get-tuple-element.39) | copy-start | bytes 18874372
  157.1 3.2 %copy-start.6 = (bf16[8448,128]{1,0:T(8,128)(2,1)S(1)}, bf16[8448,128]{1,0:T(8,128)(2,1)}, u32[]{:S(2)}) copy-start(bf16[8448,128]{1,0:T(8,128)(2,1)} %all-gather.2.cloned.1.call-done) | copy-start | bytes 6488068
  166.6 4.7 %copy-start.7 = (bf16[8448,128]{1,0:T(8,128)(2,1)S(1)}, bf16[8448,128]{1,0:T(8,128)(2,1)}, u32[]{:S(2)}) copy-start(bf16[8448,128]{1,0:T(8,128)(2,1)} %all-gather.2.cloned.1.call-done) | copy-start | bytes 6488068
  175.7 13.7 %all-to-all-start.6 = ((bf16[32,2,256]{2,1,0:T(2,128)(2,1)}), bf16[32,2,256]{2,1,0:T(2,128)(2,1)S(1)}, u32[]{:S(2)}, u32[]{:S(2)}) async-start(bf16[32,2,256]{2,1,0:T(2,128)(2,1)} %reshape.359), calls=%async_computation.6 | async-start | bytes 65536 | tf_op jit(solution)/shard_map/all_to_all | solution.py:182
Sparse Core Ops, SparseCore 0:
  58.9 85.5 all-gather.1

commit v6 on v5

--- a/solution.py
+++ b/solution.py
@@ -140,7 +140,6 @@
     )
     merged_kv = grp_gather(jnp.concatenate([mproj[1], mproj[2]], axis=1))
 
-    dquery = jnp.concatenate([tproj[0], mproj[0]], axis=0)
     query_pos = jnp.concatenate([own_text_pos, positions], axis=0)
     block = positions // tok
     seen = jnp.sum(
@@ -151,14 +150,16 @@
     )
     merged_limit = block * text_count + (positions - block * tok + 1 - seen)
     text_limit = here * text_count + jnp.arange(text_count, dtype=jnp.int32) + 1
-    limit = jnp.concatenate([text_limit, merged_limit], axis=0)
     key_row = jnp.arange(groups * (text_count + pad_rows), dtype=jnp.int32)
     key_grp = key_row // (text_count + pad_rows)
     key_in = key_row % (text_count + pad_rows)
     text_key = jnp.where(key_in < text_count, key_grp * text_count + key_in, groups * tok)
-    top_t, total_t, acc_t = attend_part(
-        dquery, text_key[None, :] < limit[:, None], text_kv[:, :DH], text_kv[:, DH:]
-    )
+    text_keys, text_values = text_kv[:, :DH], text_kv[:, DH:]
+    part_tt = attend_part(tproj[0], text_key[None, :] < text_limit[:, None], text_keys, text_values)
+    part_mt = attend_part(mproj[0], text_key[None, :] < merged_limit[:, None], text_keys, text_values)
+    part_t = [jnp.concatenate([a, b], axis=0) for a, b in zip(part_tt, part_mt)]
+    top_t, total_t, acc_t = part_t
+    dquery = jnp.concatenate([tproj[0], mproj[0]], axis=0)
     top_m, total_m, acc_m = attend_part(
         dquery, all_pos[None, :] <= query_pos[:, None], merged_kv[:, :DH], merged_kv[:, DH:]
     )

time: 199 us -> 195 us (0.980)
  waiting for transfers between devices: 69.1 us -> 63.3 us
    all_to_all x3, waiting for transfers between devices: 33.2 us -> 27.4 us  [a2a_gather(): got = lax.all_to_all(spread, axis, 0, 0, tiled=True)]
    dot_general x2 -> x3, matrix products: 4.63 us -> 6.42 us  [attend_part(): jnp.dot(query, keys.T, preferred_element_type=jnp.float32) * DH ** (-0.5)]
    dot_general x2 -> x3, matrix products: 8.05 us -> 6.65 us  [attend_part(): jnp.dot(expo.astype(jnp.bfloat16), values, preferred_element_type=jnp.flo...]
    unnamed x31 -> x33, local copies, waits for them, and re-layouts: 6.85 us -> 7.34 us
    reduce_sum x2 -> x3, other arithmetic: 4.67 us -> 4.81 us  [attend_part(): total = jnp.sum(expo, axis=1)]
  transfers between devices with their start and end apart: 8 -> 8, of which waited for: 7 -> 7; matrix products, arithmetic and copies ran while one was open for 11% -> 13% of each run, Pallas kernels for 0% -> 0%
where the time goes in v6:
time: 195 us; the launch traced here: 193 us
  waiting for transfers between devices  63.3 us (32%)
  starting transfers between devices  36.9 us (19%)
  matrix products  23.4 us (12%)
  blocking collectives  19.6 us (10%)
  other arithmetic  18 us (9%)
  local copies, waits for them, and re-layouts  17.9 us (9%)
  between operations  13.9 us (7%)
    all_to_all x3, waiting for transfers between devices, a2a_gather(): got = lax.all_to_all(spread, axis, 0, 0, tiled=True)  27.4 us
    all_to_all x1, waiting for transfers between devices, a2a_sum(): got = lax.all_to_all(parts, axis, 0, 0, tiled=True)  20.2 us
    all_to_all x2, blocking collectives, a2a_sum(): got = lax.all_to_all(parts, axis, 0, 0, tiled=True)  19.6 us
    all_to_all x3, starting transfers between devices, a2a_gather(): got = lax.all_to_all(spread, axis, 0, 0, tiled=True)  14.5 us
    all_to_all x1, starting transfers between devices, a2a_sum(): got = lax.all_to_all(parts, axis, 0, 0, tiled=True)  10.3 us
    all_to_all x1, waiting for transfers between devices, body(): got = lax.all_to_all(packed, GRP, 0, 0, tiled=True)  7.83 us
    unnamed x33, local copies, waits for them, and re-layouts  7.34 us
    dot_general x3, matrix products, attend_part(): jnp.dot(expo.astype(jnp.bfloat16), values, preferred_element_type=jnp.flo...  6.65 us
  transfers between devices with their start and end apart: 8, of which 7 were waited for; matrix products, arithmetic and copies ran while one was open for 13% of the time, Pallas kernels for 0%

profile of v6, /device:TPU:6, one launch (start us, length us, event | category | flops | bytes accessed | tf_op | source)
XLA Modules:
  0.0 193.1 jit_solution(16201566375292142830)
XLA Ops:
  6.5 3.6 %collective-permute-start.1 = (s32[512]{0:T(512)}, s32[512]{0:T(512)S(1)}, u32[]{:S(2)}, u32[]{:S(2)}) collective-permute-start(s32[512]{0:T(512)} %param.15), channel_id=1, source_target_pairs={{0,16},{16,0},{32,48},{48,32},{64,80},{80,64},{96,112},{112,96},{1... | collective-permute-start | bytes 6152 | tf_op jit(solution)/shard_map/ppermute | solution.py:100
  10.2 2.8 %copy.47 = bf16[512,1664]{0,1:T(8,128)(2,1)S(1)} copy(bf16[512,1664]{1,0:T(8,128)(2,1)} %param.14) | data formatting | bytes 3407872 | tf_op args[0]
  13.9 1.0 fusion.25
  14.9 2.4 %collective-permute-start = (bf16[2,512,104]{1,2,0:T(8,128)(2,1)S(1)}, bf16[2,512,104]{1,2,0:T(8,128)(2,1)S(1)}, u32[]{:S(2)}, u32[]{:S(2)}) collective-permute-start(bf16[2,512,104]{1,2,0:T(8,128)(2,1)S(1)} %slice.112), channel_id=1, source_target_pairs={{0,16},{16,0},{32,48},{48,32},{64,80},{80,64},{96,112},{112,96},{1... | collective-permute-start | bytes 638984 | tf_op jit(solution)/shard_map/ppermute | solution.py:100
  17.8 5.7 %collective-permute-done = bf16[2,512,104]{1,2,0:T(8,128)(2,1)S(1)} collective-permute-done((bf16[2,512,104]{1,2,0:T(8,128)(2,1)S(1)}, bf16[2,512,104]{1,2,0:T(8,128)(2,1)S(1)}, u32[]{:S(2)}, u32[]{:S(2)}) %collective-permute-start) | collective-permute-done | bytes 213024 | tf_op jit(solution)/shard_map/ppermute | solution.py:100
  24.2 1.2 copy-done.2
  25.4 0.7 fusion.30
  26.1 4.3 %fusion.13 = bf16[1664,512]{0,1:T(8,128)(2,1)} fusion(bf16[104,1664]{1,0:T(8,128)(2,1)} %param.19, f32[512,1024]{1,0:T(8,128)} %copy-done.2, f32[512]{0:T(512)S(1)} %fusion.30, f32[512]{0:T(512)S(1)} %get-tuple-element.36, s32[1024]{0:T(1024)S(1)} %pad_add_fusion, s32[512]{0:T(512)S(1)} %copy-done.4, bf16[2,512,104]{1,2,0:T(8,128)(2,1)S(1)} %slice.112, ...), kind=kOutput, calls=%fused_computation.24 | convolution fusion | flops 290738176 | bytes 4583424 | tf_op jit(solution)/shard_map/dot_general | solution.py:120
  30.4 3.6 %copy.49 = bf16[1664,512]{1,0:T(8,128)(2,1)} copy(bf16[1664,512]{0,1:T(8,128)(2,1)} %fusion.13) | data formatting | bytes 3407872 | tf_op jit(solution)/shard_map/convert_element_type | solution.py:122
  34.0 1.6 copy.50
  35.6 6.0 %all_to_all.42 = bf16[2,8,104,512]{3,2,1,0:T(8,128)(2,1)} all-to-all(bf16[2,8,104,512]{3,2,1,0:T(8,128)(2,1)S(1)} %copy.50), channel_id=1, replica_groups=mesh['gx'=4,'gy'=8,'z'=8,'core'=2] {'core'}, dimensions={0} | all-to-all | bytes 3407872 | tf_op jit(solution)/shard_map/all_to_all | solution.py:35
  41.6 2.9 %reduce_sum.176 = bf16[8,104,512]{2,1,0:T(8,128)(2,1)} reduce(bf16[2,8,104,512]{3,2,1,0:T(8,128)(2,1)} %all_to_all.42, bf16[]{:T(256)} %constant.153.clone.1), dimensions={0}, to_apply=%region_12.13 | reduce | flops 425984 | bytes 2555906 | tf_op jit(solution)/shard_map/reduce_sum | solution.py:36
  44.5 10.3 %all-to-all-start.1 = ((bf16[8,104,512]{2,1,0:T(8,128)(2,1)}), bf16[8,104,512]{2,1,0:T(8,128)(2,1)}, u32[]{:S(2)}, u32[]{:S(2)}) async-start(bf16[8,104,512]{2,1,0:T(8,128)(2,1)} %reduce_sum.176), calls=%async_computation.1 | async-start | bytes 1703936 | tf_op jit(solution)/shard_map/all_to_all | solution.py:35
  55.0 1.5 fusion.72
  56.5 0.7 copy.45
  57.3 2.2 %convert_element_type.125 = f32[512,1664]{0,1:T(8,128)} convert(bf16[512,1664]{0,1:T(8,128)(2,1)S(1)} %copy.47) | non-fusion elementwise | flops 851968 | bytes 5111808 | tf_op jit(solution)/shard_map/convert_element_type | solution.py:93
  59.5 20.2 %all-to-all-done.1 = bf16[8,104,512]{2,1,0:T(8,128)(2,1)} async-done(((bf16[8,104,512]{2,1,0:T(8,128)(2,1)}), bf16[8,104,512]{2,1,0:T(8,128)(2,1)}, u32[]{:S(2)}, u32[]{:S(2)}) %all-to-all-start.1) | async-done | bytes 852000 | tf_op jit(solution)/shard_map/all_to_all | solution.py:35
  79.7 1.3 convert_reduce_fusion.3
  81.1 1.0 fusion.96
  82.2 1.5 fusion.34
  83.7 13.6 %all_to_all.43 = bf16[16,8,1024]{2,1,0:T(8,128)(2,1)S(1)} all-to-all(bf16[16,8,1024]{2,1,0:T(8,128)(2,1)S(1)} %fusion.34), channel_id=1, replica_groups=mesh['gx'=4,'gy'=8,'z'=8,'core'=2] {'z','core'}, dimensions={0} | all-to-all | bytes 524288 | tf_op jit(solution)/shard_map/all_to_all | solution.py:35
  97.3 0.7 broadcast_in_dim.68
  98.1 3.5 %all-to-all-start.3 = ((bf16[16,8,1024]{2,1,0:T(8,128)(2,1)}), bf16[16,8,1024]{2,1,0:T(8,128)(2,1)S(1)}, u32[]{:S(2)}, u32[]{:S(2)}) async-start(bf16[16,8,1024]{2,1,0:T(8,128)(2,1)} %broadcast_in_dim.68), calls=%async_computation.3 | async-start | bytes 524288 | tf_op jit(solution)/shard_map/all_to_all | solution.py:26
  101.7 11.2 %all-to-all-done.3 = bf16[16,8,1024]{2,1,0:T(8,128)(2,1)S(1)} async-done(((bf16[16,8,1024]{2,1,0:T(8,128)(2,1)}), bf16[16,8,1024]{2,1,0:T(8,128)(2,1)S(1)}, u32[]{:S(2)}, u32[]{:S(2)}) %all-to-all-start.3) | async-done | bytes 262176 | tf_op jit(solution)/shard_map/all_to_all | solution.py:26
  114.0 0.7 broadcast_in_dim.72
  114.8 6.2 %all-to-all-start.4 = ((bf16[8,128,128]{2,1,0:T(8,128)(2,1)}), bf16[8,128,128]{2,1,0:T(8,128)(2,1)S(1)}, u32[]{:S(2)}, u32[]{:S(2)}) async-start(bf16[8,128,128]{2,1,0:T(8,128)(2,1)} %broadcast_in_dim.72), calls=%async_computation.4 | async-start | bytes 524288 | tf_op jit(solution)/shard_map/all_to_all | solution.py:26
  121.4 14.9 %all-to-all-done.4 = bf16[8,128,128]{2,1,0:T(8,128)(2,1)S(1)} async-done(((bf16[8,128,128]{2,1,0:T(8,128)(2,1)}), bf16[8,128,128]{2,1,0:T(8,128)(2,1)S(1)}, u32[]{:S(2)}, u32[]{:S(2)}) %all-to-all-start.4) | async-done | bytes 262176 | tf_op jit(solution)/shard_map/all_to_all | solution.py:26
  136.3 1.1 broadcast_in_dim.74
  137.4 4.8 %all-to-all-start.5 = ((bf16[4,1024,128]{2,1,0:T(8,128)(2,1)}), bf16[4,1024,128]{2,1,0:T(8,128)(2,1)S(1)}, u32[]{:S(2)}, u32[]{:S(2)}) async-start(bf16[4,1024,128]{2,1,0:T(8,128)(2,1)} %broadcast_in_dim.74), calls=%async_computation.5 | async-start | bytes 2097152 | tf_op jit(solution)/shard_map/all_to_all | solution.py:26
  142.2 2.2 %all-gather.2.cloned.1.call-done = bf16[8448,128]{1,0:T(8,128)(2,1)} async-done(((bf16[264,128]{1,0:T(8,128)(2,1)}), bf16[8448,128]{1,0:T(8,128)(2,1)}) %all-gather.2.cloned.1.call-update) | async-done | bytes 2162704 | tf_op jit(solution)/shard_map/all_gather | solution.py:80
  144.4 0.8 slice.106
  145.4 0.8 convert_reduce_fusion
  147.8 0.6 select_reduce_fusion.1
  148.4 2.8 %fusion.6 = (f32[128]{0:T(128)S(1)}, f32[128,8448]{1,0:T(8,128)S(1)}) fusion(s32[8448]{0:T(1024)S(1)} %fusion.118, s32[128]{0:T(128)S(1)} %get-tuple-element.32, bf16[8448,128]{1,0:T(8,128)(2,1)} %all-gather.2.cloned.1.call-done, bf16[3,128,64]{1,2,0:T(8,128)(2,1)S(1)} %convert_bitcast_fusion.3), kind=kOutput, calls=%fused_computation.16 | convolution fusion | flops 142737280 | bytes 6542336 | tf_op jit(solution)/shard_map/dot_general | solution.py:40
  151.2 2.1 %copy-done.1 = f32[128,8448]{1,0:T(8,128)} copy-done((f32[128,8448]{1,0:T(8,128)}, f32[128,8448]{1,0:T(8,128)S(1)}, u32[]{:S(2)}) %copy-start.1) | copy-done | bytes 4325400
  153.3 1.1 fusion.9
  154.3 1.2 all-to-all-done.5
  155.5 1.6 fusion.3
  157.1 1.4 fusion.4
  158.7 2.1 %fusion = (f32[256]{0:T(256)S(1)}, f32[256,8448]{1,0:T(8,128)S(1)}) fusion(s32[8448]{0:T(1024)S(1)} %fusion.118, s32[256]{0:T(256)S(1)} %add_add_fusion, bf16[8448,128]{1,0:T(8,128)(2,1)S(1)} %copy-done.6, bf16[3,256,64]{1,2,0:T(8,128)(2,1)S(1)} %convert_bitcast_fusion.2), kind=kOutput, calls=%fused_computation.4 | convolution fusion | flops 285474560 | bytes 10885120 | tf_op jit(solution)/shard_map/dot_general | solution.py:40
  160.8 2.4 %fusion.1 = f32[256]{0:T(256)S(1)} fusion(f32[256,8448]{1,0:T(8,128)S(1)} %get-tuple-element.43, f32[256]{0:T(256)S(1)} %get-tuple-element.42, s32[8448]{0:T(1024)S(1)} %fusion.118, s32[256]{0:T(256)S(1)} %add_add_fusion), kind=kLoop, calls=%fused_computation.7 | loop fusion | flops 8650496 | bytes 8687616 | tf_op jit(solution)/shard_map/reduce_sum | solution.py:43
  163.2 2.0 %fusion.14 = f32[128,64]{0,1:T(8,128)S(1)} fusion(f32[128,8448]{1,0:T(8,128)S(1)} %bitcast.123, f32[128]{0:T(128)S(1)} %get-tuple-element.40, s32[8448]{0:T(1024)S(1)} %fusion.118, s32[128]{0:T(128)S(1)} %get-tuple-element.32, bf16[8448,128]{1,0:T(8,128)(2,1)S(1)} %copy-done.6), kind=kOutput, calls=%fused_computation.28 | convolution fusion | flops 142737408 | bytes 6555648 | tf_op jit(solution)/shard_map/dot_general | solution.py:44
  165.3 2.8 %fusion.7 = f32[256,64]{0,1:T(8,128)S(1)} fusion(f32[256,8448]{1,0:T(8,128)S(1)} %get-tuple-element.43, f32[256]{0:T(256)S(1)} %get-tuple-element.42, s32[8448]{0:T(1024)S(1)} %fusion.118, s32[256]{0:T(256)S(1)} %add_add_fusion, bf16[8448,128]{1,0:T(8,128)(2,1)S(1)} %copy-done.6), kind=kOutput, calls=%fused_computation.17 | convolution fusion | flops 285474816 | bytes 10914816 | tf_op jit(solution)/shard_map/dot_general | solution.py:44
  168.1 1.8 fusion.46
  170.2 0.7 reshape.419
  170.9 6.1 %all-to-all-start.6 = ((bf16[32,2,256]{2,1,0:T(2,128)(2,1)}), bf16[32,2,256]{2,1,0:T(2,128)(2,1)S(1)}, u32[]{:S(2)}, u32[]{:S(2)}) async-start(bf16[32,2,256]{2,1,0:T(2,128)(2,1)} %reshape.419), calls=%async_computation.6 | async-start | bytes 65536 | tf_op jit(solution)/shard_map/all_to_all | solution.py:183
  177.2 7.8 %all-to-all-done.6 = bf16[32,2,256]{2,1,0:T(2,128)(2,1)S(1)} async-done(((bf16[32,2,256]{2,1,0:T(2,128)(2,1)}), bf16[32,2,256]{2,1,0:T(2,128)(2,1)S(1)}, u32[]{:S(2)}, u32[]{:S(2)}) %all-to-all-start.6) | async-done | bytes 32800 | tf_op jit(solution)/shard_map/all_to_all | solution.py:183
  185.4 0.8 fusion.42
  (95 shorter events, 6.7 us)
Async XLA Ops:
  6.5 7.3 %copy-start = (bf16[3,1664,104]{1,2,0:T(8,128)(2,1)S(1)}, bf16[3,1664,104]{1,2,0:T(8,128)(2,1)}, u32[]{:S(2)}) copy-start(bf16[3,1664,104]{1,2,0:T(8,128)(2,1)} %param.18) | copy-start | bytes 3115012
  6.5 7.3 %copy-start.9 = (f32[1664]{0:T(1024)S(1)}, f32[1664]{0:T(1024)}, u32[]{:S(2)}) copy-start(f32[1664]{0:T(1024)} %param.17) | copy-start | bytes 19972
  6.5 7.3 %copy-start.10 = (f32[1664]{0:T(1024)S(1)}, f32[1664]{0:T(1024)}, u32[]{:S(2)}) copy-start(f32[1664]{0:T(1024)} %param.16) | copy-start | bytes 19972
  6.5 11.2 %collective-permute-start.1 = (s32[512]{0:T(512)}, s32[512]{0:T(512)S(1)}, u32[]{:S(2)}, u32[]{:S(2)}) collective-permute-start(s32[512]{0:T(512)} %param.15), channel_id=1, source_target_pairs={{0,16},{16,0},{32,48},{48,32},{64,80},{80,64},{96,112},{112,96},{1... | collective-permute-start | bytes 6152 | tf_op jit(solution)/shard_map/ppermute | solution.py:100
  13.8 3.4 %copy-start.3 = (bf16[256,1024]{1,0:T(8,128)(2,1)S(1)}, bf16[256,1024]{1,0:T(8,128)(2,1)}, u32[]{:S(2)}) copy-start(bf16[256,1024]{1,0:T(8,128)(2,1)} %param.22) | copy-start | bytes 1572868
  13.9 3.9 %copy-start.5 = (s32[128]{0:T(128)S(1)}, s32[128]{0:T(128)}, u32[]{:S(2)}) copy-start(s32[128]{0:T(128)} %param.21) | copy-start | bytes 1540
  13.9 3.9 %copy-start.4 = (s32[512]{0:T(512)S(1)}, s32[512]{0:T(512)}, u32[]{:S(2)}) copy-start(s32[512]{0:T(512)} %param.15) | copy-start | bytes 6148
  14.9 8.6 %collective-permute-start = (bf16[2,512,104]{1,2,0:T(8,128)(2,1)S(1)}, bf16[2,512,104]{1,2,0:T(8,128)(2,1)S(1)}, u32[]{:S(2)}, u32[]{:S(2)}) collective-permute-start(bf16[2,512,104]{1,2,0:T(8,128)(2,1)S(1)} %slice.112), channel_id=1, source_target_pairs={{0,16},{16,0},{32,48},{48,32},{64,80},{80,64},{96,112},{112,96},{1... | collective-permute-start | bytes 638984 | tf_op jit(solution)/shard_map/ppermute | solution.py:100
  23.5 0.7 copy-start.8
  24.1 1.3 copy-start.2
  35.6 19.4 %copy-start.11 = (f32[1024]{0:T(1024)S(1)}, f32[1024]{0:T(1024)}, u32[]{:S(2)}) copy-start(f32[1024]{0:T(1024)} %param.24) | copy-start | bytes 12292
  35.6 19.4 %copy-start.12 = (f32[1024]{0:T(1024)S(1)}, f32[1024]{0:T(1024)}, u32[]{:S(2)}) copy-start(f32[1024]{0:T(1024)} %param.23) | copy-start | bytes 12292
  44.5 35.3 %all-to-all-start.1 = ((bf16[8,104,512]{2,1,0:T(8,128)(2,1)}), bf16[8,104,512]{2,1,0:T(8,128)(2,1)}, u32[]{:S(2)}, u32[]{:S(2)}) async-start(bf16[8,104,512]{2,1,0:T(8,128)(2,1)} %reduce_sum.176), calls=%async_computation.1 | async-start | bytes 1703936 | tf_op jit(solution)/shard_map/all_to_all | solution.py:35
  54.8 89.6 %all-gather.2.cloned.1.call-start = ((), (), s32[]{:S(2)}) async-start(), calls=%async_computation.7 | async-start | bytes 2230272 | tf_op jit(solution)/shard_map/all_gather | solution.py:80
  59.5 53.9 %copy-start.7 = (bf16[3,1024,64]{1,2,0:T(8,128)(2,1)S(1)}, bf16[3,1024,64]{1,2,0:T(8,128)(2,1)}, u32[]{:S(2)}) copy-start(bf16[3,1024,64]{1,2,0:T(8,128)(2,1)} %param.25) | copy-start | bytes 1179652
  98.1 14.9 %all-to-all-start.3 = ((bf16[16,8,1024]{2,1,0:T(8,128)(2,1)}), bf16[16,8,1024]{2,1,0:T(8,128)(2,1)S(1)}, u32[]{:S(2)}, u32[]{:S(2)}) async-start(bf16[16,8,1024]{2,1,0:T(8,128)(2,1)} %broadcast_in_dim.68), calls=%async_computation.3 | async-start | bytes 524288 | tf_op jit(solution)/shard_map/all_to_all | solution.py:26
  114.8 21.5 %all-to-all-start.4 = ((bf16[8,128,128]{2,1,0:T(8,128)(2,1)}), bf16[8,128,128]{2,1,0:T(8,128)(2,1)S(1)}, u32[]{:S(2)}, u32[]{:S(2)}) async-start(bf16[8,128,128]{2,1,0:T(8,128)(2,1)} %broadcast_in_dim.72), calls=%async_computation.4 | async-start | bytes 524288 | tf_op jit(solution)/shard_map/all_to_all | solution.py:26
  137.4 18.1 %all-to-all-start.5 = ((bf16[4,1024,128]{2,1,0:T(8,128)(2,1)}), bf16[4,1024,128]{2,1,0:T(8,128)(2,1)S(1)}, u32[]{:S(2)}, u32[]{:S(2)}) async-start(bf16[4,1024,128]{2,1,0:T(8,128)(2,1)} %broadcast_in_dim.74), calls=%async_computation.5 | async-start | bytes 2097152 | tf_op jit(solution)/shard_map/all_to_all | solution.py:26
  151.2 2.1 %copy-start.1 = (f32[128,8448]{1,0:T(8,128)}, f32[128,8448]{1,0:T(8,128)S(1)}, u32[]{:S(2)}) copy-start(f32[128,8448]{1,0:T(8,128)S(1)} %get-tuple-element.41) | copy-start | bytes 12976132
  157.1 1.6 copy-start.6
  157.1 6.1 %slice-start = ((s8[4325376]{0:T(1024)(128)(4,1)}), s8[4194304]{0:T(1024)(128)(4,1)S(1)}, s32[]{:S(2)}) async-start(s8[4325376]{0:T(1024)(128)(4,1)} %bitcast.122), calls=%async_computation.8 | async-start | bytes 8388608
  158.7 4.5 %slice-start.1 = ((s8[4325376]{0:T(1024)(128)(4,1)}), s8[131072]{0:T(1024)(128)(4,1)S(1)}, s32[]{:S(2)}) async-start(s8[4325376]{0:T(1024)(128)(4,1)} %bitcast.122), calls=%async_computation.9 | async-start | bytes 262144
  170.9 14.1 %all-to-all-start.6 = ((bf16[32,2,256]{2,1,0:T(2,128)(2,1)}), bf16[32,2,256]{2,1,0:T(2,128)(2,1)S(1)}, u32[]{:S(2)}, u32[]{:S(2)}) async-start(bf16[32,2,256]{2,1,0:T(2,128)(2,1)} %reshape.419), calls=%async_computation.6 | async-start | bytes 65536 | tf_op jit(solution)/shard_map/all_to_all | solution.py:183
Sparse Core Ops, SparseCore 0:
  58.9 85.5 all-gather.1

commit v7 on v6

--- a/solution.py
+++ b/solution.py
@@ -120,8 +120,14 @@
     mixed_parts = lax.dot_general(
         vis_out, attended, (((0,), (1,)), ((), ())), preferred_element_type=jnp.float32
     ).astype(jnp.bfloat16)
-    mixed_parts = mixed_parts.reshape(nz, ncore, width, rows).transpose(1, 0, 2, 3)
-    half = a2a_sum(mixed_parts, "core").astype(jnp.bfloat16)
+    mixed_parts = mixed_parts.reshape(nz, ncore, width, rows)
+    core = lax.axis_index("core")
+    keep = lax.dynamic_index_in_dim(mixed_parts, core, 1, keepdims=False)
+    send = lax.dynamic_index_in_dim(mixed_parts, 1 - core, 1, keepdims=False)
+    pair = [(i, i ^ 1) for i in range(ncore)]
+    half = (
+        keep.astype(jnp.float32) + lax.ppermute(send, "core", pair).astype(jnp.float32)
+    ).astype(jnp.bfloat16)
     mixed = a2a_sum(half, "z")
     own_cols = lax.dynamic_slice_in_dim(patches_f, lax.axis_index(TP) * width, width, 1)
     visual = (mixed + own_cols.T).astype(jnp.bfloat16)

time: 195 us -> 189 us (0.969)
  blocking collectives: 19.6 us -> 13.6 us
  starting transfers between devices: 36.9 us -> 40.5 us
    all_to_all x2 -> x1, blocking collectives: 19.6 us -> 13.6 us  [a2a_sum(): got = lax.all_to_all(parts, axis, 0, 0, tiled=True)]
    reduce_sum x3 -> x2, other arithmetic: 4.25 us -> 1.33 us  [a2a_sum(): return jnp.sum(got.astype(jnp.float32), axis=0)]
    ppermute x2, waiting for transfers between devices: 5.71 us -> 3.11 us  [body(): partner_kv, partner_ids = lax.ppermute((proj[1:], patch_image), 'gy', swap)]
    convert_element_type x0 -> x1, other arithmetic: none -> 2.57 us  [body(): half = (keep.astype(jnp.float32) + lax.ppermute(send, 'core', pair).astyp...]
    ppermute x0 -> x1, waiting for transfers between devices: none -> 2.19 us  [body(): lax.ppermute(send, 'core', pair).astype(jnp.float32)]
    squeeze x0 -> x1, local copies, waits for them, and re-layouts: none -> 2.15 us  [body(): send = lax.dynamic_index_in_dim(mixed_parts, 1 - core, 1, keepdims=False)]
    unnamed x33 -> x25, local copies, waits for them, and re-layouts: 7.34 us -> 5.69 us
  transfers between devices with their start and end apart: 8 -> 9, of which waited for: 7 -> 7; matrix products, arithmetic and copies ran while one was open for 13% -> 16% of each run, Pallas kernels for 0% -> 0%
where the time goes in v7:
time: 189 us; the launch traced here: 188 us
  waiting for transfers between devices  61.8 us (33%)
  starting transfers between devices  40.5 us (21%)
  matrix products  23.4 us (12%)
  other arithmetic  17.7 us (9%)
  local copies, waits for them, and re-layouts  16.8 us (9%)
  between operations  13.9 us (7%)
  blocking collectives  13.6 us (7%)
    all_to_all x3, waiting for transfers between devices, a2a_gather(): got = lax.all_to_all(spread, axis, 0, 0, tiled=True)  26.1 us
    all_to_all x1, waiting for transfers between devices, a2a_sum(): got = lax.all_to_all(parts, axis, 0, 0, tiled=True)  20.2 us
    all_to_all x3, starting transfers between devices, a2a_gather(): got = lax.all_to_all(spread, axis, 0, 0, tiled=True)  15.3 us
    all_to_all x1, blocking collectives, a2a_sum(): got = lax.all_to_all(parts, axis, 0, 0, tiled=True)  13.6 us
    all_to_all x1, starting transfers between devices, a2a_sum(): got = lax.all_to_all(parts, axis, 0, 0, tiled=True)  10.3 us
    all_to_all x1, waiting for transfers between devices, body(): got = lax.all_to_all(packed, GRP, 0, 0, tiled=True)  7.83 us
    all_to_all x1, starting transfers between devices, body(): got = lax.all_to_all(packed, GRP, 0, 0, tiled=True)  7.13 us
    dot_general x3, matrix products, attend_part(): jnp.dot(expo.astype(jnp.bfloat16), values, preferred_element_type=jnp.flo...  6.64 us
  transfers between devices with their start and end apart: 9, of which 7 were waited for; matrix products, arithmetic and copies ran while one was open for 16% of the time, Pallas kernels for 0%

profile of v7, /device:TPU:6, one launch (start us, length us, event | category | flops | bytes accessed | tf_op | source)
XLA Modules:
  0.0 187.7 jit_solution(15792828017669951954)
XLA Ops:
  6.5 2.9 %copy.48 = bf16[512,1664]{0,1:T(8,128)(2,1)S(1)} copy(bf16[512,1664]{1,0:T(8,128)(2,1)} %param.14) | data formatting | bytes 3407872 | tf_op args[0]
  10.3 1.0 fusion.25
  11.4 3.5 %collective-permute-start = (bf16[2,512,104]{1,2,0:T(8,128)(2,1)S(1)}, bf16[2,512,104]{1,2,0:T(8,128)(2,1)S(1)}, u32[]{:S(2)}, u32[]{:S(2)}) collective-permute-start(bf16[2,512,104]{1,2,0:T(8,128)(2,1)S(1)} %slice.112), channel_id=1, source_target_pairs={{0,16},{16,0},{32,48},{48,32},{64,80},{80,64},{96,112},{112,96},{1... | collective-permute-start | bytes 638984 | tf_op jit(solution)/shard_map/ppermute | solution.py:100
  14.9 2.4 %collective-permute-start.1 = (s32[512]{0:T(512)S(1)}, s32[512]{0:T(512)S(1)}, u32[]{:S(2)}, u32[]{:S(2)}) collective-permute-start(s32[512]{0:T(512)S(1)} %copy-done.3), channel_id=1, source_target_pairs={{0,16},{16,0},{32,48},{48,32},{64,80},{80,64},{96,112},{112,96},{1... | collective-permute-start | bytes 6152 | tf_op jit(solution)/shard_map/ppermute | solution.py:100
  17.2 3.1 %collective-permute-done.1 = s32[512]{0:T(512)S(1)} collective-permute-done((s32[512]{0:T(512)S(1)}, s32[512]{0:T(512)S(1)}, u32[]{:S(2)}, u32[]{:S(2)}) %collective-permute-start.1) | collective-permute-done | bytes 2080 | tf_op jit(solution)/shard_map/ppermute | solution.py:100
  20.4 0.6 fusion.20
  20.9 1.4 copy-done.1
  22.3 0.7 fusion.31
  23.0 4.2 %fusion.13 = bf16[1664,512]{0,1:T(8,128)(2,1)} fusion(bf16[104,1664]{1,0:T(8,128)(2,1)} %param.19, f32[512,1024]{1,0:T(8,128)} %copy-done.1, f32[512]{0:T(512)S(1)} %fusion.31, f32[512]{0:T(512)S(1)} %get-tuple-element.36, s32[1024]{0:T(1024)S(1)} %pad_add_fusion, s32[512]{0:T(512)S(1)} %copy-done.3, bf16[2,512,104]{1,2,0:T(8,128)(2,1)S(1)} %slice.112, ...), kind=kOutput, calls=%fused_computation.24 | convolution fusion | flops 290738176 | bytes 4583424 | tf_op jit(solution)/shard_map/dot_general | solution.py:120
  27.2 3.7 %copy.50 = bf16[1664,512]{1,0:T(8,128)(2,1)} copy(bf16[1664,512]{0,1:T(8,128)(2,1)} %fusion.13) | data formatting | bytes 3407872 | tf_op jit(solution)/shard_map/convert_element_type | solution.py:122
  30.9 2.1 %dynamic-slice_bitcast_fusion = bf16[8,104,512]{2,1,0:T(8,128)(2,1)} fusion(bf16[8,2,104,512]{3,2,1,0:T(8,128)(2,1)} %bitcast.124, s32[]{:T(128)S(6)} %select_n.123), kind=kLoop, calls=%fused_computation.76 | loop fusion | bytes 1703940 | tf_op jit(solution)/shard_map/jit(dynamic_index_in_dim)/squeeze | solution.py:126
  33.0 1.9 %collective-permute-start.2 = (bf16[8,104,512]{2,1,0:T(8,128)(2,1)}, bf16[8,104,512]{2,1,0:T(8,128)(2,1)}, u32[]{:S(2)}, u32[]{:S(2)}) collective-permute-start(bf16[8,104,512]{2,1,0:T(8,128)(2,1)} %dynamic-slice_bitcast_fusion), channel_id=1, source_target_pairs={{0,1},{1,0},{2,3},{3,2},{4,5},{5,4},{6,7},{7,6},{8,9},{9,8},{10,11... | collective-permute-start | bytes 2555912 | tf_op jit(solution)/shard_map/ppermute | solution.py:129
  35.5 2.2 %collective-permute-done.2 = bf16[8,104,512]{2,1,0:T(8,128)(2,1)} collective-permute-done((bf16[8,104,512]{2,1,0:T(8,128)(2,1)}, bf16[8,104,512]{2,1,0:T(8,128)(2,1)}, u32[]{:S(2)}, u32[]{:S(2)}) %collective-permute-start.2) | collective-permute-done | bytes 852000 | tf_op jit(solution)/shard_map/ppermute | solution.py:129
  37.7 2.6 %fusion.26 = bf16[8,104,512]{2,1,0:T(8,128)(2,1)} fusion(bf16[8,104,512]{2,1,0:T(8,128)(2,1)} %collective-permute-done.2, bf16[8,2,104,512]{3,2,1,0:T(8,128)(2,1)} %bitcast.125, s32[]{:T(128)S(6)} %select_n.122), kind=kLoop, calls=%fused_computation.42 | loop fusion | flops 1703936 | bytes 2555908 | tf_op jit(solution)/shard_map/convert_element_type | solution.py:130
  40.2 10.3 %all-to-all-start = ((bf16[8,104,512]{2,1,0:T(8,128)(2,1)}), bf16[8,104,512]{2,1,0:T(8,128)(2,1)}, u32[]{:S(2)}, u32[]{:S(2)}) async-start(bf16[8,104,512]{2,1,0:T(8,128)(2,1)} %fusion.26), calls=%async_computation | async-start | bytes 1703936 | tf_op jit(solution)/shard_map/all_to_all | solution.py:35
  50.7 1.5 fusion.73
  52.3 0.7 copy.46
  53.0 2.2 %convert_element_type.135 = f32[512,1664]{0,1:T(8,128)} convert(bf16[512,1664]{0,1:T(8,128)(2,1)S(1)} %copy.48) | non-fusion elementwise | flops 851968 | bytes 5111808 | tf_op jit(solution)/shard_map/convert_element_type | solution.py:93
  55.2 20.2 %all-to-all-done = bf16[8,104,512]{2,1,0:T(8,128)(2,1)} async-done(((bf16[8,104,512]{2,1,0:T(8,128)(2,1)}), bf16[8,104,512]{2,1,0:T(8,128)(2,1)}, u32[]{:S(2)}, u32[]{:S(2)}) %all-to-all-start) | async-done | bytes 852000 | tf_op jit(solution)/shard_map/all_to_all | solution.py:35
  75.5 1.3 convert_reduce_fusion.3
  76.8 1.0 fusion.97
  77.9 1.5 fusion.35
  79.4 13.6 %all_to_all.37 = bf16[16,8,1024]{2,1,0:T(8,128)(2,1)S(1)} all-to-all(bf16[16,8,1024]{2,1,0:T(8,128)(2,1)S(1)} %fusion.35), channel_id=1, replica_groups=mesh['gx'=4,'gy'=8,'z'=8,'core'=2] {'z','core'}, dimensions={0} | all-to-all | bytes 524288 | tf_op jit(solution)/shard_map/all_to_all | solution.py:35
  93.1 0.7 broadcast_in_dim.68
  93.8 3.5 %all-to-all-start.2 = ((bf16[16,8,1024]{2,1,0:T(8,128)(2,1)}), bf16[16,8,1024]{2,1,0:T(8,128)(2,1)S(1)}, u32[]{:S(2)}, u32[]{:S(2)}) async-start(bf16[16,8,1024]{2,1,0:T(8,128)(2,1)} %broadcast_in_dim.68), calls=%async_computation.2 | async-start | bytes 524288 | tf_op jit(solution)/shard_map/all_to_all | solution.py:26
  97.4 11.2 %all-to-all-done.2 = bf16[16,8,1024]{2,1,0:T(8,128)(2,1)S(1)} async-done(((bf16[16,8,1024]{2,1,0:T(8,128)(2,1)}), bf16[16,8,1024]{2,1,0:T(8,128)(2,1)S(1)}, u32[]{:S(2)}, u32[]{:S(2)}) %all-to-all-start.2) | async-done | bytes 262176 | tf_op jit(solution)/shard_map/all_to_all | solution.py:26
  109.7 0.7 broadcast_in_dim.72
  110.5 7.0 %all-to-all-start.3 = ((bf16[8,128,128]{2,1,0:T(8,128)(2,1)}), bf16[8,128,128]{2,1,0:T(8,128)(2,1)S(1)}, u32[]{:S(2)}, u32[]{:S(2)}) async-start(bf16[8,128,128]{2,1,0:T(8,128)(2,1)} %broadcast_in_dim.72), calls=%async_computation.3 | async-start | bytes 524288 | tf_op jit(solution)/shard_map/all_to_all | solution.py:26
  117.9 14.9 %all-to-all-done.3 = bf16[8,128,128]{2,1,0:T(8,128)(2,1)S(1)} async-done(((bf16[8,128,128]{2,1,0:T(8,128)(2,1)}), bf16[8,128,128]{2,1,0:T(8,128)(2,1)S(1)}, u32[]{:S(2)}, u32[]{:S(2)}) %all-to-all-start.3) | async-done | bytes 262176 | tf_op jit(solution)/shard_map/all_to_all | solution.py:26
  132.8 1.1 broadcast_in_dim.74
  133.9 4.7 %all-to-all-start.4 = ((bf16[4,1024,128]{2,1,0:T(8,128)(2,1)}), bf16[4,1024,128]{2,1,0:T(8,128)(2,1)S(1)}, u32[]{:S(2)}, u32[]{:S(2)}) async-start(bf16[4,1024,128]{2,1,0:T(8,128)(2,1)} %broadcast_in_dim.74), calls=%async_computation.4 | async-start | bytes 2097152 | tf_op jit(solution)/shard_map/all_to_all | solution.py:26
  138.7 2.3 %all-gather.2.cloned.1.call-done = bf16[8448,128]{1,0:T(8,128)(2,1)} async-done(((bf16[264,128]{1,0:T(8,128)(2,1)}), bf16[8448,128]{1,0:T(8,128)(2,1)}) %all-gather.2.cloned.1.call-update) | async-done | bytes 2162704 | tf_op jit(solution)/shard_map/all_gather | solution.py:80
  141.0 0.8 slice.106
  141.9 0.8 convert_reduce_fusion
  144.3 0.6 select_reduce_fusion.1
  144.9 2.8 %fusion.6 = (f32[128]{0:T(128)S(1)}, f32[128,8448]{1,0:T(8,128)S(1)}) fusion(s32[8448]{0:T(1024)S(1)} %fusion.119, s32[128]{0:T(128)S(1)} %get-tuple-element.32, bf16[8448,128]{1,0:T(8,128)(2,1)} %all-gather.2.cloned.1.call-done, bf16[3,128,64]{1,2,0:T(8,128)(2,1)S(1)} %convert_bitcast_fusion.3), kind=kOutput, calls=%fused_computation.16 | convolution fusion | flops 142737280 | bytes 6542336 | tf_op jit(solution)/shard_map/dot_general | solution.py:40
  147.7 1.1 fusion.9
  149.3 2.1 %fusion = (f32[256]{0:T(256)S(1)}, f32[256,8448]{1,0:T(8,128)S(1)}) fusion(s32[8448]{0:T(1024)S(1)} %fusion.119, s32[256]{0:T(256)S(1)} %add_add_fusion, bf16[8448,128]{1,0:T(8,128)(2,1)S(1)} %copy-done.5, bf16[3,256,64]{1,2,0:T(8,128)(2,1)S(1)} %convert_bitcast_fusion.2), kind=kOutput, calls=%fused_computation.4 | convolution fusion | flops 285474560 | bytes 10885120 | tf_op jit(solution)/shard_map/dot_general | solution.py:40
  151.4 2.4 %fusion.1 = f32[256]{0:T(256)S(1)} fusion(f32[256,8448]{1,0:T(8,128)S(1)} %get-tuple-element.43, f32[256]{0:T(256)S(1)} %get-tuple-element.42, s32[8448]{0:T(1024)S(1)} %fusion.119, s32[256]{0:T(256)S(1)} %add_add_fusion), kind=kLoop, calls=%fused_computation.7 | loop fusion | flops 8650496 | bytes 8687616 | tf_op jit(solution)/shard_map/reduce_sum | solution.py:43
  153.8 2.0 %fusion.14 = f32[128,64]{0,1:T(8,128)S(1)} fusion(f32[128,8448]{1,0:T(8,128)S(1)} %get-tuple-element.41, f32[128]{0:T(128)S(1)} %get-tuple-element.40, s32[8448]{0:T(1024)S(1)} %fusion.119, s32[128]{0:T(128)S(1)} %get-tuple-element.32, bf16[8448,128]{1,0:T(8,128)(2,1)S(1)} %copy-done.5), kind=kOutput, calls=%fused_computation.28 | convolution fusion | flops 142737408 | bytes 6555648 | tf_op jit(solution)/shard_map/dot_general | solution.py:44
  155.8 2.8 %fusion.7 = f32[256,64]{0,1:T(8,128)S(1)} fusion(f32[256,8448]{1,0:T(8,128)S(1)} %get-tuple-element.43, f32[256]{0:T(256)S(1)} %get-tuple-element.42, s32[8448]{0:T(1024)S(1)} %fusion.119, s32[256]{0:T(256)S(1)} %add_add_fusion, bf16[8448,128]{1,0:T(8,128)(2,1)S(1)} %copy-done.5), kind=kOutput, calls=%fused_computation.17 | convolution fusion | flops 285474816 | bytes 10914816 | tf_op jit(solution)/shard_map/dot_general | solution.py:44
  158.6 1.6 fusion.3
  160.2 1.4 fusion.4
  161.7 1.8 fusion.47
  163.8 0.7 reshape.422
  164.5 7.1 %all-to-all-start.5 = ((bf16[32,2,256]{2,1,0:T(2,128)(2,1)}), bf16[32,2,256]{2,1,0:T(2,128)(2,1)S(1)}, u32[]{:S(2)}, u32[]{:S(2)}) async-start(bf16[32,2,256]{2,1,0:T(2,128)(2,1)} %reshape.422), calls=%async_computation.5 | async-start | bytes 65536 | tf_op jit(solution)/shard_map/all_to_all | solution.py:189
  171.9 7.8 %all-to-all-done.5 = bf16[32,2,256]{2,1,0:T(2,128)(2,1)S(1)} async-done(((bf16[32,2,256]{2,1,0:T(2,128)(2,1)}), bf16[32,2,256]{2,1,0:T(2,128)(2,1)S(1)}, u32[]{:S(2)}, u32[]{:S(2)}) %all-to-all-start.5) | async-done | bytes 32800 | tf_op jit(solution)/shard_map/all_to_all | solution.py:189
  180.0 0.8 fusion.43
  (87 shorter events, 6.3 us)
Async XLA Ops:
  6.5 3.8 %copy-start = (bf16[3,1664,104]{1,2,0:T(8,128)(2,1)S(1)}, bf16[3,1664,104]{1,2,0:T(8,128)(2,1)}, u32[]{:S(2)}) copy-start(bf16[3,1664,104]{1,2,0:T(8,128)(2,1)} %param.18) | copy-start | bytes 3115012
  6.5 3.8 %copy-start.7 = (f32[1664]{0:T(1024)S(1)}, f32[1664]{0:T(1024)}, u32[]{:S(2)}) copy-start(f32[1664]{0:T(1024)} %param.17) | copy-start | bytes 19972
  6.5 3.8 %copy-start.8 = (f32[1664]{0:T(1024)S(1)}, f32[1664]{0:T(1024)}, u32[]{:S(2)}) copy-start(f32[1664]{0:T(1024)} %param.16) | copy-start | bytes 19972
  10.3 4.5 %copy-start.3 = (s32[512]{0:T(512)S(1)}, s32[512]{0:T(512)}, u32[]{:S(2)}) copy-start(s32[512]{0:T(512)} %param.15) | copy-start | bytes 6148
  11.4 9.0 %collective-permute-start = (bf16[2,512,104]{1,2,0:T(8,128)(2,1)S(1)}, bf16[2,512,104]{1,2,0:T(8,128)(2,1)S(1)}, u32[]{:S(2)}, u32[]{:S(2)}) collective-permute-start(bf16[2,512,104]{1,2,0:T(8,128)(2,1)S(1)} %slice.112), channel_id=1, source_target_pairs={{0,16},{16,0},{32,48},{48,32},{64,80},{80,64},{96,112},{112,96},{1... | collective-permute-start | bytes 638984 | tf_op jit(solution)/shard_map/ppermute | solution.py:100
  14.9 5.5 %collective-permute-start.1 = (s32[512]{0:T(512)S(1)}, s32[512]{0:T(512)S(1)}, u32[]{:S(2)}, u32[]{:S(2)}) collective-permute-start(s32[512]{0:T(512)S(1)} %copy-done.3), channel_id=1, source_target_pairs={{0,16},{16,0},{32,48},{48,32},{64,80},{80,64},{96,112},{112,96},{1... | collective-permute-start | bytes 6152 | tf_op jit(solution)/shard_map/ppermute | solution.py:100
  20.9 1.4 copy-start.1
  27.2 7.8 %copy-start.2 = (bf16[256,1024]{1,0:T(8,128)(2,1)S(1)}, bf16[256,1024]{1,0:T(8,128)(2,1)}, u32[]{:S(2)}) copy-start(bf16[256,1024]{1,0:T(8,128)(2,1)} %param.22) | copy-start | bytes 1572868
  27.2 8.2 %copy-start.4 = (s32[128]{0:T(128)S(1)}, s32[128]{0:T(128)}, u32[]{:S(2)}) copy-start(s32[128]{0:T(128)} %param.21) | copy-start | bytes 1540
  30.9 19.8 %copy-start.9 = (f32[1024]{0:T(1024)S(1)}, f32[1024]{0:T(1024)}, u32[]{:S(2)}) copy-start(f32[1024]{0:T(1024)} %param.24) | copy-start | bytes 12292
  30.9 19.8 %copy-start.10 = (f32[1024]{0:T(1024)S(1)}, f32[1024]{0:T(1024)}, u32[]{:S(2)}) copy-start(f32[1024]{0:T(1024)} %param.23) | copy-start | bytes 12292
  33.0 4.6 %collective-permute-start.2 = (bf16[8,104,512]{2,1,0:T(8,128)(2,1)}, bf16[8,104,512]{2,1,0:T(8,128)(2,1)}, u32[]{:S(2)}, u32[]{:S(2)}) collective-permute-start(bf16[8,104,512]{2,1,0:T(8,128)(2,1)} %dynamic-slice_bitcast_fusion), channel_id=1, source_target_pairs={{0,1},{1,0},{2,3},{3,2},{4,5},{5,4},{6,7},{7,6},{8,9},{9,8},{10,11... | collective-permute-start | bytes 2555912 | tf_op jit(solution)/shard_map/ppermute | solution.py:129
  40.2 35.2 %all-to-all-start = ((bf16[8,104,512]{2,1,0:T(8,128)(2,1)}), bf16[8,104,512]{2,1,0:T(8,128)(2,1)}, u32[]{:S(2)}, u32[]{:S(2)}) async-start(bf16[8,104,512]{2,1,0:T(8,128)(2,1)} %fusion.26), calls=%async_computation | async-start | bytes 1703936 | tf_op jit(solution)/shard_map/all_to_all | solution.py:35
  50.5 90.4 %all-gather.2.cloned.1.call-start = ((), (), s32[]{:S(2)}) async-start(), calls=%async_computation.6 | async-start | bytes 2230272 | tf_op jit(solution)/shard_map/all_gather | solution.py:80
  55.2 54.0 %copy-start.6 = (bf16[3,1024,64]{1,2,0:T(8,128)(2,1)S(1)}, bf16[3,1024,64]{1,2,0:T(8,128)(2,1)}, u32[]{:S(2)}) copy-start(bf16[3,1024,64]{1,2,0:T(8,128)(2,1)} %param.25) | copy-start | bytes 1179652
  93.8 14.9 %all-to-all-start.2 = ((bf16[16,8,1024]{2,1,0:T(8,128)(2,1)}), bf16[16,8,1024]{2,1,0:T(8,128)(2,1)S(1)}, u32[]{:S(2)}, u32[]{:S(2)}) async-start(bf16[16,8,1024]{2,1,0:T(8,128)(2,1)} %broadcast_in_dim.68), calls=%async_computation.2 | async-start | bytes 524288 | tf_op jit(solution)/shard_map/all_to_all | solution.py:26
  110.5 22.3 %all-to-all-start.3 = ((bf16[8,128,128]{2,1,0:T(8,128)(2,1)}), bf16[8,128,128]{2,1,0:T(8,128)(2,1)S(1)}, u32[]{:S(2)}, u32[]{:S(2)}) async-start(bf16[8,128,128]{2,1,0:T(8,128)(2,1)} %broadcast_in_dim.72), calls=%async_computation.3 | async-start | bytes 524288 | tf_op jit(solution)/shard_map/all_to_all | solution.py:26
  133.9 24.7 %all-to-all-start.4 = ((bf16[4,1024,128]{2,1,0:T(8,128)(2,1)}), bf16[4,1024,128]{2,1,0:T(8,128)(2,1)S(1)}, u32[]{:S(2)}, u32[]{:S(2)}) async-start(bf16[4,1024,128]{2,1,0:T(8,128)(2,1)} %broadcast_in_dim.74), calls=%async_computation.4 | async-start | bytes 2097152 | tf_op jit(solution)/shard_map/all_to_all | solution.py:26
  147.7 1.6 copy-start.5
  164.5 15.2 %all-to-all-start.5 = ((bf16[32,2,256]{2,1,0:T(2,128)(2,1)}), bf16[32,2,256]{2,1,0:T(2,128)(2,1)S(1)}, u32[]{:S(2)}, u32[]{:S(2)}) async-start(bf16[32,2,256]{2,1,0:T(2,128)(2,1)} %reshape.422), calls=%async_computation.5 | async-start | bytes 65536 | tf_op jit(solution)/shard_map/all_to_all | solution.py:189
Sparse Core Ops, SparseCore 0:
  54.6 86.3 all-gather.1

commit v8 on v7

--- a/solution.py
+++ b/solution.py
@@ -117,20 +117,20 @@
     nz = lax.axis_size("z")
     ncore = lax.axis_size("core")
     width = patches.shape[1] // (nz * ncore)
-    mixed_parts = lax.dot_general(
-        vis_out, attended, (((0,), (1,)), ((), ())), preferred_element_type=jnp.float32
-    ).astype(jnp.bfloat16)
-    mixed_parts = mixed_parts.reshape(nz, ncore, width, rows)
     core = lax.axis_index("core")
-    keep = lax.dynamic_index_in_dim(mixed_parts, core, 1, keepdims=False)
-    send = lax.dynamic_index_in_dim(mixed_parts, 1 - core, 1, keepdims=False)
+    vo = vis_out.reshape(vis_out.shape[0], nz, ncore, width)
+    keep_w = lax.dynamic_index_in_dim(vo, core, 2, keepdims=False)
+    send_w = lax.dynamic_index_in_dim(vo, 1 - core, 2, keepdims=False)
+    keep = jnp.einsum("pe,ezf->zfp", attended, keep_w, preferred_element_type=jnp.float32)
+    send = jnp.einsum("pe,ezf->zfp", attended, send_w, preferred_element_type=jnp.float32)
     pair = [(i, i ^ 1) for i in range(ncore)]
     half = (
-        keep.astype(jnp.float32) + lax.ppermute(send, "core", pair).astype(jnp.float32)
+        keep.astype(jnp.bfloat16).astype(jnp.float32)
+        + lax.ppermute(send.astype(jnp.bfloat16), "core", pair).astype(jnp.float32)
     ).astype(jnp.bfloat16)
     mixed = a2a_sum(half, "z")
-    own_cols = lax.dynamic_slice_in_dim(patches_f, lax.axis_index(TP) * width, width, 1)
-    visual = (mixed + own_cols.T).astype(jnp.bfloat16)
+    own_cols = lax.dynamic_slice_in_dim(patches, lax.axis_index(TP) * width, width, 1)
+    visual = (mixed + own_cols.astype(jnp.float32).T).astype(jnp.bfloat16)
     windows = visual.reshape(width, merged_count, 4)
     partial_rows = jnp.einsum(
         "cmk,kce->me", windows, merge_weight, preferred_element_type=jnp.float32

time: 189 us -> 186 us (0.984)
  matrix products: 23.4 us -> 26.8 us
  other arithmetic: 17.7 us -> 15 us
  local copies, waits for them, and re-layouts: 16.8 us -> 14.4 us
    convert_element_type x3 -> x1, other arithmetic: 5.76 us -> 0.02 us  [body(): visual = (mixed + own_cols.astype(jnp.float32).T).astype(jnp.bfloat16)]
    convert_element_type x2 -> x1, local copies, waits for them, and re-layouts: 3.8 us -> 0.12 us  [body(): visual = (mixed + own_cols.astype(jnp.float32).T).astype(jnp.bfloat16)]
    squeeze x1 -> x0, local copies, waits for them, and re-layouts: 2.15 us -> none  [body(): send = lax.dynamic_index_in_dim(mixed_parts, 1 - core, 1, keepdims=False)]
    ppermute x2, waiting for transfers between devices: 3.11 us -> 1.05 us  [body(): partner_kv, partner_ids = lax.ppermute((proj[1:], patch_image), 'gy', swap)]
    all_to_all x1, waiting for transfers between devices: 20.2 us -> 22.2 us  [a2a_sum(): got = lax.all_to_all(parts, axis, 0, 0, tiled=True)]
    dynamic_slice x0 -> x2, local copies, waits for them, and re-layouts: none -> 1.9 us  [the longest x1 1.79 us: body(): keep_w = lax.dynamic_index_in_dim(vo, core, 2, keepdims=False)]
    dot_general x1 -> x3, matrix products: 4.24 us -> 5.62 us  [the longest x1 2.48 us: body(): jnp.einsum('pe,ezf->zfp', attended, keep_w, preferred_element_type=jnp.fl...]
    unnamed x25 -> x29, local copies, waits for them, and re-layouts: 5.69 us -> 4.65 us
  transfers between devices with their start and end apart: 9 -> 9, of which waited for: 7 -> 7; matrix products, arithmetic and copies ran while one was open for 16% -> 22% of each run, Pallas kernels for 0% -> 0%
where the time goes in v8:
time: 186 us; the launch traced here: 184 us
  waiting for transfers between devices  60.1 us (32%)
  starting transfers between devices  40.3 us (22%)
  matrix products  26.8 us (14%)
  other arithmetic  15 us (8%)
  local copies, waits for them, and re-layouts  14.4 us (8%)
  between operations  13.9 us (7%)
  blocking collectives  13.6 us (7%)
    all_to_all x3, waiting for transfers between devices, a2a_gather(): got = lax.all_to_all(spread, axis, 0, 0, tiled=True)  26.1 us
    all_to_all x1, waiting for transfers between devices, a2a_sum(): got = lax.all_to_all(parts, axis, 0, 0, tiled=True)  22.2 us
    all_to_all x3, starting transfers between devices, a2a_gather(): got = lax.all_to_all(spread, axis, 0, 0, tiled=True)  14.5 us
    all_to_all x1, blocking collectives, a2a_sum(): got = lax.all_to_all(parts, axis, 0, 0, tiled=True)  13.6 us
    all_to_all x1, starting transfers between devices, a2a_sum(): got = lax.all_to_all(parts, axis, 0, 0, tiled=True)  10.3 us
    all_to_all x1, waiting for transfers between devices, body(): got = lax.all_to_all(packed, GRP, 0, 0, tiled=True)  7.83 us
    all_to_all x1, starting transfers between devices, body(): got = lax.all_to_all(packed, GRP, 0, 0, tiled=True)  7.39 us
    dot_general x3, matrix products, attend_part(): jnp.dot(expo.astype(jnp.bfloat16), values, preferred_element_type=jnp.flo...  6.64 us
  transfers between devices with their start and end apart: 9, of which 7 were waited for; matrix products, arithmetic and copies ran while one was open for 22% of the time, Pallas kernels for 0%

profile of v8, /device:TPU:6, one launch (start us, length us, event | category | flops | bytes accessed | tf_op | source)
XLA Modules:
  0.0 184.1 jit_solution(16856446739257612206)
XLA Ops:
  6.5 3.7 %collective-permute-start.1 = (s32[512]{0:T(512)}, s32[512]{0:T(512)S(1)}, u32[]{:S(2)}, u32[]{:S(2)}) collective-permute-start(s32[512]{0:T(512)} %param.15), channel_id=1, source_target_pairs={{0,16},{16,0},{32,48},{48,32},{64,80},{80,64},{96,112},{112,96},{1... | collective-permute-start | bytes 6152 | tf_op jit(solution)/shard_map/ppermute | solution.py:100
  10.3 1.8 convert_reduce_fusion.1
  12.1 2.0 %fusion.11 = f32[512]{0:T(512)S(1)} fusion(bf16[512,1664]{1,0:T(8,128)(2,1)} %param.14, f32[512]{0:T(512)S(1)} %broadcast_multiply_fusion.1), kind=kLoop, calls=%fused_computation.22 | loop fusion | flops 3407360 | bytes 1708032 | tf_op jit(solution)/shard_map/reduce_sum | solution.py:19
  14.1 1.0 fusion.30
  15.9 2.3 %collective-permute-start = (bf16[2,512,104]{1,2,0:T(8,128)(2,1)}, bf16[2,512,104]{1,2,0:T(8,128)(2,1)}, u32[]{:S(2)}, u32[]{:S(2)}) collective-permute-start(bf16[2,512,104]{1,2,0:T(8,128)(2,1)} %slice.112), channel_id=1, source_target_pairs={{0,16},{16,0},{32,48},{48,32},{64,80},{80,64},{96,112},{112,96},{1... | collective-permute-start | bytes 638984 | tf_op jit(solution)/shard_map/ppermute | solution.py:100
  18.3 1.8 reshape.400
  20.1 1.8 constant_dynamic-slice_fusion.2
  21.9 1.9 %copy.60 = bf16[104,8,1,104]{0,3,1,2:T(8,128)(2,1)} copy(bf16[104,8,1,104]{3,2,1,0:T(2,128)(2,1)} %get-tuple-element.25) | data formatting | bytes 346112
  23.8 1.1 collective-permute-done
  24.8 1.5 fusion.25
  27.1 1.9 %fusion.41 = bf16[512,104,1]{0,1,2:T(8,128)(2,1)S(1)} fusion(f32[512,1024]{1,0:T(8,128)S(1)} %get-tuple-element.39, f32[512]{0:T(512)S(1)} %fusion.36, f32[512]{0:T(512)S(1)} %get-tuple-element.38, s32[1024]{0:T(1024)S(1)} %pad_add_fusion, s32[512]{0:T(512)S(1)} %copy-done.5, bf16[2,512,104]{1,2,0:T(8,128)(2,1)} %slice.112, ...), kind=kOutput, calls=%fused_computation.61 | convolution fusion | flops 112676864 | bytes 2639872 | tf_op jit(solution)/shard_map/hpk,khe->phe/dot_general | solution.py:112
  29.0 1.3 convolution_convert_fusion
  30.3 1.9 %collective-permute-start.2 = (bf16[8,104,512]{2,1,0:T(8,128)(2,1)}, bf16[8,104,512]{2,1,0:T(8,128)(2,1)}, u32[]{:S(2)}, u32[]{:S(2)}) collective-permute-start(bf16[8,104,512]{2,1,0:T(8,128)(2,1)} %convolution_convert_fusion), channel_id=1, source_target_pairs={{0,1},{1,0},{2,3},{3,2},{4,5},{5,4},{6,7},{7,6},{8,9},{9,8},{10,11... | collective-permute-start | bytes 2555912 | tf_op jit(solution)/shard_map/ppermute | solution.py:129
  32.4 1.3 copy.59
  34.0 0.9 collective-permute-done.2
  34.9 2.5 %add_convert_fusion = bf16[8,104,512]{2,1,0:T(8,128)(2,1)} fusion(bf16[8,104,512]{2,1,0:T(8,128)(2,1)} %collective-permute-done.2, bf16[512,104,1]{0,1,2:T(8,128)(2,1)} %copy-done.4, bf16[104,8,1,104]{0,3,1,2:T(8,128)(2,1)S(1)} %copy.59), kind=kOutput, calls=%fused_computation.45 | convolution fusion | flops 90734592 | bytes 1983488 | tf_op jit(solution)/shard_map/pe,ezf->zfp/dot_general | solution.py:124
  37.4 10.3 %all-to-all-start = ((bf16[8,104,512]{2,1,0:T(8,128)(2,1)}), bf16[8,104,512]{2,1,0:T(8,128)(2,1)}, u32[]{:S(2)}, u32[]{:S(2)}) async-start(bf16[8,104,512]{2,1,0:T(8,128)(2,1)} %add_convert_fusion), calls=%async_computation | async-start | bytes 1703936 | tf_op jit(solution)/shard_map/all_to_all | solution.py:35
  47.9 1.5 fusion.68
  49.4 0.7 copy.49
  50.4 22.2 %all-to-all-done = bf16[8,104,512]{2,1,0:T(8,128)(2,1)} async-done(((bf16[8,104,512]{2,1,0:T(8,128)(2,1)}), bf16[8,104,512]{2,1,0:T(8,128)(2,1)}, u32[]{:S(2)}, u32[]{:S(2)}) %all-to-all-start) | async-done | bytes 852000 | tf_op jit(solution)/shard_map/all_to_all | solution.py:35
  72.6 1.3 convert_reduce_fusion.3
  74.1 1.5 fusion.40
  75.6 13.6 %all_to_all.37 = bf16[16,8,1024]{2,1,0:T(8,128)(2,1)S(1)} all-to-all(bf16[16,8,1024]{2,1,0:T(8,128)(2,1)S(1)} %fusion.40), channel_id=1, replica_groups=mesh['gx'=4,'gy'=8,'z'=8,'core'=2] {'z','core'}, dimensions={0} | all-to-all | bytes 524288 | tf_op jit(solution)/shard_map/all_to_all | solution.py:35
  89.3 0.7 broadcast_in_dim.68
  90.0 3.5 %all-to-all-start.2 = ((bf16[16,8,1024]{2,1,0:T(8,128)(2,1)}), bf16[16,8,1024]{2,1,0:T(8,128)(2,1)S(1)}, u32[]{:S(2)}, u32[]{:S(2)}) async-start(bf16[16,8,1024]{2,1,0:T(8,128)(2,1)} %broadcast_in_dim.68), calls=%async_computation.2 | async-start | bytes 524288 | tf_op jit(solution)/shard_map/all_to_all | solution.py:26
  93.7 11.2 %all-to-all-done.2 = bf16[16,8,1024]{2,1,0:T(8,128)(2,1)S(1)} async-done(((bf16[16,8,1024]{2,1,0:T(8,128)(2,1)}), bf16[16,8,1024]{2,1,0:T(8,128)(2,1)S(1)}, u32[]{:S(2)}, u32[]{:S(2)}) %all-to-all-start.2) | async-done | bytes 262176 | tf_op jit(solution)/shard_map/all_to_all | solution.py:26
  105.4 1.4 fusion.78
  107.0 0.8 broadcast_in_dim.72
  107.7 6.2 %all-to-all-start.3 = ((bf16[8,128,128]{2,1,0:T(8,128)(2,1)}), bf16[8,128,128]{2,1,0:T(8,128)(2,1)S(1)}, u32[]{:S(2)}, u32[]{:S(2)}) async-start(bf16[8,128,128]{2,1,0:T(8,128)(2,1)} %broadcast_in_dim.72), calls=%async_computation.3 | async-start | bytes 524288 | tf_op jit(solution)/shard_map/all_to_all | solution.py:26
  114.3 14.8 %all-to-all-done.3 = bf16[8,128,128]{2,1,0:T(8,128)(2,1)S(1)} async-done(((bf16[8,128,128]{2,1,0:T(8,128)(2,1)}), bf16[8,128,128]{2,1,0:T(8,128)(2,1)S(1)}, u32[]{:S(2)}, u32[]{:S(2)}) %all-to-all-start.3) | async-done | bytes 262176 | tf_op jit(solution)/shard_map/all_to_all | solution.py:26
  129.1 1.1 broadcast_in_dim.74
  130.3 4.8 %all-to-all-start.4 = ((bf16[4,1024,128]{2,1,0:T(8,128)(2,1)}), bf16[4,1024,128]{2,1,0:T(8,128)(2,1)S(1)}, u32[]{:S(2)}, u32[]{:S(2)}) async-start(bf16[4,1024,128]{2,1,0:T(8,128)(2,1)} %broadcast_in_dim.74), calls=%async_computation.4 | async-start | bytes 2097152 | tf_op jit(solution)/shard_map/all_to_all | solution.py:26
  135.1 2.0 %all-gather.2.cloned.1.call-done = bf16[8448,128]{1,0:T(8,128)(2,1)} async-done(((bf16[264,128]{1,0:T(8,128)(2,1)}), bf16[8448,128]{1,0:T(8,128)(2,1)}) %all-gather.2.cloned.1.call-update) | async-done | bytes 2162704 | tf_op jit(solution)/shard_map/all_gather | solution.py:80
  137.0 0.8 slice.106
  138.0 0.8 convert_reduce_fusion
  141.0 2.8 %fusion.6 = (f32[128]{0:T(128)S(1)}, f32[128,8448]{1,0:T(8,128)S(1)}) fusion(s32[8448]{0:T(1024)S(1)} %fusion.115, s32[128]{0:T(128)S(1)} %get-tuple-element.34, bf16[8448,128]{1,0:T(8,128)(2,1)} %all-gather.2.cloned.1.call-done, bf16[3,128,64]{1,2,0:T(8,128)(2,1)S(1)} %convert_bitcast_fusion.3), kind=kOutput, calls=%fused_computation.16 | convolution fusion | flops 142737280 | bytes 6542336 | tf_op jit(solution)/shard_map/dot_general | solution.py:40
  143.8 1.1 fusion.15
  145.4 2.1 %fusion = (f32[256]{0:T(256)S(1)}, f32[256,8448]{1,0:T(8,128)S(1)}) fusion(s32[8448]{0:T(1024)S(1)} %fusion.115, s32[256]{0:T(256)S(1)} %add_add_fusion, bf16[8448,128]{1,0:T(8,128)(2,1)S(1)} %copy-done.7, bf16[3,256,64]{1,2,0:T(8,128)(2,1)S(1)} %convert_bitcast_fusion.2), kind=kOutput, calls=%fused_computation.4 | convolution fusion | flops 285474560 | bytes 10885120 | tf_op jit(solution)/shard_map/dot_general | solution.py:40
  147.5 2.4 %fusion.1 = f32[256]{0:T(256)S(1)} fusion(f32[256,8448]{1,0:T(8,128)S(1)} %get-tuple-element.45, f32[256]{0:T(256)S(1)} %get-tuple-element.44, s32[8448]{0:T(1024)S(1)} %fusion.115, s32[256]{0:T(256)S(1)} %add_add_fusion), kind=kLoop, calls=%fused_computation.7 | loop fusion | flops 8650496 | bytes 8687616 | tf_op jit(solution)/shard_map/reduce_sum | solution.py:43
  149.9 2.0 %fusion.19 = f32[128,64]{0,1:T(8,128)S(1)} fusion(f32[128,8448]{1,0:T(8,128)S(1)} %get-tuple-element.43, f32[128]{0:T(128)S(1)} %get-tuple-element.42, s32[8448]{0:T(1024)S(1)} %fusion.115, s32[128]{0:T(128)S(1)} %get-tuple-element.34, bf16[8448,128]{1,0:T(8,128)(2,1)S(1)} %copy-done.7), kind=kOutput, calls=%fused_computation.31 | convolution fusion | flops 142737408 | bytes 6555648 | tf_op jit(solution)/shard_map/dot_general | solution.py:44
  151.9 2.8 %fusion.7 = f32[256,64]{0,1:T(8,128)S(1)} fusion(f32[256,8448]{1,0:T(8,128)S(1)} %get-tuple-element.45, f32[256]{0:T(256)S(1)} %get-tuple-element.44, s32[8448]{0:T(1024)S(1)} %fusion.115, s32[256]{0:T(256)S(1)} %add_add_fusion, bf16[8448,128]{1,0:T(8,128)(2,1)S(1)} %copy-done.7), kind=kOutput, calls=%fused_computation.17 | convolution fusion | flops 285474816 | bytes 10914816 | tf_op jit(solution)/shard_map/dot_general | solution.py:44
  154.7 1.6 fusion.3
  156.3 1.4 fusion.4
  157.7 1.8 fusion.52
  159.9 0.7 reshape.420
  160.6 7.4 %all-to-all-start.5 = ((bf16[32,2,256]{2,1,0:T(2,128)(2,1)}), bf16[32,2,256]{2,1,0:T(2,128)(2,1)S(1)}, u32[]{:S(2)}, u32[]{:S(2)}) async-start(bf16[32,2,256]{2,1,0:T(2,128)(2,1)} %reshape.420), calls=%async_computation.5 | async-start | bytes 65536 | tf_op jit(solution)/shard_map/all_to_all | solution.py:189
  168.2 7.8 %all-to-all-done.5 = bf16[32,2,256]{2,1,0:T(2,128)(2,1)S(1)} async-done(((bf16[32,2,256]{2,1,0:T(2,128)(2,1)}), bf16[32,2,256]{2,1,0:T(2,128)(2,1)S(1)}, u32[]{:S(2)}, u32[]{:S(2)}) %all-to-all-start.5) | async-done | bytes 32800 | tf_op jit(solution)/shard_map/all_to_all | solution.py:189
  176.4 0.8 fusion.48
  (92 shorter events, 7.4 us)
Async XLA Ops:
  6.5 7.6 %copy-start = (bf16[3,1664,104]{1,2,0:T(8,128)(2,1)S(1)}, bf16[3,1664,104]{1,2,0:T(8,128)(2,1)}, u32[]{:S(2)}) copy-start(bf16[3,1664,104]{1,2,0:T(8,128)(2,1)} %param.18) | copy-start | bytes 3115012
  6.5 7.6 %copy-start.1 = (bf16[512,1664]{1,0:T(8,128)(2,1)S(1)}, bf16[512,1664]{1,0:T(8,128)(2,1)}, u32[]{:S(2)}) copy-start(bf16[512,1664]{1,0:T(8,128)(2,1)} %param.14) | copy-start | bytes 5111812
  6.5 7.6 %copy-start.8 = (f32[1664]{0:T(1024)S(1)}, f32[1664]{0:T(1024)}, u32[]{:S(2)}) copy-start(f32[1664]{0:T(1024)} %param.17) | copy-start | bytes 19972
  6.5 7.6 %copy-start.9 = (f32[1664]{0:T(1024)S(1)}, f32[1664]{0:T(1024)}, u32[]{:S(2)}) copy-start(f32[1664]{0:T(1024)} %param.16) | copy-start | bytes 19972
  6.5 17.2 %collective-permute-start.1 = (s32[512]{0:T(512)}, s32[512]{0:T(512)S(1)}, u32[]{:S(2)}, u32[]{:S(2)}) collective-permute-start(s32[512]{0:T(512)} %param.15), channel_id=1, source_target_pairs={{0,16},{16,0},{32,48},{48,32},{64,80},{80,64},{96,112},{112,96},{1... | collective-permute-start | bytes 6152 | tf_op jit(solution)/shard_map/ppermute | solution.py:100
  15.2 8.6 %copy-start.5 = (s32[512]{0:T(512)S(1)}, s32[512]{0:T(512)}, u32[]{:S(2)}) copy-start(s32[512]{0:T(512)} %param.15) | copy-start | bytes 6148
  15.9 8.9 %collective-permute-start = (bf16[2,512,104]{1,2,0:T(8,128)(2,1)}, bf16[2,512,104]{1,2,0:T(8,128)(2,1)}, u32[]{:S(2)}, u32[]{:S(2)}) collective-permute-start(bf16[2,512,104]{1,2,0:T(8,128)(2,1)} %slice.112), channel_id=1, source_target_pairs={{0,16},{16,0},{32,48},{48,32},{64,80},{80,64},{96,112},{112,96},{1... | collective-permute-start | bytes 638984 | tf_op jit(solution)/shard_map/ppermute | solution.py:100
  27.1 1.9 %copy-start.3 = (bf16[104,8,1,104]{0,3,1,2:T(8,128)(2,1)S(1)}, bf16[104,8,1,104]{0,3,1,2:T(8,128)(2,1)}, u32[]{:S(2)}) copy-start(bf16[104,8,1,104]{0,3,1,2:T(8,128)(2,1)} %copy.60) | copy-start | bytes 519172
  27.1 5.1 %copy-start.2 = (bf16[256,1024]{1,0:T(8,128)(2,1)S(1)}, bf16[256,1024]{1,0:T(8,128)(2,1)}, u32[]{:S(2)}) copy-start(bf16[256,1024]{1,0:T(8,128)(2,1)} %param.22) | copy-start | bytes 1572868
  27.1 6.8 %copy-start.6 = (s32[128]{0:T(128)S(1)}, s32[128]{0:T(128)}, u32[]{:S(2)}) copy-start(s32[128]{0:T(128)} %param.21) | copy-start | bytes 1540
  29.0 3.4 %copy-start.4 = (bf16[512,104,1]{0,1,2:T(8,128)(2,1)}, bf16[512,104,1]{0,1,2:T(8,128)(2,1)S(1)}, u32[]{:S(2)}) copy-start(bf16[512,104,1]{0,1,2:T(8,128)(2,1)S(1)} %fusion.41) | copy-start | bytes 319492
  29.0 18.9 %copy-start.10 = (f32[1024]{0:T(1024)S(1)}, f32[1024]{0:T(1024)}, u32[]{:S(2)}) copy-start(f32[1024]{0:T(1024)} %param.24) | copy-start | bytes 12292
  29.0 18.9 %copy-start.11 = (f32[1024]{0:T(1024)S(1)}, f32[1024]{0:T(1024)}, u32[]{:S(2)}) copy-start(f32[1024]{0:T(1024)} %param.23) | copy-start | bytes 12292
  30.3 4.6 %collective-permute-start.2 = (bf16[8,104,512]{2,1,0:T(8,128)(2,1)}, bf16[8,104,512]{2,1,0:T(8,128)(2,1)}, u32[]{:S(2)}, u32[]{:S(2)}) collective-permute-start(bf16[8,104,512]{2,1,0:T(8,128)(2,1)} %convolution_convert_fusion), channel_id=1, source_target_pairs={{0,1},{1,0},{2,3},{3,2},{4,5},{5,4},{6,7},{7,6},{8,9},{9,8},{10,11... | collective-permute-start | bytes 2555912 | tf_op jit(solution)/shard_map/ppermute | solution.py:129
  37.4 35.2 %all-to-all-start = ((bf16[8,104,512]{2,1,0:T(8,128)(2,1)}), bf16[8,104,512]{2,1,0:T(8,128)(2,1)}, u32[]{:S(2)}, u32[]{:S(2)}) async-start(bf16[8,104,512]{2,1,0:T(8,128)(2,1)} %add_convert_fusion), calls=%async_computation | async-start | bytes 1703936 | tf_op jit(solution)/shard_map/all_to_all | solution.py:35
  47.7 89.4 %all-gather.2.cloned.1.call-start = ((), (), s32[]{:S(2)}) async-start(), calls=%async_computation.6 | async-start | bytes 2230272 | tf_op jit(solution)/shard_map/all_gather | solution.py:80
  90.0 14.9 %all-to-all-start.2 = ((bf16[16,8,1024]{2,1,0:T(8,128)(2,1)}), bf16[16,8,1024]{2,1,0:T(8,128)(2,1)S(1)}, u32[]{:S(2)}, u32[]{:S(2)}) async-start(bf16[16,8,1024]{2,1,0:T(8,128)(2,1)} %broadcast_in_dim.68), calls=%async_computation.2 | async-start | bytes 524288 | tf_op jit(solution)/shard_map/all_to_all | solution.py:26
  107.7 21.4 %all-to-all-start.3 = ((bf16[8,128,128]{2,1,0:T(8,128)(2,1)}), bf16[8,128,128]{2,1,0:T(8,128)(2,1)S(1)}, u32[]{:S(2)}, u32[]{:S(2)}) async-start(bf16[8,128,128]{2,1,0:T(8,128)(2,1)} %broadcast_in_dim.72), calls=%async_computation.3 | async-start | bytes 524288 | tf_op jit(solution)/shard_map/all_to_all | solution.py:26
  130.3 24.4 %all-to-all-start.4 = ((bf16[4,1024,128]{2,1,0:T(8,128)(2,1)}), bf16[4,1024,128]{2,1,0:T(8,128)(2,1)S(1)}, u32[]{:S(2)}, u32[]{:S(2)}) async-start(bf16[4,1024,128]{2,1,0:T(8,128)(2,1)} %broadcast_in_dim.74), calls=%async_computation.4 | async-start | bytes 2097152 | tf_op jit(solution)/shard_map/all_to_all | solution.py:26
  143.8 1.6 copy-start.7
  160.6 15.4 %all-to-all-start.5 = ((bf16[32,2,256]{2,1,0:T(2,128)(2,1)}), bf16[32,2,256]{2,1,0:T(2,128)(2,1)S(1)}, u32[]{:S(2)}, u32[]{:S(2)}) async-start(bf16[32,2,256]{2,1,0:T(2,128)(2,1)} %reshape.420), calls=%async_computation.5 | async-start | bytes 65536 | tf_op jit(solution)/shard_map/all_to_all | solution.py:189
Sparse Core Ops, SparseCore 0:
  51.7 85.2 all-gather.1

commit v9 on v8

--- a/solution.py
+++ b/solution.py
@@ -136,8 +136,12 @@
         "cmk,kce->me", windows, merge_weight, preferred_element_type=jnp.float32
     ).astype(jnp.bfloat16)
     ntp = nz * ncore
+    chip_rows = (
+        partial_rows.astype(jnp.float32)
+        + lax.ppermute(partial_rows, "core", pair).astype(jnp.float32)
+    ).astype(jnp.bfloat16)
     merged = a2a_gather(
-        a2a_sum(partial_rows.reshape(ntp, merged_count // ntp, -1), TP).astype(jnp.bfloat16), TP
+        a2a_sum(chip_rows.reshape(nz, merged_count // nz, -1), "z").astype(jnp.bfloat16), "z"
     )
 
     mnorm = normalize(merged.astype(jnp.float32), dec_gain, dec_bias).astype(jnp.bfloat16)

time: 186 us -> 201 us (1.081)
  waiting for transfers between devices: 60.1 us -> 77.1 us
  blocking collectives: 13.6 us -> 0 us
  starting transfers between devices: 40.3 us -> 46.5 us
  matrix products: 26.8 us -> 29.6 us
    all_gather x1, waiting for transfers between devices: 1.97 us -> 16 us  [body(): text_kv = lax.all_gather(payload, GRP, axis=0, tiled=True)]
    all_to_all x1 -> x0, blocking collectives: 13.6 us -> none  [a2a_sum(): got = lax.all_to_all(parts, axis, 0, 0, tiled=True)]
    all_to_all x1 -> x2, waiting for transfers between devices: 22.2 us -> 34.2 us  [a2a_sum(): got = lax.all_to_all(parts, axis, 0, 0, tiled=True)]
    all_to_all x3, waiting for transfers between devices: 26.1 us -> 15.4 us  [a2a_gather(): got = lax.all_to_all(spread, axis, 0, 0, tiled=True)]
    dot_general x3, matrix products: 6.64 us -> 10.6 us  [attend_part(): jnp.dot(expo.astype(jnp.bfloat16), values, preferred_element_type=jnp.flo...]
    all_to_all x1 -> x2, starting transfers between devices: 10.3 us -> 13.7 us  [a2a_sum(): got = lax.all_to_all(parts, axis, 0, 0, tiled=True)]
    unnamed x29 -> x33, local copies, waits for them, and re-layouts: 4.65 us -> 5.79 us
  transfers between devices with their start and end apart: 9 -> 11, of which waited for: 7 -> 9; matrix products, arithmetic and copies ran while one was open for 22% -> 22% of each run, Pallas kernels for 0% -> 0%
where the time goes in v9:
time: 201 us; the launch traced here: 198 us
  waiting for transfers between devices  77.1 us (38%)
  starting transfers between devices  46.5 us (23%)
  matrix products  29.6 us (15%)
  other arithmetic  15.8 us (8%)
  local copies, waits for them, and re-layouts  15.4 us (8%)
  between operations  14 us (7%)
    all_to_all x2, waiting for transfers between devices, a2a_sum(): got = lax.all_to_all(parts, axis, 0, 0, tiled=True)  34.2 us
    all_gather x1, waiting for transfers between devices, body(): text_kv = lax.all_gather(payload, GRP, axis=0, tiled=True)  16 us
    all_to_all x3, waiting for transfers between devices, a2a_gather(): got = lax.all_to_all(spread, axis, 0, 0, tiled=True)  15.4 us
    all_to_all x3, starting transfers between devices, a2a_gather(): got = lax.all_to_all(spread, axis, 0, 0, tiled=True)  14.9 us
    all_to_all x2, starting transfers between devices, a2a_sum(): got = lax.all_to_all(parts, axis, 0, 0, tiled=True)  13.7 us
    dot_general x3, matrix products, attend_part(): jnp.dot(expo.astype(jnp.bfloat16), values, preferred_element_type=jnp.flo...  10.6 us
    all_to_all x1, starting transfers between devices, body(): got = lax.all_to_all(packed, GRP, 0, 0, tiled=True)  7.94 us
    all_to_all x1, waiting for transfers between devices, body(): got = lax.all_to_all(packed, GRP, 0, 0, tiled=True)  7.83 us
  transfers between devices with their start and end apart: 11, of which 9 were waited for; matrix products, arithmetic and copies ran while one was open for 22% of the time, Pallas kernels for 0%

profile of v9, /device:TPU:6, one launch (start us, length us, event | category | flops | bytes accessed | tf_op | source)
XLA Modules:
  0.0 198.5 jit_solution(1319839759101246245)
XLA Ops:
  6.5 3.7 %collective-permute-start.1 = (s32[512]{0:T(512)}, s32[512]{0:T(512)S(1)}, u32[]{:S(2)}, u32[]{:S(2)}) collective-permute-start(s32[512]{0:T(512)} %param.15), channel_id=1, source_target_pairs={{0,16},{16,0},{32,48},{48,32},{64,80},{80,64},{96,112},{112,96},{1... | collective-permute-start | bytes 6152 | tf_op jit(solution)/shard_map/ppermute | solution.py:100
  10.3 1.8 convert_reduce_fusion.1
  12.1 2.0 %fusion.11 = f32[512]{0:T(512)S(1)} fusion(bf16[512,1664]{1,0:T(8,128)(2,1)} %param.14, f32[512]{0:T(512)S(1)} %broadcast_multiply_fusion.1), kind=kLoop, calls=%fused_computation.22 | loop fusion | flops 3407360 | bytes 1708032 | tf_op jit(solution)/shard_map/reduce_sum | solution.py:19
  14.1 1.0 fusion.30
  15.9 2.3 %collective-permute-start = (bf16[2,512,104]{1,2,0:T(8,128)(2,1)}, bf16[2,512,104]{1,2,0:T(8,128)(2,1)}, u32[]{:S(2)}, u32[]{:S(2)}) collective-permute-start(bf16[2,512,104]{1,2,0:T(8,128)(2,1)} %slice.112), channel_id=1, source_target_pairs={{0,16},{16,0},{32,48},{48,32},{64,80},{80,64},{96,112},{112,96},{1... | collective-permute-start | bytes 638984 | tf_op jit(solution)/shard_map/ppermute | solution.py:100
  18.3 1.8 reshape.400
  20.1 1.8 constant_dynamic-slice_fusion.2
  21.9 1.9 copy.60
  23.8 1.1 collective-permute-done
  24.8 1.5 fusion.25
  27.1 1.9 fusion.40
  29.0 1.3 convolution_convert_fusion
  30.3 1.9 collective-permute-start.2
  32.2 1.3 copy.59
  33.6 1.2 collective-permute-done.2
  34.9 2.5 %add_convert_fusion = bf16[8,104,512]{2,1,0:T(8,128)(2,1)} fusion(bf16[8,104,512]{2,1,0:T(8,128)(2,1)} %collective-permute-done.2, bf16[512,104,1]{0,1,2:T(8,128)(2,1)} %copy-done.5, bf16[104,8,1,104]{0,3,1,2:T(8,128)(2,1)S(1)} %copy.59), kind=kOutput, calls=%fused_computation.45 | convolution fusion | flops 90734592 | bytes 1983488 | tf_op jit(solution)/shard_map/pe,ezf->zfp/dot_general | solution.py:124
  37.4 10.3 %all-to-all-start = ((bf16[8,104,512]{2,1,0:T(8,128)(2,1)}), bf16[8,104,512]{2,1,0:T(8,128)(2,1)}, u32[]{:S(2)}, u32[]{:S(2)}) async-start(bf16[8,104,512]{2,1,0:T(8,128)(2,1)} %add_convert_fusion), calls=%async_computation | async-start | bytes 1703936 | tf_op jit(solution)/shard_map/all_to_all | solution.py:35
  48.2 1.5 fusion.60
  50.7 21.9 %all-to-all-done = bf16[8,104,512]{2,1,0:T(8,128)(2,1)} async-done(((bf16[8,104,512]{2,1,0:T(8,128)(2,1)}), bf16[8,104,512]{2,1,0:T(8,128)(2,1)}, u32[]{:S(2)}, u32[]{:S(2)}) %all-to-all-start) | async-done | bytes 852000 | tf_op jit(solution)/shard_map/all_to_all | solution.py:35
  72.6 1.3 convert_reduce_fusion.3
  74.1 1.5 fusion.39
  75.6 1.9 collective-permute-start.3
  77.5 1.5 collective-permute-done.3
  79.0 0.8 add_convert_fusion.1
  79.8 3.4 %all-to-all-start.1 = ((bf16[8,16,1024]{2,1,0:T(8,128)(2,1)}), bf16[8,16,1024]{2,1,0:T(8,128)(2,1)S(1)}, u32[]{:S(2)}, u32[]{:S(2)}) async-start(bf16[8,16,1024]{2,1,0:T(8,128)(2,1)} %bitcast.33), calls=%async_computation.1 | async-start | bytes 524288 | tf_op jit(solution)/shard_map/all_to_all | solution.py:35
  83.3 12.3 %all-to-all-done.1 = bf16[8,16,1024]{2,1,0:T(8,128)(2,1)S(1)} async-done(((bf16[8,16,1024]{2,1,0:T(8,128)(2,1)}), bf16[8,16,1024]{2,1,0:T(8,128)(2,1)S(1)}, u32[]{:S(2)}, u32[]{:S(2)}) %all-to-all-start.1) | async-done | bytes 262176 | tf_op jit(solution)/shard_map/all_to_all | solution.py:35
  96.3 3.4 %all-to-all-start.2 = ((bf16[8,16,1024]{2,1,0:T(8,128)(2,1)}), bf16[8,16,1024]{2,1,0:T(8,128)(2,1)S(1)}, u32[]{:S(2)}, u32[]{:S(2)}) async-start(bf16[8,16,1024]{2,1,0:T(8,128)(2,1)} %broadcast_in_dim.68), calls=%async_computation.2 | async-start | bytes 524288 | tf_op jit(solution)/shard_map/all_to_all | solution.py:26
  100.1 11.9 %all-to-all-done.2 = bf16[8,16,1024]{2,1,0:T(8,128)(2,1)S(1)} async-done(((bf16[8,16,1024]{2,1,0:T(8,128)(2,1)}), bf16[8,16,1024]{2,1,0:T(8,128)(2,1)S(1)}, u32[]{:S(2)}, u32[]{:S(2)}) %all-to-all-start.2) | async-done | bytes 262176 | tf_op jit(solution)/shard_map/all_to_all | solution.py:26
  114.0 6.2 %all-to-all-start.3 = ((bf16[8,128,128]{2,1,0:T(8,128)(2,1)}), bf16[8,128,128]{2,1,0:T(8,128)(2,1)S(1)}, u32[]{:S(2)}, u32[]{:S(2)}) async-start(bf16[8,128,128]{2,1,0:T(8,128)(2,1)} %broadcast_in_dim.72), calls=%async_computation.3 | async-start | bytes 524288 | tf_op jit(solution)/shard_map/all_to_all | solution.py:26
  120.2 16.0 %all-gather.2.cloned.1.call-done = bf16[8448,128]{1,0:T(8,128)(2,1)} async-done(((bf16[264,128]{1,0:T(8,128)(2,1)}), bf16[8448,128]{1,0:T(8,128)(2,1)}) %all-gather.2.cloned.1.call-update) | async-done | bytes 2162704 | tf_op jit(solution)/shard_map/all_gather | solution.py:80
  136.1 0.8 slice.106
  137.1 0.8 convert_reduce_fusion
  140.1 2.8 %fusion.6 = (f32[128]{0:T(128)S(1)}, f32[128,8448]{1,0:T(8,128)S(1)}) fusion(s32[8448]{0:T(1024)S(1)} %fusion.105, s32[128]{0:T(128)S(1)} %get-tuple-element.34, bf16[8448,128]{1,0:T(8,128)(2,1)} %all-gather.2.cloned.1.call-done, bf16[3,128,64]{1,2,0:T(8,128)(2,1)S(1)} %convert_bitcast_fusion.2), kind=kOutput, calls=%fused_computation.16 | convolution fusion | flops 142737280 | bytes 6542336 | tf_op jit(solution)/shard_map/dot_general | solution.py:40
  142.9 1.1 fusion.15
  144.5 2.1 %fusion = (f32[256]{0:T(256)S(1)}, f32[256,8448]{1,0:T(8,128)S(1)}) fusion(s32[8448]{0:T(1024)S(1)} %fusion.105, s32[256]{0:T(256)S(1)} %add_add_fusion, bf16[8448,128]{1,0:T(8,128)(2,1)S(1)} %copy-done.11, bf16[3,256,64]{1,2,0:T(8,128)(2,1)S(1)} %convert_bitcast_fusion.1), kind=kOutput, calls=%fused_computation.4 | convolution fusion | flops 285474560 | bytes 10885120 | tf_op jit(solution)/shard_map/dot_general | solution.py:40
  146.6 2.2 %fusion.1 = f32[256]{0:T(256)S(1)} fusion(f32[256,8448]{1,0:T(8,128)S(1)} %get-tuple-element.45, f32[256]{0:T(256)S(1)} %get-tuple-element.44, s32[8448]{0:T(1024)S(1)} %fusion.105, s32[256]{0:T(256)S(1)} %add_add_fusion), kind=kLoop, calls=%fused_computation.7 | loop fusion | flops 8650496 | bytes 8687616 | tf_op jit(solution)/shard_map/reduce_sum | solution.py:43
  148.8 1.1 copy-done.1
  149.9 2.0 %fusion.19 = f32[128,64]{0,1:T(8,128)S(1)} fusion(f32[128,8448]{1,0:T(8,128)S(1)} %get-tuple-element.43, f32[128]{0:T(128)S(1)} %get-tuple-element.42, s32[8448]{0:T(1024)S(1)} %fusion.105, s32[128]{0:T(128)S(1)} %get-tuple-element.34, bf16[8448,128]{1,0:T(8,128)(2,1)S(1)} %copy-done.11), kind=kOutput, calls=%fused_computation.31 | convolution fusion | flops 142737408 | bytes 6555648 | tf_op jit(solution)/shard_map/dot_general | solution.py:44
  151.9 1.1 broadcast_in_dim.74
  153.0 5.3 %all-to-all-start.4 = ((bf16[4,1024,128]{2,1,0:T(8,128)(2,1)}), bf16[4,1024,128]{2,1,0:T(8,128)(2,1)S(1)}, u32[]{:S(2)}, u32[]{:S(2)}) async-start(bf16[4,1024,128]{2,1,0:T(8,128)(2,1)} %broadcast_in_dim.74), calls=%async_computation.4 | async-start | bytes 2097152 | tf_op jit(solution)/shard_map/all_to_all | solution.py:26
  158.3 6.7 %fusion.7 = f32[256,64]{0,1:T(8,128)S(1)} fusion(f32[256,8448]{1,0:T(8,128)} %copy-done.1, f32[256]{0:T(256)S(1)} %get-tuple-element.44, s32[8448]{0:T(1024)S(1)} %fusion.105, s32[256]{0:T(256)S(1)} %add_add_fusion, bf16[8448,128]{1,0:T(8,128)(2,1)} %all-gather.2.cloned.1.call-done), kind=kOutput, calls=%fused_computation.17 | convolution fusion | flops 285474816 | bytes 10914816 | tf_op jit(solution)/shard_map/dot_general | solution.py:44
  165.1 3.5 %all-to-all-done.4 = bf16[4,1024,128]{2,1,0:T(8,128)(2,1)S(1)} async-done(((bf16[4,1024,128]{2,1,0:T(8,128)(2,1)}), bf16[4,1024,128]{2,1,0:T(8,128)(2,1)S(1)}, u32[]{:S(2)}, u32[]{:S(2)}) %all-to-all-start.4) | async-done | bytes 1048608 | tf_op jit(solution)/shard_map/all_to_all | solution.py:26
  168.6 1.6 fusion.3
  170.1 1.4 fusion.4
  171.6 1.8 fusion.51
  174.5 7.9 %all-to-all-start.5 = ((bf16[32,2,256]{2,1,0:T(2,128)(2,1)}), bf16[32,2,256]{2,1,0:T(2,128)(2,1)S(1)}, u32[]{:S(2)}, u32[]{:S(2)}) async-start(bf16[32,2,256]{2,1,0:T(2,128)(2,1)} %reshape.420), calls=%async_computation.5 | async-start | bytes 65536 | tf_op jit(solution)/shard_map/all_to_all | solution.py:193
  182.6 7.8 %all-to-all-done.5 = bf16[32,2,256]{2,1,0:T(2,128)(2,1)S(1)} async-done(((bf16[32,2,256]{2,1,0:T(2,128)(2,1)}), bf16[32,2,256]{2,1,0:T(2,128)(2,1)S(1)}, u32[]{:S(2)}, u32[]{:S(2)}) %all-to-all-start.5) | async-done | bytes 32800 | tf_op jit(solution)/shard_map/all_to_all | solution.py:193
  190.8 0.8 fusion.47
  (101 shorter events, 10.8 us)
Async XLA Ops:
  6.5 7.6 %copy-start = (bf16[3,1664,104]{1,2,0:T(8,128)(2,1)S(1)}, bf16[3,1664,104]{1,2,0:T(8,128)(2,1)}, u32[]{:S(2)}) copy-start(bf16[3,1664,104]{1,2,0:T(8,128)(2,1)} %param.18) | copy-start | bytes 3115012
  6.5 7.6 %copy-start.2 = (bf16[512,1664]{1,0:T(8,128)(2,1)S(1)}, bf16[512,1664]{1,0:T(8,128)(2,1)}, u32[]{:S(2)}) copy-start(bf16[512,1664]{1,0:T(8,128)(2,1)} %param.14) | copy-start | bytes 5111812
  6.5 7.6 %copy-start.12 = (f32[1664]{0:T(1024)S(1)}, f32[1664]{0:T(1024)}, u32[]{:S(2)}) copy-start(f32[1664]{0:T(1024)} %param.17) | copy-start | bytes 19972
  6.5 7.6 %copy-start.13 = (f32[1664]{0:T(1024)S(1)}, f32[1664]{0:T(1024)}, u32[]{:S(2)}) copy-start(f32[1664]{0:T(1024)} %param.16) | copy-start | bytes 19972
  6.5 17.2 %collective-permute-start.1 = (s32[512]{0:T(512)}, s32[512]{0:T(512)S(1)}, u32[]{:S(2)}, u32[]{:S(2)}) collective-permute-start(s32[512]{0:T(512)} %param.15), channel_id=1, source_target_pairs={{0,16},{16,0},{32,48},{48,32},{64,80},{80,64},{96,112},{112,96},{1... | collective-permute-start | bytes 6152 | tf_op jit(solution)/shard_map/ppermute | solution.py:100
  15.2 8.6 %copy-start.7 = (s32[512]{0:T(512)S(1)}, s32[512]{0:T(512)}, u32[]{:S(2)}) copy-start(s32[512]{0:T(512)} %param.15) | copy-start | bytes 6148
  15.9 8.9 %collective-permute-start = (bf16[2,512,104]{1,2,0:T(8,128)(2,1)}, bf16[2,512,104]{1,2,0:T(8,128)(2,1)}, u32[]{:S(2)}, u32[]{:S(2)}) collective-permute-start(bf16[2,512,104]{1,2,0:T(8,128)(2,1)} %slice.112), channel_id=1, source_target_pairs={{0,16},{16,0},{32,48},{48,32},{64,80},{80,64},{96,112},{112,96},{1... | collective-permute-start | bytes 638984 | tf_op jit(solution)/shard_map/ppermute | solution.py:100
  27.1 1.9 copy-start.4
  27.1 6.4 %copy-start.3 = (bf16[256,1024]{1,0:T(8,128)(2,1)S(1)}, bf16[256,1024]{1,0:T(8,128)(2,1)}, u32[]{:S(2)}) copy-start(bf16[256,1024]{1,0:T(8,128)(2,1)} %param.22) | copy-start | bytes 1572868
  27.1 6.5 %copy-start.8 = (s32[128]{0:T(128)S(1)}, s32[128]{0:T(128)}, u32[]{:S(2)}) copy-start(s32[128]{0:T(128)} %param.21) | copy-start | bytes 1540
  29.0 3.2 %copy-start.5 = (bf16[512,104,1]{0,1,2:T(8,128)(2,1)}, bf16[512,104,1]{0,1,2:T(8,128)(2,1)S(1)}, u32[]{:S(2)}) copy-start(bf16[512,104,1]{0,1,2:T(8,128)(2,1)S(1)} %fusion.40) | copy-start | bytes 319492
  29.0 19.2 %copy-start.9 = (f32[1024]{0:T(1024)S(1)}, f32[1024]{0:T(1024)}, u32[]{:S(2)}) copy-start(f32[1024]{0:T(1024)} %param.24) | copy-start | bytes 12292
  29.0 19.2 %copy-start.10 = (f32[1024]{0:T(1024)S(1)}, f32[1024]{0:T(1024)}, u32[]{:S(2)}) copy-start(f32[1024]{0:T(1024)} %param.23) | copy-start | bytes 12292
  30.3 4.6 %collective-permute-start.2 = (bf16[8,104,512]{2,1,0:T(8,128)(2,1)}, bf16[8,104,512]{2,1,0:T(8,128)(2,1)}, u32[]{:S(2)}, u32[]{:S(2)}) collective-permute-start(bf16[8,104,512]{2,1,0:T(8,128)(2,1)} %convolution_convert_fusion), channel_id=1, source_target_pairs={{0,1},{1,0},{2,3},{3,2},{4,5},{5,4},{6,7},{7,6},{8,9},{9,8},{10,11... | collective-permute-start | bytes 2555912 | tf_op jit(solution)/shard_map/ppermute | solution.py:129
  37.4 35.2 %all-to-all-start = ((bf16[8,104,512]{2,1,0:T(8,128)(2,1)}), bf16[8,104,512]{2,1,0:T(8,128)(2,1)}, u32[]{:S(2)}, u32[]{:S(2)}) async-start(bf16[8,104,512]{2,1,0:T(8,128)(2,1)} %add_convert_fusion), calls=%async_computation | async-start | bytes 1703936 | tf_op jit(solution)/shard_map/all_to_all | solution.py:35
  47.7 88.5 %all-gather.2.cloned.1.call-start = ((), (), s32[]{:S(2)}) async-start(), calls=%async_computation.6 | async-start | bytes 2230272 | tf_op jit(solution)/shard_map/all_gather | solution.py:80
  50.7 62.1 %copy-start.6 = (bf16[3,1024,64]{1,2,0:T(8,128)(2,1)S(1)}, bf16[3,1024,64]{1,2,0:T(8,128)(2,1)}, u32[]{:S(2)}) copy-start(bf16[3,1024,64]{1,2,0:T(8,128)(2,1)} %param.25) | copy-start | bytes 1179652
  75.6 3.4 %collective-permute-start.3 = (bf16[128,1024]{1,0:T(8,128)(2,1)S(1)}, bf16[128,1024]{1,0:T(8,128)(2,1)S(1)}, u32[]{:S(2)}, u32[]{:S(2)}) collective-permute-start(bf16[128,1024]{1,0:T(8,128)(2,1)S(1)} %fusion.39), channel_id=1, source_target_pairs={{0,1},{1,0},{2,3},{3,2},{4,5},{5,4},{6,7},{7,6},{8,9},{9,8},{10,11... | collective-permute-start | bytes 786440 | tf_op jit(solution)/shard_map/ppermute | solution.py:141
  79.8 15.8 %all-to-all-start.1 = ((bf16[8,16,1024]{2,1,0:T(8,128)(2,1)}), bf16[8,16,1024]{2,1,0:T(8,128)(2,1)S(1)}, u32[]{:S(2)}, u32[]{:S(2)}) async-start(bf16[8,16,1024]{2,1,0:T(8,128)(2,1)} %bitcast.33), calls=%async_computation.1 | async-start | bytes 524288 | tf_op jit(solution)/shard_map/all_to_all | solution.py:35
  96.3 15.7 %all-to-all-start.2 = ((bf16[8,16,1024]{2,1,0:T(8,128)(2,1)}), bf16[8,16,1024]{2,1,0:T(8,128)(2,1)S(1)}, u32[]{:S(2)}, u32[]{:S(2)}) async-start(bf16[8,16,1024]{2,1,0:T(8,128)(2,1)} %broadcast_in_dim.68), calls=%async_computation.2 | async-start | bytes 524288 | tf_op jit(solution)/shard_map/all_to_all | solution.py:26
  114.0 38.0 %all-to-all-start.3 = ((bf16[8,128,128]{2,1,0:T(8,128)(2,1)}), bf16[8,128,128]{2,1,0:T(8,128)(2,1)S(1)}, u32[]{:S(2)}, u32[]{:S(2)}) async-start(bf16[8,128,128]{2,1,0:T(8,128)(2,1)} %broadcast_in_dim.72), calls=%async_computation.3 | async-start | bytes 524288 | tf_op jit(solution)/shard_map/all_to_all | solution.py:26
  142.9 1.6 copy-start.11
  146.6 3.3 %copy-start.1 = (f32[256,8448]{1,0:T(8,128)}, f32[256,8448]{1,0:T(8,128)S(1)}, u32[]{:S(2)}) copy-start(f32[256,8448]{1,0:T(8,128)S(1)} %get-tuple-element.45) | copy-start | bytes 25952260
  153.0 15.5 %all-to-all-start.4 = ((bf16[4,1024,128]{2,1,0:T(8,128)(2,1)}), bf16[4,1024,128]{2,1,0:T(8,128)(2,1)S(1)}, u32[]{:S(2)}, u32[]{:S(2)}) async-start(bf16[4,1024,128]{2,1,0:T(8,128)(2,1)} %broadcast_in_dim.74), calls=%async_computation.4 | async-start | bytes 2097152 | tf_op jit(solution)/shard_map/all_to_all | solution.py:26
  174.5 16.0 %all-to-all-start.5 = ((bf16[32,2,256]{2,1,0:T(2,128)(2,1)}), bf16[32,2,256]{2,1,0:T(2,128)(2,1)S(1)}, u32[]{:S(2)}, u32[]{:S(2)}) async-start(bf16[32,2,256]{2,1,0:T(2,128)(2,1)} %reshape.420), calls=%async_computation.5 | async-start | bytes 65536 | tf_op jit(solution)/shard_map/all_to_all | solution.py:193
Sparse Core Ops, SparseCore 0:
  51.7 84.3 all-gather.1

commit v10 on v8

--- a/solution.py
+++ b/solution.py
@@ -146,7 +146,6 @@
     )
     merged_kv = grp_gather(jnp.concatenate([mproj[1], mproj[2]], axis=1))
 
-    query_pos = jnp.concatenate([own_text_pos, positions], axis=0)
     block = positions // tok
     seen = jnp.sum(
         ((all_pos[None, :] >= (block * tok)[:, None]) & (all_pos[None, :] <= positions[:, None])).astype(
@@ -161,22 +160,24 @@
     key_in = key_row % (text_count + pad_rows)
     text_key = jnp.where(key_in < text_count, key_grp * text_count + key_in, groups * tok)
     text_keys, text_values = text_kv[:, :DH], text_kv[:, DH:]
-    part_tt = attend_part(tproj[0], text_key[None, :] < text_limit[:, None], text_keys, text_values)
-    part_mt = attend_part(mproj[0], text_key[None, :] < merged_limit[:, None], text_keys, text_values)
-    part_t = [jnp.concatenate([a, b], axis=0) for a, b in zip(part_tt, part_mt)]
-    top_t, total_t, acc_t = part_t
-    dquery = jnp.concatenate([tproj[0], mproj[0]], axis=0)
-    top_m, total_m, acc_m = attend_part(
-        dquery, all_pos[None, :] <= query_pos[:, None], merged_kv[:, :DH], merged_kv[:, DH:]
-    )
-    best = jnp.maximum(top_t, top_m)
-    scale_t = jnp.exp(top_t - best)
-    scale_m = jnp.exp(top_m - best)
-    total = total_t * scale_t + total_m * scale_m
-    acc = acc_t * scale_t[:, None] + acc_m * scale_m[:, None]
-    result = (acc / total[:, None]).astype(jnp.bfloat16)
-    text_out = result[:text_count]
-    merged_out = result[text_count:]
+    merged_keys, merged_values = merged_kv[:, :DH], merged_kv[:, DH:]
+
+    def finish(part_a, part_b):
+        best = jnp.maximum(part_a[0], part_b[0])
+        scale_a = jnp.exp(part_a[0] - best)
+        scale_b = jnp.exp(part_b[0] - best)
+        total = part_a[1] * scale_a + part_b[1] * scale_b
+        acc = part_a[2] * scale_a[:, None] + part_b[2] * scale_b[:, None]
+        return (acc / total[:, None]).astype(jnp.bfloat16)
+
+    merged_out = finish(
+        attend_part(mproj[0], text_key[None, :] < merged_limit[:, None], text_keys, text_values),
+        attend_part(mproj[0], all_pos[None, :] <= positions[:, None], merged_keys, merged_values),
+    )
+    text_out = finish(
+        attend_part(tproj[0], text_key[None, :] < text_limit[:, None], text_keys, text_values),
+        attend_part(tproj[0], all_pos[None, :] <= own_text_pos[:, None], merged_keys, merged_values),
+    )
 
     target = positions // tok
     member = (target[:, None] == jnp.arange(groups, dtype=jnp.int32)[None, :]).astype(jnp.int32)

time: 186 us -> 199 us (1.070)
  matrix products: 26.8 us -> 36.5 us
  local copies, waits for them, and re-layouts: 14.4 us -> 20.8 us
  waiting for transfers between devices: 60.1 us -> 55.8 us
    dot_general x1, matrix products: 0.83 us -> 7.46 us  [body(): jnp.dot(text_land.astype(jnp.bfloat16), text_out, preferred_element_type=...]
    unnamed x29 -> x47, local copies, waits for them, and re-layouts: 4.65 us -> 11.1 us
    all_to_all x1, waiting for transfers between devices: 7.83 us -> 1.85 us  [body(): got = lax.all_to_all(packed, GRP, 0, 0, tiled=True)]
    dot_general x3 -> x4, matrix products: 6.44 us -> 11.2 us  [attend_part(): jnp.dot(query, keys.T, preferred_element_type=jnp.float32) * DH ** (-0.5)]
    dot_general x1, matrix products: 0.15 us -> 2.53 us  [body(): jnp.dot(select.astype(jnp.bfloat16), merged_out, preferred_element_type=j...]
    reduce_sum x3 -> x4, other arithmetic: 4.87 us -> 7.1 us  [attend_part(): total = jnp.sum(expo, axis=1)]
    dot_general x3 -> x2, matrix products: 6.64 us -> 4.74 us  [attend_part(): jnp.dot(expo.astype(jnp.bfloat16), values, preferred_element_type=jnp.flo...]
  transfers between devices with their start and end apart: 9 -> 9, of which waited for: 7 -> 7; matrix products, arithmetic and copies ran while one was open for 22% -> 19% of each run, Pallas kernels for 0% -> 0%
where the time goes in v10:
time: 199 us; the launch traced here: 197 us
  waiting for transfers between devices  55.8 us (28%)
  starting transfers between devices  40.9 us (21%)
  matrix products  36.5 us (18%)
  local copies, waits for them, and re-layouts  20.8 us (10%)
  other arithmetic  15.7 us (8%)
  between operations  14 us (7%)
  blocking collectives  13.6 us (7%)
    all_to_all x3, waiting for transfers between devices, a2a_gather(): got = lax.all_to_all(spread, axis, 0, 0, tiled=True)  26.1 us
    all_to_all x1, waiting for transfers between devices, a2a_sum(): got = lax.all_to_all(parts, axis, 0, 0, tiled=True)  22.2 us
    all_to_all x3, starting transfers between devices, a2a_gather(): got = lax.all_to_all(spread, axis, 0, 0, tiled=True)  14.3 us
    all_to_all x1, blocking collectives, a2a_sum(): got = lax.all_to_all(parts, axis, 0, 0, tiled=True)  13.6 us
    dot_general x4, matrix products, attend_part(): jnp.dot(query, keys.T, preferred_element_type=jnp.float32) * DH ** (-0.5)  11.2 us
    unnamed x47, local copies, waits for them, and re-layouts  11.1 us
    all_to_all x1, starting transfers between devices, a2a_sum(): got = lax.all_to_all(parts, axis, 0, 0, tiled=True)  10.3 us
    all_to_all x1, starting transfers between devices, body(): got = lax.all_to_all(packed, GRP, 0, 0, tiled=True)  8.25 us
  transfers between devices with their start and end apart: 9, of which 7 were waited for; matrix products, arithmetic and copies ran while one was open for 19% of the time, Pallas kernels for 0%

profile of v10, /device:TPU:6, one launch (start us, length us, event | category | flops | bytes accessed | tf_op | source)
XLA Modules:
  0.0 197.4 jit_solution(13896637268567794491)
XLA Ops:
  6.5 3.7 %collective-permute-start.1 = (s32[512]{0:T(512)}, s32[512]{0:T(512)S(1)}, u32[]{:S(2)}, u32[]{:S(2)}) collective-permute-start(s32[512]{0:T(512)} %param.15), channel_id=1, source_target_pairs={{0,16},{16,0},{32,48},{48,32},{64,80},{80,64},{96,112},{112,96},{1... | collective-permute-start | bytes 6152 | tf_op jit(solution)/shard_map/ppermute | solution.py:100
  10.3 1.8 convert_reduce_fusion.1
  12.7 1.0 fusion.31
  14.5 2.3 %collective-permute-start = (bf16[2,512,104]{1,2,0:T(8,128)(2,1)}, bf16[2,512,104]{1,2,0:T(8,128)(2,1)}, u32[]{:S(2)}, u32[]{:S(2)}) collective-permute-start(bf16[2,512,104]{1,2,0:T(8,128)(2,1)} %slice.101), channel_id=1, source_target_pairs={{0,16},{16,0},{32,48},{48,32},{64,80},{80,64},{96,112},{112,96},{1... | collective-permute-start | bytes 638984 | tf_op jit(solution)/shard_map/ppermute | solution.py:100
  16.8 1.8 reshape.373
  18.7 1.8 constant_dynamic-slice_fusion.2
  20.5 1.9 copy.60
  22.3 1.1 collective-permute-done
  23.4 1.5 fusion.23
  25.6 1.9 fusion.44
  27.5 1.3 convolution_convert_fusion
  28.8 1.9 collective-permute-start.2
  30.9 1.3 copy.59
  32.5 0.9 collective-permute-done.2
  33.4 2.5 %add_convert_fusion = bf16[8,104,512]{2,1,0:T(8,128)(2,1)} fusion(bf16[8,104,512]{2,1,0:T(8,128)(2,1)} %collective-permute-done.2, bf16[512,104,1]{0,1,2:T(8,128)(2,1)} %copy-done.9, bf16[104,8,1,104]{0,3,1,2:T(8,128)(2,1)S(1)} %copy.59), kind=kOutput, calls=%fused_computation.50 | convolution fusion | flops 90734592 | bytes 1983488 | tf_op jit(solution)/shard_map/pe,ezf->zfp/dot_general | solution.py:124
  35.9 10.3 %all-to-all-start = ((bf16[8,104,512]{2,1,0:T(8,128)(2,1)}), bf16[8,104,512]{2,1,0:T(8,128)(2,1)}, u32[]{:S(2)}, u32[]{:S(2)}) async-start(bf16[8,104,512]{2,1,0:T(8,128)(2,1)} %add_convert_fusion), calls=%async_computation | async-start | bytes 1703936 | tf_op jit(solution)/shard_map/all_to_all | solution.py:35
  46.4 1.5 fusion.107
  47.9 0.7 copy.49
  48.9 22.2 %all-to-all-done = bf16[8,104,512]{2,1,0:T(8,128)(2,1)} async-done(((bf16[8,104,512]{2,1,0:T(8,128)(2,1)}), bf16[8,104,512]{2,1,0:T(8,128)(2,1)}, u32[]{:S(2)}, u32[]{:S(2)}) %all-to-all-start) | async-done | bytes 852000 | tf_op jit(solution)/shard_map/all_to_all | solution.py:35
  71.1 1.3 convert_reduce_fusion.3
  73.0 13.6 %all_to_all.37 = bf16[16,8,1024]{2,1,0:T(8,128)(2,1)S(1)} all-to-all(bf16[16,8,1024]{2,1,0:T(8,128)(2,1)S(1)} %fusion.43), channel_id=1, replica_groups=mesh['gx'=4,'gy'=8,'z'=8,'core'=2] {'z','core'}, dimensions={0} | all-to-all | bytes 524288 | tf_op jit(solution)/shard_map/all_to_all | solution.py:35
  87.4 3.5 %all-to-all-start.2 = ((bf16[16,8,1024]{2,1,0:T(8,128)(2,1)}), bf16[16,8,1024]{2,1,0:T(8,128)(2,1)S(1)}, u32[]{:S(2)}, u32[]{:S(2)}) async-start(bf16[16,8,1024]{2,1,0:T(8,128)(2,1)} %broadcast_in_dim.73), calls=%async_computation.2 | async-start | bytes 524288 | tf_op jit(solution)/shard_map/all_to_all | solution.py:26
  91.0 11.2 %all-to-all-done.2 = bf16[16,8,1024]{2,1,0:T(8,128)(2,1)S(1)} async-done(((bf16[16,8,1024]{2,1,0:T(8,128)(2,1)}), bf16[16,8,1024]{2,1,0:T(8,128)(2,1)S(1)}, u32[]{:S(2)}, u32[]{:S(2)}) %all-to-all-start.2) | async-done | bytes 262176 | tf_op jit(solution)/shard_map/all_to_all | solution.py:26
  103.3 0.7 broadcast_in_dim.76
  104.0 6.2 %all-to-all-start.3 = ((bf16[8,128,128]{2,1,0:T(8,128)(2,1)}), bf16[8,128,128]{2,1,0:T(8,128)(2,1)S(1)}, u32[]{:S(2)}, u32[]{:S(2)}) async-start(bf16[8,128,128]{2,1,0:T(8,128)(2,1)} %broadcast_in_dim.76), calls=%async_computation.3 | async-start | bytes 524288 | tf_op jit(solution)/shard_map/all_to_all | solution.py:26
  110.6 14.9 %all-to-all-done.3 = bf16[8,128,128]{2,1,0:T(8,128)(2,1)S(1)} async-done(((bf16[8,128,128]{2,1,0:T(8,128)(2,1)}), bf16[8,128,128]{2,1,0:T(8,128)(2,1)S(1)}, u32[]{:S(2)}, u32[]{:S(2)}) %all-to-all-start.3) | async-done | bytes 262176 | tf_op jit(solution)/shard_map/all_to_all | solution.py:26
  125.5 1.2 broadcast_in_dim.78
  126.7 4.6 %all-to-all-start.4 = ((bf16[4,1024,128]{2,1,0:T(8,128)(2,1)}), bf16[4,1024,128]{2,1,0:T(8,128)(2,1)S(1)}, u32[]{:S(2)}, u32[]{:S(2)}) async-start(bf16[4,1024,128]{2,1,0:T(8,128)(2,1)} %broadcast_in_dim.78), calls=%async_computation.4 | async-start | bytes 2097152 | tf_op jit(solution)/shard_map/all_to_all | solution.py:26
  131.3 3.7 %all-gather.2.cloned.1.call-done = bf16[8448,128]{1,0:T(8,128)(2,1)} async-done(((bf16[264,128]{1,0:T(8,128)(2,1)}), bf16[8448,128]{1,0:T(8,128)(2,1)}) %all-gather.2.cloned.1.call-update) | async-done | bytes 2162704 | tf_op jit(solution)/shard_map/all_gather | solution.py:80
  135.0 0.8 slice.98
  135.9 0.8 convert_reduce_fusion
  139.1 2.8 %fusion.3 = (f32[128]{0:T(128)S(1)}, f32[128,8448]{1,0:T(8,128)S(1)}) fusion(s32[8448]{0:T(1024)S(1)} %fusion.151, s32[128]{0:T(128)S(1)} %get-tuple-element.36, bf16[8448,128]{1,0:T(8,128)(2,1)} %all-gather.2.cloned.1.call-done, bf16[3,128,64]{1,2,0:T(8,128)(2,1)S(1)} %convert_bitcast_fusion.3), kind=kOutput, calls=%fused_computation.14 | convolution fusion | flops 142737280 | bytes 6542336 | tf_op jit(solution)/shard_map/dot_general | solution.py:40
  141.9 2.0 %copy-done.3 = f32[128,8448]{1,0:T(8,128)} copy-done((f32[128,8448]{1,0:T(8,128)}, f32[128,8448]{1,0:T(8,128)S(1)}, u32[]{:S(2)}) %copy-start.3) | copy-done | bytes 4325400
  143.9 1.1 fusion.13
  145.5 2.1 %fusion = (f32[256]{0:T(256)S(1)}, f32[256,8448]{1,0:T(8,128)S(1)}) fusion(s32[8448]{0:T(1024)S(1)} %fusion.151, s32[256]{0:T(256)S(1)} %add_add_fusion, bf16[8448,128]{1,0:T(8,128)(2,1)S(1)} %copy-done.12, bf16[3,256,64]{1,2,0:T(8,128)(2,1)S(1)} %convert_bitcast_fusion.2), kind=kOutput, calls=%fused_computation.4 | convolution fusion | flops 285474560 | bytes 10885120 | tf_op jit(solution)/shard_map/dot_general | solution.py:40
  147.7 3.3 %copy-done.1 = f32[256,8448]{1,0:T(8,128)} copy-done((f32[256,8448]{1,0:T(8,128)}, f32[256,8448]{1,0:T(8,128)S(1)}, u32[]{:S(2)}) %copy-start.1) | copy-done | bytes 8650776
  150.9 2.1 %fusion.1 = f32[256]{0:T(256)S(1)} fusion(f32[256,8448]{1,0:T(8,128)S(1)} %get-tuple-element.48, f32[256]{0:T(256)S(1)} %get-tuple-element.47, s32[8448]{0:T(1024)S(1)} %fusion.151, s32[256]{0:T(256)S(1)} %add_add_fusion), kind=kLoop, calls=%fused_computation.5 | loop fusion | flops 8650496 | bytes 8687616 | tf_op jit(solution)/shard_map/reduce_sum | solution.py:43
  153.1 1.0 copy-done.6
  154.1 2.0 fusion.24
  156.1 4.3 %fusion.6 = (f32[256]{0:T(256)S(1)}, f32[256,4096]{1,0:T(8,128)}) fusion(s32[4096]{0:T(1024)S(1)} %get-tuple-element.33, s32[256]{0:T(256)S(1)} %broadcast_add_fusion.1, bf16[4096,128]{1,0:T(8,128)(2,1)} %bitcast.132, bf16[3,256,64]{1,2,0:T(8,128)(2,1)S(1)} %convert_bitcast_fusion.2), kind=kOutput, calls=%fused_computation.18 | convolution fusion | flops 138411776 | bytes 5294080 | tf_op jit(solution)/shard_map/dot_general | solution.py:40
  161.0 2.0 %fusion.61 = f32[128,64]{0,1:T(8,128)S(1)} fusion(bf16[8448,128]{1,0:T(8,128)(2,1)S(1)} %copy-done.13, f32[128,8448]{1,0:T(8,128)S(1)} %bitcast.129, f32[128]{0:T(128)S(1)} %get-tuple-element.41, s32[8448]{0:T(1024)S(1)} %fusion.151, s32[128]{0:T(128)S(1)} %get-tuple-element.36, f32[128]{0:T(128)S(1)} %get-tuple-element.22), kind=kOutput, calls=%fused_computation.78 | convolution fusion | flops 142745600 | bytes 6556160 | tf_op jit(solution)/shard_map/dot_general | solution.py:44
  163.1 2.5 %convolution_convert_fusion.3 = bf16[256,64]{0,1:T(8,128)(2,1)S(1)} fusion(f32[128,64]{0,1:T(8,128)S(1)} %fusion.61, f32[128,4096]{1,0:T(8,128)S(1)} %get-tuple-element.44, f32[128]{0:T(128)S(1)} %get-tuple-element.43, s32[4096]{0:T(1024)S(1)} %get-tuple-element.33, s32[128]{0:T(128)S(1)} %copy-done.11, bf16[4096,128]{1,0:T(8,128)(2,1)} %bitcast.133, ...), kind=kOutput, calls=%fused_computation.74 | convolution fusion | flops 73482240 | bytes 3230208 | tf_op jit(solution)/shard_map/dot_general | solution.py:187
  165.7 0.7 reshape.393
  166.5 8.3 %all-to-all-start.5 = ((bf16[32,2,256]{2,1,0:T(2,128)(2,1)}), bf16[32,2,256]{2,1,0:T(2,128)(2,1)S(1)}, u32[]{:S(2)}, u32[]{:S(2)}) async-start(bf16[32,2,256]{2,1,0:T(2,128)(2,1)} %reshape.393), calls=%async_computation.5 | async-start | bytes 65536 | tf_op jit(solution)/shard_map/all_to_all | solution.py:190
  174.7 3.3 %fusion.15 = f32[256]{0:T(256)S(1)} fusion(f32[256,4096]{1,0:T(8,128)} %get-tuple-element.46, f32[256]{0:T(256)S(1)} %get-tuple-element.45, s32[4096]{0:T(1024)S(1)} %get-tuple-element.33, s32[256]{0:T(256)S(1)} %broadcast_add_fusion.1), kind=kLoop, calls=%fused_computation.27 | loop fusion | flops 4194048 | bytes 4213760 | tf_op jit(solution)/shard_map/reduce_sum | solution.py:43
  178.2 2.7 %fusion.46 = f32[256,64]{0,1:T(8,128)S(1)} fusion(f32[256,4096]{1,0:T(8,128)S(1)} %copy-done.4, f32[256]{0:T(256)S(1)} %get-tuple-element.45, s32[4096]{0:T(1024)S(1)} %get-tuple-element.33, s32[256]{0:T(256)S(1)} %broadcast_add_fusion.1, bf16[4096,128]{1,0:T(8,128)(2,1)} %bitcast.134, f32[256]{0:T(256)S(1)} %get-tuple-element.19), kind=kOutput, calls=%fused_computation.71 | convolution fusion | flops 138428416 | bytes 5327872 | tf_op jit(solution)/shard_map/dot_general | solution.py:44
  180.9 1.9 all-to-all-done.5
  183.1 7.5 %fusion.45 = bf16[384,64]{0,1:T(8,128)(2,1)} fusion(f32[384,64]{0,1:T(8,128)S(1)} %fusion.114, f32[256,64]{0,1:T(8,128)S(1)} %fusion.46, bf16[8448,128]{1,0:T(8,128)(2,1)} %all-gather.2.cloned.1.call-done, f32[256,8448]{1,0:T(8,128)} %copy-done.1, f32[256]{0:T(256)S(1)} %get-tuple-element.47, s32[8448]{0:T(1024)S(1)} %fusion.151, s32[256]{0:T(256)S(1)} %add_add_fusion, ...), kind=kOutput, calls=%fused_computation.70 | convolution fusion | flops 298270720 | bytes 11065344 | tf_op jit(solution)/shard_map/dot_general | solution.py:203
  (112 shorter events, 9.9 us)
Async XLA Ops:
  6.5 6.1 %copy-start = (bf16[3,1664,104]{1,2,0:T(8,128)(2,1)S(1)}, bf16[3,1664,104]{1,2,0:T(8,128)(2,1)}, u32[]{:S(2)}) copy-start(bf16[3,1664,104]{1,2,0:T(8,128)(2,1)} %param.18) | copy-start | bytes 3115012
  6.5 5.5 %copy-start.2 = (bf16[512,1664]{1,0:T(8,128)(2,1)S(1)}, bf16[512,1664]{1,0:T(8,128)(2,1)}, u32[]{:S(2)}) copy-start(bf16[512,1664]{1,0:T(8,128)(2,1)} %param.14) | copy-start | bytes 5111812
  6.5 6.1 %copy-start.15 = (f32[1664]{0:T(1024)S(1)}, f32[1664]{0:T(1024)}, u32[]{:S(2)}) copy-start(f32[1664]{0:T(1024)} %param.17) | copy-start | bytes 19972
  6.5 6.1 %copy-start.16 = (f32[1664]{0:T(1024)S(1)}, f32[1664]{0:T(1024)}, u32[]{:S(2)}) copy-start(f32[1664]{0:T(1024)} %param.16) | copy-start | bytes 19972
  6.5 15.8 %collective-permute-start.1 = (s32[512]{0:T(512)}, s32[512]{0:T(512)S(1)}, u32[]{:S(2)}, u32[]{:S(2)}) collective-permute-start(s32[512]{0:T(512)} %param.15), channel_id=1, source_target_pairs={{0,16},{16,0},{32,48},{48,32},{64,80},{80,64},{96,112},{112,96},{1... | collective-permute-start | bytes 6152 | tf_op jit(solution)/shard_map/ppermute | solution.py:100
  13.7 8.6 %copy-start.10 = (s32[512]{0:T(512)S(1)}, s32[512]{0:T(512)}, u32[]{:S(2)}) copy-start(s32[512]{0:T(512)} %param.15) | copy-start | bytes 6148
  14.5 8.9 %collective-permute-start = (bf16[2,512,104]{1,2,0:T(8,128)(2,1)}, bf16[2,512,104]{1,2,0:T(8,128)(2,1)}, u32[]{:S(2)}, u32[]{:S(2)}) collective-permute-start(bf16[2,512,104]{1,2,0:T(8,128)(2,1)} %slice.101), channel_id=1, source_target_pairs={{0,16},{16,0},{32,48},{48,32},{64,80},{80,64},{96,112},{112,96},{1... | collective-permute-start | bytes 638984 | tf_op jit(solution)/shard_map/ppermute | solution.py:100
  25.6 1.9 copy-start.7
  25.6 5.1 %copy-start.5 = (bf16[256,1024]{1,0:T(8,128)(2,1)S(1)}, bf16[256,1024]{1,0:T(8,128)(2,1)}, u32[]{:S(2)}) copy-start(bf16[256,1024]{1,0:T(8,128)(2,1)} %param.22) | copy-start | bytes 1572868
  27.5 3.4 %copy-start.9 = (bf16[512,104,1]{0,1,2:T(8,128)(2,1)}, bf16[512,104,1]{0,1,2:T(8,128)(2,1)S(1)}, u32[]{:S(2)}) copy-start(bf16[512,104,1]{0,1,2:T(8,128)(2,1)S(1)} %fusion.44) | copy-start | bytes 319492
  27.5 4.9 %copy-start.11 = (s32[128]{0:T(128)S(1)}, s32[128]{0:T(128)}, u32[]{:S(2)}) copy-start(s32[128]{0:T(128)} %param.21) | copy-start | bytes 1540
  28.8 4.6 %collective-permute-start.2 = (bf16[8,104,512]{2,1,0:T(8,128)(2,1)}, bf16[8,104,512]{2,1,0:T(8,128)(2,1)}, u32[]{:S(2)}, u32[]{:S(2)}) collective-permute-start(bf16[8,104,512]{2,1,0:T(8,128)(2,1)} %convolution_convert_fusion), channel_id=1, source_target_pairs={{0,1},{1,0},{2,3},{3,2},{4,5},{5,4},{6,7},{7,6},{8,9},{9,8},{10,11... | collective-permute-start | bytes 2555912 | tf_op jit(solution)/shard_map/ppermute | solution.py:129
  32.1 14.3 %copy-start.17 = (f32[1024]{0:T(1024)S(1)}, f32[1024]{0:T(1024)}, u32[]{:S(2)}) copy-start(f32[1024]{0:T(1024)} %param.24) | copy-start | bytes 12292
  32.1 14.3 %copy-start.18 = (f32[1024]{0:T(1024)S(1)}, f32[1024]{0:T(1024)}, u32[]{:S(2)}) copy-start(f32[1024]{0:T(1024)} %param.23) | copy-start | bytes 12292
  35.9 35.3 %all-to-all-start = ((bf16[8,104,512]{2,1,0:T(8,128)(2,1)}), bf16[8,104,512]{2,1,0:T(8,128)(2,1)}, u32[]{:S(2)}, u32[]{:S(2)}) async-start(bf16[8,104,512]{2,1,0:T(8,128)(2,1)} %add_convert_fusion), calls=%async_computation | async-start | bytes 1703936 | tf_op jit(solution)/shard_map/all_to_all | solution.py:35
  46.2 88.8 %all-gather.2.cloned.1.call-start = ((), (), s32[]{:S(2)}) async-start(), calls=%async_computation.6 | async-start | bytes 2230272 | tf_op jit(solution)/shard_map/all_gather | solution.py:80
  48.8 23.8 %copy-start.8 = (bf16[4,104,1024]{2,1,0:T(8,128)(2,1)S(1)}, bf16[4,104,1024]{2,1,0:T(8,128)(2,1)}, u32[]{:S(2)}) copy-start(bf16[4,104,1024]{2,1,0:T(8,128)(2,1)} %param.20) | copy-start | bytes 2555908
  72.4 30.3 %copy-start.14 = (bf16[3,1024,64]{1,2,0:T(8,128)(2,1)S(1)}, bf16[3,1024,64]{1,2,0:T(8,128)(2,1)}, u32[]{:S(2)}) copy-start(bf16[3,1024,64]{1,2,0:T(8,128)(2,1)} %param.25) | copy-start | bytes 1179652
  87.4 14.9 %all-to-all-start.2 = ((bf16[16,8,1024]{2,1,0:T(8,128)(2,1)}), bf16[16,8,1024]{2,1,0:T(8,128)(2,1)S(1)}, u32[]{:S(2)}, u32[]{:S(2)}) async-start(bf16[16,8,1024]{2,1,0:T(8,128)(2,1)} %broadcast_in_dim.73), calls=%async_computation.2 | async-start | bytes 524288 | tf_op jit(solution)/shard_map/all_to_all | solution.py:26
  104.0 21.4 %all-to-all-start.3 = ((bf16[8,128,128]{2,1,0:T(8,128)(2,1)}), bf16[8,128,128]{2,1,0:T(8,128)(2,1)S(1)}, u32[]{:S(2)}, u32[]{:S(2)}) async-start(bf16[8,128,128]{2,1,0:T(8,128)(2,1)} %broadcast_in_dim.76), calls=%async_computation.3 | async-start | bytes 524288 | tf_op jit(solution)/shard_map/all_to_all | solution.py:26
  126.7 26.4 %all-to-all-start.4 = ((bf16[4,1024,128]{2,1,0:T(8,128)(2,1)}), bf16[4,1024,128]{2,1,0:T(8,128)(2,1)S(1)}, u32[]{:S(2)}, u32[]{:S(2)}) async-start(bf16[4,1024,128]{2,1,0:T(8,128)(2,1)} %broadcast_in_dim.78), calls=%async_computation.4 | async-start | bytes 2097152 | tf_op jit(solution)/shard_map/all_to_all | solution.py:26
  141.9 2.0 %copy-start.3 = (f32[128,8448]{1,0:T(8,128)}, f32[128,8448]{1,0:T(8,128)S(1)}, u32[]{:S(2)}) copy-start(f32[128,8448]{1,0:T(8,128)S(1)} %get-tuple-element.42) | copy-start | bytes 12976132
  143.9 1.6 copy-start.12
  147.6 3.3 %copy-start.1 = (f32[256,8448]{1,0:T(8,128)}, f32[256,8448]{1,0:T(8,128)S(1)}, u32[]{:S(2)}) copy-start(f32[256,8448]{1,0:T(8,128)S(1)} %get-tuple-element.48) | copy-start | bytes 25952260
  153.1 1.0 copy-start.6
  154.1 6.9 %slice-start = ((s8[4325376]{0:T(1024)(128)(4,1)}), s8[4194304]{0:T(1024)(128)(4,1)S(1)}, s32[]{:S(2)}) async-start(s8[4325376]{0:T(1024)(128)(4,1)} %bitcast.128), calls=%async_computation.7 | async-start | bytes 8388608
  156.1 4.9 %slice-start.1 = ((s8[4325376]{0:T(1024)(128)(4,1)}), s8[131072]{0:T(1024)(128)(4,1)S(1)}, s32[]{:S(2)}) async-start(s8[4325376]{0:T(1024)(128)(4,1)} %bitcast.128), calls=%async_computation.8 | async-start | bytes 262144
  156.1 4.9 %copy-start.13 = (bf16[8448,128]{1,0:T(8,128)(2,1)S(1)}, bf16[8448,128]{1,0:T(8,128)(2,1)}, u32[]{:S(2)}) copy-start(bf16[8448,128]{1,0:T(8,128)(2,1)} %all-gather.2.cloned.1.call-done) | copy-start | bytes 6488068
  166.5 16.3 %all-to-all-start.5 = ((bf16[32,2,256]{2,1,0:T(2,128)(2,1)}), bf16[32,2,256]{2,1,0:T(2,128)(2,1)S(1)}, u32[]{:S(2)}, u32[]{:S(2)}) async-start(bf16[32,2,256]{2,1,0:T(2,128)(2,1)} %reshape.393), calls=%async_computation.5 | async-start | bytes 65536 | tf_op jit(solution)/shard_map/all_to_all | solution.py:190
  174.7 3.5 %copy-start.4 = (f32[256,4096]{1,0:T(8,128)S(1)}, f32[256,4096]{1,0:T(8,128)}, u32[]{:S(2)}) copy-start(f32[256,4096]{1,0:T(8,128)} %get-tuple-element.46) | copy-start | bytes 12582916
Sparse Core Ops, SparseCore 0:
  50.2 84.7 all-gather.1

commit v11 on v8

--- a/solution.py
+++ b/solution.py
@@ -1,6 +1,7 @@
 import jax
 import jax.numpy as jnp
 from jax import lax
+from jax.experimental import pallas as pl
 from jax.sharding import Mesh
 from jax.sharding import PartitionSpec as P
 
@@ -34,6 +35,60 @@
 def a2a_sum(parts, axis):
     got = lax.all_to_all(parts, axis, 0, 0, tiled=True)
     return jnp.sum(got.astype(jnp.float32), axis=0)
+
+
+BLOCK = 256
+
+
+def text_attend_kernel(q_ref, kv_ref, rank_ref, lim_ref, top_ref, tot_ref, acc_ref):
+    q = q_ref[...]
+    lim = lim_ref[...]
+    rows = q.shape[0]
+
+    def step(i, carry):
+        best, total, acc = carry
+        start = pl.multiple_of(i * BLOCK, BLOCK)
+        kv = kv_ref[pl.ds(start, BLOCK), :]
+        keys = kv[:, :DH]
+        values = kv[:, DH:]
+        score = lax.dot_general(
+            q, keys, (((1,), (1,)), ((), ())), preferred_element_type=jnp.float32
+        ) * DH ** (-0.5)
+        allowed = rank_ref[:, pl.ds(start, BLOCK)] < lim
+        new_best = jnp.maximum(best, jnp.max(jnp.where(allowed, score, -1e30), axis=1, keepdims=True))
+        expo = jnp.where(allowed, jnp.exp(score - new_best), 0.0)
+        scale = jnp.exp(best - new_best)
+        total = total * scale + jnp.sum(expo, axis=1, keepdims=True)
+        acc = acc * scale + jnp.dot(expo.astype(jnp.bfloat16), values, preferred_element_type=jnp.float32)
+        return new_best, total, acc
+
+    init = (
+        jnp.full((rows, 1), -1e30, jnp.float32),
+        jnp.zeros((rows, 1), jnp.float32),
+        jnp.zeros((rows, DH), jnp.float32),
+    )
+    best, total, acc = lax.fori_loop(0, kv_ref.shape[0] // BLOCK, step, init)
+    top_ref[...] = best
+    tot_ref[...] = total
+    acc_ref[...] = acc
+
+
+def text_attend(query, kv, rank, limit):
+    rows = query.shape[0]
+    keys = kv.shape[0]
+    cost = pl.CostEstimate(
+        flops=4 * rows * keys * DH, transcendentals=rows * keys, bytes_accessed=kv.size * 2 + rows * DH * 6
+    )
+    top, total, acc = pl.pallas_call(
+        text_attend_kernel,
+        out_shape=(
+            jax.ShapeDtypeStruct((rows, 1), jnp.float32),
+            jax.ShapeDtypeStruct((rows, 1), jnp.float32),
+            jax.ShapeDtypeStruct((rows, DH), jnp.float32),
+        ),
+        cost_estimate=cost,
+    )(query, kv, rank.reshape(1, -1), limit.reshape(-1, 1))
+    return top[:, 0], total[:, 0], acc
 
 
 def attend_part(query, allowed, keys, values):
@@ -160,9 +215,8 @@
     key_grp = key_row // (text_count + pad_rows)
     key_in = key_row % (text_count + pad_rows)
     text_key = jnp.where(key_in < text_count, key_grp * text_count + key_in, groups * tok)
-    text_keys, text_values = text_kv[:, :DH], text_kv[:, DH:]
-    part_tt = attend_part(tproj[0], text_key[None, :] < text_limit[:, None], text_keys, text_values)
-    part_mt = attend_part(mproj[0], text_key[None, :] < merged_limit[:, None], text_keys, text_values)
+    part_tt = text_attend(tproj[0], text_kv, text_key, text_limit)
+    part_mt = text_attend(mproj[0], text_kv, text_key, merged_limit)
     part_t = [jnp.concatenate([a, b], axis=0) for a, b in zip(part_tt, part_mt)]
     top_t, total_t, acc_t = part_t
     dquery = jnp.concatenate([tproj[0], mproj[0]], axis=0)

time: 186 us -> 211 us (1.13)
  Pallas kernels: 0 us -> 36 us
  matrix products: 26.8 us -> 14.3 us
    pallas_call x0 -> x2, Pallas kernels: none -> 36 us  [text_attend(): pl.pallas_call(text_attend_kernel, out_shape=(jax.ShapeDtypeStruct((rows,...]
    dot_general x3 -> x1, matrix products: 6.44 us -> 1.24 us  [attend_part(): jnp.dot(query, keys.T, preferred_element_type=jnp.float32) * DH ** (-0.5)]
    dot_general x3 -> x1, matrix products: 6.64 us -> 1.48 us  [attend_part(): jnp.dot(expo.astype(jnp.bfloat16), values, preferred_element_type=jnp.flo...]
    pallas_call x0 -> x4, other arithmetic: none -> 3.95 us  [text_attend(): pl.pallas_call(text_attend_kernel, out_shape=(jax.ShapeDtypeStruct((rows,...]
    reduce_sum x3 -> x1, other arithmetic: 4.87 us -> 1.43 us  [attend_part(): total = jnp.sum(expo, axis=1)]
    unnamed x29 -> x39, local copies, waits for them, and re-layouts: 4.65 us -> 4.14 us
  transfers between devices with their start and end apart: 9 -> 9, of which waited for: 7 -> 7; matrix products, arithmetic and copies ran while one was open for 22% -> 15% of each run, Pallas kernels for 0% -> 17%
where the time goes in v11:
time: 211 us; the launch traced here: 209 us
  waiting for transfers between devices  59.3 us (28%)
  starting transfers between devices  40.2 us (19%)
  Pallas kernels  36 us (17%)
  other arithmetic  16.2 us (8%)
  local copies, waits for them, and re-layouts  15.1 us (7%)
  matrix products  14.3 us (7%)
  between operations  14 us (7%)
  blocking collectives  13.6 us (6%)
    pallas_call x2, Pallas kernels, text_attend(): pl.pallas_call(text_attend_kernel, out_shape=(jax.ShapeDtypeStruct((rows,...  36 us
    all_to_all x3, waiting for transfers between devices, a2a_gather(): got = lax.all_to_all(spread, axis, 0, 0, tiled=True)  24.5 us
    all_to_all x1, waiting for transfers between devices, a2a_sum(): got = lax.all_to_all(parts, axis, 0, 0, tiled=True)  21.2 us
    all_to_all x3, starting transfers between devices, a2a_gather(): got = lax.all_to_all(spread, axis, 0, 0, tiled=True)  14.4 us
    all_to_all x1, blocking collectives, a2a_sum(): got = lax.all_to_all(parts, axis, 0, 0, tiled=True)  13.6 us
    all_to_all x1, starting transfers between devices, a2a_sum(): got = lax.all_to_all(parts, axis, 0, 0, tiled=True)  10.4 us
    all_to_all x1, waiting for transfers between devices, body(): got = lax.all_to_all(packed, GRP, 0, 0, tiled=True)  7.83 us
    all_to_all x1, starting transfers between devices, body(): got = lax.all_to_all(packed, GRP, 0, 0, tiled=True)  7.34 us
  transfers between devices with their start and end apart: 9, of which 7 were waited for; matrix products, arithmetic and copies ran while one was open for 15% of the time, Pallas kernels for 17%

profile of v11, /device:TPU:6, one launch (start us, length us, event | category | flops | bytes accessed | tf_op | source)
XLA Modules:
  0.0 208.8 jit_solution(10373151904942312545)
XLA Ops:
  6.5 3.7 %collective-permute-start.1 = (s32[512]{0:T(512)}, s32[512]{0:T(512)S(1)}, u32[]{:S(2)}, u32[]{:S(2)}) collective-permute-start(s32[512]{0:T(512)} %param.15), channel_id=1, source_target_pairs={{0,16},{16,0},{32,48},{48,32},{64,80},{80,64},{96,112},{112,96},{1... | collective-permute-start | bytes 6152 | tf_op jit(solution)/shard_map/ppermute | solution.py:155
  10.3 1.8 convert_reduce_fusion.1
  12.7 1.0 fusion.12
  13.8 0.7 slice.102
  14.5 2.3 %collective-permute-start = (bf16[2,512,104]{1,2,0:T(8,128)(2,1)}, bf16[2,512,104]{1,2,0:T(8,128)(2,1)}, u32[]{:S(2)}, u32[]{:S(2)}) collective-permute-start(bf16[2,512,104]{1,2,0:T(8,128)(2,1)} %slice.102), channel_id=1, source_target_pairs={{0,16},{16,0},{32,48},{48,32},{64,80},{80,64},{96,112},{112,96},{1... | collective-permute-start | bytes 638984 | tf_op jit(solution)/shard_map/ppermute | solution.py:155
  16.8 1.8 reshape.453
  18.7 1.8 constant_dynamic-slice_fusion.2
  20.5 1.9 copy.76
  22.3 1.1 collective-permute-done
  23.4 1.5 fusion.11
  25.6 1.8 fusion.29
  27.5 1.3 convolution_convert_fusion
  28.8 1.9 collective-permute-start.2
  30.7 1.3 copy.75
  32.1 1.2 collective-permute-done.2
  33.4 2.5 %add_convert_fusion = bf16[8,104,512]{2,1,0:T(8,128)(2,1)} fusion(bf16[8,104,512]{2,1,0:T(8,128)(2,1)} %collective-permute-done.2, bf16[512,104,1]{0,1,2:T(8,128)(2,1)} %copy-done.5, bf16[104,8,1,104]{0,3,1,2:T(8,128)(2,1)S(1)} %copy.75), kind=kOutput, calls=%fused_computation.23 | convolution fusion | flops 90734592 | bytes 1983488 | tf_op jit(solution)/shard_map/pe,ezf->zfp/dot_general | solution.py:179
  35.9 10.4 %all-to-all-start = ((bf16[8,104,512]{2,1,0:T(8,128)(2,1)}), bf16[8,104,512]{2,1,0:T(8,128)(2,1)}, u32[]{:S(2)}, u32[]{:S(2)}) async-start(bf16[8,104,512]{2,1,0:T(8,128)(2,1)} %add_convert_fusion), calls=%async_computation | async-start | bytes 1703936 | tf_op jit(solution)/shard_map/all_to_all | solution.py:36
  46.7 1.5 fusion.50
  49.0 0.7 pad_maximum_fusion.1
  50.0 21.2 %all-to-all-done = bf16[8,104,512]{2,1,0:T(8,128)(2,1)} async-done(((bf16[8,104,512]{2,1,0:T(8,128)(2,1)}), bf16[8,104,512]{2,1,0:T(8,128)(2,1)}, u32[]{:S(2)}, u32[]{:S(2)}) %all-to-all-start) | async-done | bytes 852000 | tf_op jit(solution)/shard_map/all_to_all | solution.py:36
  71.2 1.3 convert_reduce_fusion.3
  73.1 13.6 %all_to_all.37 = bf16[16,8,1024]{2,1,0:T(8,128)(2,1)S(1)} all-to-all(bf16[16,8,1024]{2,1,0:T(8,128)(2,1)S(1)} %fusion.22), channel_id=1, replica_groups=mesh['gx'=4,'gy'=8,'z'=8,'core'=2] {'z','core'}, dimensions={0} | all-to-all | bytes 524288 | tf_op jit(solution)/shard_map/all_to_all | solution.py:36
  86.7 0.7 broadcast_in_dim.52
  87.5 3.5 %all-to-all-start.2 = ((bf16[16,8,1024]{2,1,0:T(8,128)(2,1)}), bf16[16,8,1024]{2,1,0:T(8,128)(2,1)S(1)}, u32[]{:S(2)}, u32[]{:S(2)}) async-start(bf16[16,8,1024]{2,1,0:T(8,128)(2,1)} %broadcast_in_dim.52), calls=%async_computation.2 | async-start | bytes 524288 | tf_op jit(solution)/shard_map/all_to_all | solution.py:27
  91.0 0.8 compare_select_fusion.4.rank_ref
  91.8 10.6 %all-to-all-done.2 = bf16[16,8,1024]{2,1,0:T(8,128)(2,1)S(1)} async-done(((bf16[16,8,1024]{2,1,0:T(8,128)(2,1)}), bf16[16,8,1024]{2,1,0:T(8,128)(2,1)S(1)}, u32[]{:S(2)}, u32[]{:S(2)}) %all-to-all-start.2) | async-done | bytes 262176 | tf_op jit(solution)/shard_map/all_to_all | solution.py:27
  104.1 0.8 broadcast_in_dim.54
  104.9 6.2 %all-to-all-start.3 = ((bf16[8,128,128]{2,1,0:T(8,128)(2,1)}), bf16[8,128,128]{2,1,0:T(8,128)(2,1)S(1)}, u32[]{:S(2)}, u32[]{:S(2)}) async-start(bf16[8,128,128]{2,1,0:T(8,128)(2,1)} %broadcast_in_dim.54), calls=%async_computation.3 | async-start | bytes 524288 | tf_op jit(solution)/shard_map/all_to_all | solution.py:27
  112.2 13.9 %all-to-all-done.3 = bf16[8,128,128]{2,1,0:T(8,128)(2,1)S(1)} async-done(((bf16[8,128,128]{2,1,0:T(8,128)(2,1)}), bf16[8,128,128]{2,1,0:T(8,128)(2,1)S(1)}, u32[]{:S(2)}, u32[]{:S(2)}) %all-to-all-start.3) | async-done | bytes 262176 | tf_op jit(solution)/shard_map/all_to_all | solution.py:27
  126.1 1.1 broadcast_in_dim.56
  127.2 4.7 %all-to-all-start.4 = ((bf16[4,1024,128]{2,1,0:T(8,128)(2,1)}), bf16[4,1024,128]{2,1,0:T(8,128)(2,1)S(1)}, u32[]{:S(2)}, u32[]{:S(2)}) async-start(bf16[4,1024,128]{2,1,0:T(8,128)(2,1)} %broadcast_in_dim.56), calls=%async_computation.4 | async-start | bytes 2097152 | tf_op jit(solution)/shard_map/all_to_all | solution.py:27
  131.9 3.5 %all-gather.2.cloned.1.call-done.kv_ref = bf16[8448,128]{1,0:T(8,128)(2,1)} async-done(((bf16[264,128]{1,0:T(8,128)(2,1)}), bf16[8448,128]{1,0:T(8,128)(2,1)}) %all-gather.2.cloned.1.call-update) | async-done | bytes 2162704 | tf_op jit(solution)/shard_map/all_gather | solution.py:135
  135.4 0.8 slice.98
  136.3 0.8 convert_reduce_fusion
  138.7 0.7 copy.70.lim_ref
  139.4 19.6 %shard_map.118 = (f32[256,1]{1,0:T(8,128)}, f32[256,1]{1,0:T(8,128)}, f32[256,64]{1,0:T(8,128)}) custom-call(bf16[256,64]{1,0:T(8,128)(2,1)} %get-tuple-element.38.q_ref, bf16[8448,128]{1,0:T(8,128)(2,1)} %all-gather.2.cloned.1.call-done.kv_ref, s32[1,8448]{1,0:T(1,128)} %compare_select_fusion.4.rank_ref, s32[256,1]{1,0:T(8,128)} %add_add_fusion.lim_ref), custom_call_target="tpu_custom_call" | custom-call | flops 553648128 | bytes 2260992 | tf_op jit(solution)/shard_map/pallas_call | solution.py:82
  159.0 1.0 reduce.9
  160.0 1.0 reduce.12
  161.0 16.4 %shard_map.119 = (f32[128,1]{1,0:T(8,128)}, f32[128,1]{1,0:T(8,128)}, f32[128,64]{1,0:T(8,128)}) custom-call(bf16[128,64]{1,0:T(8,128)(2,1)} %get-tuple-element.41.q_ref, bf16[8448,128]{1,0:T(8,128)(2,1)} %all-gather.2.cloned.1.call-done.kv_ref, s32[1,8448]{1,0:T(1,128)} %compare_select_fusion.4.rank_ref, s32[128,1]{1,0:T(8,128)} %copy.70.lim_ref), custom_call_target="tpu_custom_call" | custom-call | flops 276824064 | bytes 2211840 | tf_op jit(solution)/shard_map/pallas_call | solution.py:82
  177.5 0.9 reduce.10
  178.4 1.0 reduce.13
  180.1 1.2 fusion
  181.3 1.4 fusion.1
  182.8 1.5 fusion.34
  184.6 0.7 reshape.478
  185.3 7.3 %all-to-all-start.5 = ((bf16[32,2,256]{2,1,0:T(2,128)(2,1)}), bf16[32,2,256]{2,1,0:T(2,128)(2,1)S(1)}, u32[]{:S(2)}, u32[]{:S(2)}) async-start(bf16[32,2,256]{2,1,0:T(2,128)(2,1)} %reshape.478), calls=%async_computation.5 | async-start | bytes 65536 | tf_op jit(solution)/shard_map/all_to_all | solution.py:243
  192.9 7.8 %all-to-all-done.5 = bf16[32,2,256]{2,1,0:T(2,128)(2,1)S(1)} async-done(((bf16[32,2,256]{2,1,0:T(2,128)(2,1)}), bf16[32,2,256]{2,1,0:T(2,128)(2,1)S(1)}, u32[]{:S(2)}, u32[]{:S(2)}) %all-to-all-start.5) | async-done | bytes 32800 | tf_op jit(solution)/shard_map/all_to_all | solution.py:243
  201.1 0.8 fusion.30
  (102 shorter events, 9.4 us)
Async XLA Ops:
  6.5 6.1 %copy-start = (bf16[3,1664,104]{1,2,0:T(8,128)(2,1)S(1)}, bf16[3,1664,104]{1,2,0:T(8,128)(2,1)}, u32[]{:S(2)}) copy-start(bf16[3,1664,104]{1,2,0:T(8,128)(2,1)} %param.18) | copy-start | bytes 3115012
  6.5 5.5 %copy-start.1 = (bf16[512,1664]{1,0:T(8,128)(2,1)S(1)}, bf16[512,1664]{1,0:T(8,128)(2,1)}, u32[]{:S(2)}) copy-start(bf16[512,1664]{1,0:T(8,128)(2,1)} %param.14) | copy-start | bytes 5111812
  6.5 6.1 %copy-start.12 = (f32[1664]{0:T(1024)S(1)}, f32[1664]{0:T(1024)}, u32[]{:S(2)}) copy-start(f32[1664]{0:T(1024)} %param.17) | copy-start | bytes 19972
  6.5 6.1 %copy-start.13 = (f32[1664]{0:T(1024)S(1)}, f32[1664]{0:T(1024)}, u32[]{:S(2)}) copy-start(f32[1664]{0:T(1024)} %param.16) | copy-start | bytes 19972
  6.5 15.8 %collective-permute-start.1 = (s32[512]{0:T(512)}, s32[512]{0:T(512)S(1)}, u32[]{:S(2)}, u32[]{:S(2)}) collective-permute-start(s32[512]{0:T(512)} %param.15), channel_id=1, source_target_pairs={{0,16},{16,0},{32,48},{48,32},{64,80},{80,64},{96,112},{112,96},{1... | collective-permute-start | bytes 6152 | tf_op jit(solution)/shard_map/ppermute | solution.py:155
  13.7 8.6 %copy-start.8 = (s32[512]{0:T(512)S(1)}, s32[512]{0:T(512)}, u32[]{:S(2)}) copy-start(s32[512]{0:T(512)} %param.15) | copy-start | bytes 6148
  14.5 8.9 %collective-permute-start = (bf16[2,512,104]{1,2,0:T(8,128)(2,1)}, bf16[2,512,104]{1,2,0:T(8,128)(2,1)}, u32[]{:S(2)}, u32[]{:S(2)}) collective-permute-start(bf16[2,512,104]{1,2,0:T(8,128)(2,1)} %slice.102), channel_id=1, source_target_pairs={{0,16},{16,0},{32,48},{48,32},{64,80},{80,64},{96,112},{112,96},{1... | collective-permute-start | bytes 638984 | tf_op jit(solution)/shard_map/ppermute | solution.py:155
  25.6 1.9 copy-start.3
  27.5 3.2 %copy-start.5 = (bf16[512,104,1]{0,1,2:T(8,128)(2,1)}, bf16[512,104,1]{0,1,2:T(8,128)(2,1)S(1)}, u32[]{:S(2)}) copy-start(bf16[512,104,1]{0,1,2:T(8,128)(2,1)S(1)} %fusion.29) | copy-start | bytes 319492
  27.5 4.5 %copy-start.2 = (bf16[256,1024]{1,0:T(8,128)(2,1)S(1)}, bf16[256,1024]{1,0:T(8,128)(2,1)}, u32[]{:S(2)}) copy-start(bf16[256,1024]{1,0:T(8,128)(2,1)} %param.22) | copy-start | bytes 1572868
  28.8 4.6 %collective-permute-start.2 = (bf16[8,104,512]{2,1,0:T(8,128)(2,1)}, bf16[8,104,512]{2,1,0:T(8,128)(2,1)}, u32[]{:S(2)}, u32[]{:S(2)}) collective-permute-start(bf16[8,104,512]{2,1,0:T(8,128)(2,1)} %convolution_convert_fusion), channel_id=1, source_target_pairs={{0,1},{1,0},{2,3},{3,2},{4,5},{5,4},{6,7},{7,6},{8,9},{9,8},{10,11... | collective-permute-start | bytes 2555912 | tf_op jit(solution)/shard_map/ppermute | solution.py:184
  32.1 14.5 %copy-start.14 = (f32[1024]{0:T(1024)S(1)}, f32[1024]{0:T(1024)}, u32[]{:S(2)}) copy-start(f32[1024]{0:T(1024)} %param.24) | copy-start | bytes 12292
  32.1 14.5 %copy-start.15 = (f32[1024]{0:T(1024)S(1)}, f32[1024]{0:T(1024)}, u32[]{:S(2)}) copy-start(f32[1024]{0:T(1024)} %param.23) | copy-start | bytes 12292
  35.9 12.5 %copy-start.9 = (s32[128]{0:T(128)S(1)}, s32[128]{0:T(128)}, u32[]{:S(2)}) copy-start(s32[128]{0:T(128)} %param.21) | copy-start | bytes 1540
  35.9 35.4 %all-to-all-start = ((bf16[8,104,512]{2,1,0:T(8,128)(2,1)}), bf16[8,104,512]{2,1,0:T(8,128)(2,1)}, u32[]{:S(2)}, u32[]{:S(2)}) async-start(bf16[8,104,512]{2,1,0:T(8,128)(2,1)} %add_convert_fusion), calls=%async_computation | async-start | bytes 1703936 | tf_op jit(solution)/shard_map/all_to_all | solution.py:36
  46.3 89.1 %all-gather.2.cloned.1.call-start = ((), (), s32[]{:S(2)}) async-start(), calls=%async_computation.6 | async-start | bytes 2230272 | tf_op jit(solution)/shard_map/all_gather | solution.py:135
  49.9 22.8 %copy-start.4 = (bf16[4,104,1024]{2,1,0:T(8,128)(2,1)S(1)}, bf16[4,104,1024]{2,1,0:T(8,128)(2,1)}, u32[]{:S(2)}) copy-start(bf16[4,104,1024]{2,1,0:T(8,128)(2,1)} %param.20) | copy-start | bytes 2555908
  72.5 30.4 %copy-start.10 = (bf16[3,1024,64]{1,2,0:T(8,128)(2,1)S(1)}, bf16[3,1024,64]{1,2,0:T(8,128)(2,1)}, u32[]{:S(2)}) copy-start(bf16[3,1024,64]{1,2,0:T(8,128)(2,1)} %param.25) | copy-start | bytes 1179652
  87.5 14.9 %all-to-all-start.2 = ((bf16[16,8,1024]{2,1,0:T(8,128)(2,1)}), bf16[16,8,1024]{2,1,0:T(8,128)(2,1)S(1)}, u32[]{:S(2)}, u32[]{:S(2)}) async-start(bf16[16,8,1024]{2,1,0:T(8,128)(2,1)} %broadcast_in_dim.52), calls=%async_computation.2 | async-start | bytes 524288 | tf_op jit(solution)/shard_map/all_to_all | solution.py:27
  104.9 21.2 %all-to-all-start.3 = ((bf16[8,128,128]{2,1,0:T(8,128)(2,1)}), bf16[8,128,128]{2,1,0:T(8,128)(2,1)S(1)}, u32[]{:S(2)}, u32[]{:S(2)}) async-start(bf16[8,128,128]{2,1,0:T(8,128)(2,1)} %broadcast_in_dim.54), calls=%async_computation.3 | async-start | bytes 524288 | tf_op jit(solution)/shard_map/all_to_all | solution.py:27
  127.2 52.8 %all-to-all-start.4 = ((bf16[4,1024,128]{2,1,0:T(8,128)(2,1)}), bf16[4,1024,128]{2,1,0:T(8,128)(2,1)S(1)}, u32[]{:S(2)}, u32[]{:S(2)}) async-start(bf16[4,1024,128]{2,1,0:T(8,128)(2,1)} %broadcast_in_dim.56), calls=%async_computation.4 | async-start | bytes 2097152 | tf_op jit(solution)/shard_map/all_to_all | solution.py:27
  159.0 21.1 %copy-start.6 = (bf16[128,64]{1,0:T(8,128)(2,1)S(1)}, bf16[128,64]{1,0:T(8,128)(2,1)}, u32[]{:S(2)}) copy-start(bf16[128,64]{1,0:T(8,128)(2,1)} %get-tuple-element.41.q_ref) | copy-start | bytes 49156
  159.0 21.1 %copy-start.7 = (bf16[256,64]{1,0:T(8,128)(2,1)S(1)}, bf16[256,64]{1,0:T(8,128)(2,1)}, u32[]{:S(2)}) copy-start(bf16[256,64]{1,0:T(8,128)(2,1)} %get-tuple-element.38.q_ref) | copy-start | bytes 98308
  181.3 1.5 copy-start.11
  181.3 1.5 copy-start.16
  185.3 15.4 %all-to-all-start.5 = ((bf16[32,2,256]{2,1,0:T(2,128)(2,1)}), bf16[32,2,256]{2,1,0:T(2,128)(2,1)S(1)}, u32[]{:S(2)}, u32[]{:S(2)}) async-start(bf16[32,2,256]{2,1,0:T(2,128)(2,1)} %reshape.478), calls=%async_computation.5 | async-start | bytes 65536 | tf_op jit(solution)/shard_map/all_to_all | solution.py:243
Sparse Core Ops, SparseCore 0:
  50.3 85.0 all-gather.1

commit v12 on v11

--- a/solution.py
+++ b/solution.py
@@ -37,29 +37,28 @@
     return jnp.sum(got.astype(jnp.float32), axis=0)
 
 
-BLOCK = 256
-
-
-def text_attend_kernel(q_ref, kv_ref, rank_ref, lim_ref, top_ref, tot_ref, acc_ref):
+BLOCK = 1408
+
+
+def text_attend_kernel(q_ref, kt_ref, v_ref, rank_ref, lim_ref, top_ref, tot_ref, acc_ref):
     q = q_ref[...]
     lim = lim_ref[...]
     rows = q.shape[0]
 
     def step(i, carry):
         best, total, acc = carry
-        start = pl.multiple_of(i * BLOCK, BLOCK)
-        kv = kv_ref[pl.ds(start, BLOCK), :]
-        keys = kv[:, :DH]
-        values = kv[:, DH:]
-        score = lax.dot_general(
-            q, keys, (((1,), (1,)), ((), ())), preferred_element_type=jnp.float32
-        ) * DH ** (-0.5)
+        start = pl.multiple_of(i * BLOCK, 128)
+        score = jnp.dot(q, kt_ref[:, pl.ds(start, BLOCK)], preferred_element_type=jnp.float32) * (
+            DH ** (-0.5)
+        )
         allowed = rank_ref[:, pl.ds(start, BLOCK)] < lim
         new_best = jnp.maximum(best, jnp.max(jnp.where(allowed, score, -1e30), axis=1, keepdims=True))
         expo = jnp.where(allowed, jnp.exp(score - new_best), 0.0)
         scale = jnp.exp(best - new_best)
         total = total * scale + jnp.sum(expo, axis=1, keepdims=True)
-        acc = acc * scale + jnp.dot(expo.astype(jnp.bfloat16), values, preferred_element_type=jnp.float32)
+        acc = acc * scale + jnp.dot(
+            expo.astype(jnp.bfloat16), v_ref[pl.ds(start, BLOCK), :], preferred_element_type=jnp.float32
+        )
         return new_best, total, acc
 
     init = (
@@ -67,17 +66,17 @@
         jnp.zeros((rows, 1), jnp.float32),
         jnp.zeros((rows, DH), jnp.float32),
     )
-    best, total, acc = lax.fori_loop(0, kv_ref.shape[0] // BLOCK, step, init)
+    best, total, acc = lax.fori_loop(0, kt_ref.shape[1] // BLOCK, step, init, unroll=True)
     top_ref[...] = best
     tot_ref[...] = total
     acc_ref[...] = acc
 
 
-def text_attend(query, kv, rank, limit):
+def text_attend(query, keys_t, values, rank, limit):
     rows = query.shape[0]
-    keys = kv.shape[0]
+    keys = keys_t.shape[1]
     cost = pl.CostEstimate(
-        flops=4 * rows * keys * DH, transcendentals=rows * keys, bytes_accessed=kv.size * 2 + rows * DH * 6
+        flops=4 * rows * keys * DH, transcendentals=rows * keys, bytes_accessed=keys * DH * 4 + rows * DH * 6
     )
     top, total, acc = pl.pallas_call(
         text_attend_kernel,
@@ -87,7 +86,7 @@
             jax.ShapeDtypeStruct((rows, DH), jnp.float32),
         ),
         cost_estimate=cost,
-    )(query, kv, rank.reshape(1, -1), limit.reshape(-1, 1))
+    )(query, keys_t, values, rank.reshape(1, -1), limit.reshape(-1, 1))
     return top[:, 0], total[:, 0], acc
 
 
@@ -215,8 +214,9 @@
     key_grp = key_row // (text_count + pad_rows)
     key_in = key_row % (text_count + pad_rows)
     text_key = jnp.where(key_in < text_count, key_grp * text_count + key_in, groups * tok)
-    part_tt = text_attend(tproj[0], text_kv, text_key, text_limit)
-    part_mt = text_attend(mproj[0], text_kv, text_key, merged_limit)
+    text_keys_t, text_values = text_kv[:, :DH].T, text_kv[:, DH:]
+    part_tt = text_attend(tproj[0], text_keys_t, text_values, text_key, text_limit)
+    part_mt = text_attend(mproj[0], text_keys_t, text_values, text_key, merged_limit)
     part_t = [jnp.concatenate([a, b], axis=0) for a, b in zip(part_tt, part_mt)]
     top_t, total_t, acc_t = part_t
     dquery = jnp.concatenate([tproj[0], mproj[0]], axis=0)

time: 211 us -> 197 us (0.934)
  Pallas kernels: 36 us -> 13.4 us
  local copies, waits for them, and re-layouts: 15.1 us -> 21.2 us
  matrix products: 14.3 us -> 16.7 us
    pallas_call x2, Pallas kernels: 36 us -> 13.4 us  [text_attend(): pl.pallas_call(text_attend_kernel, out_shape=(jax.ShapeDtypeStruct((rows,...]
    slice x0 -> x1, local copies, waits for them, and re-layouts: none -> 4.06 us  [body(): text_keys_t, text_values = (text_kv[:, :DH].T, text_kv[:, DH:])]
    transpose x0 -> x1, local copies, waits for them, and re-layouts: none -> 2.13 us  [body(): text_keys_t, text_values = (text_kv[:, :DH].T, text_kv[:, DH:])]
  transfers between devices with their start and end apart: 9 -> 9, of which waited for: 7 -> 7; matrix products, arithmetic and copies ran while one was open for 15% -> 19% of each run, Pallas kernels for 17% -> 7%
where the time goes in v12:
time: 197 us; the launch traced here: 195 us
  waiting for transfers between devices  58.6 us (30%)
  starting transfers between devices  40.9 us (21%)
  local copies, waits for them, and re-layouts  21.2 us (11%)
  matrix products  16.7 us (8%)
  other arithmetic  16.1 us (8%)
  between operations  14 us (7%)
  blocking collectives  13.6 us (7%)
  Pallas kernels  13.4 us (7%)
    all_to_all x3, waiting for transfers between devices, a2a_gather(): got = lax.all_to_all(spread, axis, 0, 0, tiled=True)  24.5 us
    all_to_all x1, waiting for transfers between devices, a2a_sum(): got = lax.all_to_all(parts, axis, 0, 0, tiled=True)  21.3 us
    all_to_all x3, starting transfers between devices, a2a_gather(): got = lax.all_to_all(spread, axis, 0, 0, tiled=True)  14.9 us
    all_to_all x1, blocking collectives, a2a_sum(): got = lax.all_to_all(parts, axis, 0, 0, tiled=True)  13.6 us
    pallas_call x2, Pallas kernels, text_attend(): pl.pallas_call(text_attend_kernel, out_shape=(jax.ShapeDtypeStruct((rows,...  13.4 us
    all_to_all x1, starting transfers between devices, a2a_sum(): got = lax.all_to_all(parts, axis, 0, 0, tiled=True)  10.5 us
    all_to_all x1, waiting for transfers between devices, body(): got = lax.all_to_all(packed, GRP, 0, 0, tiled=True)  7.83 us
    all_to_all x1, starting transfers between devices, body(): got = lax.all_to_all(packed, GRP, 0, 0, tiled=True)  7.54 us
  transfers between devices with their start and end apart: 9, of which 7 were waited for; matrix products, arithmetic and copies ran while one was open for 19% of the time, Pallas kernels for 7%

profile of v12, /device:TPU:6, one launch (start us, length us, event | category | flops | bytes accessed | tf_op | source)
XLA Modules:
  0.0 194.6 jit_solution(10872605723322082320)
XLA Ops:
  6.5 3.7 %collective-permute-start.1 = (s32[512]{0:T(512)}, s32[512]{0:T(512)S(1)}, u32[]{:S(2)}, u32[]{:S(2)}) collective-permute-start(s32[512]{0:T(512)} %param.15), channel_id=1, source_target_pairs={{0,16},{16,0},{32,48},{48,32},{64,80},{80,64},{96,112},{112,96},{1... | collective-permute-start | bytes 6152 | tf_op jit(solution)/shard_map/ppermute | solution.py:154
  10.3 1.8 convert_reduce_fusion.1
  12.7 1.0 fusion.12
  14.5 2.3 %collective-permute-start = (bf16[2,512,104]{1,2,0:T(8,128)(2,1)}, bf16[2,512,104]{1,2,0:T(8,128)(2,1)}, u32[]{:S(2)}, u32[]{:S(2)}) collective-permute-start(bf16[2,512,104]{1,2,0:T(8,128)(2,1)} %slice.112), channel_id=1, source_target_pairs={{0,16},{16,0},{32,48},{48,32},{64,80},{80,64},{96,112},{112,96},{1... | collective-permute-start | bytes 638984 | tf_op jit(solution)/shard_map/ppermute | solution.py:154
  16.8 1.8 reshape.453
  18.7 1.8 constant_dynamic-slice_fusion.2
  20.5 1.9 copy.88
  22.3 1.1 collective-permute-done
  23.4 1.5 fusion.11
  25.6 1.8 fusion.29
  27.5 1.3 convolution_convert_fusion
  28.7 1.9 collective-permute-start.2
  30.7 1.3 copy.87
  32.1 1.2 collective-permute-done.2
  33.4 2.5 %add_convert_fusion = bf16[8,104,512]{2,1,0:T(8,128)(2,1)} fusion(bf16[8,104,512]{2,1,0:T(8,128)(2,1)} %collective-permute-done.2, bf16[512,104,1]{0,1,2:T(8,128)(2,1)} %copy-done.5, bf16[104,8,1,104]{0,3,1,2:T(8,128)(2,1)S(1)} %copy.87), kind=kOutput, calls=%fused_computation.24 | convolution fusion | flops 90734592 | bytes 1983488 | tf_op jit(solution)/shard_map/pe,ezf->zfp/dot_general | solution.py:178
  35.8 10.5 %all-to-all-start = ((bf16[8,104,512]{2,1,0:T(8,128)(2,1)}), bf16[8,104,512]{2,1,0:T(8,128)(2,1)}, u32[]{:S(2)}, u32[]{:S(2)}) async-start(bf16[8,104,512]{2,1,0:T(8,128)(2,1)} %add_convert_fusion), calls=%async_computation | async-start | bytes 1703936 | tf_op jit(solution)/shard_map/all_to_all | solution.py:36
  46.7 1.4 fusion.50
  50.0 21.3 %all-to-all-done = bf16[8,104,512]{2,1,0:T(8,128)(2,1)} async-done(((bf16[8,104,512]{2,1,0:T(8,128)(2,1)}), bf16[8,104,512]{2,1,0:T(8,128)(2,1)}, u32[]{:S(2)}, u32[]{:S(2)}) %all-to-all-start) | async-done | bytes 852000 | tf_op jit(solution)/shard_map/all_to_all | solution.py:36
  71.2 1.3 convert_reduce_fusion.3
  73.1 13.6 %all_to_all.37 = bf16[16,8,1024]{2,1,0:T(8,128)(2,1)S(1)} all-to-all(bf16[16,8,1024]{2,1,0:T(8,128)(2,1)S(1)} %fusion.22), channel_id=1, replica_groups=mesh['gx'=4,'gy'=8,'z'=8,'core'=2] {'z','core'}, dimensions={0} | all-to-all | bytes 524288 | tf_op jit(solution)/shard_map/all_to_all | solution.py:36
  86.7 0.7 broadcast_in_dim.52
  87.5 3.5 %all-to-all-start.2 = ((bf16[16,8,1024]{2,1,0:T(8,128)(2,1)}), bf16[16,8,1024]{2,1,0:T(8,128)(2,1)S(1)}, u32[]{:S(2)}, u32[]{:S(2)}) async-start(bf16[16,8,1024]{2,1,0:T(8,128)(2,1)} %broadcast_in_dim.52), calls=%async_computation.2 | async-start | bytes 524288 | tf_op jit(solution)/shard_map/all_to_all | solution.py:27
  91.0 0.8 compare_select_fusion.4.rank_ref
  91.8 10.6 %all-to-all-done.2 = bf16[16,8,1024]{2,1,0:T(8,128)(2,1)S(1)} async-done(((bf16[16,8,1024]{2,1,0:T(8,128)(2,1)}), bf16[16,8,1024]{2,1,0:T(8,128)(2,1)S(1)}, u32[]{:S(2)}, u32[]{:S(2)}) %all-to-all-start.2) | async-done | bytes 262176 | tf_op jit(solution)/shard_map/all_to_all | solution.py:27
  104.1 0.7 broadcast_in_dim.54
  104.8 6.2 %all-to-all-start.3 = ((bf16[8,128,128]{2,1,0:T(8,128)(2,1)}), bf16[8,128,128]{2,1,0:T(8,128)(2,1)S(1)}, u32[]{:S(2)}, u32[]{:S(2)}) async-start(bf16[8,128,128]{2,1,0:T(8,128)(2,1)} %broadcast_in_dim.54), calls=%async_computation.3 | async-start | bytes 524288 | tf_op jit(solution)/shard_map/all_to_all | solution.py:27
  112.1 13.9 %all-to-all-done.3 = bf16[8,128,128]{2,1,0:T(8,128)(2,1)S(1)} async-done(((bf16[8,128,128]{2,1,0:T(8,128)(2,1)}), bf16[8,128,128]{2,1,0:T(8,128)(2,1)S(1)}, u32[]{:S(2)}, u32[]{:S(2)}) %all-to-all-start.3) | async-done | bytes 262176 | tf_op jit(solution)/shard_map/all_to_all | solution.py:27
  126.0 1.1 broadcast_in_dim.56
  127.2 5.2 %all-to-all-start.4 = ((bf16[4,1024,128]{2,1,0:T(8,128)(2,1)}), bf16[4,1024,128]{2,1,0:T(8,128)(2,1)}, u32[]{:S(2)}, u32[]{:S(2)}) async-start(bf16[4,1024,128]{2,1,0:T(8,128)(2,1)} %broadcast_in_dim.56), calls=%async_computation.4 | async-start | bytes 2097152 | tf_op jit(solution)/shard_map/all_to_all | solution.py:27
  132.3 2.7 %all-gather.2.cloned.1.call-done = bf16[8448,128]{1,0:T(8,128)(2,1)} async-done(((bf16[264,128]{1,0:T(8,128)(2,1)}), bf16[8448,128]{1,0:T(8,128)(2,1)}) %all-gather.2.cloned.1.call-update) | async-done | bytes 2162704 | tf_op jit(solution)/shard_map/all_gather | solution.py:134
  135.1 0.8 slice.106
  136.0 0.8 convert_reduce_fusion
  138.1 4.1 %fusion.113 = (bf16[8448,64]{1,0:T(8,128)(2,1)}, bf16[64,8448]{0,1:T(8,128)(2,1)S(1)}) fusion(bf16[8448,128]{1,0:T(8,128)(2,1)} %all-gather.2.cloned.1.call-done), kind=kLoop, calls=%fused_computation.192 | loop fusion | bytes 4325376 | tf_op jit(solution)/shard_map/slice | solution.py:217
  142.4 0.7 copy.82.lim_ref
  143.1 2.1 %copy.74.kt_ref = bf16[64,8448]{1,0:T(8,128)(2,1)} copy(bf16[64,8448]{0,1:T(8,128)(2,1)S(1)} %get-tuple-element.37) | data formatting | bytes 2162688 | tf_op jit(solution)/shard_map/transpose | solution.py:217
  145.3 5.7 %shard_map.119 = (f32[128,1]{1,0:T(8,128)}, f32[128,1]{1,0:T(8,128)}, f32[128,64]{1,0:T(8,128)}) custom-call(bf16[128,64]{1,0:T(8,128)(2,1)} %get-tuple-element.43.q_ref, bf16[64,8448]{1,0:T(8,128)(2,1)} %copy.74.kt_ref, bf16[8448,64]{1,0:T(8,128)(2,1)} %get-tuple-element.36.v_ref, s32[1,8448]{1,0:T(1,128)} %compare_select_fusion.4.rank_ref, ...), custom_call_target="tpu_custom_call" | custom-call | flops 276824064 | bytes 2211840 | tf_op jit(solution)/shard_map/pallas_call | solution.py:81
  150.9 0.9 reduce.10
  151.9 1.0 reduce.13
  152.9 7.8 %shard_map.118 = (f32[256,1]{1,0:T(8,128)}, f32[256,1]{1,0:T(8,128)}, f32[256,64]{1,0:T(8,128)}) custom-call(bf16[256,64]{1,0:T(8,128)(2,1)} %get-tuple-element.40.q_ref, bf16[64,8448]{1,0:T(8,128)(2,1)} %copy.74.kt_ref, bf16[8448,64]{1,0:T(8,128)(2,1)} %get-tuple-element.36.v_ref, s32[1,8448]{1,0:T(1,128)} %compare_select_fusion.4.rank_ref, ...), custom_call_target="tpu_custom_call" | custom-call | flops 553648128 | bytes 2260992 | tf_op jit(solution)/shard_map/pallas_call | solution.py:81
  160.6 1.0 reduce.9
  161.6 1.0 reduce.12
  163.3 2.4 %fusion = (f32[384]{0:T(512)S(1)}, f32[384,4096]{1,0:T(8,128)S(1)}) fusion(s32[4096]{0:T(1024)S(1)} %get-tuple-element.46, s32[384]{0:T(512)S(1)} %pad_add_fusion.1, bf16[4096,128]{1,0:T(8,128)(2,1)} %bitcast.47, bf16[128,64]{1,0:T(8,128)(2,1)S(1)} %copy-done.6, bf16[256,64]{1,0:T(8,128)(2,1)S(1)} %copy-done.7), kind=kOutput, calls=%fused_computation.2 | convolution fusion | flops 207715968 | bytes 7408640 | tf_op jit(solution)/shard_map/dot_general | solution.py:94
  165.8 1.4 fusion.1
  167.2 2.7 %fusion.34 = bf16[384,64]{1,0:T(8,128)(2,1)S(1)} fusion(f32[384,4096]{1,0:T(8,128)S(1)} %get-tuple-element.55, f32[384]{0:T(512)S(1)} %get-tuple-element.54, s32[4096]{0:T(1024)S(1)} %get-tuple-element.46, s32[384]{0:T(512)S(1)} %pad_add_fusion.1, bf16[4096,128]{1,0:T(8,128)(2,1)} %bitcast.47, f32[128,64]{1,0:T(8,128)S(1)} %copy-done.11, ...), kind=kOutput, calls=%fused_computation.47 | convolution fusion | flops 207765504 | bytes 7511552 | tf_op jit(solution)/shard_map/dot_general | solution.py:98
  170.3 0.7 reshape.478
  171.0 7.5 %all-to-all-start.5 = ((bf16[32,2,256]{2,1,0:T(2,128)(2,1)}), bf16[32,2,256]{2,1,0:T(2,128)(2,1)S(1)}, u32[]{:S(2)}, u32[]{:S(2)}) async-start(bf16[32,2,256]{2,1,0:T(2,128)(2,1)} %reshape.478), calls=%async_computation.5 | async-start | bytes 65536 | tf_op jit(solution)/shard_map/all_to_all | solution.py:243
  178.7 7.8 %all-to-all-done.5 = bf16[32,2,256]{2,1,0:T(2,128)(2,1)S(1)} async-done(((bf16[32,2,256]{2,1,0:T(2,128)(2,1)}), bf16[32,2,256]{2,1,0:T(2,128)(2,1)S(1)}, u32[]{:S(2)}, u32[]{:S(2)}) %all-to-all-start.5) | async-done | bytes 32800 | tf_op jit(solution)/shard_map/all_to_all | solution.py:243
  186.9 0.8 fusion.30
  (104 shorter events, 10.8 us)
Async XLA Ops:
  6.5 6.1 %copy-start = (bf16[3,1664,104]{1,2,0:T(8,128)(2,1)S(1)}, bf16[3,1664,104]{1,2,0:T(8,128)(2,1)}, u32[]{:S(2)}) copy-start(bf16[3,1664,104]{1,2,0:T(8,128)(2,1)} %param.18) | copy-start | bytes 3115012
  6.5 5.5 %copy-start.1 = (bf16[512,1664]{1,0:T(8,128)(2,1)S(1)}, bf16[512,1664]{1,0:T(8,128)(2,1)}, u32[]{:S(2)}) copy-start(bf16[512,1664]{1,0:T(8,128)(2,1)} %param.14) | copy-start | bytes 5111812
  6.5 6.1 %copy-start.12 = (f32[1664]{0:T(1024)S(1)}, f32[1664]{0:T(1024)}, u32[]{:S(2)}) copy-start(f32[1664]{0:T(1024)} %param.17) | copy-start | bytes 19972
  6.5 6.1 %copy-start.13 = (f32[1664]{0:T(1024)S(1)}, f32[1664]{0:T(1024)}, u32[]{:S(2)}) copy-start(f32[1664]{0:T(1024)} %param.16) | copy-start | bytes 19972
  6.5 15.8 %collective-permute-start.1 = (s32[512]{0:T(512)}, s32[512]{0:T(512)S(1)}, u32[]{:S(2)}, u32[]{:S(2)}) collective-permute-start(s32[512]{0:T(512)} %param.15), channel_id=1, source_target_pairs={{0,16},{16,0},{32,48},{48,32},{64,80},{80,64},{96,112},{112,96},{1... | collective-permute-start | bytes 6152 | tf_op jit(solution)/shard_map/ppermute | solution.py:154
  13.7 8.6 %copy-start.8 = (s32[512]{0:T(512)S(1)}, s32[512]{0:T(512)}, u32[]{:S(2)}) copy-start(s32[512]{0:T(512)} %param.15) | copy-start | bytes 6148
  14.5 8.9 %collective-permute-start = (bf16[2,512,104]{1,2,0:T(8,128)(2,1)}, bf16[2,512,104]{1,2,0:T(8,128)(2,1)}, u32[]{:S(2)}, u32[]{:S(2)}) collective-permute-start(bf16[2,512,104]{1,2,0:T(8,128)(2,1)} %slice.112), channel_id=1, source_target_pairs={{0,16},{16,0},{32,48},{48,32},{64,80},{80,64},{96,112},{112,96},{1... | collective-permute-start | bytes 638984 | tf_op jit(solution)/shard_map/ppermute | solution.py:154
  25.6 1.9 copy-start.3
  27.5 3.2 %copy-start.5 = (bf16[512,104,1]{0,1,2:T(8,128)(2,1)}, bf16[512,104,1]{0,1,2:T(8,128)(2,1)S(1)}, u32[]{:S(2)}) copy-start(bf16[512,104,1]{0,1,2:T(8,128)(2,1)S(1)} %fusion.29) | copy-start | bytes 319492
  27.5 4.5 %copy-start.2 = (bf16[256,1024]{1,0:T(8,128)(2,1)S(1)}, bf16[256,1024]{1,0:T(8,128)(2,1)}, u32[]{:S(2)}) copy-start(bf16[256,1024]{1,0:T(8,128)(2,1)} %param.22) | copy-start | bytes 1572868
  28.7 4.6 %collective-permute-start.2 = (bf16[8,104,512]{2,1,0:T(8,128)(2,1)}, bf16[8,104,512]{2,1,0:T(8,128)(2,1)}, u32[]{:S(2)}, u32[]{:S(2)}) collective-permute-start(bf16[8,104,512]{2,1,0:T(8,128)(2,1)} %convolution_convert_fusion), channel_id=1, source_target_pairs={{0,1},{1,0},{2,3},{3,2},{4,5},{5,4},{6,7},{7,6},{8,9},{9,8},{10,11... | collective-permute-start | bytes 2555912 | tf_op jit(solution)/shard_map/ppermute | solution.py:183
  32.1 14.5 %copy-start.14 = (f32[1024]{0:T(1024)S(1)}, f32[1024]{0:T(1024)}, u32[]{:S(2)}) copy-start(f32[1024]{0:T(1024)} %param.24) | copy-start | bytes 12292
  32.1 14.5 %copy-start.15 = (f32[1024]{0:T(1024)S(1)}, f32[1024]{0:T(1024)}, u32[]{:S(2)}) copy-start(f32[1024]{0:T(1024)} %param.23) | copy-start | bytes 12292
  35.8 12.5 %copy-start.9 = (s32[128]{0:T(128)S(1)}, s32[128]{0:T(128)}, u32[]{:S(2)}) copy-start(s32[128]{0:T(128)} %param.21) | copy-start | bytes 1540
  35.8 35.4 %all-to-all-start = ((bf16[8,104,512]{2,1,0:T(8,128)(2,1)}), bf16[8,104,512]{2,1,0:T(8,128)(2,1)}, u32[]{:S(2)}, u32[]{:S(2)}) async-start(bf16[8,104,512]{2,1,0:T(8,128)(2,1)} %add_convert_fusion), calls=%async_computation | async-start | bytes 1703936 | tf_op jit(solution)/shard_map/all_to_all | solution.py:36
  46.3 88.8 %all-gather.2.cloned.1.call-start = ((), (), s32[]{:S(2)}) async-start(), calls=%async_computation.6 | async-start | bytes 2230272 | tf_op jit(solution)/shard_map/all_gather | solution.py:134
  49.8 22.9 %copy-start.4 = (bf16[4,104,1024]{2,1,0:T(8,128)(2,1)S(1)}, bf16[4,104,1024]{2,1,0:T(8,128)(2,1)}, u32[]{:S(2)}) copy-start(bf16[4,104,1024]{2,1,0:T(8,128)(2,1)} %param.20) | copy-start | bytes 2555908
  72.5 30.3 %copy-start.10 = (bf16[3,1024,64]{1,2,0:T(8,128)(2,1)S(1)}, bf16[3,1024,64]{1,2,0:T(8,128)(2,1)}, u32[]{:S(2)}) copy-start(bf16[3,1024,64]{1,2,0:T(8,128)(2,1)} %param.25) | copy-start | bytes 1179652
  87.5 14.9 %all-to-all-start.2 = ((bf16[16,8,1024]{2,1,0:T(8,128)(2,1)}), bf16[16,8,1024]{2,1,0:T(8,128)(2,1)S(1)}, u32[]{:S(2)}, u32[]{:S(2)}) async-start(bf16[16,8,1024]{2,1,0:T(8,128)(2,1)} %broadcast_in_dim.52), calls=%async_computation.2 | async-start | bytes 524288 | tf_op jit(solution)/shard_map/all_to_all | solution.py:27
  104.8 21.2 %all-to-all-start.3 = ((bf16[8,128,128]{2,1,0:T(8,128)(2,1)}), bf16[8,128,128]{2,1,0:T(8,128)(2,1)S(1)}, u32[]{:S(2)}, u32[]{:S(2)}) async-start(bf16[8,128,128]{2,1,0:T(8,128)(2,1)} %broadcast_in_dim.54), calls=%async_computation.3 | async-start | bytes 524288 | tf_op jit(solution)/shard_map/all_to_all | solution.py:27
  127.2 36.1 %all-to-all-start.4 = ((bf16[4,1024,128]{2,1,0:T(8,128)(2,1)}), bf16[4,1024,128]{2,1,0:T(8,128)(2,1)}, u32[]{:S(2)}, u32[]{:S(2)}) async-start(bf16[4,1024,128]{2,1,0:T(8,128)(2,1)} %broadcast_in_dim.56), calls=%async_computation.4 | async-start | bytes 2097152 | tf_op jit(solution)/shard_map/all_to_all | solution.py:27
  152.8 10.5 %copy-start.6 = (bf16[128,64]{1,0:T(8,128)(2,1)S(1)}, bf16[128,64]{1,0:T(8,128)(2,1)}, u32[]{:S(2)}) copy-start(bf16[128,64]{1,0:T(8,128)(2,1)} %get-tuple-element.43.q_ref) | copy-start | bytes 49156
  152.8 10.5 %copy-start.7 = (bf16[256,64]{1,0:T(8,128)(2,1)S(1)}, bf16[256,64]{1,0:T(8,128)(2,1)}, u32[]{:S(2)}) copy-start(bf16[256,64]{1,0:T(8,128)(2,1)} %get-tuple-element.40.q_ref) | copy-start | bytes 98308
  165.8 1.5 copy-start.11
  165.8 1.5 copy-start.16
  171.0 15.6 %all-to-all-start.5 = ((bf16[32,2,256]{2,1,0:T(2,128)(2,1)}), bf16[32,2,256]{2,1,0:T(2,128)(2,1)S(1)}, u32[]{:S(2)}, u32[]{:S(2)}) async-start(bf16[32,2,256]{2,1,0:T(2,128)(2,1)} %reshape.478), calls=%async_computation.5 | async-start | bytes 65536 | tf_op jit(solution)/shard_map/all_to_all | solution.py:243
Sparse Core Ops, SparseCore 0:
  50.3 84.6 all-gather.1

commit v13 on v8

--- a/solution.py
+++ b/solution.py
@@ -97,7 +97,14 @@
     )
     query = proj[0].reshape(rows, heads, HD)
     swap = [(i, i ^ 1) for i in range(lax.axis_size("gy"))]
-    partner_kv, partner_ids = lax.ppermute((proj[1:], patch_image), "gy", swap)
+    id_digit = 64
+    id_plane = jnp.zeros((1, rows, HD), jnp.bfloat16)
+    id_plane = id_plane.at[0, :, 0].set((patch_image // id_digit).astype(jnp.bfloat16))
+    id_plane = id_plane.at[0, :, 1].set((patch_image % id_digit).astype(jnp.bfloat16))
+    partner_all = lax.ppermute(jnp.concatenate([proj[1:], id_plane], axis=0), "gy", swap)
+    partner_kv = partner_all[:2]
+    partner_digits = partner_all[2, :, :2].astype(jnp.int32)
+    partner_ids = partner_digits[:, 0] * id_digit + partner_digits[:, 1]
     both_kv = jnp.concatenate([proj[1:], partner_kv], axis=1)
     both_ids = jnp.concatenate([patch_image, partner_ids], axis=0)
     keys = both_kv[0].reshape(2 * rows, heads, HD)

time: 186 us -> 191 us (1.027)
  other arithmetic: 15 us -> 19.5 us
    another operation x2 -> x4, other arithmetic: 0.34 us -> 3.17 us
    ppermute x2 -> x1, starting transfers between devices: 6.09 us -> 3.47 us  [body(): lax.ppermute(jnp.concatenate([proj[1:], id_plane], axis=0), 'gy', swap)]
    unnamed x29 -> x35, local copies, waits for them, and re-layouts: 4.65 us -> 4.73 us
  transfers between devices with their start and end apart: 9 -> 8, of which waited for: 7 -> 7; matrix products, arithmetic and copies ran while one was open for 22% -> 19% of each run, Pallas kernels for 0% -> 0%
where the time goes in v13:
time: 191 us; the launch traced here: 189 us
  waiting for transfers between devices  61.5 us (32%)
  starting transfers between devices  38.8 us (20%)
  matrix products  25.7 us (13%)
  other arithmetic  19.5 us (10%)
  local copies, waits for them, and re-layouts  16 us (8%)
  between operations  14 us (7%)
  blocking collectives  13.6 us (7%)
    all_to_all x3, waiting for transfers between devices, a2a_gather(): got = lax.all_to_all(spread, axis, 0, 0, tiled=True)  26.2 us
    all_to_all x1, waiting for transfers between devices, a2a_sum(): got = lax.all_to_all(parts, axis, 0, 0, tiled=True)  22.2 us
    all_to_all x3, starting transfers between devices, a2a_gather(): got = lax.all_to_all(spread, axis, 0, 0, tiled=True)  15.4 us
    all_to_all x1, blocking collectives, a2a_sum(): got = lax.all_to_all(parts, axis, 0, 0, tiled=True)  13.6 us
    all_to_all x1, starting transfers between devices, a2a_sum(): got = lax.all_to_all(parts, axis, 0, 0, tiled=True)  10.3 us
    all_to_all x1, waiting for transfers between devices, body(): got = lax.all_to_all(packed, GRP, 0, 0, tiled=True)  7.83 us
    all_to_all x1, starting transfers between devices, body(): got = lax.all_to_all(packed, GRP, 0, 0, tiled=True)  7.63 us
    dot_general x3, matrix products, attend_part(): jnp.dot(expo.astype(jnp.bfloat16), values, preferred_element_type=jnp.flo...  6.64 us
  transfers between devices with their start and end apart: 8, of which 7 were waited for; matrix products, arithmetic and copies ran while one was open for 19% of the time, Pallas kernels for 0%

profile of v13, /device:TPU:6, one launch (start us, length us, event | category | flops | bytes accessed | tf_op | source)
XLA Modules:
  0.0 189.2 jit_solution(7591203276370428843)
XLA Ops:
  7.1 2.0 %convert_reduce_fusion.1 = f32[512]{0:T(512)S(1)} fusion(bf16[512,1664]{1,0:T(8,128)(2,1)} %param.18), kind=kLoop, calls=%fused_computation.19 | loop fusion | flops 1703424 | bytes 1705984 | tf_op jit(solution)/shard_map/reduce_sum | solution.py:17
  9.2 2.0 %fusion.11 = f32[512]{0:T(512)S(1)} fusion(bf16[512,1664]{1,0:T(8,128)(2,1)} %param.18, f32[512]{0:T(512)S(1)} %broadcast_multiply_fusion.1), kind=kLoop, calls=%fused_computation.22 | loop fusion | flops 3407360 | bytes 1708032 | tf_op jit(solution)/shard_map/reduce_sum | solution.py:19
  11.3 1.0 fusion.30
  12.5 1.5 and_reduce_fusion
  13.9 1.3 broadcast_select_fusion
  16.0 0.8 pad_maximum_fusion
  16.7 3.5 %collective-permute-start = (bf16[3,512,104]{1,2,0:T(8,128)(2,1)}, bf16[3,512,104]{1,2,0:T(8,128)(2,1)}, u32[]{:S(2)}, u32[]{:S(2)}) collective-permute-start(bf16[3,512,104]{1,2,0:T(8,128)(2,1)} %pad_maximum_fusion), channel_id=1, source_target_pairs={{0,16},{16,0},{32,48},{48,32},{64,80},{80,64},{96,112},{112,96},{1... | collective-permute-start | bytes 958472 | tf_op jit(solution)/shard_map/ppermute | solution.py:104
  20.2 1.8 reshape.467
  22.1 1.8 constant_dynamic-slice_fusion.2
  23.9 1.9 copy.60
  25.7 2.5 %collective-permute-done = bf16[3,512,104]{1,2,0:T(8,128)(2,1)} collective-permute-done((bf16[3,512,104]{1,2,0:T(8,128)(2,1)}, bf16[3,512,104]{1,2,0:T(8,128)(2,1)}, u32[]{:S(2)}, u32[]{:S(2)}) %collective-permute-start) | collective-permute-done | bytes 319520 | tf_op jit(solution)/shard_map/ppermute | solution.py:104
  28.9 0.9 slice.175
  29.9 1.5 fusion.25
  32.1 0.9 fusion.41
  33.0 1.3 convolution_convert_fusion
  34.3 1.9 %collective-permute-start.1 = (bf16[8,104,512]{2,1,0:T(8,128)(2,1)}, bf16[8,104,512]{2,1,0:T(8,128)(2,1)}, u32[]{:S(2)}, u32[]{:S(2)}) collective-permute-start(bf16[8,104,512]{2,1,0:T(8,128)(2,1)} %convolution_convert_fusion), channel_id=1, source_target_pairs={{0,1},{1,0},{2,3},{3,2},{4,5},{5,4},{6,7},{7,6},{8,9},{9,8},{10,11... | collective-permute-start | bytes 2555912 | tf_op jit(solution)/shard_map/ppermute | solution.py:136
  36.4 1.3 copy.59
  38.0 0.9 collective-permute-done.1
  38.9 2.5 %add_convert_fusion = bf16[8,104,512]{2,1,0:T(8,128)(2,1)} fusion(bf16[8,104,512]{2,1,0:T(8,128)(2,1)} %collective-permute-done.1, bf16[512,104,1]{0,1,2:T(8,128)(2,1)} %copy-done.6, bf16[104,8,1,104]{0,3,1,2:T(8,128)(2,1)S(1)} %copy.59), kind=kOutput, calls=%fused_computation.45 | convolution fusion | flops 90734592 | bytes 1983488 | tf_op jit(solution)/shard_map/pe,ezf->zfp/dot_general | solution.py:131
  41.4 10.3 %all-to-all-start = ((bf16[8,104,512]{2,1,0:T(8,128)(2,1)}), bf16[8,104,512]{2,1,0:T(8,128)(2,1)}, u32[]{:S(2)}, u32[]{:S(2)}) async-start(bf16[8,104,512]{2,1,0:T(8,128)(2,1)} %add_convert_fusion), calls=%async_computation | async-start | bytes 1703936 | tf_op jit(solution)/shard_map/all_to_all | solution.py:35
  51.9 1.4 fusion.68
  54.4 22.2 %all-to-all-done = bf16[8,104,512]{2,1,0:T(8,128)(2,1)} async-done(((bf16[8,104,512]{2,1,0:T(8,128)(2,1)}), bf16[8,104,512]{2,1,0:T(8,128)(2,1)}, u32[]{:S(2)}, u32[]{:S(2)}) %all-to-all-start) | async-done | bytes 852000 | tf_op jit(solution)/shard_map/all_to_all | solution.py:35
  76.6 1.3 convert_reduce_fusion.3
  78.1 1.5 fusion.40
  79.6 13.6 %all_to_all.37 = bf16[16,8,1024]{2,1,0:T(8,128)(2,1)S(1)} all-to-all(bf16[16,8,1024]{2,1,0:T(8,128)(2,1)S(1)} %fusion.40), channel_id=1, replica_groups=mesh['gx'=4,'gy'=8,'z'=8,'core'=2] {'z','core'}, dimensions={0} | all-to-all | bytes 524288 | tf_op jit(solution)/shard_map/all_to_all | solution.py:35
  94.0 3.5 %all-to-all-start.2 = ((bf16[16,8,1024]{2,1,0:T(8,128)(2,1)}), bf16[16,8,1024]{2,1,0:T(8,128)(2,1)S(1)}, u32[]{:S(2)}, u32[]{:S(2)}) async-start(bf16[16,8,1024]{2,1,0:T(8,128)(2,1)} %broadcast_in_dim.68), calls=%async_computation.2 | async-start | bytes 524288 | tf_op jit(solution)/shard_map/all_to_all | solution.py:26
  97.6 11.2 %all-to-all-done.2 = bf16[16,8,1024]{2,1,0:T(8,128)(2,1)S(1)} async-done(((bf16[16,8,1024]{2,1,0:T(8,128)(2,1)}), bf16[16,8,1024]{2,1,0:T(8,128)(2,1)S(1)}, u32[]{:S(2)}, u32[]{:S(2)}) %all-to-all-start.2) | async-done | bytes 262176 | tf_op jit(solution)/shard_map/all_to_all | solution.py:26
  109.4 1.4 fusion.78
  110.9 0.8 broadcast_in_dim.72
  111.7 7.1 %all-to-all-start.3 = ((bf16[8,128,128]{2,1,0:T(8,128)(2,1)}), bf16[8,128,128]{2,1,0:T(8,128)(2,1)S(1)}, u32[]{:S(2)}, u32[]{:S(2)}) async-start(bf16[8,128,128]{2,1,0:T(8,128)(2,1)} %broadcast_in_dim.72), calls=%async_computation.3 | async-start | bytes 524288 | tf_op jit(solution)/shard_map/all_to_all | solution.py:26
  119.2 14.9 %all-to-all-done.3 = bf16[8,128,128]{2,1,0:T(8,128)(2,1)S(1)} async-done(((bf16[8,128,128]{2,1,0:T(8,128)(2,1)}), bf16[8,128,128]{2,1,0:T(8,128)(2,1)S(1)}, u32[]{:S(2)}, u32[]{:S(2)}) %all-to-all-start.3) | async-done | bytes 262176 | tf_op jit(solution)/shard_map/all_to_all | solution.py:26
  134.1 1.1 broadcast_in_dim.74
  135.3 4.8 %all-to-all-start.4 = ((bf16[4,1024,128]{2,1,0:T(8,128)(2,1)}), bf16[4,1024,128]{2,1,0:T(8,128)(2,1)S(1)}, u32[]{:S(2)}, u32[]{:S(2)}) async-start(bf16[4,1024,128]{2,1,0:T(8,128)(2,1)} %broadcast_in_dim.74), calls=%async_computation.4 | async-start | bytes 2097152 | tf_op jit(solution)/shard_map/all_to_all | solution.py:26
  140.1 1.9 all-gather.2.cloned.1.call-done
  141.9 0.8 slice.168
  142.8 0.8 convert_reduce_fusion
  145.9 2.8 %fusion.6 = (f32[128]{0:T(128)S(1)}, f32[128,8448]{1,0:T(8,128)S(1)}) fusion(s32[8448]{0:T(1024)S(1)} %fusion.115, s32[128]{0:T(128)S(1)} %get-tuple-element.60, bf16[8448,128]{1,0:T(8,128)(2,1)} %all-gather.2.cloned.1.call-done, bf16[3,128,64]{1,2,0:T(8,128)(2,1)S(1)} %convert_bitcast_fusion.3), kind=kOutput, calls=%fused_computation.16 | convolution fusion | flops 142737280 | bytes 6542336 | tf_op jit(solution)/shard_map/dot_general | solution.py:40
  148.6 1.1 fusion.15
  150.2 2.1 %fusion = (f32[256]{0:T(256)S(1)}, f32[256,8448]{1,0:T(8,128)S(1)}) fusion(s32[8448]{0:T(1024)S(1)} %fusion.115, s32[256]{0:T(256)S(1)} %add_add_fusion, bf16[8448,128]{1,0:T(8,128)(2,1)S(1)} %copy-done.10, bf16[3,256,64]{1,2,0:T(8,128)(2,1)S(1)} %convert_bitcast_fusion.2), kind=kOutput, calls=%fused_computation.4 | convolution fusion | flops 285474560 | bytes 10885120 | tf_op jit(solution)/shard_map/dot_general | solution.py:40
  152.4 2.4 %fusion.1 = f32[256]{0:T(256)S(1)} fusion(f32[256,8448]{1,0:T(8,128)S(1)} %get-tuple-element.71, f32[256]{0:T(256)S(1)} %get-tuple-element.70, s32[8448]{0:T(1024)S(1)} %fusion.115, s32[256]{0:T(256)S(1)} %add_add_fusion), kind=kLoop, calls=%fused_computation.7 | loop fusion | flops 8650496 | bytes 8687616 | tf_op jit(solution)/shard_map/reduce_sum | solution.py:43
  154.7 2.0 %fusion.19 = f32[128,64]{0,1:T(8,128)S(1)} fusion(f32[128,8448]{1,0:T(8,128)S(1)} %get-tuple-element.69, f32[128]{0:T(128)S(1)} %get-tuple-element.68, s32[8448]{0:T(1024)S(1)} %fusion.115, s32[128]{0:T(128)S(1)} %get-tuple-element.60, bf16[8448,128]{1,0:T(8,128)(2,1)S(1)} %copy-done.10), kind=kOutput, calls=%fused_computation.31 | convolution fusion | flops 142737408 | bytes 6555648 | tf_op jit(solution)/shard_map/dot_general | solution.py:44
  156.8 2.8 %fusion.7 = f32[256,64]{0,1:T(8,128)S(1)} fusion(f32[256,8448]{1,0:T(8,128)S(1)} %get-tuple-element.71, f32[256]{0:T(256)S(1)} %get-tuple-element.70, s32[8448]{0:T(1024)S(1)} %fusion.115, s32[256]{0:T(256)S(1)} %add_add_fusion, bf16[8448,128]{1,0:T(8,128)(2,1)S(1)} %copy-done.10), kind=kOutput, calls=%fused_computation.17 | convolution fusion | flops 285474816 | bytes 10914816 | tf_op jit(solution)/shard_map/dot_general | solution.py:44
  159.6 1.6 fusion.3
  161.2 1.4 fusion.4
  162.6 1.8 fusion.52
  165.5 7.6 %all-to-all-start.5 = ((bf16[32,2,256]{2,1,0:T(2,128)(2,1)}), bf16[32,2,256]{2,1,0:T(2,128)(2,1)S(1)}, u32[]{:S(2)}, u32[]{:S(2)}) async-start(bf16[32,2,256]{2,1,0:T(2,128)(2,1)} %reshape.492), calls=%async_computation.5 | async-start | bytes 65536 | tf_op jit(solution)/shard_map/all_to_all | solution.py:196
  173.3 7.8 %all-to-all-done.5 = bf16[32,2,256]{2,1,0:T(2,128)(2,1)S(1)} async-done(((bf16[32,2,256]{2,1,0:T(2,128)(2,1)}), bf16[32,2,256]{2,1,0:T(2,128)(2,1)S(1)}, u32[]{:S(2)}, u32[]{:S(2)}) %all-to-all-start.5) | async-done | bytes 32800 | tf_op jit(solution)/shard_map/all_to_all | solution.py:196
  181.5 0.8 fusion.48
  (109 shorter events, 10.9 us)
Async XLA Ops:
  6.5 4.7 %copy-start = (bf16[3,1664,104]{1,2,0:T(8,128)(2,1)S(1)}, bf16[3,1664,104]{1,2,0:T(8,128)(2,1)}, u32[]{:S(2)}) copy-start(bf16[3,1664,104]{1,2,0:T(8,128)(2,1)} %param.22) | copy-start | bytes 3115012
  6.5 4.7 %copy-start.1 = (bf16[512,1664]{1,0:T(8,128)(2,1)S(1)}, bf16[512,1664]{1,0:T(8,128)(2,1)}, u32[]{:S(2)}) copy-start(bf16[512,1664]{1,0:T(8,128)(2,1)} %param.18) | copy-start | bytes 5111812
  6.5 4.7 %copy-start.7 = (s32[512]{0:T(512)S(1)}, s32[512]{0:T(512)}, u32[]{:S(2)}) copy-start(s32[512]{0:T(512)} %param.19) | copy-start | bytes 6148
  6.5 4.7 %copy-start.11 = (f32[1664]{0:T(1024)S(1)}, f32[1664]{0:T(1024)}, u32[]{:S(2)}) copy-start(f32[1664]{0:T(1024)} %param.21) | copy-start | bytes 19972
  6.5 4.7 %copy-start.12 = (f32[1664]{0:T(1024)S(1)}, f32[1664]{0:T(1024)}, u32[]{:S(2)}) copy-start(f32[1664]{0:T(1024)} %param.20) | copy-start | bytes 19972
  11.3 1.2 copy-start.9
  12.4 7.8 %copy-start.4 = (bf16[2,512,104]{1,2,0:T(8,128)(2,1)}, bf16[2,512,104]{1,2,0:T(8,128)(2,1)S(1)}, u32[]{:S(2)}) copy-start(bf16[2,512,104]{1,2,0:T(8,128)(2,1)S(1)} %slice.174) | copy-start | bytes 638980
  16.7 11.5 %collective-permute-start = (bf16[3,512,104]{1,2,0:T(8,128)(2,1)}, bf16[3,512,104]{1,2,0:T(8,128)(2,1)}, u32[]{:S(2)}, u32[]{:S(2)}) collective-permute-start(bf16[3,512,104]{1,2,0:T(8,128)(2,1)} %pad_maximum_fusion), channel_id=1, source_target_pairs={{0,16},{16,0},{32,48},{48,32},{64,80},{80,64},{96,112},{112,96},{1... | collective-permute-start | bytes 958472 | tf_op jit(solution)/shard_map/ppermute | solution.py:104
  23.9 8.2 %copy-start.5 = (bf16[2,512,104]{1,2,0:T(8,128)(2,1)S(1)}, bf16[2,512,104]{1,2,0:T(8,128)(2,1)}, u32[]{:S(2)}) copy-start(bf16[2,512,104]{1,2,0:T(8,128)(2,1)} %copy-done.4) | copy-start | bytes 638980
  32.1 0.9 copy-start.3
  32.1 4.1 %copy-start.2 = (bf16[256,1024]{1,0:T(8,128)(2,1)S(1)}, bf16[256,1024]{1,0:T(8,128)(2,1)}, u32[]{:S(2)}) copy-start(bf16[256,1024]{1,0:T(8,128)(2,1)} %param.26) | copy-start | bytes 1572868
  32.1 5.8 %copy-start.8 = (s32[128]{0:T(128)S(1)}, s32[128]{0:T(128)}, u32[]{:S(2)}) copy-start(s32[128]{0:T(128)} %param.25) | copy-start | bytes 1540
  33.0 3.4 %copy-start.6 = (bf16[512,104,1]{0,1,2:T(8,128)(2,1)}, bf16[512,104,1]{0,1,2:T(8,128)(2,1)S(1)}, u32[]{:S(2)}) copy-start(bf16[512,104,1]{0,1,2:T(8,128)(2,1)S(1)} %fusion.41) | copy-start | bytes 319492
  33.0 18.9 %copy-start.13 = (f32[1024]{0:T(1024)S(1)}, f32[1024]{0:T(1024)}, u32[]{:S(2)}) copy-start(f32[1024]{0:T(1024)} %param.28) | copy-start | bytes 12292
  33.0 18.9 %copy-start.14 = (f32[1024]{0:T(1024)S(1)}, f32[1024]{0:T(1024)}, u32[]{:S(2)}) copy-start(f32[1024]{0:T(1024)} %param.27) | copy-start | bytes 12292
  34.3 4.6 %collective-permute-start.1 = (bf16[8,104,512]{2,1,0:T(8,128)(2,1)}, bf16[8,104,512]{2,1,0:T(8,128)(2,1)}, u32[]{:S(2)}, u32[]{:S(2)}) collective-permute-start(bf16[8,104,512]{2,1,0:T(8,128)(2,1)} %convolution_convert_fusion), channel_id=1, source_target_pairs={{0,1},{1,0},{2,3},{3,2},{4,5},{5,4},{6,7},{7,6},{8,9},{9,8},{10,11... | collective-permute-start | bytes 2555912 | tf_op jit(solution)/shard_map/ppermute | solution.py:136
  41.4 35.2 %all-to-all-start = ((bf16[8,104,512]{2,1,0:T(8,128)(2,1)}), bf16[8,104,512]{2,1,0:T(8,128)(2,1)}, u32[]{:S(2)}, u32[]{:S(2)}) async-start(bf16[8,104,512]{2,1,0:T(8,128)(2,1)} %add_convert_fusion), calls=%async_computation | async-start | bytes 1703936 | tf_op jit(solution)/shard_map/all_to_all | solution.py:35
  51.7 90.2 %all-gather.2.cloned.1.call-start = ((), (), s32[]{:S(2)}) async-start(), calls=%async_computation.6 | async-start | bytes 2230272 | tf_op jit(solution)/shard_map/all_gather | solution.py:80
  94.0 14.9 %all-to-all-start.2 = ((bf16[16,8,1024]{2,1,0:T(8,128)(2,1)}), bf16[16,8,1024]{2,1,0:T(8,128)(2,1)S(1)}, u32[]{:S(2)}, u32[]{:S(2)}) async-start(bf16[16,8,1024]{2,1,0:T(8,128)(2,1)} %broadcast_in_dim.68), calls=%async_computation.2 | async-start | bytes 524288 | tf_op jit(solution)/shard_map/all_to_all | solution.py:26
  111.7 22.4 %all-to-all-start.3 = ((bf16[8,128,128]{2,1,0:T(8,128)(2,1)}), bf16[8,128,128]{2,1,0:T(8,128)(2,1)S(1)}, u32[]{:S(2)}, u32[]{:S(2)}) async-start(bf16[8,128,128]{2,1,0:T(8,128)(2,1)} %broadcast_in_dim.72), calls=%async_computation.3 | async-start | bytes 524288 | tf_op jit(solution)/shard_map/all_to_all | solution.py:26
  135.3 24.3 %all-to-all-start.4 = ((bf16[4,1024,128]{2,1,0:T(8,128)(2,1)}), bf16[4,1024,128]{2,1,0:T(8,128)(2,1)S(1)}, u32[]{:S(2)}, u32[]{:S(2)}) async-start(bf16[4,1024,128]{2,1,0:T(8,128)(2,1)} %broadcast_in_dim.74), calls=%async_computation.4 | async-start | bytes 2097152 | tf_op jit(solution)/shard_map/all_to_all | solution.py:26
  148.6 1.6 copy-start.10
  165.5 15.7 %all-to-all-start.5 = ((bf16[32,2,256]{2,1,0:T(2,128)(2,1)}), bf16[32,2,256]{2,1,0:T(2,128)(2,1)S(1)}, u32[]{:S(2)}, u32[]{:S(2)}) async-start(bf16[32,2,256]{2,1,0:T(2,128)(2,1)} %reshape.492), calls=%async_computation.5 | async-start | bytes 65536 | tf_op jit(solution)/shard_map/all_to_all | solution.py:196
Sparse Core Ops, SparseCore 0:
  55.7 86.1 all-gather.1

commit v14 on v8

--- a/solution.py
+++ b/solution.py
@@ -39,9 +39,9 @@
 def attend_part(query, allowed, keys, values):
     score = jnp.dot(query, keys.T, preferred_element_type=jnp.float32) * DH ** (-0.5)
     top = jnp.max(jnp.where(allowed, score, -1e30), axis=1)
-    expo = jnp.where(allowed, jnp.exp(score - top[:, None]), 0.0)
-    total = jnp.sum(expo, axis=1)
-    acc = jnp.dot(expo.astype(jnp.bfloat16), values, preferred_element_type=jnp.float32)
+    expo = jnp.where(allowed, jnp.exp(score - top[:, None]), 0.0).astype(jnp.bfloat16)
+    total = jnp.sum(expo.astype(jnp.float32), axis=1)
+    acc = jnp.dot(expo, values, preferred_element_type=jnp.float32)
     return top, total, acc
 
 

time: 186 us -> 185 us (level)
  no operation moved by 1% of the time
where the time goes in v14:
time: 185 us; the launch traced here: 184 us
  waiting for transfers between devices  60.1 us (32%)
  starting transfers between devices  40.3 us (22%)
  matrix products  26.1 us (14%)
  other arithmetic  15.5 us (8%)
  local copies, waits for them, and re-layouts  14.2 us (8%)
  between operations  13.9 us (8%)
  blocking collectives  13.6 us (7%)
    all_to_all x3, waiting for transfers between devices, a2a_gather(): got = lax.all_to_all(spread, axis, 0, 0, tiled=True)  26.1 us
    all_to_all x1, waiting for transfers between devices, a2a_sum(): got = lax.all_to_all(parts, axis, 0, 0, tiled=True)  22.2 us
    all_to_all x3, starting transfers between devices, a2a_gather(): got = lax.all_to_all(spread, axis, 0, 0, tiled=True)  14.5 us
    all_to_all x1, blocking collectives, a2a_sum(): got = lax.all_to_all(parts, axis, 0, 0, tiled=True)  13.6 us
    all_to_all x1, starting transfers between devices, a2a_sum(): got = lax.all_to_all(parts, axis, 0, 0, tiled=True)  10.3 us
    all_to_all x1, waiting for transfers between devices, body(): got = lax.all_to_all(packed, GRP, 0, 0, tiled=True)  7.83 us
    all_to_all x1, starting transfers between devices, body(): got = lax.all_to_all(packed, GRP, 0, 0, tiled=True)  7.38 us
    dot_general x3, matrix products, attend_part(): jnp.dot(query, keys.T, preferred_element_type=jnp.float32) * DH ** (-0.5)  6.41 us
  transfers between devices with their start and end apart: 9, of which 7 were waited for; matrix products, arithmetic and copies ran while one was open for 22% of the time, Pallas kernels for 0%

profile of v14, /device:TPU:6, one launch (start us, length us, event | category | flops | bytes accessed | tf_op | source)
XLA Modules:
  0.0 183.7 jit_solution(2304241290033616744)
XLA Ops:
  6.5 3.7 %collective-permute-start.1 = (s32[512]{0:T(512)}, s32[512]{0:T(512)S(1)}, u32[]{:S(2)}, u32[]{:S(2)}) collective-permute-start(s32[512]{0:T(512)} %param.15), channel_id=1, source_target_pairs={{0,16},{16,0},{32,48},{48,32},{64,80},{80,64},{96,112},{112,96},{1... | collective-permute-start | bytes 6152 | tf_op jit(solution)/shard_map/ppermute | solution.py:100
  10.3 1.8 convert_reduce_fusion.4
  12.1 2.0 %fusion.8 = f32[512]{0:T(512)S(1)} fusion(bf16[512,1664]{1,0:T(8,128)(2,1)} %param.14, f32[512]{0:T(512)S(1)} %broadcast_multiply_fusion.1), kind=kLoop, calls=%fused_computation.23 | loop fusion | flops 3407360 | bytes 1708032 | tf_op jit(solution)/shard_map/reduce_sum | solution.py:19
  14.1 1.0 fusion.19
  15.9 2.3 %collective-permute-start = (bf16[2,512,104]{1,2,0:T(8,128)(2,1)}, bf16[2,512,104]{1,2,0:T(8,128)(2,1)}, u32[]{:S(2)}, u32[]{:S(2)}) collective-permute-start(bf16[2,512,104]{1,2,0:T(8,128)(2,1)} %slice.112), channel_id=1, source_target_pairs={{0,16},{16,0},{32,48},{48,32},{64,80},{80,64},{96,112},{112,96},{1... | collective-permute-start | bytes 638984 | tf_op jit(solution)/shard_map/ppermute | solution.py:100
  18.3 1.8 reshape.400
  20.1 1.8 constant_dynamic-slice_fusion.2
  21.9 1.9 %copy.60 = bf16[104,8,1,104]{0,3,1,2:T(8,128)(2,1)} copy(bf16[104,8,1,104]{3,2,1,0:T(2,128)(2,1)} %get-tuple-element.31) | data formatting | bytes 346112
  23.8 1.1 collective-permute-done
  24.8 1.5 fusion.12
  27.1 1.9 %fusion.30 = bf16[512,104,1]{0,1,2:T(8,128)(2,1)S(1)} fusion(f32[512,1024]{1,0:T(8,128)S(1)} %get-tuple-element.45, f32[512]{0:T(512)S(1)} %fusion.25, f32[512]{0:T(512)S(1)} %get-tuple-element.44, s32[1024]{0:T(1024)S(1)} %pad_add_fusion, s32[512]{0:T(512)S(1)} %copy-done.6, bf16[2,512,104]{1,2,0:T(8,128)(2,1)} %slice.112, ...), kind=kOutput, calls=%fused_computation.56 | convolution fusion | flops 112676864 | bytes 2639872 | tf_op jit(solution)/shard_map/hpk,khe->phe/dot_general | solution.py:112
  29.0 1.3 convolution_convert_fusion
  30.3 1.9 %collective-permute-start.2 = (bf16[8,104,512]{2,1,0:T(8,128)(2,1)}, bf16[8,104,512]{2,1,0:T(8,128)(2,1)}, u32[]{:S(2)}, u32[]{:S(2)}) collective-permute-start(bf16[8,104,512]{2,1,0:T(8,128)(2,1)} %convolution_convert_fusion), channel_id=1, source_target_pairs={{0,1},{1,0},{2,3},{3,2},{4,5},{5,4},{6,7},{7,6},{8,9},{9,8},{10,11... | collective-permute-start | bytes 2555912 | tf_op jit(solution)/shard_map/ppermute | solution.py:129
  32.4 1.3 copy.59
  34.0 0.9 collective-permute-done.2
  34.9 2.5 %add_convert_fusion = bf16[8,104,512]{2,1,0:T(8,128)(2,1)} fusion(bf16[8,104,512]{2,1,0:T(8,128)(2,1)} %collective-permute-done.2, bf16[512,104,1]{0,1,2:T(8,128)(2,1)} %copy-done.5, bf16[104,8,1,104]{0,3,1,2:T(8,128)(2,1)S(1)} %copy.59), kind=kOutput, calls=%fused_computation.40 | convolution fusion | flops 90734592 | bytes 1983488 | tf_op jit(solution)/shard_map/pe,ezf->zfp/dot_general | solution.py:124
  37.4 10.3 %all-to-all-start = ((bf16[8,104,512]{2,1,0:T(8,128)(2,1)}), bf16[8,104,512]{2,1,0:T(8,128)(2,1)}, u32[]{:S(2)}, u32[]{:S(2)}) async-start(bf16[8,104,512]{2,1,0:T(8,128)(2,1)} %add_convert_fusion), calls=%async_computation | async-start | bytes 1703936 | tf_op jit(solution)/shard_map/all_to_all | solution.py:35
  47.9 1.5 fusion.48
  49.4 0.7 copy.49
  50.4 22.2 %all-to-all-done = bf16[8,104,512]{2,1,0:T(8,128)(2,1)} async-done(((bf16[8,104,512]{2,1,0:T(8,128)(2,1)}), bf16[8,104,512]{2,1,0:T(8,128)(2,1)}, u32[]{:S(2)}, u32[]{:S(2)}) %all-to-all-start) | async-done | bytes 852000 | tf_op jit(solution)/shard_map/all_to_all | solution.py:35
  72.6 1.3 convert_reduce_fusion.6
  74.1 1.5 fusion.29
  75.6 13.6 %all_to_all.37 = bf16[16,8,1024]{2,1,0:T(8,128)(2,1)S(1)} all-to-all(bf16[16,8,1024]{2,1,0:T(8,128)(2,1)S(1)} %fusion.29), channel_id=1, replica_groups=mesh['gx'=4,'gy'=8,'z'=8,'core'=2] {'z','core'}, dimensions={0} | all-to-all | bytes 524288 | tf_op jit(solution)/shard_map/all_to_all | solution.py:35
  89.3 0.7 broadcast_in_dim.68
  90.0 3.5 %all-to-all-start.2 = ((bf16[16,8,1024]{2,1,0:T(8,128)(2,1)}), bf16[16,8,1024]{2,1,0:T(8,128)(2,1)S(1)}, u32[]{:S(2)}, u32[]{:S(2)}) async-start(bf16[16,8,1024]{2,1,0:T(8,128)(2,1)} %broadcast_in_dim.68), calls=%async_computation.2 | async-start | bytes 524288 | tf_op jit(solution)/shard_map/all_to_all | solution.py:26
  93.7 11.2 %all-to-all-done.2 = bf16[16,8,1024]{2,1,0:T(8,128)(2,1)S(1)} async-done(((bf16[16,8,1024]{2,1,0:T(8,128)(2,1)}), bf16[16,8,1024]{2,1,0:T(8,128)(2,1)S(1)}, u32[]{:S(2)}, u32[]{:S(2)}) %all-to-all-start.2) | async-done | bytes 262176 | tf_op jit(solution)/shard_map/all_to_all | solution.py:26
  105.4 1.4 fusion.58
  107.0 0.8 broadcast_in_dim.72
  107.7 6.2 %all-to-all-start.3 = ((bf16[8,128,128]{2,1,0:T(8,128)(2,1)}), bf16[8,128,128]{2,1,0:T(8,128)(2,1)S(1)}, u32[]{:S(2)}, u32[]{:S(2)}) async-start(bf16[8,128,128]{2,1,0:T(8,128)(2,1)} %broadcast_in_dim.72), calls=%async_computation.3 | async-start | bytes 524288 | tf_op jit(solution)/shard_map/all_to_all | solution.py:26
  114.3 14.8 %all-to-all-done.3 = bf16[8,128,128]{2,1,0:T(8,128)(2,1)S(1)} async-done(((bf16[8,128,128]{2,1,0:T(8,128)(2,1)}), bf16[8,128,128]{2,1,0:T(8,128)(2,1)S(1)}, u32[]{:S(2)}, u32[]{:S(2)}) %all-to-all-start.3) | async-done | bytes 262176 | tf_op jit(solution)/shard_map/all_to_all | solution.py:26
  129.1 1.1 broadcast_in_dim.74
  130.3 4.8 %all-to-all-start.4 = ((bf16[4,1024,128]{2,1,0:T(8,128)(2,1)}), bf16[4,1024,128]{2,1,0:T(8,128)(2,1)S(1)}, u32[]{:S(2)}, u32[]{:S(2)}) async-start(bf16[4,1024,128]{2,1,0:T(8,128)(2,1)} %broadcast_in_dim.74), calls=%async_computation.4 | async-start | bytes 2097152 | tf_op jit(solution)/shard_map/all_to_all | solution.py:26
  135.1 2.0 %all-gather.2.cloned.1.call-done = bf16[8448,128]{1,0:T(8,128)(2,1)} async-done(((bf16[264,128]{1,0:T(8,128)(2,1)}), bf16[8448,128]{1,0:T(8,128)(2,1)}) %all-gather.2.cloned.1.call-update) | async-done | bytes 2162704 | tf_op jit(solution)/shard_map/all_gather | solution.py:80
  137.0 0.8 slice.106
  138.0 0.8 convert_reduce_fusion.2
  141.0 2.7 %fusion.4 = (f32[128]{0:T(128)S(1)}, f32[128,8448]{1,0:T(8,128)S(1)}) fusion(s32[8448]{0:T(1024)S(1)} %fusion.95, s32[128]{0:T(128)S(1)} %get-tuple-element.40, bf16[8448,128]{1,0:T(8,128)(2,1)} %all-gather.2.cloned.1.call-done, bf16[3,128,64]{1,2,0:T(8,128)(2,1)S(1)} %convert_bitcast_fusion.3), kind=kOutput, calls=%fused_computation.16 | convolution fusion | flops 142737280 | bytes 6542336 | tf_op jit(solution)/shard_map/dot_general | solution.py:40
  143.8 1.2 convert_reduce_fusion.3
  145.4 2.1 %fusion = (f32[256]{0:T(256)S(1)}, f32[256,8448]{1,0:T(8,128)S(1)}) fusion(s32[8448]{0:T(1024)S(1)} %fusion.95, s32[256]{0:T(256)S(1)} %add_add_fusion, bf16[8448,128]{1,0:T(8,128)(2,1)S(1)} %copy-done.1, bf16[3,256,64]{1,2,0:T(8,128)(2,1)S(1)} %convert_bitcast_fusion.2), kind=kOutput, calls=%fused_computation.4 | convolution fusion | flops 285474560 | bytes 10885120 | tf_op jit(solution)/shard_map/dot_general | solution.py:40
  147.5 2.7 %convert_reduce_fusion = (f32[256]{0:T(256)S(1)}, bf16[256,8448]{1,0:T(8,128)(2,1)S(1)}) fusion(f32[256,8448]{1,0:T(8,128)S(1)} %get-tuple-element.51, f32[256]{0:T(256)S(1)} %get-tuple-element.50, s32[256]{0:T(256)S(1)} %add_add_fusion, s32[8448]{0:T(1024)S(1)} %fusion.95), kind=kLoop, calls=%fused_computation.6 | loop fusion | flops 12975872 | bytes 13012992 | tf_op jit(solution)/shard_map/reduce_sum | solution.py:43
  150.2 2.0 %fusion.13 = f32[128,64]{0,1:T(8,128)S(1)} fusion(bf16[128,8448]{1,0:T(8,128)(2,1)S(1)} %get-tuple-element.25, bf16[8448,128]{1,0:T(8,128)(2,1)S(1)} %copy-done.1), kind=kOutput, calls=%fused_computation.32 | convolution fusion | flops 138412032 | bytes 4358144 | tf_op jit(solution)/shard_map/dot_general | solution.py:44
  152.1 2.5 %fusion.15 = f32[256,64]{0,1:T(8,128)S(1)} fusion(bf16[256,8448]{1,0:T(8,128)(2,1)S(1)} %get-tuple-element.23, bf16[8448,128]{1,0:T(8,128)(2,1)S(1)} %copy-done.1), kind=kOutput, calls=%fused_computation.34 | convolution fusion | flops 276824064 | bytes 6553600 | tf_op jit(solution)/shard_map/dot_general | solution.py:44
  154.6 1.6 fusion.2
  156.2 1.5 convert_reduce_fusion.1
  157.7 1.5 fusion.34
  159.5 0.7 reshape.420
  160.2 7.4 %all-to-all-start.5 = ((bf16[32,2,256]{2,1,0:T(2,128)(2,1)}), bf16[32,2,256]{2,1,0:T(2,128)(2,1)S(1)}, u32[]{:S(2)}, u32[]{:S(2)}) async-start(bf16[32,2,256]{2,1,0:T(2,128)(2,1)} %reshape.420), calls=%async_computation.5 | async-start | bytes 65536 | tf_op jit(solution)/shard_map/all_to_all | solution.py:189
  167.8 7.8 %all-to-all-done.5 = bf16[32,2,256]{2,1,0:T(2,128)(2,1)S(1)} async-done(((bf16[32,2,256]{2,1,0:T(2,128)(2,1)}), bf16[32,2,256]{2,1,0:T(2,128)(2,1)S(1)}, u32[]{:S(2)}, u32[]{:S(2)}) %all-to-all-start.5) | async-done | bytes 32800 | tf_op jit(solution)/shard_map/all_to_all | solution.py:189
  176.0 0.8 fusion.33
  (92 shorter events, 7.2 us)
Async XLA Ops:
  6.5 7.6 %copy-start = (bf16[3,1664,104]{1,2,0:T(8,128)(2,1)S(1)}, bf16[3,1664,104]{1,2,0:T(8,128)(2,1)}, u32[]{:S(2)}) copy-start(bf16[3,1664,104]{1,2,0:T(8,128)(2,1)} %param.18) | copy-start | bytes 3115012
  6.5 7.6 %copy-start.2 = (bf16[512,1664]{1,0:T(8,128)(2,1)S(1)}, bf16[512,1664]{1,0:T(8,128)(2,1)}, u32[]{:S(2)}) copy-start(bf16[512,1664]{1,0:T(8,128)(2,1)} %param.14) | copy-start | bytes 5111812
  6.5 7.6 %copy-start.8 = (f32[1664]{0:T(1024)S(1)}, f32[1664]{0:T(1024)}, u32[]{:S(2)}) copy-start(f32[1664]{0:T(1024)} %param.17) | copy-start | bytes 19972
  6.5 7.6 %copy-start.9 = (f32[1664]{0:T(1024)S(1)}, f32[1664]{0:T(1024)}, u32[]{:S(2)}) copy-start(f32[1664]{0:T(1024)} %param.16) | copy-start | bytes 19972
  6.5 17.2 %collective-permute-start.1 = (s32[512]{0:T(512)}, s32[512]{0:T(512)S(1)}, u32[]{:S(2)}, u32[]{:S(2)}) collective-permute-start(s32[512]{0:T(512)} %param.15), channel_id=1, source_target_pairs={{0,16},{16,0},{32,48},{48,32},{64,80},{80,64},{96,112},{112,96},{1... | collective-permute-start | bytes 6152 | tf_op jit(solution)/shard_map/ppermute | solution.py:100
  15.2 8.6 %copy-start.6 = (s32[512]{0:T(512)S(1)}, s32[512]{0:T(512)}, u32[]{:S(2)}) copy-start(s32[512]{0:T(512)} %param.15) | copy-start | bytes 6148
  15.9 8.9 %collective-permute-start = (bf16[2,512,104]{1,2,0:T(8,128)(2,1)}, bf16[2,512,104]{1,2,0:T(8,128)(2,1)}, u32[]{:S(2)}, u32[]{:S(2)}) collective-permute-start(bf16[2,512,104]{1,2,0:T(8,128)(2,1)} %slice.112), channel_id=1, source_target_pairs={{0,16},{16,0},{32,48},{48,32},{64,80},{80,64},{96,112},{112,96},{1... | collective-permute-start | bytes 638984 | tf_op jit(solution)/shard_map/ppermute | solution.py:100
  27.1 1.9 %copy-start.4 = (bf16[104,8,1,104]{0,3,1,2:T(8,128)(2,1)S(1)}, bf16[104,8,1,104]{0,3,1,2:T(8,128)(2,1)}, u32[]{:S(2)}) copy-start(bf16[104,8,1,104]{0,3,1,2:T(8,128)(2,1)} %copy.60) | copy-start | bytes 519172
  27.1 5.1 %copy-start.3 = (bf16[256,1024]{1,0:T(8,128)(2,1)S(1)}, bf16[256,1024]{1,0:T(8,128)(2,1)}, u32[]{:S(2)}) copy-start(bf16[256,1024]{1,0:T(8,128)(2,1)} %param.22) | copy-start | bytes 1572868
  27.1 6.8 %copy-start.7 = (s32[128]{0:T(128)S(1)}, s32[128]{0:T(128)}, u32[]{:S(2)}) copy-start(s32[128]{0:T(128)} %param.21) | copy-start | bytes 1540
  29.0 3.4 %copy-start.5 = (bf16[512,104,1]{0,1,2:T(8,128)(2,1)}, bf16[512,104,1]{0,1,2:T(8,128)(2,1)S(1)}, u32[]{:S(2)}) copy-start(bf16[512,104,1]{0,1,2:T(8,128)(2,1)S(1)} %fusion.30) | copy-start | bytes 319492
  29.0 18.9 %copy-start.10 = (f32[1024]{0:T(1024)S(1)}, f32[1024]{0:T(1024)}, u32[]{:S(2)}) copy-start(f32[1024]{0:T(1024)} %param.24) | copy-start | bytes 12292
  29.0 18.9 %copy-start.11 = (f32[1024]{0:T(1024)S(1)}, f32[1024]{0:T(1024)}, u32[]{:S(2)}) copy-start(f32[1024]{0:T(1024)} %param.23) | copy-start | bytes 12292
  30.3 4.6 %collective-permute-start.2 = (bf16[8,104,512]{2,1,0:T(8,128)(2,1)}, bf16[8,104,512]{2,1,0:T(8,128)(2,1)}, u32[]{:S(2)}, u32[]{:S(2)}) collective-permute-start(bf16[8,104,512]{2,1,0:T(8,128)(2,1)} %convolution_convert_fusion), channel_id=1, source_target_pairs={{0,1},{1,0},{2,3},{3,2},{4,5},{5,4},{6,7},{7,6},{8,9},{9,8},{10,11... | collective-permute-start | bytes 2555912 | tf_op jit(solution)/shard_map/ppermute | solution.py:129
  37.4 35.2 %all-to-all-start = ((bf16[8,104,512]{2,1,0:T(8,128)(2,1)}), bf16[8,104,512]{2,1,0:T(8,128)(2,1)}, u32[]{:S(2)}, u32[]{:S(2)}) async-start(bf16[8,104,512]{2,1,0:T(8,128)(2,1)} %add_convert_fusion), calls=%async_computation | async-start | bytes 1703936 | tf_op jit(solution)/shard_map/all_to_all | solution.py:35
  47.7 89.4 %all-gather.2.cloned.1.call-start = ((), (), s32[]{:S(2)}) async-start(), calls=%async_computation.6 | async-start | bytes 2230272 | tf_op jit(solution)/shard_map/all_gather | solution.py:80
  90.0 14.9 %all-to-all-start.2 = ((bf16[16,8,1024]{2,1,0:T(8,128)(2,1)}), bf16[16,8,1024]{2,1,0:T(8,128)(2,1)S(1)}, u32[]{:S(2)}, u32[]{:S(2)}) async-start(bf16[16,8,1024]{2,1,0:T(8,128)(2,1)} %broadcast_in_dim.68), calls=%async_computation.2 | async-start | bytes 524288 | tf_op jit(solution)/shard_map/all_to_all | solution.py:26
  107.7 21.4 %all-to-all-start.3 = ((bf16[8,128,128]{2,1,0:T(8,128)(2,1)}), bf16[8,128,128]{2,1,0:T(8,128)(2,1)S(1)}, u32[]{:S(2)}, u32[]{:S(2)}) async-start(bf16[8,128,128]{2,1,0:T(8,128)(2,1)} %broadcast_in_dim.72), calls=%async_computation.3 | async-start | bytes 524288 | tf_op jit(solution)/shard_map/all_to_all | solution.py:26
  130.3 24.3 %all-to-all-start.4 = ((bf16[4,1024,128]{2,1,0:T(8,128)(2,1)}), bf16[4,1024,128]{2,1,0:T(8,128)(2,1)S(1)}, u32[]{:S(2)}, u32[]{:S(2)}) async-start(bf16[4,1024,128]{2,1,0:T(8,128)(2,1)} %broadcast_in_dim.74), calls=%async_computation.4 | async-start | bytes 2097152 | tf_op jit(solution)/shard_map/all_to_all | solution.py:26
  143.8 1.6 copy-start.1
  160.2 15.4 %all-to-all-start.5 = ((bf16[32,2,256]{2,1,0:T(2,128)(2,1)}), bf16[32,2,256]{2,1,0:T(2,128)(2,1)S(1)}, u32[]{:S(2)}, u32[]{:S(2)}) async-start(bf16[32,2,256]{2,1,0:T(2,128)(2,1)} %reshape.420), calls=%async_computation.5 | async-start | bytes 65536 | tf_op jit(solution)/shard_map/all_to_all | solution.py:189
Sparse Core Ops, SparseCore 0:
  51.7 85.2 all-gather.1

commit v15 on v14

--- a/solution.py
+++ b/solution.py
@@ -186,7 +186,9 @@
     packed = jnp.dot(
         select.astype(jnp.bfloat16), merged_out, preferred_element_type=jnp.float32
     ).astype(jnp.bfloat16)
-    got = lax.all_to_all(packed, GRP, 0, 0, tiled=True)
+    wide = jnp.concatenate([packed, jnp.zeros_like(packed)], axis=1)
+    got = lax.all_to_all(wide.reshape(groups, cap, 2 * DH), GRP, 0, 0, tiled=True)
+    got = got.reshape(groups * cap, 2 * DH)[:, :DH]
 
     src_pos = all_pos.reshape(groups, merged_count)
     to_me = (src_pos // tok) == here

time: 185 us -> 192 us (1.038)
  matrix products: 26.1 us -> 30.3 us
  other arithmetic: 15.5 us -> 17.6 us
    dot_general x3, matrix products: 5.94 us -> 8.93 us  [attend_part(): acc = jnp.dot(expo, values, preferred_element_type=jnp.float32)]
    reduce_sum x3, other arithmetic: 5.37 us -> 7.55 us  [attend_part(): total = jnp.sum(expo.astype(jnp.float32), axis=1)]
    unnamed x29 -> x30, local copies, waits for them, and re-layouts: 4.51 us -> 3.41 us
  transfers between devices with their start and end apart: 9 -> 9, of which waited for: 7 -> 7; matrix products, arithmetic and copies ran while one was open for 22% -> 24% of each run, Pallas kernels for 0% -> 0%
where the time goes in v15:
time: 192 us; the launch traced here: 190 us
  waiting for transfers between devices  60.3 us (31%)
  starting transfers between devices  40.2 us (21%)
  matrix products  30.3 us (16%)
  other arithmetic  17.6 us (9%)
  between operations  13.9 us (7%)
  local copies, waits for them, and re-layouts  13.7 us (7%)
  blocking collectives  13.6 us (7%)
    all_to_all x3, waiting for transfers between devices, a2a_gather(): got = lax.all_to_all(spread, axis, 0, 0, tiled=True)  26.2 us
    all_to_all x1, waiting for transfers between devices, a2a_sum(): got = lax.all_to_all(parts, axis, 0, 0, tiled=True)  22.2 us
    all_to_all x3, starting transfers between devices, a2a_gather(): got = lax.all_to_all(spread, axis, 0, 0, tiled=True)  14.4 us
    all_to_all x1, blocking collectives, a2a_sum(): got = lax.all_to_all(parts, axis, 0, 0, tiled=True)  13.6 us
    all_to_all x1, starting transfers between devices, a2a_sum(): got = lax.all_to_all(parts, axis, 0, 0, tiled=True)  10.3 us
    dot_general x3, matrix products, attend_part(): acc = jnp.dot(expo, values, preferred_element_type=jnp.float32)  8.93 us
    all_to_all x1, waiting for transfers between devices, body(): lax.all_to_all(wide.reshape(groups, cap, 2 * DH), GRP, 0, 0, tiled=True)  8.03 us
    dot_general x3, matrix products, attend_part(): jnp.dot(query, keys.T, preferred_element_type=jnp.float32) * DH ** (-0.5)  7.64 us
  transfers between devices with their start and end apart: 9, of which 7 were waited for; matrix products, arithmetic and copies ran while one was open for 24% of the time, Pallas kernels for 0%

profile of v15, /device:TPU:6, one launch (start us, length us, event | category | flops | bytes accessed | tf_op | source)
XLA Modules:
  0.0 189.6 jit_solution(10427370874046159835)
XLA Ops:
  6.5 3.7 %collective-permute-start.1 = (s32[512]{0:T(512)}, s32[512]{0:T(512)S(1)}, u32[]{:S(2)}, u32[]{:S(2)}) collective-permute-start(s32[512]{0:T(512)} %param.15), channel_id=1, source_target_pairs={{0,16},{16,0},{32,48},{48,32},{64,80},{80,64},{96,112},{112,96},{1... | collective-permute-start | bytes 6152 | tf_op jit(solution)/shard_map/ppermute | solution.py:100
  10.3 1.8 convert_reduce_fusion.4
  12.1 2.0 %fusion.8 = f32[512]{0:T(512)S(1)} fusion(bf16[512,1664]{1,0:T(8,128)(2,1)} %param.14, f32[512]{0:T(512)S(1)} %broadcast_multiply_fusion.1), kind=kLoop, calls=%fused_computation.23 | loop fusion | flops 3407360 | bytes 1708032 | tf_op jit(solution)/shard_map/reduce_sum | solution.py:19
  14.1 1.0 fusion.19
  15.2 0.7 slice.116
  15.9 2.3 %collective-permute-start = (bf16[2,512,104]{1,2,0:T(8,128)(2,1)}, bf16[2,512,104]{1,2,0:T(8,128)(2,1)}, u32[]{:S(2)}, u32[]{:S(2)}) collective-permute-start(bf16[2,512,104]{1,2,0:T(8,128)(2,1)} %slice.116), channel_id=1, source_target_pairs={{0,16},{16,0},{32,48},{48,32},{64,80},{80,64},{96,112},{112,96},{1... | collective-permute-start | bytes 638984 | tf_op jit(solution)/shard_map/ppermute | solution.py:100
  18.3 1.8 reshape.404
  20.1 1.8 constant_dynamic-slice_fusion.2
  21.9 1.9 copy.60
  23.8 1.1 collective-permute-done
  24.8 1.5 fusion.12
  27.1 1.9 fusion.30
  29.0 1.3 convolution_convert_fusion
  30.3 1.9 %collective-permute-start.2 = (bf16[8,104,512]{2,1,0:T(8,128)(2,1)}, bf16[8,104,512]{2,1,0:T(8,128)(2,1)}, u32[]{:S(2)}, u32[]{:S(2)}) collective-permute-start(bf16[8,104,512]{2,1,0:T(8,128)(2,1)} %convolution_convert_fusion), channel_id=1, source_target_pairs={{0,1},{1,0},{2,3},{3,2},{4,5},{5,4},{6,7},{7,6},{8,9},{9,8},{10,11... | collective-permute-start | bytes 2555912 | tf_op jit(solution)/shard_map/ppermute | solution.py:129
  32.4 1.3 copy.59
  34.0 0.9 collective-permute-done.2
  34.9 2.5 %add_convert_fusion = bf16[8,104,512]{2,1,0:T(8,128)(2,1)} fusion(bf16[8,104,512]{2,1,0:T(8,128)(2,1)} %collective-permute-done.2, bf16[512,104,1]{0,1,2:T(8,128)(2,1)} %copy-done.6, bf16[104,8,1,104]{0,3,1,2:T(8,128)(2,1)S(1)} %copy.59), kind=kOutput, calls=%fused_computation.40 | convolution fusion | flops 90734592 | bytes 1983488 | tf_op jit(solution)/shard_map/pe,ezf->zfp/dot_general | solution.py:124
  37.4 10.3 %all-to-all-start = ((bf16[8,104,512]{2,1,0:T(8,128)(2,1)}), bf16[8,104,512]{2,1,0:T(8,128)(2,1)}, u32[]{:S(2)}, u32[]{:S(2)}) async-start(bf16[8,104,512]{2,1,0:T(8,128)(2,1)} %add_convert_fusion), calls=%async_computation | async-start | bytes 1703936 | tf_op jit(solution)/shard_map/all_to_all | solution.py:35
  47.9 1.5 fusion.48
  49.4 0.7 copy.49
  50.4 22.2 %all-to-all-done = bf16[8,104,512]{2,1,0:T(8,128)(2,1)} async-done(((bf16[8,104,512]{2,1,0:T(8,128)(2,1)}), bf16[8,104,512]{2,1,0:T(8,128)(2,1)}, u32[]{:S(2)}, u32[]{:S(2)}) %all-to-all-start) | async-done | bytes 852000 | tf_op jit(solution)/shard_map/all_to_all | solution.py:35
  72.6 1.3 convert_reduce_fusion.6
  74.1 1.5 fusion.29
  75.6 13.6 %all_to_all.30 = bf16[16,8,1024]{2,1,0:T(8,128)(2,1)S(1)} all-to-all(bf16[16,8,1024]{2,1,0:T(8,128)(2,1)S(1)} %fusion.29), channel_id=1, replica_groups=mesh['gx'=4,'gy'=8,'z'=8,'core'=2] {'z','core'}, dimensions={0} | all-to-all | bytes 524288 | tf_op jit(solution)/shard_map/all_to_all | solution.py:35
  89.3 0.7 broadcast_in_dim.68
  90.0 3.5 %all-to-all-start.2 = ((bf16[16,8,1024]{2,1,0:T(8,128)(2,1)}), bf16[16,8,1024]{2,1,0:T(8,128)(2,1)S(1)}, u32[]{:S(2)}, u32[]{:S(2)}) async-start(bf16[16,8,1024]{2,1,0:T(8,128)(2,1)} %broadcast_in_dim.68), calls=%async_computation.2 | async-start | bytes 524288 | tf_op jit(solution)/shard_map/all_to_all | solution.py:26
  93.7 11.2 %all-to-all-done.2 = bf16[16,8,1024]{2,1,0:T(8,128)(2,1)S(1)} async-done(((bf16[16,8,1024]{2,1,0:T(8,128)(2,1)}), bf16[16,8,1024]{2,1,0:T(8,128)(2,1)S(1)}, u32[]{:S(2)}, u32[]{:S(2)}) %all-to-all-start.2) | async-done | bytes 262176 | tf_op jit(solution)/shard_map/all_to_all | solution.py:26
  105.4 1.4 fusion.58
  107.0 0.8 broadcast_in_dim.72
  107.7 6.2 %all-to-all-start.3 = ((bf16[8,128,128]{2,1,0:T(8,128)(2,1)}), bf16[8,128,128]{2,1,0:T(8,128)(2,1)S(1)}, u32[]{:S(2)}, u32[]{:S(2)}) async-start(bf16[8,128,128]{2,1,0:T(8,128)(2,1)} %broadcast_in_dim.72), calls=%async_computation.3 | async-start | bytes 524288 | tf_op jit(solution)/shard_map/all_to_all | solution.py:26
  114.3 14.9 %all-to-all-done.3 = bf16[8,128,128]{2,1,0:T(8,128)(2,1)S(1)} async-done(((bf16[8,128,128]{2,1,0:T(8,128)(2,1)}), bf16[8,128,128]{2,1,0:T(8,128)(2,1)S(1)}, u32[]{:S(2)}, u32[]{:S(2)}) %all-to-all-start.3) | async-done | bytes 262176 | tf_op jit(solution)/shard_map/all_to_all | solution.py:26
  129.2 1.2 broadcast_in_dim.74
  130.4 4.7 %all-to-all-start.4 = ((bf16[4,1024,128]{2,1,0:T(8,128)(2,1)}), bf16[4,1024,128]{2,1,0:T(8,128)(2,1)}, u32[]{:S(2)}, u32[]{:S(2)}) async-start(bf16[4,1024,128]{2,1,0:T(8,128)(2,1)} %broadcast_in_dim.74), calls=%async_computation.4 | async-start | bytes 2097152 | tf_op jit(solution)/shard_map/all_to_all | solution.py:26
  135.1 1.9 all-gather.2.cloned.1.call-done
  137.0 0.8 slice.110
  137.9 0.8 convert_reduce_fusion.2
  140.9 2.7 %fusion.4 = (f32[128]{0:T(128)S(1)}, f32[128,8448]{1,0:T(8,128)S(1)}) fusion(s32[8448]{0:T(1024)S(1)} %fusion.95, s32[128]{0:T(128)S(1)} %get-tuple-element.40, bf16[8448,128]{1,0:T(8,128)(2,1)} %all-gather.2.cloned.1.call-done, bf16[3,128,64]{1,2,0:T(8,128)(2,1)S(1)} %convert_bitcast_fusion.3), kind=kOutput, calls=%fused_computation.16 | convolution fusion | flops 142737280 | bytes 6542336 | tf_op jit(solution)/shard_map/dot_general | solution.py:40
  143.7 2.5 %convert_reduce_fusion.3 = (f32[128]{0:T(128)S(1)}, bf16[128,8448]{1,0:T(8,128)(2,1)}) fusion(f32[128,8448]{1,0:T(8,128)S(1)} %get-tuple-element.49, f32[128]{0:T(128)S(1)} %get-tuple-element.48, s32[128]{0:T(128)S(1)} %get-tuple-element.40, s32[8448]{0:T(1024)S(1)} %fusion.95), kind=kLoop, calls=%fused_computation.18 | loop fusion | flops 6487936 | bytes 6523392 | tf_op jit(solution)/shard_map/reduce_sum | solution.py:43
  146.2 2.1 %fusion = (f32[256]{0:T(256)S(1)}, f32[256,8448]{1,0:T(8,128)S(1)}) fusion(s32[8448]{0:T(1024)S(1)} %fusion.95, s32[256]{0:T(256)S(1)} %add_add_fusion, bf16[8448,128]{1,0:T(8,128)(2,1)S(1)} %copy-done.2, bf16[3,256,64]{1,2,0:T(8,128)(2,1)S(1)} %convert_bitcast_fusion.2), kind=kOutput, calls=%fused_computation.4 | convolution fusion | flops 285474560 | bytes 10885120 | tf_op jit(solution)/shard_map/dot_general | solution.py:40
  148.3 3.6 %convert_reduce_fusion = (f32[256]{0:T(256)S(1)}, bf16[256,8448]{1,0:T(8,128)(2,1)}) fusion(f32[256,8448]{1,0:T(8,128)S(1)} %get-tuple-element.51, f32[256]{0:T(256)S(1)} %get-tuple-element.50, s32[256]{0:T(256)S(1)} %add_add_fusion, s32[8448]{0:T(1024)S(1)} %fusion.95), kind=kLoop, calls=%fused_computation.6 | loop fusion | flops 12975872 | bytes 13012992 | tf_op jit(solution)/shard_map/reduce_sum | solution.py:43
  152.0 3.7 %fusion.13 = f32[128,64]{0,1:T(8,128)S(1)} fusion(bf16[128,8448]{1,0:T(8,128)(2,1)} %get-tuple-element.25, bf16[8448,128]{1,0:T(8,128)(2,1)S(1)} %copy-done.2), kind=kOutput, calls=%fused_computation.32 | convolution fusion | flops 138412032 | bytes 4358144 | tf_op jit(solution)/shard_map/dot_general | solution.py:44
  155.7 2.5 %fusion.15 = f32[256,64]{0,1:T(8,128)S(1)} fusion(bf16[256,8448]{1,0:T(8,128)(2,1)S(1)} %copy-done.1, bf16[8448,128]{1,0:T(8,128)(2,1)S(1)} %copy-done.2), kind=kOutput, calls=%fused_computation.34 | convolution fusion | flops 276824064 | bytes 6553600 | tf_op jit(solution)/shard_map/dot_general | solution.py:44
  158.2 2.8 %fusion.2 = (f32[384]{0:T(512)S(1)}, f32[384,4096]{1,0:T(8,128)S(1)}) fusion(s32[4096]{0:T(1024)S(1)} %get-tuple-element.38, s32[384]{0:T(512)S(1)} %pad_add_fusion.1, bf16[4096,128]{1,0:T(8,128)(2,1)} %bitcast.45, bf16[128,64]{0,1:T(8,128)(2,1)S(1)} %get-tuple-element.35, bf16[256,64]{0,1:T(8,128)(2,1)S(1)} %get-tuple-element.32), kind=kOutput, calls=%fused_computation.9 | convolution fusion | flops 207715968 | bytes 7408640 | tf_op jit(solution)/shard_map/dot_general | solution.py:40
  161.0 1.5 convert_reduce_fusion.1
  162.5 2.8 %fusion.34 = bf16[384,64]{0,1:T(8,128)(2,1)S(1)} fusion(bf16[384,4096]{1,0:T(8,128)(2,1)S(1)} %get-tuple-element.21, bf16[4096,128]{1,0:T(8,128)(2,1)} %bitcast.45, f32[128,64]{0,1:T(8,128)S(1)} %fusion.13, f32[256,64]{0,1:T(8,128)S(1)} %fusion.15, f32[384]{0:T(512)S(1)} %get-tuple-element.17, f32[384]{0:T(512)S(1)} %get-tuple-element.18, ...), kind=kOutput, calls=%fused_computation.62 | convolution fusion | flops 201474048 | bytes 4346368 | tf_op jit(solution)/shard_map/dot_general | solution.py:44
  166.2 7.4 %all-to-all-start.5 = ((bf16[32,8,128]{2,1,0:T(8,128)(2,1)}), bf16[32,8,128]{2,1,0:T(8,128)(2,1)S(1)}, u32[]{:S(2)}, u32[]{:S(2)}) async-start(bf16[32,8,128]{2,1,0:T(8,128)(2,1)} %pad_bitcast_fusion), calls=%async_computation.5 | async-start | bytes 131072 | tf_op jit(solution)/shard_map/all_to_all | solution.py:190
  173.7 8.0 %all-to-all-done.5 = bf16[32,8,128]{2,1,0:T(8,128)(2,1)S(1)} async-done(((bf16[32,8,128]{2,1,0:T(8,128)(2,1)}), bf16[32,8,128]{2,1,0:T(8,128)(2,1)S(1)}, u32[]{:S(2)}, u32[]{:S(2)}) %all-to-all-start.5) | async-done | bytes 65568 | tf_op jit(solution)/shard_map/all_to_all | solution.py:190
  182.0 0.8 fusion.33
  (93 shorter events, 6.7 us)
Async XLA Ops:
  6.5 7.6 %copy-start = (bf16[3,1664,104]{1,2,0:T(8,128)(2,1)S(1)}, bf16[3,1664,104]{1,2,0:T(8,128)(2,1)}, u32[]{:S(2)}) copy-start(bf16[3,1664,104]{1,2,0:T(8,128)(2,1)} %param.18) | copy-start | bytes 3115012
  6.5 7.6 %copy-start.3 = (bf16[512,1664]{1,0:T(8,128)(2,1)S(1)}, bf16[512,1664]{1,0:T(8,128)(2,1)}, u32[]{:S(2)}) copy-start(bf16[512,1664]{1,0:T(8,128)(2,1)} %param.14) | copy-start | bytes 5111812
  6.5 7.6 %copy-start.9 = (f32[1664]{0:T(1024)S(1)}, f32[1664]{0:T(1024)}, u32[]{:S(2)}) copy-start(f32[1664]{0:T(1024)} %param.17) | copy-start | bytes 19972
  6.5 7.6 %copy-start.10 = (f32[1664]{0:T(1024)S(1)}, f32[1664]{0:T(1024)}, u32[]{:S(2)}) copy-start(f32[1664]{0:T(1024)} %param.16) | copy-start | bytes 19972
  6.5 17.2 %collective-permute-start.1 = (s32[512]{0:T(512)}, s32[512]{0:T(512)S(1)}, u32[]{:S(2)}, u32[]{:S(2)}) collective-permute-start(s32[512]{0:T(512)} %param.15), channel_id=1, source_target_pairs={{0,16},{16,0},{32,48},{48,32},{64,80},{80,64},{96,112},{112,96},{1... | collective-permute-start | bytes 6152 | tf_op jit(solution)/shard_map/ppermute | solution.py:100
  15.2 8.6 %copy-start.7 = (s32[512]{0:T(512)S(1)}, s32[512]{0:T(512)}, u32[]{:S(2)}) copy-start(s32[512]{0:T(512)} %param.15) | copy-start | bytes 6148
  15.9 8.9 %collective-permute-start = (bf16[2,512,104]{1,2,0:T(8,128)(2,1)}, bf16[2,512,104]{1,2,0:T(8,128)(2,1)}, u32[]{:S(2)}, u32[]{:S(2)}) collective-permute-start(bf16[2,512,104]{1,2,0:T(8,128)(2,1)} %slice.116), channel_id=1, source_target_pairs={{0,16},{16,0},{32,48},{48,32},{64,80},{80,64},{96,112},{112,96},{1... | collective-permute-start | bytes 638984 | tf_op jit(solution)/shard_map/ppermute | solution.py:100
  27.1 1.9 %copy-start.5 = (bf16[104,8,1,104]{0,3,1,2:T(8,128)(2,1)S(1)}, bf16[104,8,1,104]{0,3,1,2:T(8,128)(2,1)}, u32[]{:S(2)}) copy-start(bf16[104,8,1,104]{0,3,1,2:T(8,128)(2,1)} %copy.60) | copy-start | bytes 519172
  27.1 5.1 %copy-start.4 = (bf16[256,1024]{1,0:T(8,128)(2,1)S(1)}, bf16[256,1024]{1,0:T(8,128)(2,1)}, u32[]{:S(2)}) copy-start(bf16[256,1024]{1,0:T(8,128)(2,1)} %param.22) | copy-start | bytes 1572868
  27.1 6.8 %copy-start.8 = (s32[128]{0:T(128)S(1)}, s32[128]{0:T(128)}, u32[]{:S(2)}) copy-start(s32[128]{0:T(128)} %param.21) | copy-start | bytes 1540
  29.0 3.4 %copy-start.6 = (bf16[512,104,1]{0,1,2:T(8,128)(2,1)}, bf16[512,104,1]{0,1,2:T(8,128)(2,1)S(1)}, u32[]{:S(2)}) copy-start(bf16[512,104,1]{0,1,2:T(8,128)(2,1)S(1)} %fusion.30) | copy-start | bytes 319492
  29.0 18.9 %copy-start.11 = (f32[1024]{0:T(1024)S(1)}, f32[1024]{0:T(1024)}, u32[]{:S(2)}) copy-start(f32[1024]{0:T(1024)} %param.24) | copy-start | bytes 12292
  29.0 18.9 %copy-start.12 = (f32[1024]{0:T(1024)S(1)}, f32[1024]{0:T(1024)}, u32[]{:S(2)}) copy-start(f32[1024]{0:T(1024)} %param.23) | copy-start | bytes 12292
  30.3 4.6 %collective-permute-start.2 = (bf16[8,104,512]{2,1,0:T(8,128)(2,1)}, bf16[8,104,512]{2,1,0:T(8,128)(2,1)}, u32[]{:S(2)}, u32[]{:S(2)}) collective-permute-start(bf16[8,104,512]{2,1,0:T(8,128)(2,1)} %convolution_convert_fusion), channel_id=1, source_target_pairs={{0,1},{1,0},{2,3},{3,2},{4,5},{5,4},{6,7},{7,6},{8,9},{9,8},{10,11... | collective-permute-start | bytes 2555912 | tf_op jit(solution)/shard_map/ppermute | solution.py:129
  37.4 35.2 %all-to-all-start = ((bf16[8,104,512]{2,1,0:T(8,128)(2,1)}), bf16[8,104,512]{2,1,0:T(8,128)(2,1)}, u32[]{:S(2)}, u32[]{:S(2)}) async-start(bf16[8,104,512]{2,1,0:T(8,128)(2,1)} %add_convert_fusion), calls=%async_computation | async-start | bytes 1703936 | tf_op jit(solution)/shard_map/all_to_all | solution.py:35
  47.7 89.3 %all-gather.2.cloned.1.call-start = ((), (), s32[]{:S(2)}) async-start(), calls=%async_computation.6 | async-start | bytes 2230272 | tf_op jit(solution)/shard_map/all_gather | solution.py:80
  90.0 14.9 %all-to-all-start.2 = ((bf16[16,8,1024]{2,1,0:T(8,128)(2,1)}), bf16[16,8,1024]{2,1,0:T(8,128)(2,1)S(1)}, u32[]{:S(2)}, u32[]{:S(2)}) async-start(bf16[16,8,1024]{2,1,0:T(8,128)(2,1)} %broadcast_in_dim.68), calls=%async_computation.2 | async-start | bytes 524288 | tf_op jit(solution)/shard_map/all_to_all | solution.py:26
  107.7 21.5 %all-to-all-start.3 = ((bf16[8,128,128]{2,1,0:T(8,128)(2,1)}), bf16[8,128,128]{2,1,0:T(8,128)(2,1)S(1)}, u32[]{:S(2)}, u32[]{:S(2)}) async-start(bf16[8,128,128]{2,1,0:T(8,128)(2,1)} %broadcast_in_dim.72), calls=%async_computation.3 | async-start | bytes 524288 | tf_op jit(solution)/shard_map/all_to_all | solution.py:26
  130.4 27.8 %all-to-all-start.4 = ((bf16[4,1024,128]{2,1,0:T(8,128)(2,1)}), bf16[4,1024,128]{2,1,0:T(8,128)(2,1)}, u32[]{:S(2)}, u32[]{:S(2)}) async-start(bf16[4,1024,128]{2,1,0:T(8,128)(2,1)} %broadcast_in_dim.74), calls=%async_computation.4 | async-start | bytes 2097152 | tf_op jit(solution)/shard_map/all_to_all | solution.py:26
  143.7 2.5 %copy-start.2 = (bf16[8448,128]{1,0:T(8,128)(2,1)S(1)}, bf16[8448,128]{1,0:T(8,128)(2,1)}, u32[]{:S(2)}) copy-start(bf16[8448,128]{1,0:T(8,128)(2,1)} %all-gather.2.cloned.1.call-done) | copy-start | bytes 6488068
  152.0 3.7 %copy-start.1 = (bf16[256,8448]{1,0:T(8,128)(2,1)S(1)}, bf16[256,8448]{1,0:T(8,128)(2,1)}, u32[]{:S(2)}) copy-start(bf16[256,8448]{1,0:T(8,128)(2,1)} %get-tuple-element.23) | copy-start | bytes 12976132
  166.2 15.6 %all-to-all-start.5 = ((bf16[32,8,128]{2,1,0:T(8,128)(2,1)}), bf16[32,8,128]{2,1,0:T(8,128)(2,1)S(1)}, u32[]{:S(2)}, u32[]{:S(2)}) async-start(bf16[32,8,128]{2,1,0:T(8,128)(2,1)} %pad_bitcast_fusion), calls=%async_computation.5 | async-start | bytes 131072 | tf_op jit(solution)/shard_map/all_to_all | solution.py:190
Sparse Core Ops, SparseCore 0:
  51.7 85.2 all-gather.1

commit v16 on v14

--- a/solution.py
+++ b/solution.py
@@ -144,7 +144,7 @@
     mproj = jnp.einsum("td,sde->ste", mnorm, dec_qkv, preferred_element_type=jnp.float32).astype(
         jnp.bfloat16
     )
-    merged_kv = grp_gather(jnp.concatenate([mproj[1], mproj[2]], axis=1))
+    merged_kv = a2a_gather(jnp.concatenate([mproj[1], mproj[2]], axis=1), GRP)
 
     query_pos = jnp.concatenate([own_text_pos, positions], axis=0)
     block = positions // tok

time: 185 us -> 191 us (1.032)
  waiting for transfers between devices: 60.1 us -> 74.9 us
  blocking collectives: 13.6 us -> 0 us
  starting transfers between devices: 40.3 us -> 47.1 us
  matrix products: 26.1 us -> 23.6 us
    all_gather x1, waiting for transfers between devices: 1.97 us -> 19.9 us  [body(): text_kv = lax.all_gather(payload, GRP, axis=0, tiled=True)]
    all_to_all x3 -> x2, waiting for transfers between devices: 26.1 us -> 10.9 us  [a2a_gather(): got = lax.all_to_all(spread, axis, 0, 0, tiled=True)]
    all_to_all x1 -> x0, blocking collectives: 13.6 us -> none  [a2a_sum(): got = lax.all_to_all(parts, axis, 0, 0, tiled=True)]
    all_to_all x1 -> x2, waiting for transfers between devices: 22.2 us -> 34.6 us  [a2a_sum(): got = lax.all_to_all(parts, axis, 0, 0, tiled=True)]
    all_to_all x1, starting transfers between devices: 7.38 us -> 11.4 us  [body(): got = lax.all_to_all(packed, GRP, 0, 0, tiled=True)]
    all_to_all x1 -> x2, starting transfers between devices: 10.3 us -> 13.8 us  [a2a_sum(): got = lax.all_to_all(parts, axis, 0, 0, tiled=True)]
    all_to_all x3 -> x2, starting transfers between devices: 14.5 us -> 13.9 us  [a2a_gather(): got = lax.all_to_all(spread, axis, 0, 0, tiled=True)]
    unnamed x29 -> x31, local copies, waits for them, and re-layouts: 4.51 us -> 4.6 us
  transfers between devices with their start and end apart: 9 -> 9, of which waited for: 7 -> 6; matrix products, arithmetic and copies ran while one was open for 22% -> 20% of each run, Pallas kernels for 0% -> 0%
where the time goes in v16:
time: 191 us; the launch traced here: 188 us
  waiting for transfers between devices  74.9 us (39%)
  starting transfers between devices  47.1 us (25%)
  matrix products  23.6 us (12%)
  other arithmetic  15.5 us (8%)
  between operations  14 us (7%)
  local copies, waits for them, and re-layouts  13 us (7%)
    all_to_all x2, waiting for transfers between devices, a2a_sum(): got = lax.all_to_all(parts, axis, 0, 0, tiled=True)  34.6 us
    all_gather x1, waiting for transfers between devices, body(): text_kv = lax.all_gather(payload, GRP, axis=0, tiled=True)  19.9 us
    all_to_all x2, starting transfers between devices, a2a_gather(): got = lax.all_to_all(spread, axis, 0, 0, tiled=True)  13.9 us
    all_to_all x2, starting transfers between devices, a2a_sum(): got = lax.all_to_all(parts, axis, 0, 0, tiled=True)  13.8 us
    all_to_all x1, starting transfers between devices, body(): got = lax.all_to_all(packed, GRP, 0, 0, tiled=True)  11.4 us
    all_to_all x2, waiting for transfers between devices, a2a_gather(): got = lax.all_to_all(spread, axis, 0, 0, tiled=True)  10.9 us
    all_to_all x1, waiting for transfers between devices, body(): got = lax.all_to_all(packed, GRP, 0, 0, tiled=True)  7.83 us
    dot_general x3, matrix products, attend_part(): jnp.dot(query, keys.T, preferred_element_type=jnp.float32) * DH ** (-0.5)  6.42 us
  transfers between devices with their start and end apart: 9, of which 6 were waited for; matrix products, arithmetic and copies ran while one was open for 20% of the time, Pallas kernels for 0%

profile of v16, /device:TPU:6, one launch (start us, length us, event | category | flops | bytes accessed | tf_op | source)
XLA Modules:
  0.0 188.1 jit_solution(11396565254781635454)
XLA Ops:
  6.5 3.7 %collective-permute-start.1 = (s32[512]{0:T(512)}, s32[512]{0:T(512)S(1)}, u32[]{:S(2)}, u32[]{:S(2)}) collective-permute-start(s32[512]{0:T(512)} %param.15), channel_id=1, source_target_pairs={{0,16},{16,0},{32,48},{48,32},{64,80},{80,64},{96,112},{112,96},{1... | collective-permute-start | bytes 6152 | tf_op jit(solution)/shard_map/ppermute | solution.py:100
  10.3 1.8 convert_reduce_fusion.4
  12.1 2.0 %fusion.8 = f32[512]{0:T(512)S(1)} fusion(bf16[512,1664]{1,0:T(8,128)(2,1)} %param.14, f32[512]{0:T(512)S(1)} %broadcast_multiply_fusion.1), kind=kLoop, calls=%fused_computation.23 | loop fusion | flops 3407360 | bytes 1708032 | tf_op jit(solution)/shard_map/reduce_sum | solution.py:19
  14.2 1.0 fusion.19
  15.3 0.7 copy-done.5
  16.0 2.4 %collective-permute-start = (bf16[2,512,104]{1,2,0:T(8,128)(2,1)S(1)}, bf16[2,512,104]{1,2,0:T(8,128)(2,1)}, u32[]{:S(2)}, u32[]{:S(2)}) collective-permute-start(bf16[2,512,104]{1,2,0:T(8,128)(2,1)S(1)} %slice.112), channel_id=1, source_target_pairs={{0,16},{16,0},{32,48},{48,32},{64,80},{80,64},{96,112},{112,96},{1... | collective-permute-start | bytes 638984 | tf_op jit(solution)/shard_map/ppermute | solution.py:100
  18.6 1.8 reshape.399
  20.4 1.8 constant_dynamic-slice_fusion.2
  22.2 1.2 copy.59
  23.4 1.3 copy.60
  24.8 1.5 fusion.12
  26.3 0.7 fusion.25
  27.0 1.8 fusion.30
  29.2 1.9 %collective-permute-start.2 = (bf16[8,104,512]{2,1,0:T(8,128)(2,1)S(1)}, bf16[8,104,512]{2,1,0:T(8,128)(2,1)S(1)}, u32[]{:S(2)}, u32[]{:S(2)}) collective-permute-start(bf16[8,104,512]{2,1,0:T(8,128)(2,1)S(1)} %convolution_convert_fusion), channel_id=1, source_target_pairs={{0,1},{1,0},{2,3},{3,2},{4,5},{5,4},{6,7},{7,6},{8,9},{9,8},{10,11... | collective-permute-start | bytes 2555912 | tf_op jit(solution)/shard_map/ppermute | solution.py:129
  31.5 0.4 fusion.48
  31.9 1.5 collective-permute-done.2
  33.5 1.3 add_convert_fusion
  34.8 10.3 %all-to-all-start = ((bf16[8,104,512]{2,1,0:T(8,128)(2,1)}), bf16[8,104,512]{2,1,0:T(8,128)(2,1)}, u32[]{:S(2)}, u32[]{:S(2)}) async-start(bf16[8,104,512]{2,1,0:T(8,128)(2,1)} %add_convert_fusion), calls=%async_computation | async-start | bytes 1703936 | tf_op jit(solution)/shard_map/all_to_all | solution.py:35
  45.3 0.7 copy.49
  46.3 23.7 %all-to-all-done = bf16[8,104,512]{2,1,0:T(8,128)(2,1)} async-done(((bf16[8,104,512]{2,1,0:T(8,128)(2,1)}), bf16[8,104,512]{2,1,0:T(8,128)(2,1)}, u32[]{:S(2)}, u32[]{:S(2)}) %all-to-all-start) | async-done | bytes 852000 | tf_op jit(solution)/shard_map/all_to_all | solution.py:35
  70.0 1.3 convert_reduce_fusion.6
  71.5 2.2 %fusion.29 = bf16[16,8,1024]{2,1,0:T(8,128)(2,1)} fusion(bf16[4,104,1024]{2,1,0:T(8,128)(2,1)} %param.20, bf16[104,128,4]{0,2,1:T(4,128)(2,1)S(1)} %bitcast.128), kind=kOutput, calls=%fused_computation.54 | convolution fusion | flops 109182976 | bytes 1220608 | tf_op jit(solution)/shard_map/cmk,kce->me/dot_general | solution.py:135
  73.7 3.5 %all-to-all-start.1 = ((bf16[16,8,1024]{2,1,0:T(8,128)(2,1)}), bf16[16,8,1024]{2,1,0:T(8,128)(2,1)S(1)}, u32[]{:S(2)}, u32[]{:S(2)}) async-start(bf16[16,8,1024]{2,1,0:T(8,128)(2,1)} %fusion.29), calls=%async_computation.1 | async-start | bytes 524288 | tf_op jit(solution)/shard_map/all_to_all | solution.py:35
  77.3 10.9 %all-to-all-done.1 = bf16[16,8,1024]{2,1,0:T(8,128)(2,1)S(1)} async-done(((bf16[16,8,1024]{2,1,0:T(8,128)(2,1)}), bf16[16,8,1024]{2,1,0:T(8,128)(2,1)S(1)}, u32[]{:S(2)}, u32[]{:S(2)}) %all-to-all-start.1) | async-done | bytes 262176 | tf_op jit(solution)/shard_map/all_to_all | solution.py:35
  88.3 0.7 broadcast_in_dim.64
  89.0 3.5 %all-to-all-start.2 = ((bf16[16,8,1024]{2,1,0:T(8,128)(2,1)}), bf16[16,8,1024]{2,1,0:T(8,128)(2,1)S(1)}, u32[]{:S(2)}, u32[]{:S(2)}) async-start(bf16[16,8,1024]{2,1,0:T(8,128)(2,1)} %broadcast_in_dim.64), calls=%async_computation.2 | async-start | bytes 524288 | tf_op jit(solution)/shard_map/all_to_all | solution.py:26
  93.0 10.9 %all-to-all-done.2 = bf16[16,8,1024]{2,1,0:T(8,128)(2,1)S(1)} async-done(((bf16[16,8,1024]{2,1,0:T(8,128)(2,1)}), bf16[16,8,1024]{2,1,0:T(8,128)(2,1)S(1)}, u32[]{:S(2)}, u32[]{:S(2)}) %all-to-all-start.2) | async-done | bytes 262176 | tf_op jit(solution)/shard_map/all_to_all | solution.py:26
  104.4 1.4 fusion.58
  106.0 1.2 broadcast_in_dim.68
  107.2 10.3 %all-to-all-start.3 = ((bf16[32,128,128]{2,1,0:T(8,128)(2,1)}), bf16[32,128,128]{2,1,0:T(8,128)(2,1)S(1)}, u32[]{:S(2)}, u32[]{:S(2)}) async-start(bf16[32,128,128]{2,1,0:T(8,128)(2,1)} %broadcast_in_dim.68), calls=%async_computation.3 | async-start | bytes 2097152 | tf_op jit(solution)/shard_map/all_to_all | solution.py:26
  117.6 19.9 %all-gather.2.cloned.1.call-done = bf16[8448,128]{1,0:T(8,128)(2,1)} async-done(((bf16[264,128]{1,0:T(8,128)(2,1)}), bf16[8448,128]{1,0:T(8,128)(2,1)}) %all-gather.2.cloned.1.call-update) | async-done | bytes 2162704 | tf_op jit(solution)/shard_map/all_gather | solution.py:80
  137.5 0.8 slice.106
  138.4 0.8 convert_reduce_fusion.2
  139.5 0.5 convert_reduce_fusion.5
  140.8 0.6 select_reduce_fusion.1
  141.4 2.7 %fusion.4 = (f32[128]{0:T(128)S(1)}, f32[128,8448]{1,0:T(8,128)S(1)}) fusion(s32[8448]{0:T(1024)S(1)} %fusion.95, s32[128]{0:T(128)S(1)} %get-tuple-element.40, bf16[8448,128]{1,0:T(8,128)(2,1)} %all-gather.2.cloned.1.call-done, bf16[3,128,64]{1,2,0:T(8,128)(2,1)S(1)} %convert_bitcast_fusion.3), kind=kOutput, calls=%fused_computation.16 | convolution fusion | flops 142737280 | bytes 6542336 | tf_op jit(solution)/shard_map/dot_general | solution.py:40
  144.2 1.2 convert_reduce_fusion.3
  145.8 2.0 %fusion.13 = f32[128,64]{0,1:T(8,128)S(1)} fusion(bf16[128,8448]{1,0:T(8,128)(2,1)S(1)} %get-tuple-element.25, bf16[8448,128]{1,0:T(8,128)(2,1)S(1)} %copy-done.1), kind=kOutput, calls=%fused_computation.32 | convolution fusion | flops 138412032 | bytes 4358144 | tf_op jit(solution)/shard_map/dot_general | solution.py:44
  147.8 2.1 %fusion = (f32[256]{0:T(256)S(1)}, f32[256,8448]{1,0:T(8,128)S(1)}) fusion(s32[8448]{0:T(1024)S(1)} %fusion.95, s32[256]{0:T(256)S(1)} %add_add_fusion, bf16[8448,128]{1,0:T(8,128)(2,1)S(1)} %copy-done.1, bf16[3,256,64]{1,2,0:T(8,128)(2,1)S(1)} %convert_bitcast_fusion.2), kind=kOutput, calls=%fused_computation.4 | convolution fusion | flops 285474560 | bytes 10885120 | tf_op jit(solution)/shard_map/dot_general | solution.py:40
  149.9 2.7 %convert_reduce_fusion = (f32[256]{0:T(256)S(1)}, bf16[256,8448]{1,0:T(8,128)(2,1)S(1)}) fusion(f32[256,8448]{1,0:T(8,128)S(1)} %get-tuple-element.51, f32[256]{0:T(256)S(1)} %get-tuple-element.50, s32[256]{0:T(256)S(1)} %add_add_fusion, s32[8448]{0:T(1024)S(1)} %fusion.95), kind=kLoop, calls=%fused_computation.6 | loop fusion | flops 12975872 | bytes 13012992 | tf_op jit(solution)/shard_map/reduce_sum | solution.py:43
  152.6 2.5 %fusion.15 = f32[256,64]{0,1:T(8,128)S(1)} fusion(bf16[256,8448]{1,0:T(8,128)(2,1)S(1)} %get-tuple-element.23, bf16[8448,128]{1,0:T(8,128)(2,1)S(1)} %copy-done.1), kind=kOutput, calls=%fused_computation.34 | convolution fusion | flops 276824064 | bytes 6553600 | tf_op jit(solution)/shard_map/dot_general | solution.py:44
  155.0 1.6 fusion.2
  156.6 1.5 convert_reduce_fusion.1
  158.1 1.5 fusion.34
  159.9 0.7 reshape.419
  160.7 11.4 %all-to-all-start.4 = ((bf16[32,2,256]{2,1,0:T(2,128)(2,1)}), bf16[32,2,256]{2,1,0:T(2,128)(2,1)S(1)}, u32[]{:S(2)}, u32[]{:S(2)}) async-start(bf16[32,2,256]{2,1,0:T(2,128)(2,1)} %reshape.419), calls=%async_computation.4 | async-start | bytes 65536 | tf_op jit(solution)/shard_map/all_to_all | solution.py:189
  172.2 7.8 %all-to-all-done.4 = bf16[32,2,256]{2,1,0:T(2,128)(2,1)S(1)} async-done(((bf16[32,2,256]{2,1,0:T(2,128)(2,1)}), bf16[32,2,256]{2,1,0:T(2,128)(2,1)S(1)}, u32[]{:S(2)}, u32[]{:S(2)}) %all-to-all-start.4) | async-done | bytes 32800 | tf_op jit(solution)/shard_map/all_to_all | solution.py:189
  180.4 0.8 fusion.33
  (92 shorter events, 5.1 us)
Async XLA Ops:
  6.5 7.6 %copy-start = (bf16[3,1664,104]{1,2,0:T(8,128)(2,1)S(1)}, bf16[3,1664,104]{1,2,0:T(8,128)(2,1)}, u32[]{:S(2)}) copy-start(bf16[3,1664,104]{1,2,0:T(8,128)(2,1)} %param.18) | copy-start | bytes 3115012
  6.5 7.6 %copy-start.2 = (bf16[512,1664]{1,0:T(8,128)(2,1)S(1)}, bf16[512,1664]{1,0:T(8,128)(2,1)}, u32[]{:S(2)}) copy-start(bf16[512,1664]{1,0:T(8,128)(2,1)} %param.14) | copy-start | bytes 5111812
  6.5 7.6 %copy-start.9 = (f32[1664]{0:T(1024)S(1)}, f32[1664]{0:T(1024)}, u32[]{:S(2)}) copy-start(f32[1664]{0:T(1024)} %param.17) | copy-start | bytes 19972
  6.5 7.6 %copy-start.10 = (f32[1664]{0:T(1024)S(1)}, f32[1664]{0:T(1024)}, u32[]{:S(2)}) copy-start(f32[1664]{0:T(1024)} %param.16) | copy-start | bytes 19972
  6.5 18.2 %collective-permute-start.1 = (s32[512]{0:T(512)}, s32[512]{0:T(512)S(1)}, u32[]{:S(2)}, u32[]{:S(2)}) collective-permute-start(s32[512]{0:T(512)} %param.15), channel_id=1, source_target_pairs={{0,16},{16,0},{32,48},{48,32},{64,80},{80,64},{96,112},{112,96},{1... | collective-permute-start | bytes 6152 | tf_op jit(solution)/shard_map/ppermute | solution.py:100
  14.1 4.2 %copy-start.3 = (bf16[256,1024]{1,0:T(8,128)(2,1)S(1)}, bf16[256,1024]{1,0:T(8,128)(2,1)}, u32[]{:S(2)}) copy-start(bf16[256,1024]{1,0:T(8,128)(2,1)} %param.22) | copy-start | bytes 1572868
  14.2 4.4 %copy-start.7 = (s32[128]{0:T(128)S(1)}, s32[128]{0:T(128)}, u32[]{:S(2)}) copy-start(s32[128]{0:T(128)} %param.21) | copy-start | bytes 1540
  15.2 9.5 %copy-start.6 = (s32[512]{0:T(512)S(1)}, s32[512]{0:T(512)}, u32[]{:S(2)}) copy-start(s32[512]{0:T(512)} %param.15) | copy-start | bytes 6148
  15.3 0.7 copy-start.5
  16.0 8.8 %collective-permute-start = (bf16[2,512,104]{1,2,0:T(8,128)(2,1)S(1)}, bf16[2,512,104]{1,2,0:T(8,128)(2,1)}, u32[]{:S(2)}, u32[]{:S(2)}) collective-permute-start(bf16[2,512,104]{1,2,0:T(8,128)(2,1)S(1)} %slice.112), channel_id=1, source_target_pairs={{0,16},{16,0},{32,48},{48,32},{64,80},{80,64},{96,112},{112,96},{1... | collective-permute-start | bytes 638984 | tf_op jit(solution)/shard_map/ppermute | solution.py:100
  27.0 4.2 %copy-start.4 = (bf16[256,1024]{1,0:T(8,128)(2,1)S(1)}, bf16[256,1024]{1,0:T(8,128)(2,1)}, u32[]{:S(2)}) copy-start(bf16[256,1024]{1,0:T(8,128)(2,1)} %param.22) | copy-start | bytes 1572868
  27.0 4.5 %copy-start.8 = (bf16[3,1024,64]{1,2,0:T(8,128)(2,1)S(1)}, bf16[3,1024,64]{1,2,0:T(8,128)(2,1)}, u32[]{:S(2)}) copy-start(bf16[3,1024,64]{1,2,0:T(8,128)(2,1)} %param.25) | copy-start | bytes 1179652
  27.0 4.5 %copy-start.11 = (f32[1024]{0:T(1024)S(1)}, f32[1024]{0:T(1024)}, u32[]{:S(2)}) copy-start(f32[1024]{0:T(1024)} %param.24) | copy-start | bytes 12292
  27.0 4.5 %copy-start.12 = (f32[1024]{0:T(1024)S(1)}, f32[1024]{0:T(1024)}, u32[]{:S(2)}) copy-start(f32[1024]{0:T(1024)} %param.23) | copy-start | bytes 12292
  29.2 4.3 %collective-permute-start.2 = (bf16[8,104,512]{2,1,0:T(8,128)(2,1)S(1)}, bf16[8,104,512]{2,1,0:T(8,128)(2,1)S(1)}, u32[]{:S(2)}, u32[]{:S(2)}) collective-permute-start(bf16[8,104,512]{2,1,0:T(8,128)(2,1)S(1)} %convolution_convert_fusion), channel_id=1, source_target_pairs={{0,1},{1,0},{2,3},{3,2},{4,5},{5,4},{6,7},{7,6},{8,9},{9,8},{10,11... | collective-permute-start | bytes 2555912 | tf_op jit(solution)/shard_map/ppermute | solution.py:129
  34.8 35.2 %all-to-all-start = ((bf16[8,104,512]{2,1,0:T(8,128)(2,1)}), bf16[8,104,512]{2,1,0:T(8,128)(2,1)}, u32[]{:S(2)}, u32[]{:S(2)}) async-start(bf16[8,104,512]{2,1,0:T(8,128)(2,1)} %add_convert_fusion), calls=%async_computation | async-start | bytes 1703936 | tf_op jit(solution)/shard_map/all_to_all | solution.py:35
  45.1 92.4 %all-gather.2.cloned.1.call-start = ((), (), s32[]{:S(2)}) async-start(), calls=%async_computation.5 | async-start | bytes 2230272 | tf_op jit(solution)/shard_map/all_gather | solution.py:80
  73.7 14.5 %all-to-all-start.1 = ((bf16[16,8,1024]{2,1,0:T(8,128)(2,1)}), bf16[16,8,1024]{2,1,0:T(8,128)(2,1)S(1)}, u32[]{:S(2)}, u32[]{:S(2)}) async-start(bf16[16,8,1024]{2,1,0:T(8,128)(2,1)} %fusion.29), calls=%async_computation.1 | async-start | bytes 524288 | tf_op jit(solution)/shard_map/all_to_all | solution.py:35
  89.0 14.9 %all-to-all-start.2 = ((bf16[16,8,1024]{2,1,0:T(8,128)(2,1)}), bf16[16,8,1024]{2,1,0:T(8,128)(2,1)S(1)}, u32[]{:S(2)}, u32[]{:S(2)}) async-start(bf16[16,8,1024]{2,1,0:T(8,128)(2,1)} %broadcast_in_dim.64), calls=%async_computation.2 | async-start | bytes 524288 | tf_op jit(solution)/shard_map/all_to_all | solution.py:26
  107.2 47.8 %all-to-all-start.3 = ((bf16[32,128,128]{2,1,0:T(8,128)(2,1)}), bf16[32,128,128]{2,1,0:T(8,128)(2,1)S(1)}, u32[]{:S(2)}, u32[]{:S(2)}) async-start(bf16[32,128,128]{2,1,0:T(8,128)(2,1)} %broadcast_in_dim.68), calls=%async_computation.3 | async-start | bytes 2097152 | tf_op jit(solution)/shard_map/all_to_all | solution.py:26
  144.2 1.6 copy-start.1
  160.7 19.4 %all-to-all-start.4 = ((bf16[32,2,256]{2,1,0:T(2,128)(2,1)}), bf16[32,2,256]{2,1,0:T(2,128)(2,1)S(1)}, u32[]{:S(2)}, u32[]{:S(2)}) async-start(bf16[32,2,256]{2,1,0:T(2,128)(2,1)} %reshape.419), calls=%async_computation.4 | async-start | bytes 65536 | tf_op jit(solution)/shard_map/all_to_all | solution.py:189
Sparse Core Ops, SparseCore 0:
  49.1 88.3 all-gather.1

commit v17 on v14

--- a/solution.py
+++ b/solution.py
@@ -18,6 +18,15 @@
     centred = values - mean
     spread = jnp.mean(centred * centred, axis=-1, keepdims=True)
     return centred * lax.rsqrt(spread + layer_eps) * gain + bias
+
+
+def normalize_shifted(values, gain, bias):
+    shift = values[:, :1]
+    moved = values - shift
+    first = jnp.mean(moved, axis=-1, keepdims=True)
+    second = jnp.mean(moved * moved, axis=-1, keepdims=True)
+    spread = jnp.maximum(second - first * first, 0.0)
+    return (moved - first) * lax.rsqrt(spread + layer_eps) * gain + bias
 
 
 def a2a_gather(value, axis):
@@ -91,7 +100,7 @@
 
     heads = vis_qkv.shape[2] // HD
     patches_f = patches.astype(jnp.float32)
-    normed = normalize(patches_f, vis_gain, vis_bias).astype(jnp.bfloat16)
+    normed = normalize_shifted(patches_f, vis_gain, vis_bias).astype(jnp.bfloat16)
     proj = jnp.einsum("pd,sde->spe", normed, vis_qkv, preferred_element_type=jnp.float32).astype(
         jnp.bfloat16
     )

time: 185 us -> 184 us (level)
    reduce_sum x3 -> x2, other arithmetic: 2.53 us -> 0.5 us  [normalize(): spread = jnp.mean(centred * centred, axis=-1, keepdims=True)]
where the time goes in v17:
time: 184 us; the launch traced here: 183 us
  waiting for transfers between devices  60.1 us (33%)
  starting transfers between devices  40.2 us (22%)
  matrix products  26.2 us (14%)
  local copies, waits for them, and re-layouts  14.4 us (8%)
  other arithmetic  14.1 us (8%)
  between operations  13.9 us (8%)
  blocking collectives  13.6 us (7%)
    all_to_all x3, waiting for transfers between devices, a2a_gather(): got = lax.all_to_all(spread, axis, 0, 0, tiled=True)  26.1 us
    all_to_all x1, waiting for transfers between devices, a2a_sum(): got = lax.all_to_all(parts, axis, 0, 0, tiled=True)  22.2 us
    all_to_all x3, starting transfers between devices, a2a_gather(): got = lax.all_to_all(spread, axis, 0, 0, tiled=True)  14.5 us
    all_to_all x1, blocking collectives, a2a_sum(): got = lax.all_to_all(parts, axis, 0, 0, tiled=True)  13.6 us
    all_to_all x1, starting transfers between devices, a2a_sum(): got = lax.all_to_all(parts, axis, 0, 0, tiled=True)  10.3 us
    all_to_all x1, waiting for transfers between devices, body(): got = lax.all_to_all(packed, GRP, 0, 0, tiled=True)  7.83 us
    all_to_all x1, starting transfers between devices, body(): got = lax.all_to_all(packed, GRP, 0, 0, tiled=True)  7.36 us
    dot_general x3, matrix products, attend_part(): jnp.dot(query, keys.T, preferred_element_type=jnp.float32) * DH ** (-0.5)  6.41 us
  transfers between devices with their start and end apart: 9, of which 7 were waited for; matrix products, arithmetic and copies ran while one was open for 22% of the time, Pallas kernels for 0%

profile of v17, /device:TPU:6, one launch (start us, length us, event | category | flops | bytes accessed | tf_op | source)
XLA Modules:
  0.0 182.6 jit_solution(12911014576404263719)
XLA Ops:
  6.5 3.7 %collective-permute-start.1 = (s32[512]{0:T(512)}, s32[512]{0:T(512)S(1)}, u32[]{:S(2)}, u32[]{:S(2)}) collective-permute-start(s32[512]{0:T(512)} %param.15), channel_id=1, source_target_pairs={{0,16},{16,0},{32,48},{48,32},{64,80},{80,64},{96,112},{112,96},{1... | collective-permute-start | bytes 6152 | tf_op jit(solution)/shard_map/ppermute | solution.py:109
  10.3 1.7 convert_element_type.142
  12.1 0.7 subtract_reduce_fusion
  12.9 1.2 fusion.13
  14.8 2.3 %collective-permute-start = (bf16[2,512,104]{1,2,0:T(8,128)(2,1)}, bf16[2,512,104]{1,2,0:T(8,128)(2,1)}, u32[]{:S(2)}, u32[]{:S(2)}) collective-permute-start(bf16[2,512,104]{1,2,0:T(8,128)(2,1)} %slice.117), channel_id=1, source_target_pairs={{0,16},{16,0},{32,48},{48,32},{64,80},{80,64},{96,112},{112,96},{1... | collective-permute-start | bytes 638984 | tf_op jit(solution)/shard_map/ppermute | solution.py:109
  17.2 1.8 %reshape.408 = bf16[104,8,2,104]{3,2,1,0:T(2,128)(2,1)S(1)} reshape(bf16[104,1664]{1,0:T(8,128)(2,1)} %param.19) | data formatting | bytes 692224 | tf_op jit(solution)/shard_map/reshape | solution.py:130
  19.0 1.8 constant_dynamic-slice_fusion.2
  20.8 1.9 %copy.60 = bf16[104,8,1,104]{0,3,1,2:T(8,128)(2,1)} copy(bf16[104,8,1,104]{3,2,1,0:T(2,128)(2,1)} %get-tuple-element.33) | data formatting | bytes 346112
  22.7 1.0 collective-permute-done
  23.7 1.5 fusion.6
  26.0 1.9 %fusion.19 = bf16[512,104,1]{0,1,2:T(8,128)(2,1)S(1)} fusion(f32[512,1024]{1,0:T(8,128)S(1)} %get-tuple-element.49, f32[512]{0:T(512)S(1)} %fusion.14, f32[512]{0:T(512)S(1)} %get-tuple-element.48, s32[1024]{0:T(1024)S(1)} %pad_add_fusion, s32[512]{0:T(512)S(1)} %copy-done.6, bf16[2,512,104]{1,2,0:T(8,128)(2,1)} %slice.117, ...), kind=kOutput, calls=%fused_computation.47 | convolution fusion | flops 112676864 | bytes 2639872 | tf_op jit(solution)/shard_map/hpk,khe->phe/dot_general | solution.py:121
  27.9 1.3 convolution_convert_fusion
  29.2 1.9 %collective-permute-start.2 = (bf16[8,104,512]{2,1,0:T(8,128)(2,1)}, bf16[8,104,512]{2,1,0:T(8,128)(2,1)}, u32[]{:S(2)}, u32[]{:S(2)}) collective-permute-start(bf16[8,104,512]{2,1,0:T(8,128)(2,1)} %convolution_convert_fusion), channel_id=1, source_target_pairs={{0,1},{1,0},{2,3},{3,2},{4,5},{5,4},{6,7},{7,6},{8,9},{9,8},{10,11... | collective-permute-start | bytes 2555912 | tf_op jit(solution)/shard_map/ppermute | solution.py:138
  31.3 1.3 copy.59
  32.9 0.9 collective-permute-done.2
  33.8 2.5 %add_convert_fusion.1 = bf16[8,104,512]{2,1,0:T(8,128)(2,1)} fusion(bf16[8,104,512]{2,1,0:T(8,128)(2,1)} %collective-permute-done.2, bf16[512,104,1]{0,1,2:T(8,128)(2,1)} %copy-done.5, bf16[104,8,1,104]{0,3,1,2:T(8,128)(2,1)S(1)} %copy.59), kind=kOutput, calls=%fused_computation.34 | convolution fusion | flops 90734592 | bytes 1983488 | tf_op jit(solution)/shard_map/pe,ezf->zfp/dot_general | solution.py:133
  36.3 10.3 %all-to-all-start = ((bf16[8,104,512]{2,1,0:T(8,128)(2,1)}), bf16[8,104,512]{2,1,0:T(8,128)(2,1)}, u32[]{:S(2)}, u32[]{:S(2)}) async-start(bf16[8,104,512]{2,1,0:T(8,128)(2,1)} %add_convert_fusion.1), calls=%async_computation | async-start | bytes 1703936 | tf_op jit(solution)/shard_map/all_to_all | solution.py:44
  46.8 1.5 fusion.37
  48.3 0.7 copy.49
  49.3 22.2 %all-to-all-done = bf16[8,104,512]{2,1,0:T(8,128)(2,1)} async-done(((bf16[8,104,512]{2,1,0:T(8,128)(2,1)}), bf16[8,104,512]{2,1,0:T(8,128)(2,1)}, u32[]{:S(2)}, u32[]{:S(2)}) %all-to-all-start) | async-done | bytes 852000 | tf_op jit(solution)/shard_map/all_to_all | solution.py:44
  71.5 1.3 convert_reduce_fusion.5
  73.0 1.5 fusion.18
  74.5 13.6 %all_to_all.37 = bf16[16,8,1024]{2,1,0:T(8,128)(2,1)S(1)} all-to-all(bf16[16,8,1024]{2,1,0:T(8,128)(2,1)S(1)} %fusion.18), channel_id=1, replica_groups=mesh['gx'=4,'gy'=8,'z'=8,'core'=2] {'z','core'}, dimensions={0} | all-to-all | bytes 524288 | tf_op jit(solution)/shard_map/all_to_all | solution.py:44
  88.2 0.7 broadcast_in_dim.68
  88.9 3.5 %all-to-all-start.2 = ((bf16[16,8,1024]{2,1,0:T(8,128)(2,1)}), bf16[16,8,1024]{2,1,0:T(8,128)(2,1)S(1)}, u32[]{:S(2)}, u32[]{:S(2)}) async-start(bf16[16,8,1024]{2,1,0:T(8,128)(2,1)} %broadcast_in_dim.68), calls=%async_computation.2 | async-start | bytes 524288 | tf_op jit(solution)/shard_map/all_to_all | solution.py:35
  92.6 11.2 %all-to-all-done.2 = bf16[16,8,1024]{2,1,0:T(8,128)(2,1)S(1)} async-done(((bf16[16,8,1024]{2,1,0:T(8,128)(2,1)}), bf16[16,8,1024]{2,1,0:T(8,128)(2,1)S(1)}, u32[]{:S(2)}, u32[]{:S(2)}) %all-to-all-start.2) | async-done | bytes 262176 | tf_op jit(solution)/shard_map/all_to_all | solution.py:35
  104.3 1.4 fusion.47
  105.9 0.8 broadcast_in_dim.72
  106.6 6.2 %all-to-all-start.3 = ((bf16[8,128,128]{2,1,0:T(8,128)(2,1)}), bf16[8,128,128]{2,1,0:T(8,128)(2,1)S(1)}, u32[]{:S(2)}, u32[]{:S(2)}) async-start(bf16[8,128,128]{2,1,0:T(8,128)(2,1)} %broadcast_in_dim.72), calls=%async_computation.3 | async-start | bytes 524288 | tf_op jit(solution)/shard_map/all_to_all | solution.py:35
  113.2 14.8 %all-to-all-done.3 = bf16[8,128,128]{2,1,0:T(8,128)(2,1)S(1)} async-done(((bf16[8,128,128]{2,1,0:T(8,128)(2,1)}), bf16[8,128,128]{2,1,0:T(8,128)(2,1)S(1)}, u32[]{:S(2)}, u32[]{:S(2)}) %all-to-all-start.3) | async-done | bytes 262176 | tf_op jit(solution)/shard_map/all_to_all | solution.py:35
  128.1 1.1 broadcast_in_dim.74
  129.2 4.8 %all-to-all-start.4 = ((bf16[4,1024,128]{2,1,0:T(8,128)(2,1)}), bf16[4,1024,128]{2,1,0:T(8,128)(2,1)S(1)}, u32[]{:S(2)}, u32[]{:S(2)}) async-start(bf16[4,1024,128]{2,1,0:T(8,128)(2,1)} %broadcast_in_dim.74), calls=%async_computation.4 | async-start | bytes 2097152 | tf_op jit(solution)/shard_map/all_to_all | solution.py:35
  134.0 2.0 %all-gather.2.cloned.1.call-done = bf16[8448,128]{1,0:T(8,128)(2,1)} async-done(((bf16[264,128]{1,0:T(8,128)(2,1)}), bf16[8448,128]{1,0:T(8,128)(2,1)}) %all-gather.2.cloned.1.call-update) | async-done | bytes 2162704 | tf_op jit(solution)/shard_map/all_gather | solution.py:89
  136.0 0.8 slice.110
  136.9 0.8 convert_reduce_fusion.2
  139.9 2.7 %fusion.4 = (f32[128]{0:T(128)S(1)}, f32[128,8448]{1,0:T(8,128)S(1)}) fusion(s32[8448]{0:T(1024)S(1)} %fusion.84, s32[128]{0:T(128)S(1)} %get-tuple-element.44, bf16[8448,128]{1,0:T(8,128)(2,1)} %all-gather.2.cloned.1.call-done, bf16[3,128,64]{1,2,0:T(8,128)(2,1)S(1)} %convert_bitcast_fusion.3), kind=kOutput, calls=%fused_computation.16 | convolution fusion | flops 142737280 | bytes 6542336 | tf_op jit(solution)/shard_map/dot_general | solution.py:49
  142.7 1.2 convert_reduce_fusion.3
  144.3 2.1 %fusion = (f32[256]{0:T(256)S(1)}, f32[256,8448]{1,0:T(8,128)S(1)}) fusion(s32[8448]{0:T(1024)S(1)} %fusion.84, s32[256]{0:T(256)S(1)} %add_add_fusion, bf16[8448,128]{1,0:T(8,128)(2,1)S(1)} %copy-done.1, bf16[3,256,64]{1,2,0:T(8,128)(2,1)S(1)} %convert_bitcast_fusion.2), kind=kOutput, calls=%fused_computation.4 | convolution fusion | flops 285474560 | bytes 10885120 | tf_op jit(solution)/shard_map/dot_general | solution.py:49
  146.4 2.7 %convert_reduce_fusion = (f32[256]{0:T(256)S(1)}, bf16[256,8448]{1,0:T(8,128)(2,1)S(1)}) fusion(f32[256,8448]{1,0:T(8,128)S(1)} %get-tuple-element.55, f32[256]{0:T(256)S(1)} %get-tuple-element.54, s32[256]{0:T(256)S(1)} %add_add_fusion, s32[8448]{0:T(1024)S(1)} %fusion.84), kind=kLoop, calls=%fused_computation.6 | loop fusion | flops 12975872 | bytes 13012992 | tf_op jit(solution)/shard_map/reduce_sum | solution.py:52
  149.1 2.0 %fusion.7 = f32[128,64]{0,1:T(8,128)S(1)} fusion(bf16[128,8448]{1,0:T(8,128)(2,1)S(1)} %get-tuple-element.27, bf16[8448,128]{1,0:T(8,128)(2,1)S(1)} %copy-done.1), kind=kOutput, calls=%fused_computation.27 | convolution fusion | flops 138412032 | bytes 4358144 | tf_op jit(solution)/shard_map/dot_general | solution.py:53
  151.1 2.5 %fusion.9 = f32[256,64]{0,1:T(8,128)S(1)} fusion(bf16[256,8448]{1,0:T(8,128)(2,1)S(1)} %get-tuple-element.25, bf16[8448,128]{1,0:T(8,128)(2,1)S(1)} %copy-done.1), kind=kOutput, calls=%fused_computation.29 | convolution fusion | flops 276824064 | bytes 6553600 | tf_op jit(solution)/shard_map/dot_general | solution.py:53
  153.5 1.6 fusion.2
  155.1 1.5 convert_reduce_fusion.1
  156.6 1.5 fusion.23
  158.4 0.7 reshape.429
  159.2 7.4 %all-to-all-start.5 = ((bf16[32,2,256]{2,1,0:T(2,128)(2,1)}), bf16[32,2,256]{2,1,0:T(2,128)(2,1)S(1)}, u32[]{:S(2)}, u32[]{:S(2)}) async-start(bf16[32,2,256]{2,1,0:T(2,128)(2,1)} %reshape.429), calls=%async_computation.5 | async-start | bytes 65536 | tf_op jit(solution)/shard_map/all_to_all | solution.py:198
  166.7 7.8 %all-to-all-done.5 = bf16[32,2,256]{2,1,0:T(2,128)(2,1)S(1)} async-done(((bf16[32,2,256]{2,1,0:T(2,128)(2,1)}), bf16[32,2,256]{2,1,0:T(2,128)(2,1)S(1)}, u32[]{:S(2)}, u32[]{:S(2)}) %all-to-all-start.5) | async-done | bytes 32800 | tf_op jit(solution)/shard_map/all_to_all | solution.py:198
  174.9 0.8 fusion.22
  (92 shorter events, 7.3 us)
Async XLA Ops:
  6.5 6.3 %copy-start = (bf16[3,1664,104]{1,2,0:T(8,128)(2,1)S(1)}, bf16[3,1664,104]{1,2,0:T(8,128)(2,1)}, u32[]{:S(2)}) copy-start(bf16[3,1664,104]{1,2,0:T(8,128)(2,1)} %param.18) | copy-start | bytes 3115012
  6.5 5.6 %copy-start.2 = (bf16[512,1664]{1,0:T(8,128)(2,1)S(1)}, bf16[512,1664]{1,0:T(8,128)(2,1)}, u32[]{:S(2)}) copy-start(bf16[512,1664]{1,0:T(8,128)(2,1)} %param.14) | copy-start | bytes 5111812
  6.5 6.3 %copy-start.8 = (f32[1664]{0:T(1024)S(1)}, f32[1664]{0:T(1024)}, u32[]{:S(2)}) copy-start(f32[1664]{0:T(1024)} %param.17) | copy-start | bytes 19972
  6.5 6.3 %copy-start.9 = (f32[1664]{0:T(1024)S(1)}, f32[1664]{0:T(1024)}, u32[]{:S(2)}) copy-start(f32[1664]{0:T(1024)} %param.16) | copy-start | bytes 19972
  6.5 16.1 %collective-permute-start.1 = (s32[512]{0:T(512)}, s32[512]{0:T(512)S(1)}, u32[]{:S(2)}, u32[]{:S(2)}) collective-permute-start(s32[512]{0:T(512)} %param.15), channel_id=1, source_target_pairs={{0,16},{16,0},{32,48},{48,32},{64,80},{80,64},{96,112},{112,96},{1... | collective-permute-start | bytes 6152 | tf_op jit(solution)/shard_map/ppermute | solution.py:109
  14.1 8.6 %copy-start.6 = (s32[512]{0:T(512)S(1)}, s32[512]{0:T(512)}, u32[]{:S(2)}) copy-start(s32[512]{0:T(512)} %param.15) | copy-start | bytes 6148
  14.8 8.9 %collective-permute-start = (bf16[2,512,104]{1,2,0:T(8,128)(2,1)}, bf16[2,512,104]{1,2,0:T(8,128)(2,1)}, u32[]{:S(2)}, u32[]{:S(2)}) collective-permute-start(bf16[2,512,104]{1,2,0:T(8,128)(2,1)} %slice.117), channel_id=1, source_target_pairs={{0,16},{16,0},{32,48},{48,32},{64,80},{80,64},{96,112},{112,96},{1... | collective-permute-start | bytes 638984 | tf_op jit(solution)/shard_map/ppermute | solution.py:109
  26.0 1.9 %copy-start.4 = (bf16[104,8,1,104]{0,3,1,2:T(8,128)(2,1)S(1)}, bf16[104,8,1,104]{0,3,1,2:T(8,128)(2,1)}, u32[]{:S(2)}) copy-start(bf16[104,8,1,104]{0,3,1,2:T(8,128)(2,1)} %copy.60) | copy-start | bytes 519172
  26.0 5.1 %copy-start.3 = (bf16[256,1024]{1,0:T(8,128)(2,1)S(1)}, bf16[256,1024]{1,0:T(8,128)(2,1)}, u32[]{:S(2)}) copy-start(bf16[256,1024]{1,0:T(8,128)(2,1)} %param.22) | copy-start | bytes 1572868
  26.0 6.8 %copy-start.7 = (s32[128]{0:T(128)S(1)}, s32[128]{0:T(128)}, u32[]{:S(2)}) copy-start(s32[128]{0:T(128)} %param.21) | copy-start | bytes 1540
  27.9 3.4 %copy-start.5 = (bf16[512,104,1]{0,1,2:T(8,128)(2,1)}, bf16[512,104,1]{0,1,2:T(8,128)(2,1)S(1)}, u32[]{:S(2)}) copy-start(bf16[512,104,1]{0,1,2:T(8,128)(2,1)S(1)} %fusion.19) | copy-start | bytes 319492
  27.9 18.9 %copy-start.10 = (f32[1024]{0:T(1024)S(1)}, f32[1024]{0:T(1024)}, u32[]{:S(2)}) copy-start(f32[1024]{0:T(1024)} %param.24) | copy-start | bytes 12292
  27.9 18.9 %copy-start.11 = (f32[1024]{0:T(1024)S(1)}, f32[1024]{0:T(1024)}, u32[]{:S(2)}) copy-start(f32[1024]{0:T(1024)} %param.23) | copy-start | bytes 12292
  29.2 4.6 %collective-permute-start.2 = (bf16[8,104,512]{2,1,0:T(8,128)(2,1)}, bf16[8,104,512]{2,1,0:T(8,128)(2,1)}, u32[]{:S(2)}, u32[]{:S(2)}) collective-permute-start(bf16[8,104,512]{2,1,0:T(8,128)(2,1)} %convolution_convert_fusion), channel_id=1, source_target_pairs={{0,1},{1,0},{2,3},{3,2},{4,5},{5,4},{6,7},{7,6},{8,9},{9,8},{10,11... | collective-permute-start | bytes 2555912 | tf_op jit(solution)/shard_map/ppermute | solution.py:138
  36.3 35.3 %all-to-all-start = ((bf16[8,104,512]{2,1,0:T(8,128)(2,1)}), bf16[8,104,512]{2,1,0:T(8,128)(2,1)}, u32[]{:S(2)}, u32[]{:S(2)}) async-start(bf16[8,104,512]{2,1,0:T(8,128)(2,1)} %add_convert_fusion.1), calls=%async_computation | async-start | bytes 1703936 | tf_op jit(solution)/shard_map/all_to_all | solution.py:44
  46.6 89.4 %all-gather.2.cloned.1.call-start = ((), (), s32[]{:S(2)}) async-start(), calls=%async_computation.6 | async-start | bytes 2230272 | tf_op jit(solution)/shard_map/all_gather | solution.py:89
  88.9 14.9 %all-to-all-start.2 = ((bf16[16,8,1024]{2,1,0:T(8,128)(2,1)}), bf16[16,8,1024]{2,1,0:T(8,128)(2,1)S(1)}, u32[]{:S(2)}, u32[]{:S(2)}) async-start(bf16[16,8,1024]{2,1,0:T(8,128)(2,1)} %broadcast_in_dim.68), calls=%async_computation.2 | async-start | bytes 524288 | tf_op jit(solution)/shard_map/all_to_all | solution.py:35
  106.6 21.4 %all-to-all-start.3 = ((bf16[8,128,128]{2,1,0:T(8,128)(2,1)}), bf16[8,128,128]{2,1,0:T(8,128)(2,1)S(1)}, u32[]{:S(2)}, u32[]{:S(2)}) async-start(bf16[8,128,128]{2,1,0:T(8,128)(2,1)} %broadcast_in_dim.72), calls=%async_computation.3 | async-start | bytes 524288 | tf_op jit(solution)/shard_map/all_to_all | solution.py:35
  129.2 24.3 %all-to-all-start.4 = ((bf16[4,1024,128]{2,1,0:T(8,128)(2,1)}), bf16[4,1024,128]{2,1,0:T(8,128)(2,1)S(1)}, u32[]{:S(2)}, u32[]{:S(2)}) async-start(bf16[4,1024,128]{2,1,0:T(8,128)(2,1)} %broadcast_in_dim.74), calls=%async_computation.4 | async-start | bytes 2097152 | tf_op jit(solution)/shard_map/all_to_all | solution.py:35
  142.7 1.6 copy-start.1
  159.2 15.4 %all-to-all-start.5 = ((bf16[32,2,256]{2,1,0:T(2,128)(2,1)}), bf16[32,2,256]{2,1,0:T(2,128)(2,1)S(1)}, u32[]{:S(2)}, u32[]{:S(2)}) async-start(bf16[32,2,256]{2,1,0:T(2,128)(2,1)} %reshape.429), calls=%async_computation.5 | async-start | bytes 65536 | tf_op jit(solution)/shard_map/all_to_all | solution.py:198
Sparse Core Ops, SparseCore 0:
  50.6 85.2 all-gather.1

commit v18 on v17

--- a/solution.py
+++ b/solution.py
@@ -149,7 +149,7 @@
         a2a_sum(partial_rows.reshape(ntp, merged_count // ntp, -1), TP).astype(jnp.bfloat16), TP
     )
 
-    mnorm = normalize(merged.astype(jnp.float32), dec_gain, dec_bias).astype(jnp.bfloat16)
+    mnorm = normalize_shifted(merged.astype(jnp.float32), dec_gain, dec_bias).astype(jnp.bfloat16)
     mproj = jnp.einsum("td,sde->ste", mnorm, dec_qkv, preferred_element_type=jnp.float32).astype(
         jnp.bfloat16
     )

time: 184 us -> 184 us (level)
    unnamed x29 -> x31, local copies, waits for them, and re-layouts: 4.51 us -> 4.51 us
  transfers between devices with their start and end apart: 9 -> 9, of which waited for: 7 -> 7; matrix products, arithmetic and copies ran while one was open for 22% -> 21% of each run, Pallas kernels for 0% -> 0%
where the time goes in v18:
time: 184 us; the launch traced here: 183 us
  waiting for transfers between devices  60.5 us (33%)
  starting transfers between devices  40.7 us (22%)
  matrix products  25.2 us (14%)
  local copies, waits for them, and re-layouts  14.5 us (8%)
  other arithmetic  14 us (8%)
  between operations  14 us (8%)
  blocking collectives  13.6 us (7%)
    all_to_all x3, waiting for transfers between devices, a2a_gather(): got = lax.all_to_all(spread, axis, 0, 0, tiled=True)  25.9 us
    all_to_all x1, waiting for transfers between devices, a2a_sum(): got = lax.all_to_all(parts, axis, 0, 0, tiled=True)  22 us
    all_to_all x3, starting transfers between devices, a2a_gather(): got = lax.all_to_all(spread, axis, 0, 0, tiled=True)  14.6 us
    all_to_all x1, blocking collectives, a2a_sum(): got = lax.all_to_all(parts, axis, 0, 0, tiled=True)  13.6 us
    all_to_all x1, starting transfers between devices, a2a_sum(): got = lax.all_to_all(parts, axis, 0, 0, tiled=True)  10.3 us
    all_to_all x1, waiting for transfers between devices, body(): got = lax.all_to_all(packed, GRP, 0, 0, tiled=True)  7.83 us
    all_to_all x1, starting transfers between devices, body(): got = lax.all_to_all(packed, GRP, 0, 0, tiled=True)  7.74 us
    dot_general x3, matrix products, attend_part(): jnp.dot(query, keys.T, preferred_element_type=jnp.float32) * DH ** (-0.5)  6.42 us
  transfers between devices with their start and end apart: 9, of which 7 were waited for; matrix products, arithmetic and copies ran while one was open for 21% of the time, Pallas kernels for 0%

profile of v18, /device:TPU:6, one launch (start us, length us, event | category | flops | bytes accessed | tf_op | source)
XLA Modules:
  0.0 182.6 jit_solution(16507496278063242355)
XLA Ops:
  6.5 3.7 %collective-permute-start.1 = (s32[512]{0:T(512)}, s32[512]{0:T(512)S(1)}, u32[]{:S(2)}, u32[]{:S(2)}) collective-permute-start(s32[512]{0:T(512)} %param.15), channel_id=1, source_target_pairs={{0,16},{16,0},{32,48},{48,32},{64,80},{80,64},{96,112},{112,96},{1... | collective-permute-start | bytes 6152 | tf_op jit(solution)/shard_map/ppermute | solution.py:109
  10.3 1.7 convert_element_type.142
  12.1 0.7 subtract_reduce_fusion
  12.9 1.2 fusion.13
  14.1 0.7 slice.121
  14.8 2.3 %collective-permute-start = (bf16[2,512,104]{1,2,0:T(8,128)(2,1)}, bf16[2,512,104]{1,2,0:T(8,128)(2,1)}, u32[]{:S(2)}, u32[]{:S(2)}) collective-permute-start(bf16[2,512,104]{1,2,0:T(8,128)(2,1)} %slice.121), channel_id=1, source_target_pairs={{0,16},{16,0},{32,48},{48,32},{64,80},{80,64},{96,112},{112,96},{1... | collective-permute-start | bytes 638984 | tf_op jit(solution)/shard_map/ppermute | solution.py:109
  17.2 1.8 %reshape.420 = bf16[104,8,2,104]{3,2,1,0:T(2,128)(2,1)S(1)} reshape(bf16[104,1664]{1,0:T(8,128)(2,1)} %param.19) | data formatting | bytes 692224 | tf_op jit(solution)/shard_map/reshape | solution.py:130
  19.0 1.8 constant_dynamic-slice_fusion.2
  20.8 1.9 %copy.70 = bf16[104,8,1,104]{0,3,1,2:T(8,128)(2,1)} copy(bf16[104,8,1,104]{3,2,1,0:T(2,128)(2,1)} %get-tuple-element.35) | data formatting | bytes 346112
  22.7 1.0 collective-permute-done
  23.7 1.5 fusion.6
  26.0 1.9 %fusion.19 = bf16[512,104,1]{0,1,2:T(8,128)(2,1)S(1)} fusion(f32[512,1024]{1,0:T(8,128)S(1)} %get-tuple-element.51, f32[512]{0:T(512)S(1)} %fusion.14, f32[512]{0:T(512)S(1)} %get-tuple-element.50, s32[1024]{0:T(1024)S(1)} %pad_add_fusion, s32[512]{0:T(512)S(1)} %copy-done.6, bf16[2,512,104]{1,2,0:T(8,128)(2,1)} %slice.121, ...), kind=kOutput, calls=%fused_computation.47 | convolution fusion | flops 112676864 | bytes 2639872 | tf_op jit(solution)/shard_map/hpk,khe->phe/dot_general | solution.py:121
  27.9 1.3 convolution_convert_fusion
  29.2 1.9 %collective-permute-start.2 = (bf16[8,104,512]{2,1,0:T(8,128)(2,1)}, bf16[8,104,512]{2,1,0:T(8,128)(2,1)}, u32[]{:S(2)}, u32[]{:S(2)}) collective-permute-start(bf16[8,104,512]{2,1,0:T(8,128)(2,1)} %convolution_convert_fusion), channel_id=1, source_target_pairs={{0,1},{1,0},{2,3},{3,2},{4,5},{5,4},{6,7},{7,6},{8,9},{9,8},{10,11... | collective-permute-start | bytes 2555912 | tf_op jit(solution)/shard_map/ppermute | solution.py:138
  31.3 1.2 copy.69
  32.7 1.1 collective-permute-done.2
  33.8 2.5 %add_convert_fusion.1 = bf16[8,104,512]{2,1,0:T(8,128)(2,1)} fusion(bf16[8,104,512]{2,1,0:T(8,128)(2,1)} %collective-permute-done.2, bf16[512,104,1]{0,1,2:T(8,128)(2,1)} %copy-done.5, bf16[104,8,1,104]{0,3,1,2:T(8,128)(2,1)S(1)} %copy.69), kind=kOutput, calls=%fused_computation.34 | convolution fusion | flops 90734592 | bytes 1983488 | tf_op jit(solution)/shard_map/pe,ezf->zfp/dot_general | solution.py:133
  36.3 10.3 %all-to-all-start = ((bf16[8,104,512]{2,1,0:T(8,128)(2,1)}), bf16[8,104,512]{2,1,0:T(8,128)(2,1)}, u32[]{:S(2)}, u32[]{:S(2)}) async-start(bf16[8,104,512]{2,1,0:T(8,128)(2,1)} %add_convert_fusion.1), calls=%async_computation | async-start | bytes 1703936 | tf_op jit(solution)/shard_map/all_to_all | solution.py:44
  47.0 1.5 fusion.33
  48.5 0.7 copy.59
  49.5 22.0 %all-to-all-done = bf16[8,104,512]{2,1,0:T(8,128)(2,1)} async-done(((bf16[8,104,512]{2,1,0:T(8,128)(2,1)}), bf16[8,104,512]{2,1,0:T(8,128)(2,1)}, u32[]{:S(2)}, u32[]{:S(2)}) %all-to-all-start) | async-done | bytes 852000 | tf_op jit(solution)/shard_map/all_to_all | solution.py:44
  71.5 1.3 convert_reduce_fusion.5
  73.0 1.5 fusion.18
  74.5 13.6 %all_to_all.37 = bf16[16,8,1024]{2,1,0:T(8,128)(2,1)S(1)} all-to-all(bf16[16,8,1024]{2,1,0:T(8,128)(2,1)S(1)} %fusion.18), channel_id=1, replica_groups=mesh['gx'=4,'gy'=8,'z'=8,'core'=2] {'z','core'}, dimensions={0} | all-to-all | bytes 524288 | tf_op jit(solution)/shard_map/all_to_all | solution.py:44
  88.2 0.7 broadcast_in_dim.68
  88.9 3.5 %all-to-all-start.2 = ((bf16[16,8,1024]{2,1,0:T(8,128)(2,1)}), bf16[16,8,1024]{2,1,0:T(8,128)(2,1)S(1)}, u32[]{:S(2)}, u32[]{:S(2)}) async-start(bf16[16,8,1024]{2,1,0:T(8,128)(2,1)} %broadcast_in_dim.68), calls=%async_computation.2 | async-start | bytes 524288 | tf_op jit(solution)/shard_map/all_to_all | solution.py:35
  92.6 11.2 %all-to-all-done.2 = bf16[16,8,1024]{2,1,0:T(8,128)(2,1)S(1)} async-done(((bf16[16,8,1024]{2,1,0:T(8,128)(2,1)}), bf16[16,8,1024]{2,1,0:T(8,128)(2,1)S(1)}, u32[]{:S(2)}, u32[]{:S(2)}) %all-to-all-start.2) | async-done | bytes 262176 | tf_op jit(solution)/shard_map/all_to_all | solution.py:35
  105.1 0.8 broadcast_in_dim.72
  105.8 6.2 %all-to-all-start.3 = ((bf16[8,128,128]{2,1,0:T(8,128)(2,1)}), bf16[8,128,128]{2,1,0:T(8,128)(2,1)S(1)}, u32[]{:S(2)}, u32[]{:S(2)}) async-start(bf16[8,128,128]{2,1,0:T(8,128)(2,1)} %broadcast_in_dim.72), calls=%async_computation.3 | async-start | bytes 524288 | tf_op jit(solution)/shard_map/all_to_all | solution.py:35
  112.4 14.6 %all-to-all-done.3 = bf16[8,128,128]{2,1,0:T(8,128)(2,1)S(1)} async-done(((bf16[8,128,128]{2,1,0:T(8,128)(2,1)}), bf16[8,128,128]{2,1,0:T(8,128)(2,1)S(1)}, u32[]{:S(2)}, u32[]{:S(2)}) %all-to-all-start.3) | async-done | bytes 262176 | tf_op jit(solution)/shard_map/all_to_all | solution.py:35
  127.0 1.1 broadcast_in_dim.74
  128.2 4.9 %all-to-all-start.4 = ((bf16[4,1024,128]{2,1,0:T(8,128)(2,1)}), bf16[4,1024,128]{2,1,0:T(8,128)(2,1)S(1)}, u32[]{:S(2)}, u32[]{:S(2)}) async-start(bf16[4,1024,128]{2,1,0:T(8,128)(2,1)} %broadcast_in_dim.74), calls=%async_computation.4 | async-start | bytes 2097152 | tf_op jit(solution)/shard_map/all_to_all | solution.py:35
  133.0 2.6 %all-gather.2.cloned.1.call-done = bf16[8448,128]{1,0:T(8,128)(2,1)} async-done(((bf16[264,128]{1,0:T(8,128)(2,1)}), bf16[8448,128]{1,0:T(8,128)(2,1)}) %all-gather.2.cloned.1.call-update) | async-done | bytes 2162704 | tf_op jit(solution)/shard_map/all_gather | solution.py:89
  135.6 0.8 slice.114
  136.6 0.8 convert_reduce_fusion.2
  139.6 2.7 %fusion.4 = (f32[128]{0:T(128)S(1)}, f32[128,8448]{1,0:T(8,128)S(1)}) fusion(s32[8448]{0:T(1024)S(1)} %fusion.80, s32[128]{0:T(128)S(1)} %get-tuple-element.46, bf16[8448,128]{1,0:T(8,128)(2,1)} %all-gather.2.cloned.1.call-done, bf16[3,128,64]{1,2,0:T(8,128)(2,1)S(1)} %convert_bitcast_fusion.4), kind=kOutput, calls=%fused_computation.16 | convolution fusion | flops 142737280 | bytes 6542336 | tf_op jit(solution)/shard_map/dot_general | solution.py:49
  142.4 1.2 convert_reduce_fusion.3
  144.0 2.1 %fusion = (f32[256]{0:T(256)S(1)}, f32[256,8448]{1,0:T(8,128)S(1)}) fusion(s32[8448]{0:T(1024)S(1)} %fusion.80, s32[256]{0:T(256)S(1)} %add_add_fusion, bf16[8448,128]{1,0:T(8,128)(2,1)S(1)} %copy-done.1, bf16[3,256,64]{1,2,0:T(8,128)(2,1)S(1)} %convert_bitcast_fusion.3), kind=kOutput, calls=%fused_computation.4 | convolution fusion | flops 285474560 | bytes 10885120 | tf_op jit(solution)/shard_map/dot_general | solution.py:49
  146.1 2.7 %convert_reduce_fusion = (f32[256]{0:T(256)S(1)}, bf16[256,8448]{1,0:T(8,128)(2,1)S(1)}) fusion(f32[256,8448]{1,0:T(8,128)S(1)} %get-tuple-element.57, f32[256]{0:T(256)S(1)} %get-tuple-element.56, s32[256]{0:T(256)S(1)} %add_add_fusion, s32[8448]{0:T(1024)S(1)} %fusion.80), kind=kLoop, calls=%fused_computation.6 | loop fusion | flops 12975872 | bytes 13012992 | tf_op jit(solution)/shard_map/reduce_sum | solution.py:52
  148.8 2.0 %fusion.7 = f32[128,64]{0,1:T(8,128)S(1)} fusion(bf16[128,8448]{1,0:T(8,128)(2,1)S(1)} %get-tuple-element.29, bf16[8448,128]{1,0:T(8,128)(2,1)S(1)} %copy-done.1), kind=kOutput, calls=%fused_computation.27 | convolution fusion | flops 138412032 | bytes 4358144 | tf_op jit(solution)/shard_map/dot_general | solution.py:53
  150.7 2.5 %fusion.9 = f32[256,64]{0,1:T(8,128)S(1)} fusion(bf16[256,8448]{1,0:T(8,128)(2,1)S(1)} %get-tuple-element.27, bf16[8448,128]{1,0:T(8,128)(2,1)S(1)} %copy-done.1), kind=kOutput, calls=%fused_computation.29 | convolution fusion | flops 276824064 | bytes 6553600 | tf_op jit(solution)/shard_map/dot_general | solution.py:53
  153.2 1.6 fusion.2
  154.8 1.5 convert_reduce_fusion.1
  156.3 1.5 fusion.23
  158.1 0.7 reshape.443
  158.8 7.7 %all-to-all-start.5 = ((bf16[32,2,256]{2,1,0:T(2,128)(2,1)}), bf16[32,2,256]{2,1,0:T(2,128)(2,1)S(1)}, u32[]{:S(2)}, u32[]{:S(2)}) async-start(bf16[32,2,256]{2,1,0:T(2,128)(2,1)} %reshape.443), calls=%async_computation.5 | async-start | bytes 65536 | tf_op jit(solution)/shard_map/all_to_all | solution.py:198
  166.8 7.8 %all-to-all-done.5 = bf16[32,2,256]{2,1,0:T(2,128)(2,1)S(1)} async-done(((bf16[32,2,256]{2,1,0:T(2,128)(2,1)}), bf16[32,2,256]{2,1,0:T(2,128)(2,1)S(1)}, u32[]{:S(2)}, u32[]{:S(2)}) %all-to-all-start.5) | async-done | bytes 32800 | tf_op jit(solution)/shard_map/all_to_all | solution.py:198
  175.0 0.8 fusion.22
  (96 shorter events, 7.2 us)
Async XLA Ops:
  6.5 6.3 %copy-start = (bf16[3,1664,104]{1,2,0:T(8,128)(2,1)S(1)}, bf16[3,1664,104]{1,2,0:T(8,128)(2,1)}, u32[]{:S(2)}) copy-start(bf16[3,1664,104]{1,2,0:T(8,128)(2,1)} %param.18) | copy-start | bytes 3115012
  6.5 5.6 %copy-start.2 = (bf16[512,1664]{1,0:T(8,128)(2,1)S(1)}, bf16[512,1664]{1,0:T(8,128)(2,1)}, u32[]{:S(2)}) copy-start(bf16[512,1664]{1,0:T(8,128)(2,1)} %param.14) | copy-start | bytes 5111812
  6.5 6.3 %copy-start.9 = (f32[1664]{0:T(1024)S(1)}, f32[1664]{0:T(1024)}, u32[]{:S(2)}) copy-start(f32[1664]{0:T(1024)} %param.17) | copy-start | bytes 19972
  6.5 6.3 %copy-start.10 = (f32[1664]{0:T(1024)S(1)}, f32[1664]{0:T(1024)}, u32[]{:S(2)}) copy-start(f32[1664]{0:T(1024)} %param.16) | copy-start | bytes 19972
  6.5 16.1 %collective-permute-start.1 = (s32[512]{0:T(512)}, s32[512]{0:T(512)S(1)}, u32[]{:S(2)}, u32[]{:S(2)}) collective-permute-start(s32[512]{0:T(512)} %param.15), channel_id=1, source_target_pairs={{0,16},{16,0},{32,48},{48,32},{64,80},{80,64},{96,112},{112,96},{1... | collective-permute-start | bytes 6152 | tf_op jit(solution)/shard_map/ppermute | solution.py:109
  14.1 8.6 %copy-start.6 = (s32[512]{0:T(512)S(1)}, s32[512]{0:T(512)}, u32[]{:S(2)}) copy-start(s32[512]{0:T(512)} %param.15) | copy-start | bytes 6148
  14.8 8.9 %collective-permute-start = (bf16[2,512,104]{1,2,0:T(8,128)(2,1)}, bf16[2,512,104]{1,2,0:T(8,128)(2,1)}, u32[]{:S(2)}, u32[]{:S(2)}) collective-permute-start(bf16[2,512,104]{1,2,0:T(8,128)(2,1)} %slice.121), channel_id=1, source_target_pairs={{0,16},{16,0},{32,48},{48,32},{64,80},{80,64},{96,112},{112,96},{1... | collective-permute-start | bytes 638984 | tf_op jit(solution)/shard_map/ppermute | solution.py:109
  26.0 1.9 %copy-start.4 = (bf16[104,8,1,104]{0,3,1,2:T(8,128)(2,1)S(1)}, bf16[104,8,1,104]{0,3,1,2:T(8,128)(2,1)}, u32[]{:S(2)}) copy-start(bf16[104,8,1,104]{0,3,1,2:T(8,128)(2,1)} %copy.70) | copy-start | bytes 519172
  26.0 5.1 %copy-start.7 = (s32[128]{0:T(128)S(1)}, s32[128]{0:T(128)}, u32[]{:S(2)}) copy-start(s32[128]{0:T(128)} %param.21) | copy-start | bytes 1540
  26.0 6.6 %copy-start.3 = (bf16[256,1024]{1,0:T(8,128)(2,1)S(1)}, bf16[256,1024]{1,0:T(8,128)(2,1)}, u32[]{:S(2)}) copy-start(bf16[256,1024]{1,0:T(8,128)(2,1)} %param.22) | copy-start | bytes 1572868
  27.9 1.3 copy-start.5
  27.9 19.1 %copy-start.11 = (f32[1024]{0:T(1024)S(1)}, f32[1024]{0:T(1024)}, u32[]{:S(2)}) copy-start(f32[1024]{0:T(1024)} %param.24) | copy-start | bytes 12292
  27.9 19.1 %copy-start.12 = (f32[1024]{0:T(1024)S(1)}, f32[1024]{0:T(1024)}, u32[]{:S(2)}) copy-start(f32[1024]{0:T(1024)} %param.23) | copy-start | bytes 12292
  29.2 4.6 %collective-permute-start.2 = (bf16[8,104,512]{2,1,0:T(8,128)(2,1)}, bf16[8,104,512]{2,1,0:T(8,128)(2,1)}, u32[]{:S(2)}, u32[]{:S(2)}) collective-permute-start(bf16[8,104,512]{2,1,0:T(8,128)(2,1)} %convolution_convert_fusion), channel_id=1, source_target_pairs={{0,1},{1,0},{2,3},{3,2},{4,5},{5,4},{6,7},{7,6},{8,9},{9,8},{10,11... | collective-permute-start | bytes 2555912 | tf_op jit(solution)/shard_map/ppermute | solution.py:138
  36.3 35.3 %all-to-all-start = ((bf16[8,104,512]{2,1,0:T(8,128)(2,1)}), bf16[8,104,512]{2,1,0:T(8,128)(2,1)}, u32[]{:S(2)}, u32[]{:S(2)}) async-start(bf16[8,104,512]{2,1,0:T(8,128)(2,1)} %add_convert_fusion.1), calls=%async_computation | async-start | bytes 1703936 | tf_op jit(solution)/shard_map/all_to_all | solution.py:44
  46.6 89.0 %all-gather.2.cloned.1.call-start = ((), (), s32[]{:S(2)}) async-start(), calls=%async_computation.6 | async-start | bytes 2230272 | tf_op jit(solution)/shard_map/all_gather | solution.py:89
  49.2 55.3 %copy-start.8 = (bf16[3,1024,64]{1,2,0:T(8,128)(2,1)S(1)}, bf16[3,1024,64]{1,2,0:T(8,128)(2,1)}, u32[]{:S(2)}) copy-start(bf16[3,1024,64]{1,2,0:T(8,128)(2,1)} %param.25) | copy-start | bytes 1179652
  88.9 14.9 %all-to-all-start.2 = ((bf16[16,8,1024]{2,1,0:T(8,128)(2,1)}), bf16[16,8,1024]{2,1,0:T(8,128)(2,1)S(1)}, u32[]{:S(2)}, u32[]{:S(2)}) async-start(bf16[16,8,1024]{2,1,0:T(8,128)(2,1)} %broadcast_in_dim.68), calls=%async_computation.2 | async-start | bytes 524288 | tf_op jit(solution)/shard_map/all_to_all | solution.py:35
  105.8 21.2 %all-to-all-start.3 = ((bf16[8,128,128]{2,1,0:T(8,128)(2,1)}), bf16[8,128,128]{2,1,0:T(8,128)(2,1)S(1)}, u32[]{:S(2)}, u32[]{:S(2)}) async-start(bf16[8,128,128]{2,1,0:T(8,128)(2,1)} %broadcast_in_dim.72), calls=%async_computation.3 | async-start | bytes 524288 | tf_op jit(solution)/shard_map/all_to_all | solution.py:35
  128.2 25.0 %all-to-all-start.4 = ((bf16[4,1024,128]{2,1,0:T(8,128)(2,1)}), bf16[4,1024,128]{2,1,0:T(8,128)(2,1)S(1)}, u32[]{:S(2)}, u32[]{:S(2)}) async-start(bf16[4,1024,128]{2,1,0:T(8,128)(2,1)} %broadcast_in_dim.74), calls=%async_computation.4 | async-start | bytes 2097152 | tf_op jit(solution)/shard_map/all_to_all | solution.py:35
  142.4 1.6 copy-start.1
  158.8 15.8 %all-to-all-start.5 = ((bf16[32,2,256]{2,1,0:T(2,128)(2,1)}), bf16[32,2,256]{2,1,0:T(2,128)(2,1)S(1)}, u32[]{:S(2)}, u32[]{:S(2)}) async-start(bf16[32,2,256]{2,1,0:T(2,128)(2,1)} %reshape.443), calls=%async_computation.5 | async-start | bytes 65536 | tf_op jit(solution)/shard_map/all_to_all | solution.py:198
Sparse Core Ops, SparseCore 0:
  50.6 84.9 all-gather.1

commit v19 on v18

--- a/solution.py
+++ b/solution.py
@@ -76,7 +76,7 @@
     tok = text_count + merged_count
     cap = merged_count // min(groups, 16)
 
-    tnorm = normalize(text.astype(jnp.float32), dec_gain, dec_bias).astype(jnp.bfloat16)
+    tnorm = normalize_shifted(text.astype(jnp.float32), dec_gain, dec_bias).astype(jnp.bfloat16)
     tproj = jnp.einsum("td,sde->ste", tnorm, dec_qkv, preferred_element_type=jnp.float32).astype(
         jnp.bfloat16
     )

time: 184 us -> 184 us (level)
  no operation moved by 1% of the time
where the time goes in v19:
time: 184 us; the launch traced here: 183 us
  waiting for transfers between devices  60.5 us (33%)
  starting transfers between devices  40.5 us (22%)
  matrix products  25.3 us (14%)
  local copies, waits for them, and re-layouts  14.7 us (8%)
  other arithmetic  14.1 us (8%)
  between operations  14 us (8%)
  blocking collectives  13.6 us (7%)
    all_to_all x3, waiting for transfers between devices, a2a_gather(): got = lax.all_to_all(spread, axis, 0, 0, tiled=True)  25.8 us
    all_to_all x1, waiting for transfers between devices, a2a_sum(): got = lax.all_to_all(parts, axis, 0, 0, tiled=True)  22 us
    all_to_all x3, starting transfers between devices, a2a_gather(): got = lax.all_to_all(spread, axis, 0, 0, tiled=True)  14.6 us
    all_to_all x1, blocking collectives, a2a_sum(): got = lax.all_to_all(parts, axis, 0, 0, tiled=True)  13.6 us
    all_to_all x1, starting transfers between devices, a2a_sum(): got = lax.all_to_all(parts, axis, 0, 0, tiled=True)  10.3 us
    all_to_all x1, waiting for transfers between devices, body(): got = lax.all_to_all(packed, GRP, 0, 0, tiled=True)  7.83 us
    all_to_all x1, starting transfers between devices, body(): got = lax.all_to_all(packed, GRP, 0, 0, tiled=True)  7.49 us
    dot_general x3, matrix products, attend_part(): jnp.dot(query, keys.T, preferred_element_type=jnp.float32) * DH ** (-0.5)  6.41 us
  transfers between devices with their start and end apart: 9, of which 7 were waited for; matrix products, arithmetic and copies ran while one was open for 21% of the time, Pallas kernels for 0%

profile of v19, /device:TPU:6, one launch (start us, length us, event | category | flops | bytes accessed | tf_op | source)
XLA Modules:
  0.0 182.6 jit_solution(13798144796747754634)
XLA Ops:
  6.5 3.7 %collective-permute-start.1 = (s32[512]{0:T(512)}, s32[512]{0:T(512)S(1)}, u32[]{:S(2)}, u32[]{:S(2)}) collective-permute-start(s32[512]{0:T(512)} %param.15), channel_id=1, source_target_pairs={{0,16},{16,0},{32,48},{48,32},{64,80},{80,64},{96,112},{112,96},{1... | collective-permute-start | bytes 6152 | tf_op jit(solution)/shard_map/ppermute | solution.py:109
  10.3 1.7 convert_element_type.142
  12.1 0.7 subtract_reduce_fusion
  12.9 1.2 fusion.13
  14.1 0.7 slice.126
  14.8 2.3 %collective-permute-start = (bf16[2,512,104]{1,2,0:T(8,128)(2,1)}, bf16[2,512,104]{1,2,0:T(8,128)(2,1)}, u32[]{:S(2)}, u32[]{:S(2)}) collective-permute-start(bf16[2,512,104]{1,2,0:T(8,128)(2,1)} %slice.126), channel_id=1, source_target_pairs={{0,16},{16,0},{32,48},{48,32},{64,80},{80,64},{96,112},{112,96},{1... | collective-permute-start | bytes 638984 | tf_op jit(solution)/shard_map/ppermute | solution.py:109
  17.2 1.8 %reshape.428 = bf16[104,8,2,104]{3,2,1,0:T(2,128)(2,1)S(1)} reshape(bf16[104,1664]{1,0:T(8,128)(2,1)} %param.19) | data formatting | bytes 692224 | tf_op jit(solution)/shard_map/reshape | solution.py:130
  19.0 1.8 constant_dynamic-slice_fusion.2
  20.8 1.9 %copy.70 = bf16[104,8,1,104]{0,3,1,2:T(8,128)(2,1)} copy(bf16[104,8,1,104]{3,2,1,0:T(2,128)(2,1)} %get-tuple-element.37) | data formatting | bytes 346112
  22.7 1.0 collective-permute-done
  23.7 1.5 fusion.6
  26.0 1.9 %fusion.17 = bf16[512,104,1]{0,1,2:T(8,128)(2,1)S(1)} fusion(f32[512,1024]{1,0:T(8,128)S(1)} %get-tuple-element.55, f32[512]{0:T(512)S(1)} %fusion.14, f32[512]{0:T(512)S(1)} %get-tuple-element.54, s32[1024]{0:T(1024)S(1)} %pad_add_fusion, s32[512]{0:T(512)S(1)} %copy-done.6, bf16[2,512,104]{1,2,0:T(8,128)(2,1)} %slice.126, ...), kind=kOutput, calls=%fused_computation.43 | convolution fusion | flops 112676864 | bytes 2639872 | tf_op jit(solution)/shard_map/hpk,khe->phe/dot_general | solution.py:121
  27.9 1.3 convolution_convert_fusion
  29.2 1.9 %collective-permute-start.2 = (bf16[8,104,512]{2,1,0:T(8,128)(2,1)}, bf16[8,104,512]{2,1,0:T(8,128)(2,1)}, u32[]{:S(2)}, u32[]{:S(2)}) collective-permute-start(bf16[8,104,512]{2,1,0:T(8,128)(2,1)} %convolution_convert_fusion), channel_id=1, source_target_pairs={{0,1},{1,0},{2,3},{3,2},{4,5},{5,4},{6,7},{7,6},{8,9},{9,8},{10,11... | collective-permute-start | bytes 2555912 | tf_op jit(solution)/shard_map/ppermute | solution.py:138
  31.3 1.2 copy.69
  32.8 1.0 collective-permute-done.2
  33.8 2.5 %add_convert_fusion.1 = bf16[8,104,512]{2,1,0:T(8,128)(2,1)} fusion(bf16[8,104,512]{2,1,0:T(8,128)(2,1)} %collective-permute-done.2, bf16[512,104,1]{0,1,2:T(8,128)(2,1)} %copy-done.5, bf16[104,8,1,104]{0,3,1,2:T(8,128)(2,1)S(1)} %copy.69), kind=kOutput, calls=%fused_computation.34 | convolution fusion | flops 90734592 | bytes 1983488 | tf_op jit(solution)/shard_map/pe,ezf->zfp/dot_general | solution.py:133
  36.3 10.3 %all-to-all-start = ((bf16[8,104,512]{2,1,0:T(8,128)(2,1)}), bf16[8,104,512]{2,1,0:T(8,128)(2,1)}, u32[]{:S(2)}, u32[]{:S(2)}) async-start(bf16[8,104,512]{2,1,0:T(8,128)(2,1)} %add_convert_fusion.1), calls=%async_computation | async-start | bytes 1703936 | tf_op jit(solution)/shard_map/all_to_all | solution.py:44
  47.0 1.5 fusion.27
  48.5 0.7 copy.59
  49.6 22.0 %all-to-all-done = bf16[8,104,512]{2,1,0:T(8,128)(2,1)} async-done(((bf16[8,104,512]{2,1,0:T(8,128)(2,1)}), bf16[8,104,512]{2,1,0:T(8,128)(2,1)}, u32[]{:S(2)}, u32[]{:S(2)}) %all-to-all-start) | async-done | bytes 852000 | tf_op jit(solution)/shard_map/all_to_all | solution.py:44
  71.5 1.3 convert_reduce_fusion.5
  73.0 1.5 fusion.16
  74.5 13.6 %all_to_all.37 = bf16[16,8,1024]{2,1,0:T(8,128)(2,1)S(1)} all-to-all(bf16[16,8,1024]{2,1,0:T(8,128)(2,1)S(1)} %fusion.16), channel_id=1, replica_groups=mesh['gx'=4,'gy'=8,'z'=8,'core'=2] {'z','core'}, dimensions={0} | all-to-all | bytes 524288 | tf_op jit(solution)/shard_map/all_to_all | solution.py:44
  88.2 0.7 broadcast_in_dim.68
  88.9 3.5 %all-to-all-start.2 = ((bf16[16,8,1024]{2,1,0:T(8,128)(2,1)}), bf16[16,8,1024]{2,1,0:T(8,128)(2,1)S(1)}, u32[]{:S(2)}, u32[]{:S(2)}) async-start(bf16[16,8,1024]{2,1,0:T(8,128)(2,1)} %broadcast_in_dim.68), calls=%async_computation.2 | async-start | bytes 524288 | tf_op jit(solution)/shard_map/all_to_all | solution.py:35
  92.5 11.2 %all-to-all-done.2 = bf16[16,8,1024]{2,1,0:T(8,128)(2,1)S(1)} async-done(((bf16[16,8,1024]{2,1,0:T(8,128)(2,1)}), bf16[16,8,1024]{2,1,0:T(8,128)(2,1)S(1)}, u32[]{:S(2)}, u32[]{:S(2)}) %all-to-all-start.2) | async-done | bytes 262176 | tf_op jit(solution)/shard_map/all_to_all | solution.py:35
  105.0 0.8 broadcast_in_dim.72
  105.8 6.2 %all-to-all-start.3 = ((bf16[8,128,128]{2,1,0:T(8,128)(2,1)}), bf16[8,128,128]{2,1,0:T(8,128)(2,1)S(1)}, u32[]{:S(2)}, u32[]{:S(2)}) async-start(bf16[8,128,128]{2,1,0:T(8,128)(2,1)} %broadcast_in_dim.72), calls=%async_computation.3 | async-start | bytes 524288 | tf_op jit(solution)/shard_map/all_to_all | solution.py:35
  112.4 14.5 %all-to-all-done.3 = bf16[8,128,128]{2,1,0:T(8,128)(2,1)S(1)} async-done(((bf16[8,128,128]{2,1,0:T(8,128)(2,1)}), bf16[8,128,128]{2,1,0:T(8,128)(2,1)S(1)}, u32[]{:S(2)}, u32[]{:S(2)}) %all-to-all-start.3) | async-done | bytes 262176 | tf_op jit(solution)/shard_map/all_to_all | solution.py:35
  126.9 1.1 broadcast_in_dim.74
  128.0 4.9 %all-to-all-start.4 = ((bf16[4,1024,128]{2,1,0:T(8,128)(2,1)}), bf16[4,1024,128]{2,1,0:T(8,128)(2,1)S(1)}, u32[]{:S(2)}, u32[]{:S(2)}) async-start(bf16[4,1024,128]{2,1,0:T(8,128)(2,1)} %broadcast_in_dim.74), calls=%async_computation.4 | async-start | bytes 2097152 | tf_op jit(solution)/shard_map/all_to_all | solution.py:35
  132.9 2.9 %all-gather.2.cloned.1.call-done = bf16[8448,128]{1,0:T(8,128)(2,1)} async-done(((bf16[264,128]{1,0:T(8,128)(2,1)}), bf16[8448,128]{1,0:T(8,128)(2,1)}) %all-gather.2.cloned.1.call-update) | async-done | bytes 2162704 | tf_op jit(solution)/shard_map/all_gather | solution.py:89
  135.9 0.8 slice.119
  136.8 0.8 convert_reduce_fusion.2
  139.8 2.7 %fusion.4 = (f32[128]{0:T(128)S(1)}, f32[128,8448]{1,0:T(8,128)S(1)}) fusion(s32[8448]{0:T(1024)S(1)} %fusion.74, s32[128]{0:T(128)S(1)} %get-tuple-element.50, bf16[8448,128]{1,0:T(8,128)(2,1)} %all-gather.2.cloned.1.call-done, bf16[3,128,64]{1,2,0:T(8,128)(2,1)S(1)} %convert_bitcast_fusion.4), kind=kOutput, calls=%fused_computation.16 | convolution fusion | flops 142737280 | bytes 6542336 | tf_op jit(solution)/shard_map/dot_general | solution.py:49
  142.6 1.2 convert_reduce_fusion.3
  144.2 2.1 %fusion = (f32[256]{0:T(256)S(1)}, f32[256,8448]{1,0:T(8,128)S(1)}) fusion(s32[8448]{0:T(1024)S(1)} %fusion.74, s32[256]{0:T(256)S(1)} %add_add_fusion, bf16[8448,128]{1,0:T(8,128)(2,1)S(1)} %copy-done.1, bf16[3,256,64]{1,2,0:T(8,128)(2,1)S(1)} %convert_bitcast_fusion.3), kind=kOutput, calls=%fused_computation.4 | convolution fusion | flops 285474560 | bytes 10885120 | tf_op jit(solution)/shard_map/dot_general | solution.py:49
  146.3 2.7 %convert_reduce_fusion = (f32[256]{0:T(256)S(1)}, bf16[256,8448]{1,0:T(8,128)(2,1)S(1)}) fusion(f32[256,8448]{1,0:T(8,128)S(1)} %get-tuple-element.61, f32[256]{0:T(256)S(1)} %get-tuple-element.60, s32[256]{0:T(256)S(1)} %add_add_fusion, s32[8448]{0:T(1024)S(1)} %fusion.74), kind=kLoop, calls=%fused_computation.6 | loop fusion | flops 12975872 | bytes 13012992 | tf_op jit(solution)/shard_map/reduce_sum | solution.py:52
  149.0 2.0 %fusion.7 = f32[128,64]{0,1:T(8,128)S(1)} fusion(bf16[128,8448]{1,0:T(8,128)(2,1)S(1)} %get-tuple-element.31, bf16[8448,128]{1,0:T(8,128)(2,1)S(1)} %copy-done.1), kind=kOutput, calls=%fused_computation.27 | convolution fusion | flops 138412032 | bytes 4358144 | tf_op jit(solution)/shard_map/dot_general | solution.py:53
  151.0 2.5 %fusion.9 = f32[256,64]{0,1:T(8,128)S(1)} fusion(bf16[256,8448]{1,0:T(8,128)(2,1)S(1)} %get-tuple-element.29, bf16[8448,128]{1,0:T(8,128)(2,1)S(1)} %copy-done.1), kind=kOutput, calls=%fused_computation.29 | convolution fusion | flops 276824064 | bytes 6553600 | tf_op jit(solution)/shard_map/dot_general | solution.py:53
  153.4 1.6 fusion.2
  155.0 1.5 convert_reduce_fusion.1
  156.5 1.5 fusion.21
  158.3 0.7 reshape.452
  159.1 7.5 %all-to-all-start.5 = ((bf16[32,2,256]{2,1,0:T(2,128)(2,1)}), bf16[32,2,256]{2,1,0:T(2,128)(2,1)S(1)}, u32[]{:S(2)}, u32[]{:S(2)}) async-start(bf16[32,2,256]{2,1,0:T(2,128)(2,1)} %reshape.452), calls=%async_computation.5 | async-start | bytes 65536 | tf_op jit(solution)/shard_map/all_to_all | solution.py:198
  166.8 7.8 %all-to-all-done.5 = bf16[32,2,256]{2,1,0:T(2,128)(2,1)S(1)} async-done(((bf16[32,2,256]{2,1,0:T(2,128)(2,1)}), bf16[32,2,256]{2,1,0:T(2,128)(2,1)S(1)}, u32[]{:S(2)}, u32[]{:S(2)}) %all-to-all-start.5) | async-done | bytes 32800 | tf_op jit(solution)/shard_map/all_to_all | solution.py:198
  174.9 0.8 fusion.20
  (96 shorter events, 7.3 us)
Async XLA Ops:
  6.5 6.3 %copy-start = (bf16[3,1664,104]{1,2,0:T(8,128)(2,1)S(1)}, bf16[3,1664,104]{1,2,0:T(8,128)(2,1)}, u32[]{:S(2)}) copy-start(bf16[3,1664,104]{1,2,0:T(8,128)(2,1)} %param.18) | copy-start | bytes 3115012
  6.5 5.6 %copy-start.2 = (bf16[512,1664]{1,0:T(8,128)(2,1)S(1)}, bf16[512,1664]{1,0:T(8,128)(2,1)}, u32[]{:S(2)}) copy-start(bf16[512,1664]{1,0:T(8,128)(2,1)} %param.14) | copy-start | bytes 5111812
  6.5 6.3 %copy-start.9 = (f32[1664]{0:T(1024)S(1)}, f32[1664]{0:T(1024)}, u32[]{:S(2)}) copy-start(f32[1664]{0:T(1024)} %param.17) | copy-start | bytes 19972
  6.5 6.3 %copy-start.10 = (f32[1664]{0:T(1024)S(1)}, f32[1664]{0:T(1024)}, u32[]{:S(2)}) copy-start(f32[1664]{0:T(1024)} %param.16) | copy-start | bytes 19972
  6.5 16.1 %collective-permute-start.1 = (s32[512]{0:T(512)}, s32[512]{0:T(512)S(1)}, u32[]{:S(2)}, u32[]{:S(2)}) collective-permute-start(s32[512]{0:T(512)} %param.15), channel_id=1, source_target_pairs={{0,16},{16,0},{32,48},{48,32},{64,80},{80,64},{96,112},{112,96},{1... | collective-permute-start | bytes 6152 | tf_op jit(solution)/shard_map/ppermute | solution.py:109
  14.1 8.6 %copy-start.6 = (s32[512]{0:T(512)S(1)}, s32[512]{0:T(512)}, u32[]{:S(2)}) copy-start(s32[512]{0:T(512)} %param.15) | copy-start | bytes 6148
  14.8 8.9 %collective-permute-start = (bf16[2,512,104]{1,2,0:T(8,128)(2,1)}, bf16[2,512,104]{1,2,0:T(8,128)(2,1)}, u32[]{:S(2)}, u32[]{:S(2)}) collective-permute-start(bf16[2,512,104]{1,2,0:T(8,128)(2,1)} %slice.126), channel_id=1, source_target_pairs={{0,16},{16,0},{32,48},{48,32},{64,80},{80,64},{96,112},{112,96},{1... | collective-permute-start | bytes 638984 | tf_op jit(solution)/shard_map/ppermute | solution.py:109
  26.0 1.9 %copy-start.4 = (bf16[104,8,1,104]{0,3,1,2:T(8,128)(2,1)S(1)}, bf16[104,8,1,104]{0,3,1,2:T(8,128)(2,1)}, u32[]{:S(2)}) copy-start(bf16[104,8,1,104]{0,3,1,2:T(8,128)(2,1)} %copy.70) | copy-start | bytes 519172
  26.0 5.1 %copy-start.7 = (s32[128]{0:T(128)S(1)}, s32[128]{0:T(128)}, u32[]{:S(2)}) copy-start(s32[128]{0:T(128)} %param.21) | copy-start | bytes 1540
  26.0 6.5 %copy-start.3 = (bf16[256,1024]{1,0:T(8,128)(2,1)S(1)}, bf16[256,1024]{1,0:T(8,128)(2,1)}, u32[]{:S(2)}) copy-start(bf16[256,1024]{1,0:T(8,128)(2,1)} %param.22) | copy-start | bytes 1572868
  27.9 1.3 copy-start.5
  29.2 4.6 %collective-permute-start.2 = (bf16[8,104,512]{2,1,0:T(8,128)(2,1)}, bf16[8,104,512]{2,1,0:T(8,128)(2,1)}, u32[]{:S(2)}, u32[]{:S(2)}) collective-permute-start(bf16[8,104,512]{2,1,0:T(8,128)(2,1)} %convolution_convert_fusion), channel_id=1, source_target_pairs={{0,1},{1,0},{2,3},{3,2},{4,5},{5,4},{6,7},{7,6},{8,9},{9,8},{10,11... | collective-permute-start | bytes 2555912 | tf_op jit(solution)/shard_map/ppermute | solution.py:138
  32.5 14.4 %copy-start.11 = (f32[1024]{0:T(1024)S(1)}, f32[1024]{0:T(1024)}, u32[]{:S(2)}) copy-start(f32[1024]{0:T(1024)} %param.24) | copy-start | bytes 12292
  32.5 14.4 %copy-start.12 = (f32[1024]{0:T(1024)S(1)}, f32[1024]{0:T(1024)}, u32[]{:S(2)}) copy-start(f32[1024]{0:T(1024)} %param.23) | copy-start | bytes 12292
  36.3 35.3 %all-to-all-start = ((bf16[8,104,512]{2,1,0:T(8,128)(2,1)}), bf16[8,104,512]{2,1,0:T(8,128)(2,1)}, u32[]{:S(2)}, u32[]{:S(2)}) async-start(bf16[8,104,512]{2,1,0:T(8,128)(2,1)} %add_convert_fusion.1), calls=%async_computation | async-start | bytes 1703936 | tf_op jit(solution)/shard_map/all_to_all | solution.py:44
  46.6 89.3 %all-gather.2.cloned.1.call-start = ((), (), s32[]{:S(2)}) async-start(), calls=%async_computation.6 | async-start | bytes 2230272 | tf_op jit(solution)/shard_map/all_gather | solution.py:89
  49.3 55.2 %copy-start.8 = (bf16[3,1024,64]{1,2,0:T(8,128)(2,1)S(1)}, bf16[3,1024,64]{1,2,0:T(8,128)(2,1)}, u32[]{:S(2)}) copy-start(bf16[3,1024,64]{1,2,0:T(8,128)(2,1)} %param.25) | copy-start | bytes 1179652
  88.9 14.9 %all-to-all-start.2 = ((bf16[16,8,1024]{2,1,0:T(8,128)(2,1)}), bf16[16,8,1024]{2,1,0:T(8,128)(2,1)S(1)}, u32[]{:S(2)}, u32[]{:S(2)}) async-start(bf16[16,8,1024]{2,1,0:T(8,128)(2,1)} %broadcast_in_dim.68), calls=%async_computation.2 | async-start | bytes 524288 | tf_op jit(solution)/shard_map/all_to_all | solution.py:35
  105.8 21.1 %all-to-all-start.3 = ((bf16[8,128,128]{2,1,0:T(8,128)(2,1)}), bf16[8,128,128]{2,1,0:T(8,128)(2,1)S(1)}, u32[]{:S(2)}, u32[]{:S(2)}) async-start(bf16[8,128,128]{2,1,0:T(8,128)(2,1)} %broadcast_in_dim.72), calls=%async_computation.3 | async-start | bytes 524288 | tf_op jit(solution)/shard_map/all_to_all | solution.py:35
  128.0 25.4 %all-to-all-start.4 = ((bf16[4,1024,128]{2,1,0:T(8,128)(2,1)}), bf16[4,1024,128]{2,1,0:T(8,128)(2,1)S(1)}, u32[]{:S(2)}, u32[]{:S(2)}) async-start(bf16[4,1024,128]{2,1,0:T(8,128)(2,1)} %broadcast_in_dim.74), calls=%async_computation.4 | async-start | bytes 2097152 | tf_op jit(solution)/shard_map/all_to_all | solution.py:35
  142.6 1.6 copy-start.1
  159.1 15.5 %all-to-all-start.5 = ((bf16[32,2,256]{2,1,0:T(2,128)(2,1)}), bf16[32,2,256]{2,1,0:T(2,128)(2,1)S(1)}, u32[]{:S(2)}, u32[]{:S(2)}) async-start(bf16[32,2,256]{2,1,0:T(2,128)(2,1)} %reshape.452), calls=%async_computation.5 | async-start | bytes 65536 | tf_op jit(solution)/shard_map/all_to_all | solution.py:198
Sparse Core Ops, SparseCore 0:
  50.6 85.2 all-gather.1
